TPU v7x, 32 devices: a whole 2x2x4 slice. The times are simulated.
32 devices in a mesh: grp: 2 (over x), lat: 16 (over z, y, core).
Axes of the slice: x: 2, y: 2, z: 4, core: 2. Of those that a mesh axis runs over, the one named last changes fastest.
Arguments:
- activations: bfloat16 [64, 1440, 384], P(('grp', 'lat')), parts along dimension 0, may hold values from -6 to 6
- upstream: bfloat16 [64, 1440, 384], P(('grp', 'lat')), parts along dimension 0, may hold values from -6 to 6
- skip_weight: bfloat16 [384, 384], replicated, may hold values from -0.3125 to 0.3125
- spectral_weight: bfloat16 [32, 2, 384, 384], P('lat'), may hold values from -2.5 to 2.5
- slot_degree: int32 [32], replicated, may hold values from 0 to 31, each once
Outputs:
- grad_activations: bfloat16 [64, 1440, 384], P(('grp', 'lat')), parts along dimension 0
- grad_spectral: bfloat16 [64, 2, 384, 384], P(('grp', 'lat')), parts along dimension 0
- grad_skip: float32 [768, 384], P(('grp', 'lat')), parts along dimension 0
There are 2 independent parts, one for each index of `grp`. A program takes and returns all parts, laid end to end along the dimension named above; an argument that names none is the same for every part. Nothing has to cross between parts.
Inputs may be any that keep to these rules, and one draw needn't show every extreme that they name: `slot_degree`: device d holds slots d * 2 to (d + 1) * 2 - 1 of spectral_weight and grad_spectral; every degree appears in exactly one slot.
All inputs are finite; a program needn't handle non-finite values.
Results may differ from a plain program's by a relative error of at most 0.013.
Values may be sent and summed in bfloat16 or wider, within the bound.
No kernel may reach another device: no remote copies, remote signals or barrier semaphores. Data moves between devices by JAX's collectives and lax.ppermute only.
A program may use at most 64 MiB of HBM per device.

v0:
```python
import math

import jax
import jax.numpy as jnp
from jax import lax
from jax.sharding import PartitionSpec as P

ORDERS = 4


highest = lax.Precision.HIGHEST


def fourier_table(lon_total, orders):
    lon_ids = jnp.arange(lon_total, dtype=jnp.int32)[:, None]
    order_ids = jnp.arange(orders, dtype=jnp.int32)[None, :]
    angles = (lon_ids * order_ids % lon_total).astype(jnp.float32) * (2.0 * math.pi / lon_total)
    amplitude = math.sqrt(2.0 / lon_total)
    return jnp.concatenate(
        [amplitude * jnp.cos(angles), -amplitude * jnp.sin(angles)], axis=1
    ).astype(jnp.bfloat16)


def colatitudes(row_ids, lat_total):
    mirror = jnp.minimum(row_ids, lat_total - 1 - row_ids)
    colatitude = (mirror.astype(jnp.float32) + 0.5) * (math.pi / lat_total)
    cosines = jnp.where(row_ids < lat_total // 2, jnp.cos(colatitude), -jnp.cos(colatitude))
    return (cosines, jnp.sin(colatitude))


def legendre_table(cosines, sines, degrees, orders):
    order_col = jnp.arange(orders, dtype=jnp.float32)[:, None]
    factors = [math.sqrt(0.5)]
    for order_num in range(1, orders):
        factors.append(factors[-1] * math.sqrt((2.0 * order_num + 1.0) / (2.0 * order_num)))
    diagonal_start = jnp.array(factors, dtype=jnp.float32)[:, None] * jnp.power(
        sines[None, :], order_col
    )
    next_start = jnp.sqrt(2.0 * order_col + 3.0) * cosines[None, :] * diagonal_start

    def advance(state_pair, degree):
        previous, earlier = state_pair
        deg_value = degree.astype(jnp.float32)
        deg_below = deg_value - 1.0
        ratio_up = jnp.sqrt(
            jnp.maximum(4.0 * deg_value * deg_value - 1.0, 1.0)
            / jnp.maximum(deg_value * deg_value - order_col * order_col, 1.0)
        )
        ratio_down = jnp.sqrt(
            jnp.maximum(deg_below * deg_below - order_col * order_col, 0.0)
            / jnp.maximum(4.0 * deg_below * deg_below - 1.0, 1.0)
        )
        recurred = ratio_up * (cosines[None, :] * previous - ratio_down * earlier)
        current = jnp.where(
            deg_value == order_col,
            diagonal_start,
            jnp.where(
                deg_value == order_col + 1.0,
                next_start,
                jnp.where(deg_value > order_col + 1.0, recurred, 0.0),
            ),
        )
        return ((current, previous), current)

    zeroed = jnp.zeros((orders, cosines.shape[0]), jnp.float32)
    _, stacked = lax.scan(advance, (zeroed, zeroed), jnp.arange(degrees, dtype=jnp.int32))
    return jnp.concatenate([stacked, stacked], axis=1)


def gelu_tanh(values):
    return jax.nn.gelu(values, approximate=True)


def complex_apply(coeffs, weights, orders):
    real_in, imag_in = (coeffs[:, :orders], coeffs[:, orders:])
    real_w, imag_w = (weights[:, 0], weights[:, 1])

    def complex_term(operand_a, operand_b):
        return jnp.einsum("smc,scd->smd", operand_a, operand_b, preferred_element_type=jnp.float32)

    real_out = complex_term(real_in, real_w) - complex_term(imag_in, imag_w)
    imag_out = complex_term(real_in, imag_w) + complex_term(imag_in, real_w)
    return jnp.concatenate([real_out, imag_out], axis=1)


def complex_adjoint(coeffs, cotangents, weights, orders):
    real_in, imag_in = (coeffs[:, :orders], coeffs[:, orders:])
    real_g, imag_g = (cotangents[:, :orders], cotangents[:, orders:])
    real_w, imag_w = (weights[:, 0], weights[:, 1])

    def outer_sum(operand_a, operand_b):
        return jnp.einsum("smc,smd->scd", operand_a, operand_b, preferred_element_type=jnp.float32)

    def back_term(operand_a, operand_b):
        return jnp.einsum("smd,scd->smc", operand_a, operand_b, preferred_element_type=jnp.float32)

    grad_real = outer_sum(real_in, real_g) + outer_sum(imag_in, imag_g)
    grad_imag = outer_sum(real_in, imag_g) - outer_sum(imag_in, real_g)
    back_real = back_term(real_g, real_w) + back_term(imag_g, imag_w)
    back_imag = back_term(imag_g, real_w) - back_term(real_g, imag_w)
    return (
        jnp.stack([grad_real, grad_imag], axis=1),
        jnp.concatenate([back_real, back_imag], axis=1),
    )


def local(activations, upstream, skip_weight, spectral_weight, slot_degree):
    groups = lax.axis_size("lat")
    lat_rows = activations.shape[0]
    lon_total = activations.shape[1]
    lat_total = lat_rows * groups
    per_owner = spectral_weight.shape[0]
    degrees = per_owner * groups
    orders = ORDERS
    fourier = fourier_table(lon_total, orders)
    spectrum = jnp.einsum("jkc,kf->jfc", activations, fourier, preferred_element_type=jnp.float32)
    all_rows = jnp.arange(lat_total, dtype=jnp.int32)
    cos_all, sin_all = colatitudes(all_rows, lat_total)
    slot_plm = jnp.take(legendre_table(cos_all, sin_all, degrees, orders), slot_degree, axis=0)
    slot_quad = slot_plm * (math.pi / lat_total * sin_all)[None, None, :]

    def to_channels(values):
        return lax.all_to_all(values, "lat", split_axis=2, concat_axis=0, tiled=True)

    def to_owners(values):
        return lax.all_to_all(values, "lat", split_axis=0, concat_axis=2, tiled=True)

    def from_owners(values):
        return lax.all_to_all(values, "lat", split_axis=2, concat_axis=0, tiled=True)

    def to_rows(values):
        return lax.all_to_all(values, "lat", split_axis=0, concat_axis=2, tiled=True)

    by_channel = to_channels(spectrum)
    coeffs = to_owners(
        jnp.einsum("sfj,jfc->sfc", slot_quad, by_channel, precision=highest).astype(jnp.bfloat16)
    )
    filtered = complex_apply(coeffs, spectral_weight, orders).astype(jnp.bfloat16)
    spread = from_owners(filtered).astype(jnp.float32)
    grid_modes = to_rows(
        jnp.einsum("sfj,sfc->jfc", slot_plm, spread, precision=highest).astype(jnp.bfloat16)
    )
    spatial = jnp.einsum("jfc,kf->jkc", grid_modes, fourier, preferred_element_type=jnp.float32)
    skip_out = jnp.einsum(
        "jkc,cd->jkd", activations, skip_weight, preferred_element_type=jnp.float32
    )
    _, pullback = jax.vjp(gelu_tanh, spatial + skip_out)
    slope_b = pullback(upstream.astype(jnp.float32))[0].astype(jnp.bfloat16)
    grad_skip = lax.psum_scatter(
        jnp.einsum("jkc,jkd->cd", activations, slope_b, preferred_element_type=jnp.float32),
        "lat",
        scatter_dimension=0,
        tiled=True,
    ) * (1.0 / math.sqrt(lat_total * lon_total))
    through_skip = jnp.einsum(
        "jkd,cd->jkc", slope_b, skip_weight, preferred_element_type=jnp.float32
    )
    mode_grads = jnp.einsum("jkc,kf->jfc", slope_b, fourier, preferred_element_type=jnp.float32)
    grads_by_channel = to_channels(mode_grads)
    coeff_grads = to_owners(
        jnp.einsum("sfj,jfc->sfc", slot_plm, grads_by_channel, precision=highest).astype(
            jnp.bfloat16
        )
    )
    weight_grads, back_coeffs = complex_adjoint(coeffs, coeff_grads, spectral_weight, orders)
    back_b = back_coeffs.astype(jnp.bfloat16)
    back_spread = from_owners(back_b).astype(jnp.float32)
    row_grads = to_rows(
        jnp.einsum("sfj,sfc->jfc", slot_quad, back_spread, precision=highest).astype(jnp.bfloat16)
    )
    through_modes = jnp.einsum(
        "jfc,kf->jkc", row_grads, fourier, preferred_element_type=jnp.float32
    )
    grad_activations = (upstream.astype(jnp.float32) + through_skip + through_modes).astype(
        jnp.bfloat16
    )
    return (grad_activations, weight_grads.astype(jnp.bfloat16), grad_skip)


def solution(mesh):
    in_specs = (
        P(("grp", "lat"), None, None),
        P(("grp", "lat"), None, None),
        P(),
        P("lat", None, None, None),
        P(),
    )
    out_specs = (
        P(("grp", "lat"), None, None),
        P(("grp", "lat"), None, None, None),
        P(("grp", "lat"), None),
    )
    return jax.shard_map(local, mesh=mesh, in_specs=in_specs, out_specs=out_specs, check_vma=False)
```

profile of v0, /device:TPU:0, one launch (start us, length us, event | category | flops | bytes accessed | tf_op | source)
XLA Modules:
  0.0 300.9 jit_solution(992449923088837298)
XLA Ops:
  10.1 2.2 reshape.143
  12.3 7.4 %all-to-all-start = ((f32[16,1,384]{2,1,0:T(1,128)}), f32[16,1,384]{2,1,0:T(1,128)}, u32[]{:S(2)}, u32[]{:S(2)}) async-start(f32[16,1,384]{2,1,0:T(1,128)} %reshape.143), calls=%async_computation | async-start | bytes 49152 | tf_op jit(solution)/shard_map/all_to_all | solution.py:123
  20.0 67.6 %while.21 = (s32[]{:T(128)}, f32[4,32]{1,0:T(4,128)S(1)}, f32[4,32]{1,0:T(4,128)S(1)}, f32[32,4,32]{2,1,0:T(4,128)}, s32[32]{0:T(128)S(1)}, /*index=5*/f32[32]{0...) while((s32[]{:T(128)}, f32[4,32]{1,0:T(4,128)S(1)}, ...), condition=%wide.region_1.2_spmd.clone.clone.clone.clone, body=%wide.region_0.1_spmd.clone.clone.clone.clone.sunk | while | flops 1723 | bytes 5059 | solution.py:66
  91.9 2.0 reduce
  93.9 2.1 reshape.144
  96.0 1.8 copy.50
  97.8 1.9 fusion.43
  102.8 12.4 %all_to_all.144 = bf16[16,2,192]{2,1,0:T(2,128)(2,1)} all-to-all(bf16[16,2,192]{2,1,0:T(2,128)(2,1)} %reshape.145), channel_id=1, replica_groups=mesh['grp'=2,'lat'=16] {'lat'}, dimensions={0} | all-to-all | bytes 24576 | tf_op jit(solution)/shard_map/all_to_all | solution.py:126
  122.1 1.8 reshape.147
  123.9 10.5 %all_to_all.145 = bf16[16,2,192]{2,1,0:T(2,128)(2,1)} all-to-all(bf16[16,2,192]{2,1,0:T(2,128)(2,1)} %reshape.147), channel_id=1, replica_groups=mesh['grp'=2,'lat'=16] {'lat'}, dimensions={0} | all-to-all | bytes 24576 | tf_op jit(solution)/shard_map/all_to_all | solution.py:129
  135.9 1.7 copy.58
  137.6 1.8 fusion.44
  142.6 10.5 %all_to_all.146 = bf16[16,2,192]{2,1,0:T(2,128)(2,1)} all-to-all(bf16[16,2,192]{2,1,0:T(2,128)(2,1)} %reshape.149), channel_id=1, replica_groups=mesh['grp'=2,'lat'=16] {'lat'}, dimensions={0} | all-to-all | bytes 24576 | tf_op jit(solution)/shard_map/all_to_all | solution.py:132
  159.2 4.4 %fusion.33 = bf16[2,1440,384]{2,1,0:T(8,128)(2,1)S(1)} fusion(bf16[2,1440,384]{2,1,0:T(8,128)(2,1)S(1)} %copy-done.5, f32[1440,2,384]{2,0,1:T(8,128)S(1)} %fusion.109, bf16[2,1440,384]{2,1,0:T(8,128)(2,1)S(1)} %copy-done, bf16[384,384]{1,0:T(8,128)(2,1)S(1)} %copy-done.12), kind=kOutput, calls=%fused_computation.45 | convolution fusion | flops 873676800 | bytes 11354112 | tf_op jit(solution)/shard_map/jkc,cd->jkd/dot_general | solution.py:144
  167.7 2.2 reshape.151
  169.9 4.1 %all-to-all-start.4 = ((f32[16,1,384]{2,1,0:T(1,128)}), f32[16,1,384]{2,1,0:T(1,128)}, u32[]{:S(2)}, u32[]{:S(2)}) async-start(f32[16,1,384]{2,1,0:T(1,128)} %reshape.151), calls=%async_computation.4 | async-start | bytes 49152 | tf_op jit(solution)/shard_map/all_to_all | solution.py:123
  175.3 5.3 %all-to-all-done.4 = f32[16,1,384]{2,1,0:T(1,128)} async-done(((f32[16,1,384]{2,1,0:T(1,128)}), f32[16,1,384]{2,1,0:T(1,128)}, u32[]{:S(2)}, u32[]{:S(2)}) %all-to-all-start.4) | async-done | bytes 24608 | tf_op jit(solution)/shard_map/all_to_all | solution.py:123
  180.6 2.0 reduce.1
  182.6 2.1 reshape.152
  184.7 1.8 copy.64
  186.5 2.0 fusion.45
  191.6 3.5 %all-to-all-start.5 = ((bf16[16,2,192]{2,1,0:T(2,128)(2,1)}), bf16[16,2,192]{2,1,0:T(2,128)(2,1)S(1)}, u32[]{:S(2)}, u32[]{:S(2)}) async-start(bf16[16,2,192]{2,1,0:T(2,128)(2,1)} %reshape.153), calls=%async_computation.5 | async-start | bytes 32768 | tf_op jit(solution)/shard_map/all_to_all | solution.py:126
  195.3 3.8 %convolution_bitcast_fusion = f32[384,384]{0,1:T(8,128)} fusion(bf16[2,1440,384]{2,1,0:T(8,128)(2,1)} %copy-done.1, bf16[2,1440,384]{2,1,0:T(8,128)(2,1)S(1)} %copy-done), kind=kOutput, calls=%fused_computation.56 | convolution fusion | flops 849346560 | bytes 5013504 | tf_op jit(solution)/shard_map/jkc,jkd->cd/dot_general | solution.py:150
  199.2 2.4 all-to-all-done.5
  210.8 1.8 reshape.155
  212.6 4.1 %all-to-all-start.6 = ((bf16[16,2,192]{2,1,0:T(2,128)(2,1)}), bf16[16,2,192]{2,1,0:T(2,128)(2,1)}, u32[]{:S(2)}, u32[]{:S(2)}) async-start(bf16[16,2,192]{2,1,0:T(2,128)(2,1)} %reshape.155), calls=%async_computation.6 | async-start | bytes 32768 | tf_op jit(solution)/shard_map/all_to_all | solution.py:129
  216.6 2.5 fusion.41
  220.3 2.9 all-to-all-done.6
  225.4 3.5 %all-to-all-start.7 = ((bf16[16,2,192]{2,1,0:T(2,128)(2,1)}), bf16[16,2,192]{2,1,0:T(2,128)(2,1)S(1)}, u32[]{:S(2)}, u32[]{:S(2)}) async-start(bf16[16,2,192]{2,1,0:T(2,128)(2,1)} %reshape.157), calls=%async_computation.7 | async-start | bytes 32768 | tf_op jit(solution)/shard_map/all_to_all | solution.py:132
  231.5 3.9 %all-to-all-done.7 = bf16[16,2,192]{2,1,0:T(2,128)(2,1)S(1)} async-done(((bf16[16,2,192]{2,1,0:T(2,128)(2,1)}), bf16[16,2,192]{2,1,0:T(2,128)(2,1)S(1)}, u32[]{:S(2)}, u32[]{:S(2)}) %all-to-all-start.7) | async-done | bytes 12320 | tf_op jit(solution)/shard_map/all_to_all | solution.py:132
  238.0 3.9 %fusion.38 = bf16[2,1440,384]{2,1,0:T(8,128)(2,1)} fusion(bf16[2,1440,384]{2,1,0:T(8,128)(2,1)S(1)} %copy-done.6, f32[1440,2,384]{2,0,1:T(8,128)S(1)} %fusion.108, bf16[2,1440,384]{2,1,0:T(8,128)(2,1)S(1)} %copy-done.2, bf16[384,384]{1,0:T(8,128)(2,1)} %param.10), kind=kOutput, calls=%fused_computation.50 | convolution fusion | flops 853770240 | bytes 11354112 | tf_op jit(solution)/shard_map/jkd,cd->jkc/dot_general | solution.py:155
  241.9 50.3 %all-reduce.3.cloned.1.call-done = f32[384,384]{0,1:T(8,128)} async-done(((f32[384,384]{0,1:T(8,128)}), f32[384,384]{0,1:T(8,128)}) %all-reduce.3.cloned.1.call-update) | async-done | bytes 589840
  (292 shorter events, 100.5 us)
Async XLA Ops:
  7.2 1.7 copy-start
  7.2 12.8 %copy-start.13 = (f32[4]{0:T(128)S(1)}, f32[4]{0:T(128)}, u32[]{:S(2)}) copy-start(f32[4]{0:T(128)} %constant.106.clone) | copy-start | bytes 52
  7.2 12.7 %copy-start.14 = (s32[32]{0:T(128)S(1)}, s32[32]{0:T(128)}, u32[]{:S(2)}) copy-start(s32[32]{0:T(128)} %param.12) | copy-start | bytes 388
  7.4 0.6 copy-start.9
  7.4 156.2 %copy-start.7 = (bf16[1440,4]{0,1:T(4,128)(2,1)}, bf16[1440,4]{0,1:T(4,128)(2,1)S(1)}, u32[]{:S(2)}) copy-start(bf16[1440,4]{0,1:T(4,128)(2,1)S(1)} %get-tuple-element.333) | copy-start | bytes 34564
  9.2 109.9 %copy-start.3 = (bf16[2,2,384,384]{3,2,1,0:T(8,128)(2,1)S(1)}, bf16[2,2,384,384]{3,2,1,0:T(8,128)(2,1)}, u32[]{:S(2)}) copy-start(bf16[2,2,384,384]{3,2,1,0:T(8,128)(2,1)} %param.11) | copy-start | bytes 3538948
  12.3 79.1 %all-to-all-start = ((f32[16,1,384]{2,1,0:T(1,128)}), f32[16,1,384]{2,1,0:T(1,128)}, u32[]{:S(2)}, u32[]{:S(2)}) async-start(f32[16,1,384]{2,1,0:T(1,128)} %reshape.143), calls=%async_computation | async-start | bytes 49152 | tf_op jit(solution)/shard_map/all_to_all | solution.py:123
  157.6 1.7 copy-start.5
  157.6 1.7 copy-start.12
  159.2 5.8 %copy-start.10 = (bf16[1440,4]{0,1:T(4,128)(2,1)S(1)}, bf16[1440,4]{0,1:T(4,128)(2,1)}, u32[]{:S(2)}) copy-start(bf16[1440,4]{0,1:T(4,128)(2,1)} %copy-done.9) | copy-start | bytes 34564
  163.7 1.4 copy-start.1
  165.0 9.0 %copy-start.15 = (u32[32]{0:T(128)S(1)}, u32[32]{0:T(128)}, u32[]{:S(2)}) copy-start(u32[32]{0:T(128)} %constant.112) | copy-start | bytes 388
  169.9 10.7 %all-to-all-start.4 = ((f32[16,1,384]{2,1,0:T(1,128)}), f32[16,1,384]{2,1,0:T(1,128)}, u32[]{:S(2)}, u32[]{:S(2)}) async-start(f32[16,1,384]{2,1,0:T(1,128)} %reshape.151), calls=%async_computation.4 | async-start | bytes 49152 | tf_op jit(solution)/shard_map/all_to_all | solution.py:123
  191.6 10.0 %all-to-all-start.5 = ((bf16[16,2,192]{2,1,0:T(2,128)(2,1)}), bf16[16,2,192]{2,1,0:T(2,128)(2,1)S(1)}, u32[]{:S(2)}, u32[]{:S(2)}) async-start(bf16[16,2,192]{2,1,0:T(2,128)(2,1)} %reshape.153), calls=%async_computation.5 | async-start | bytes 32768 | tf_op jit(solution)/shard_map/all_to_all | solution.py:126
  195.1 97.1 %all-reduce.3.cloned.1.call-start = ((), (), s32[]{:S(2)}) async-start(), calls=%async_computation.8 | async-start | bytes 1179648
  208.6 10.5 %copy-start.4 = (f32[2,384,384]{2,1,0:T(8,128)S(1)}, f32[2,384,384]{2,1,0:T(8,128)}, u32[]{:S(2)}) copy-start(f32[2,384,384]{2,1,0:T(8,128)} %fusion.92) | copy-start | bytes 3538948
  212.6 10.6 %all-to-all-start.6 = ((bf16[16,2,192]{2,1,0:T(2,128)(2,1)}), bf16[16,2,192]{2,1,0:T(2,128)(2,1)}, u32[]{:S(2)}, u32[]{:S(2)}) async-start(bf16[16,2,192]{2,1,0:T(2,128)(2,1)} %reshape.155), calls=%async_computation.6 | async-start | bytes 32768 | tf_op jit(solution)/shard_map/all_to_all | solution.py:129
  225.4 10.0 %all-to-all-start.7 = ((bf16[16,2,192]{2,1,0:T(2,128)(2,1)}), bf16[16,2,192]{2,1,0:T(2,128)(2,1)S(1)}, u32[]{:S(2)}, u32[]{:S(2)}) async-start(bf16[16,2,192]{2,1,0:T(2,128)(2,1)} %reshape.157), calls=%async_computation.7 | async-start | bytes 32768 | tf_op jit(solution)/shard_map/all_to_all | solution.py:132
  228.9 6.7 %copy-start.8 = (bf16[1440,4]{0,1:T(4,128)(2,1)S(1)}, bf16[1440,4]{0,1:T(4,128)(2,1)}, u32[]{:S(2)}) copy-start(bf16[1440,4]{0,1:T(4,128)(2,1)} %copy-done.7) | copy-start | bytes 34564
  228.9 6.7 %copy-start.11 = (bf16[1440,4]{0,1:T(4,128)(2,1)S(1)}, bf16[1440,4]{0,1:T(4,128)(2,1)}, u32[]{:S(2)}) copy-start(bf16[1440,4]{0,1:T(4,128)(2,1)} %copy-done.9) | copy-start | bytes 34564
  235.7 1.6 copy-start.2
  235.7 2.3 copy-start.6
Sparse Core Ops, SparseCore 0:
  199.3 92.8 all-reduce.2
where the time goes:
time: 303 us; the launch traced here: 301 us
  local copies, waits for them, and re-layouts  76.7 us (25%)
  waiting for transfers between devices  64.8 us (21%)
  other arithmetic  34.8 us (11%)
  blocking collectives  33.4 us (11%)
  matrix products  30.5 us (10%)
  starting transfers between devices  22.9 us (8%)
  loops' own time  22.8 us (8%)
  between operations  15 us (5%)
    unnamed x2, waiting for transfers between devices  50.3 us
    unnamed x51, local copies, waits for them, and re-layouts  30.5 us
    another operation x1, loops' own time, legendre_table(): lax.scan(advance, (zeroed, zeroed), jnp.arange(degrees, dtype=jnp.int32))  22.8 us
    dynamic_update_slice x32, other arithmetic, legendre_table(): lax.scan(advance, (zeroed, zeroed), jnp.arange(degrees, dtype=jnp.int32))  21.2 us
    dynamic_slice x32, local copies, waits for them, and re-layouts, legendre_table(): lax.scan(advance, (zeroed, zeroed), jnp.arange(degrees, dtype=jnp.int32))  20.7 us
    all_to_all x1, blocking collectives, to_owners(): lax.all_to_all(values, 'lat', split_axis=0, concat_axis=2, tiled=True)  12.4 us
    all_to_all x2, starting transfers between devices, to_channels(): lax.all_to_all(values, 'lat', split_axis=2, concat_axis=0, tiled=True)  11.6 us
    all_to_all x1, blocking collectives, from_owners(): lax.all_to_all(values, 'lat', split_axis=2, concat_axis=0, tiled=True)  10.5 us
  transfers between devices with their start and end apart: 6, of which 5 were waited for; matrix products, arithmetic and copies ran while one was open for 25% of the time, Pallas kernels for 0%

commit v1 on v0

v1 whole, which is shorter than its diff:
```python
import math

import jax
import jax.numpy as jnp
import ml_dtypes
import numpy as np
from jax import lax
from jax.sharding import PartitionSpec as P

ORDERS = 4


def fourier_table(lon_total, orders):
    lon_ids = np.arange(lon_total, dtype=np.int64)[:, None]
    order_ids = np.arange(orders, dtype=np.int64)[None, :]
    angles = (lon_ids * order_ids % lon_total).astype(np.float64) * (2.0 * math.pi / lon_total)
    amplitude = math.sqrt(2.0 / lon_total)
    table = np.concatenate([amplitude * np.cos(angles), -amplitude * np.sin(angles)], axis=1)
    return table.astype(ml_dtypes.bfloat16)


def colatitudes(lat_total):
    row_ids = np.arange(lat_total)
    mirror = np.minimum(row_ids, lat_total - 1 - row_ids)
    colatitude = (mirror.astype(np.float64) + 0.5) * (math.pi / lat_total)
    cosines = np.where(row_ids < lat_total // 2, np.cos(colatitude), -np.cos(colatitude))
    return cosines, np.sin(colatitude)


def legendre_table(cosines, sines, degrees, orders):
    rows = cosines.shape[0]
    table = np.zeros((degrees, orders, rows), np.float64)
    factor = math.sqrt(0.5)
    for m in range(orders):
        if m > 0:
            factor *= math.sqrt((2.0 * m + 1.0) / (2.0 * m))
        diagonal = factor * sines**m
        if m < degrees:
            table[m, m] = diagonal
        if m + 1 < degrees:
            table[m + 1, m] = math.sqrt(2.0 * m + 3.0) * cosines * diagonal
        for l in range(m + 2, degrees):
            a = math.sqrt((4.0 * l * l - 1.0) / (l * l - m * m))
            b = math.sqrt(((l - 1.0) ** 2 - m * m) / (4.0 * (l - 1.0) ** 2 - 1.0))
            table[l, m] = a * (cosines * table[l - 1, m] - b * table[l - 2, m])
    return np.concatenate([table, table], axis=1)


def legendre_scan(cosines_np, sines_np, degrees, orders):
    cosines = jnp.asarray(cosines_np.astype(np.float32))
    sines = jnp.asarray(sines_np.astype(np.float32))
    order_col = jnp.arange(orders, dtype=jnp.float32)[:, None]
    factors = [math.sqrt(0.5)]
    for order_num in range(1, orders):
        factors.append(factors[-1] * math.sqrt((2.0 * order_num + 1.0) / (2.0 * order_num)))
    diagonal_start = jnp.array(factors, dtype=jnp.float32)[:, None] * jnp.power(sines[None, :], order_col)
    next_start = jnp.sqrt(2.0 * order_col + 3.0) * cosines[None, :] * diagonal_start

    def advance(state_pair, degree):
        previous, earlier = state_pair
        deg_value = degree.astype(jnp.float32)
        deg_below = deg_value - 1.0
        ratio_up = jnp.sqrt(
            jnp.maximum(4.0 * deg_value * deg_value - 1.0, 1.0)
            / jnp.maximum(deg_value * deg_value - order_col * order_col, 1.0)
        )
        ratio_down = jnp.sqrt(
            jnp.maximum(deg_below * deg_below - order_col * order_col, 0.0)
            / jnp.maximum(4.0 * deg_below * deg_below - 1.0, 1.0)
        )
        recurred = ratio_up * (cosines[None, :] * previous - ratio_down * earlier)
        current = jnp.where(
            deg_value == order_col,
            diagonal_start,
            jnp.where(
                deg_value == order_col + 1.0,
                next_start,
                jnp.where(deg_value > order_col + 1.0, recurred, 0.0),
            ),
        )
        return ((current, previous), current)

    zeroed = jnp.zeros((orders, cosines.shape[0]), jnp.float32)
    _, stacked = lax.scan(advance, (zeroed, zeroed), jnp.arange(degrees, dtype=jnp.int32))
    return jnp.concatenate([stacked, stacked], axis=1)


def gelu_tanh(values):
    return jax.nn.gelu(values, approximate=True)


def xor_gather(x, axis_name, groups):
    bits = groups.bit_length() - 1
    cur = x[None]
    low = 0
    while low < bits:
        width = min(2, bits - low)
        parts = [cur]
        for k in range(1, 1 << width):
            mask = k << low
            parts.append(lax.ppermute(cur, axis_name, [(i, i ^ mask) for i in range(groups)]))
        cur = jnp.concatenate(parts, axis=0)
        low += width
    return cur


def xor_reduce_scatter(part, axis_name, groups, me):
    bits = groups.bit_length() - 1
    cur = part.reshape((groups, part.shape[0] // groups) + part.shape[1:])
    for b in range(bits):
        pairs = cur.reshape((cur.shape[0] // 2, 2) + cur.shape[1:])
        bit = (me >> b) & 1
        keep = jnp.where(bit == 0, pairs[:, 0], pairs[:, 1])
        send = jnp.where(bit == 0, pairs[:, 1], pairs[:, 0])
        mask = 1 << b
        cur = keep + lax.ppermute(send, axis_name, [(i, i ^ mask) for i in range(groups)])
    return cur.reshape(cur.shape[1:])


def complex_apply(coeffs, weights, orders):
    real_in, imag_in = (coeffs[:, :orders], coeffs[:, orders:])
    real_w, imag_w = (weights[:, 0], weights[:, 1])

    def complex_term(operand_a, operand_b):
        return jnp.einsum("smc,scd->smd", operand_a, operand_b, preferred_element_type=jnp.float32)

    real_out = complex_term(real_in, real_w) - complex_term(imag_in, imag_w)
    imag_out = complex_term(real_in, imag_w) + complex_term(imag_in, real_w)
    return jnp.concatenate([real_out, imag_out], axis=1)


def complex_adjoint(coeffs, cotangents, weights, orders):
    real_in, imag_in = (coeffs[:, :orders], coeffs[:, orders:])
    real_g, imag_g = (cotangents[:, :orders], cotangents[:, orders:])
    real_w, imag_w = (weights[:, 0], weights[:, 1])

    def outer_sum(operand_a, operand_b):
        return jnp.einsum("smc,smd->scd", operand_a, operand_b, preferred_element_type=jnp.float32)

    def back_term(operand_a, operand_b):
        return jnp.einsum("smd,scd->smc", operand_a, operand_b, preferred_element_type=jnp.float32)

    grad_real = outer_sum(real_in, real_g) + outer_sum(imag_in, imag_g)
    grad_imag = outer_sum(real_in, imag_g) - outer_sum(imag_in, real_g)
    back_real = back_term(real_g, real_w) + back_term(imag_g, imag_w)
    back_imag = back_term(imag_g, real_w) - back_term(real_g, imag_w)
    return (
        jnp.stack([grad_real, grad_imag], axis=1),
        jnp.concatenate([back_real, back_imag], axis=1),
    )


def local(activations, upstream, skip_weight, spectral_weight, slot_degree):
    groups = lax.axis_size("lat")
    me = lax.axis_index("lat")
    lat_rows = activations.shape[0]
    lon_total = activations.shape[1]
    lat_total = lat_rows * groups
    per_owner = spectral_weight.shape[0]
    degrees = per_owner * groups
    orders = ORDERS
    highest = lax.Precision.HIGHEST

    fourier = jnp.asarray(fourier_table(lon_total, orders))
    cosines, sines = colatitudes(lat_total)
    plm_np = legendre_table(cosines, sines, degrees, orders)
    quad_np = plm_np * (math.pi / lat_total * sines)[None, None, :]
    if degrees * lat_total <= 64 * 64:
        plm_all = jnp.asarray(plm_np.astype(np.float32))
        quad_all = jnp.asarray(quad_np.astype(np.float32))
    else:
        plm_all = legendre_scan(cosines, sines, degrees, orders)
        quad_all = plm_all * jnp.asarray((math.pi / lat_total * sines).astype(np.float32))[None, None, :]

    row_ids = jnp.arange(lat_total, dtype=jnp.int32)
    row_cols = jnp.bitwise_xor(me, row_ids // lat_rows) * lat_rows + row_ids % lat_rows
    slot_ids = jnp.arange(degrees, dtype=jnp.int32)
    slot_src = jnp.bitwise_xor(me, slot_ids // per_owner) * per_owner + slot_ids % per_owner
    slot_deg = jnp.take(slot_degree, slot_src, axis=0)
    own_deg = lax.dynamic_slice_in_dim(slot_degree, me * per_owner, per_owner)

    own_quad = jnp.take(jnp.take(quad_all, own_deg, axis=0), row_cols, axis=2)
    own_plm = jnp.take(jnp.take(plm_all, own_deg, axis=0), row_cols, axis=2)
    rows_plm = jnp.take(lax.dynamic_slice_in_dim(plm_all, me * lat_rows, lat_rows, axis=2), slot_deg, axis=0)
    rows_quad = jnp.take(lax.dynamic_slice_in_dim(quad_all, me * lat_rows, lat_rows, axis=2), slot_deg, axis=0)

    def gather(values):
        out = xor_gather(values, "lat", groups)
        return out.reshape((-1,) + out.shape[2:])

    spectrum = jnp.einsum("jkc,kf->jfc", activations, fourier, preferred_element_type=jnp.float32)
    all_spectrum = gather(spectrum)
    coeffs = jnp.einsum("sfj,jfc->sfc", own_quad, all_spectrum, precision=highest).astype(jnp.bfloat16)
    filtered = complex_apply(coeffs, spectral_weight, orders).astype(jnp.bfloat16)
    all_filtered = gather(filtered).astype(jnp.float32)
    grid_modes = jnp.einsum("sfj,sfc->jfc", rows_plm, all_filtered, precision=highest).astype(jnp.bfloat16)

    spatial = jnp.einsum("jfc,kf->jkc", grid_modes, fourier, preferred_element_type=jnp.float32)
    skip_out = jnp.einsum("jkc,cd->jkd", activations, skip_weight, preferred_element_type=jnp.float32)
    _, pullback = jax.vjp(gelu_tanh, spatial + skip_out)
    slope_b = pullback(upstream.astype(jnp.float32))[0].astype(jnp.bfloat16)

    skip_terms = jnp.einsum("jkc,jkd->cd", activations, slope_b, preferred_element_type=jnp.float32)
    grad_skip = xor_reduce_scatter(skip_terms, "lat", groups, me) * (1.0 / math.sqrt(lat_total * lon_total))
    through_skip = jnp.einsum("jkd,cd->jkc", slope_b, skip_weight, preferred_element_type=jnp.float32)

    mode_grads = jnp.einsum("jkc,kf->jfc", slope_b, fourier, preferred_element_type=jnp.float32)
    all_mode_grads = gather(mode_grads)
    coeff_grads = jnp.einsum("sfj,jfc->sfc", own_plm, all_mode_grads, precision=highest).astype(jnp.bfloat16)
    weight_grads, back_coeffs = complex_adjoint(coeffs, coeff_grads, spectral_weight, orders)
    back_b = back_coeffs.astype(jnp.bfloat16)
    all_back = gather(back_b).astype(jnp.float32)
    row_grads = jnp.einsum("sfj,sfc->jfc", rows_quad, all_back, precision=highest).astype(jnp.bfloat16)
    through_modes = jnp.einsum("jfc,kf->jkc", row_grads, fourier, preferred_element_type=jnp.float32)
    grad_activations = (upstream.astype(jnp.float32) + through_skip + through_modes).astype(jnp.bfloat16)
    return (grad_activations, weight_grads.astype(jnp.bfloat16), grad_skip)


def solution(mesh):
    in_specs = (
        P(("grp", "lat"), None, None),
        P(("grp", "lat"), None, None),
        P(),
        P("lat", None, None, None),
        P(),
    )
    out_specs = (
        P(("grp", "lat"), None, None),
        P(("grp", "lat"), None, None, None),
        P(("grp", "lat"), None),
    )
    return jax.shard_map(local, mesh=mesh, in_specs=in_specs, out_specs=out_specs, check_vma=False)
```

time: 303 us -> 108 us (0.36)
  local copies, waits for them, and re-layouts: 76.7 us -> 25.9 us
  waiting for transfers between devices: 64.8 us -> 21.9 us
  blocking collectives: 33.4 us -> 0 us
  other arithmetic: 34.8 us -> 6.82 us
  loops' own time: 22.8 us -> 0 us
  between operations: 15 us -> 1.01 us
  matrix products: 30.5 us -> 19 us
  starting transfers between devices: 22.9 us -> 32 us
    unnamed x2 -> x0, waiting for transfers between devices: 50.3 us -> none
    all_to_all x3 -> x0, blocking collectives: 33.4 us -> none  [the longest x1 12.4 us: to_owners(): lax.all_to_all(values, 'lat', split_axis=0, concat_axis=2, tiled=True)]
    ppermute x0 -> x28, starting transfers between devices: none -> 32 us  [the longest x24 26.6 us: xor_gather(): lax.ppermute(cur, axis_name, [(i, i ^ mask) for i in range(groups)])]
    another operation x1 -> x0, loops' own time: 22.8 us -> none  [legendre_table(): lax.scan(advance, (zeroed, zeroed), jnp.arange(degrees, dtype=jnp.int32))]
    all_to_all x5 -> x0, starting transfers between devices: 22.6 us -> none  [the longest x2 11.6 us: to_channels(): lax.all_to_all(values, 'lat', split_axis=2, concat_axis=0, tiled=True)]
    ppermute x0 -> x28, waiting for transfers between devices: none -> 21.9 us  [the longest x24 15.8 us: xor_gather(): lax.ppermute(cur, axis_name, [(i, i ^ mask) for i in range(groups)])]
    dynamic_update_slice x32 -> x0, other arithmetic: 21.2 us -> none  [legendre_table(): lax.scan(advance, (zeroed, zeroed), jnp.arange(degrees, dtype=jnp.int32))]
    dynamic_slice x32 -> x1, local copies, waits for them, and re-layouts: 20.7 us -> 1 us  [local(): lax.dynamic_slice_in_dim(quad_all, me * lat_rows, lat_rows, axis=2)]
  transfers between devices with their start and end apart: 6 -> 28, of which waited for: 5 -> 9; matrix products, arithmetic and copies ran while one was open for 25% -> 32% of each run, Pallas kernels for 0% -> 0%
where the time goes in v1:
time: 108 us; the launch traced here: 107 us
  starting transfers between devices  32 us (30%)
  local copies, waits for them, and re-layouts  25.9 us (24%)
  waiting for transfers between devices  21.9 us (20%)
  matrix products  19 us (18%)
  other arithmetic  6.82 us (6%)
    ppermute x24, starting transfers between devices, xor_gather(): lax.ppermute(cur, axis_name, [(i, i ^ mask) for i in range(groups)])  26.6 us
    ppermute x24, waiting for transfers between devices, xor_gather(): lax.ppermute(cur, axis_name, [(i, i ^ mask) for i in range(groups)])  15.8 us
    unnamed x33, local copies, waits for them, and re-layouts  14.2 us
    ppermute x4, waiting for transfers between devices, xor_reduce_scatter(): lax.ppermute(send, axis_name, [(i, i ^ mask) for i in range(groups)])  6.14 us
    ppermute x4, starting transfers between devices, xor_reduce_scatter(): lax.ppermute(send, axis_name, [(i, i ^ mask) for i in range(groups)])  5.44 us
    dot_general x1, matrix products, local(): jnp.einsum('jkc,cd->jkd', activations, skip_weight, preferred_element_typ...  4.4 us
    dot_general x1, matrix products, local(): jnp.einsum('jkd,cd->jkc', slope_b, skip_weight, preferred_element_type=jn...  2.97 us
    gather x2, local copies, waits for them, and re-layouts, local(): own_quad = jnp.take(jnp.take(quad_all, own_deg, axis=0), row_cols, axis=2)  2.68 us
  transfers between devices with their start and end apart: 28, of which 9 were waited for; matrix products, arithmetic and copies ran while one was open for 32% of the time, Pallas kernels for 0%

profile of v1, /device:TPU:0, one launch (start us, length us, event | category | flops | bytes accessed | tf_op | source)
XLA Modules:
  0.0 106.7 jit_solution(1629644429673139895)
XLA Ops:
  0.7 1.6 %copy-done = bf16[2,1440,384]{2,1,0:T(8,128)(2,1)S(1)} copy-done((bf16[2,1440,384]{2,1,0:T(8,128)(2,1)S(1)}, bf16[2,1440,384]{2,1,0:T(8,128)(2,1)}, u32[]{:S(2)}) %copy-start) | copy-done | bytes 2211864
  2.3 1.7 %constant_dynamic-update-slice_fusion.6 = (f32[16,2,8,384]{3,2,1,0:T(8,128)}, f32[1,2,8,384]{3,2,1,0:T(8,128)S(1)}) fusion(bf16[1440,8,1]{0,1,2:T(8,128)(2,1)} %constant.122, bf16[2,1440,384]{2,1,0:T(8,128)(2,1)S(1)} %copy-done), kind=kOutput, calls=%fused_computation.101 | convolution fusion | flops 17694720 | bytes 2284032 | tf_op jit(solution)/shard_map/jkc,kf->jfc/dot_general | solution.py:191
  4.5 2.5 %collective-permute-start.1 = (f32[1,2,8,384]{3,2,1,0:T(8,128)S(1)}, f32[1,2,8,384]{3,2,1,0:T(8,128)}, u32[]{:S(2)}, u32[]{:S(2)}) collective-permute-start(f32[1,2,8,384]{3,2,1,0:T(8,128)S(1)} %get-tuple-element.37), channel_id=1, source_target_pairs={{0,2},{1,3},{2,0},{3,1},{4,6},{5,7},{6,4},{7,5},{8,10},{9,11},{10,... | collective-permute-start | bytes 73736 | tf_op jit(solution)/shard_map/ppermute | solution.py:101
  8.5 1.5 %gather_fusion.1 = f32[2,8,32]{2,1,0:T(8,128)S(1)} fusion(f32[32,8,32]{2,1,0:T(8,128)} %constant.118.clone2.1, s32[1024]{0:T(1024)S(1)} %get-tuple-element.44), kind=kCustom, calls=%fused_computation.clone | custom fusion | bytes 4104 | tf_op jit(solution)/shard_map/jit(_take)/gather | solution.py:182
  10.0 1.5 %gather_fusion.4 = f32[2,8,32]{2,1,0:T(8,128)S(1)} fusion(f32[32,8,32]{2,1,0:T(8,128)} %constant.117.clone2.1, s32[1024]{0:T(1024)S(1)} %get-tuple-element.44), kind=kCustom, calls=%fused_computation.3.clone | custom fusion | bytes 4104 | tf_op jit(solution)/shard_map/jit(_take)/gather | solution.py:183
  14.6 1.5 %select_bitcast_fusion.5 = (f32[2,8,32]{1,0,2:T(2,128)}, f32[2,8,32]{1,0,2:T(2,128)S(1)}) fusion(f32[32,2,8]{2,1,0:T(2,128)} %gather_fusion.2, pred[32]{0:T(512)(128)(4,1)S(1)} %get-tuple-element.40, f32[32,2,8]{2,1,0:T(2,128)S(1)} %gather_fusion.5), kind=kLoop, calls=%fused_computation.130 | loop fusion | flops 1024 | bytes 8224 | tf_op jit(solution)/shard_map/jit(_take)/select_n | solution.py:182
  18.9 1.8 %collective-permute-start.3 = (f32[4,2,8,384]{3,2,1,0:T(8,128)S(1)}, f32[4,2,8,384]{3,2,1,0:T(8,128)S(1)}, u32[]{:S(2)}, u32[]{:S(2)}) collective-permute-start(f32[4,2,8,384]{3,2,1,0:T(8,128)S(1)} %pad_maximum_fusion.1), channel_id=1, source_target_pairs={{0,4},{1,5},{2,6},{3,7},{4,0},{5,1},{6,2},{7,3},{8,12},{9,13},{10,... | collective-permute-start | bytes 294920 | tf_op jit(solution)/shard_map/ppermute | solution.py:101
  20.7 2.6 %collective-permute-start.4 = (f32[4,2,8,384]{3,2,1,0:T(8,128)S(1)}, f32[4,2,8,384]{3,2,1,0:T(8,128)S(1)}, u32[]{:S(2)}, u32[]{:S(2)}) collective-permute-start(f32[4,2,8,384]{3,2,1,0:T(8,128)S(1)} %pad_maximum_fusion.1), channel_id=1, source_target_pairs={{0,8},{1,9},{2,10},{3,11},{4,12},{5,13},{6,14},{7,15},{8,0},{9,1},... | collective-permute-start | bytes 294920 | tf_op jit(solution)/shard_map/ppermute | solution.py:101
  23.3 1.3 %constant_dynamic-update-slice_fusion.5 = f32[16,2,8,384]{3,2,1,0:T(8,128)} fusion(f32[16,2,8,384]{3,2,1,0:T(8,128)} %get-tuple-element.36, f32[1,2,8,384]{3,2,1,0:T(8,128)} %collective-permute-done), kind=kLoop, calls=%fused_computation.100 | loop fusion | bytes 49152
  24.7 1.3 %constant_dynamic-update-slice_fusion.4 = f32[16,2,8,384]{3,2,1,0:T(8,128)} fusion(f32[16,2,8,384]{3,2,1,0:T(8,128)} %constant_dynamic-update-slice_fusion.5, f32[1,2,8,384]{3,2,1,0:T(8,128)} %collective-permute-done.1), kind=kLoop, calls=%fused_computation.99 | loop fusion | bytes 49152
  26.0 1.3 %constant_dynamic-update-slice_fusion.3 = f32[16,2,8,384]{3,2,1,0:T(8,128)} fusion(f32[16,2,8,384]{3,2,1,0:T(8,128)} %constant_dynamic-update-slice_fusion.4, f32[1,2,8,384]{3,2,1,0:T(8,128)} %collective-permute-done.2), kind=kLoop, calls=%fused_computation.98 | loop fusion | bytes 49152
  28.0 3.3 %collective-permute-done.4 = f32[4,2,8,384]{3,2,1,0:T(8,128)S(1)} collective-permute-done((f32[4,2,8,384]{3,2,1,0:T(8,128)S(1)}, f32[4,2,8,384]{3,2,1,0:T(8,128)S(1)}, u32[]{:S(2)}, u32[]{:S(2)}) %collective-permute-start.4) | collective-permute-done | bytes 98336 | tf_op jit(solution)/shard_map/ppermute | solution.py:101
  32.6 1.4 %fusion.18 = bf16[2,8,384]{2,0,1:T(2,128)(2,1)S(1)} fusion(f32[2,8,32]{2,0,1:T(2,128)S(1)} %copy.112, f32[32,8,384]{2,1,0:T(8,128)} %bitcast.167), kind=kOutput, calls=%fused_computation.44 | convolution fusion | flops 2365440 | bytes 407552 | tf_op jit(solution)/shard_map/sfj,jfc->sfc/dot_general | solution.py:193
  35.5 1.5 %collective-permute-start.7 = (bf16[1,2,8,384]{3,2,1,0:T(8,128)(2,1)}, bf16[1,2,8,384]{3,2,1,0:T(8,128)(2,1)}, u32[]{:S(2)}, u32[]{:S(2)}) collective-permute-start(bf16[1,2,8,384]{3,2,1,0:T(8,128)(2,1)} %get-tuple-element.26), channel_id=1, source_target_pairs={{0,2},{1,3},{2,0},{3,1},{4,6},{5,7},{6,4},{7,5},{8,10},{9,11},{10,... | collective-permute-start | bytes 36872 | tf_op jit(solution)/shard_map/ppermute | solution.py:101
  37.4 1.4 %broadcast_select_fusion.1 = (f32[32,8,2]{1,2,0:T(2,128)}, f32[32,8,2]{1,2,0:T(2,128)}) fusion(f32[32,8,2]{1,2,0:T(2,128)S(1)} %gather_fusion.3, pred[32]{0:T(512)(128)(4,1)} %get-tuple-element.20, f32[32,8,2]{1,2,0:T(2,128)S(1)} %gather_fusion.6), kind=kLoop, calls=%fused_computation.132 | loop fusion | flops 1024 | bytes 8224 | tf_op jit(solution)/shard_map/jit(_take)/select_n | solution.py:184
  42.5 2.0 %collective-permute-start.10 = (bf16[4,2,8,384]{3,2,1,0:T(8,128)(2,1)S(1)}, bf16[4,2,8,384]{3,2,1,0:T(8,128)(2,1)S(1)}, u32[]{:S(2)}, u32[]{:S(2)}) collective-permute-start(bf16[4,2,8,384]{3,2,1,0:T(8,128)(2,1)S(1)} %pad_maximum_fusion.3), channel_id=1, source_target_pairs={{0,8},{1,9},{2,10},{3,11},{4,12},{5,13},{6,14},{7,15},{8,0},{9,1},... | collective-permute-start | bytes 147464 | tf_op jit(solution)/shard_map/ppermute | solution.py:101
  45.7 1.3 %constant_dynamic-update-slice_fusion.12 = bf16[16,2,8,384]{3,2,1,0:T(8,128)(2,1)} fusion(bf16[16,2,8,384]{3,2,1,0:T(8,128)(2,1)} %get-tuple-element.27, bf16[1,2,8,384]{3,2,1,0:T(8,128)(2,1)} %collective-permute-done.6), kind=kLoop, calls=%fused_computation.107 | loop fusion | bytes 24576
  47.0 1.3 %constant_dynamic-update-slice_fusion.11 = bf16[16,2,8,384]{3,2,1,0:T(8,128)(2,1)} fusion(bf16[16,2,8,384]{3,2,1,0:T(8,128)(2,1)} %constant_dynamic-update-slice_fusion.12, bf16[1,2,8,384]{3,2,1,0:T(8,128)(2,1)} %collective-permute-done.7), kind=kLoop, calls=%fused_computation.106 | loop fusion | bytes 24576
  48.3 1.3 %constant_dynamic-update-slice_fusion.10 = bf16[16,2,8,384]{3,2,1,0:T(8,128)(2,1)} fusion(bf16[16,2,8,384]{3,2,1,0:T(8,128)(2,1)} %constant_dynamic-update-slice_fusion.11, bf16[1,2,8,384]{3,2,1,0:T(8,128)(2,1)} %collective-permute-done.8), kind=kLoop, calls=%fused_computation.105 | loop fusion | bytes 24576
  54.3 4.4 %fusion.6 = bf16[2,1440,384]{2,1,0:T(8,128)(2,1)S(1)} fusion(bf16[2,1440,384]{2,1,0:T(8,128)(2,1)S(1)} %copy-done.3, f32[2,384,1440]{1,2,0:T(8,128)S(1)} %fusion.63, bf16[2,1440,384]{2,1,0:T(8,128)(2,1)S(1)} %copy-done, bf16[384,384]{1,0:T(8,128)(2,1)S(1)} %copy-done.5), kind=kOutput, calls=%fused_computation.18 | convolution fusion | flops 873676800 | bytes 11354112 | tf_op jit(solution)/shard_map/jkc,cd->jkd/dot_general | solution.py:199
  59.1 1.6 %collective-permute-start.13 = (f32[1,2,8,384]{3,2,1,0:T(8,128)S(1)}, f32[1,2,8,384]{3,2,1,0:T(8,128)S(1)}, u32[]{:S(2)}, u32[]{:S(2)}) collective-permute-start(f32[1,2,8,384]{3,2,1,0:T(8,128)S(1)} %get-tuple-element.39), channel_id=1, source_target_pairs={{0,2},{1,3},{2,0},{3,1},{4,6},{5,7},{6,4},{7,5},{8,10},{9,11},{10,... | collective-permute-start | bytes 73736 | tf_op jit(solution)/shard_map/ppermute | solution.py:101
  61.0 1.4 %fusion.92 = f32[384,384,1]{0,1,2:T(8,128)S(1)} fusion(bf16[2,1440,384]{2,1,0:T(8,128)(2,1)S(1)} %fusion.6, bf16[2,1440,384]{2,1,0:T(8,128)(2,1)S(1)} %copy-done), kind=kOutput, calls=%fused_computation.191 | convolution fusion | flops 849346560 | bytes 5013504 | tf_op jit(solution)/shard_map/jkc,jkd->cd/dot_general | solution.py:203
  64.3 2.9 %collective-permute-start.16 = (f32[4,2,8,384]{3,2,1,0:T(8,128)S(1)}, f32[4,2,8,384]{3,2,1,0:T(8,128)S(1)}, u32[]{:S(2)}, u32[]{:S(2)}) collective-permute-start(f32[4,2,8,384]{3,2,1,0:T(8,128)S(1)} %pad_maximum_fusion.2), channel_id=1, source_target_pairs={{0,8},{1,9},{2,10},{3,11},{4,12},{5,13},{6,14},{7,15},{8,0},{9,1},... | collective-permute-start | bytes 294920 | tf_op jit(solution)/shard_map/ppermute | solution.py:101
  68.4 2.1 %collective-permute-done.15 = f32[4,2,8,384]{3,2,1,0:T(8,128)S(1)} collective-permute-done((f32[4,2,8,384]{3,2,1,0:T(8,128)S(1)}, f32[4,2,8,384]{3,2,1,0:T(8,128)S(1)}, u32[]{:S(2)}, u32[]{:S(2)}) %collective-permute-start.15) | collective-permute-done | bytes 98336 | tf_op jit(solution)/shard_map/ppermute | solution.py:101
  70.5 4.7 %collective-permute-done.16 = f32[4,2,8,384]{3,2,1,0:T(8,128)S(1)} collective-permute-done((f32[4,2,8,384]{3,2,1,0:T(8,128)S(1)}, f32[4,2,8,384]{3,2,1,0:T(8,128)S(1)}, u32[]{:S(2)}, u32[]{:S(2)}) %collective-permute-start.16) | collective-permute-done | bytes 98336 | tf_op jit(solution)/shard_map/ppermute | solution.py:101
  81.5 2.0 %collective-permute-start.21 = (bf16[4,2,8,384]{3,2,1,0:T(8,128)(2,1)S(1)}, bf16[4,2,8,384]{3,2,1,0:T(8,128)(2,1)S(1)}, u32[]{:S(2)}, u32[]{:S(2)}) collective-permute-start(bf16[4,2,8,384]{3,2,1,0:T(8,128)(2,1)S(1)} %pad_maximum_fusion.4), channel_id=1, source_target_pairs={{0,4},{1,5},{2,6},{3,7},{4,0},{5,1},{6,2},{7,3},{8,12},{9,13},{10,... | collective-permute-start | bytes 147464 | tf_op jit(solution)/shard_map/ppermute | solution.py:101
  86.0 4.1 %collective-permute-done.22 = bf16[4,2,8,384]{3,2,1,0:T(8,128)(2,1)S(1)} collective-permute-done((bf16[4,2,8,384]{3,2,1,0:T(8,128)(2,1)S(1)}, bf16[4,2,8,384]{3,2,1,0:T(8,128)(2,1)S(1)}, u32[]{:S(2)}, u32[]{:S(2)}) %collective-permute-start.22) | collective-permute-done | bytes 49184 | tf_op jit(solution)/shard_map/ppermute | solution.py:101
  91.9 4.1 %collective-permute-done.25 = f32[4,24,384]{2,1,0:T(8,128)S(1)} collective-permute-done((f32[4,24,384]{2,1,0:T(8,128)S(1)}, f32[4,24,384]{2,1,0:T(8,128)S(1)}, u32[]{:S(2)}, u32[]{:S(2)}) %collective-permute-start.25) | collective-permute-done | bytes 147488 | tf_op jit(solution)/shard_map/ppermute | solution.py:116
  96.1 1.6 %collective-permute-start.26 = (f32[2,24,384]{2,1,0:T(8,128)S(1)}, f32[2,24,384]{2,1,0:T(8,128)S(1)}, u32[]{:S(2)}, u32[]{:S(2)}) collective-permute-start(f32[2,24,384]{2,1,0:T(8,128)S(1)} %select_bitcast_fusion.2), channel_id=1, source_target_pairs={{0,4},{1,5},{2,6},{3,7},{4,0},{5,1},{6,2},{7,3},{8,12},{9,13},{10,... | collective-permute-start | bytes 221192 | tf_op jit(solution)/shard_map/ppermute | solution.py:116
  98.5 2.0 %collective-permute-done.26 = f32[2,24,384]{2,1,0:T(8,128)S(1)} collective-permute-done((f32[2,24,384]{2,1,0:T(8,128)S(1)}, f32[2,24,384]{2,1,0:T(8,128)S(1)}, u32[]{:S(2)}, u32[]{:S(2)}) %collective-permute-start.26) | collective-permute-done | bytes 73760 | tf_op jit(solution)/shard_map/ppermute | solution.py:116
  100.5 2.6 %collective-permute-start.27 = (f32[1,24,384]{2,1,0:T(8,128)S(1)}, f32[1,24,384]{2,1,0:T(8,128)S(1)}, u32[]{:S(2)}, u32[]{:S(2)}) collective-permute-start(f32[1,24,384]{2,1,0:T(8,128)S(1)} %select_bitcast_fusion.3), channel_id=1, source_target_pairs={{0,8},{1,9},{2,10},{3,11},{4,12},{5,13},{6,14},{7,15},{8,0},{9,1},... | collective-permute-start | bytes 110600 | tf_op jit(solution)/shard_map/ppermute | solution.py:116
  103.1 3.0 %fusion.11 = bf16[2,1440,384]{2,1,0:T(8,128)(2,1)} fusion(bf16[2,1440,384]{2,1,0:T(8,128)(2,1)S(1)} %copy-done.3, f32[2,384,1440]{1,2,0:T(8,128)S(1)} %fusion.61, bf16[2,1440,384]{2,1,0:T(8,128)(2,1)S(1)} %fusion.6, bf16[384,384]{1,0:T(8,128)(2,1)S(1)} %copy-done.5), kind=kOutput, calls=%fused_computation.23 | convolution fusion | flops 853770240 | bytes 11354112 | tf_op jit(solution)/shard_map/jkd,cd->jkc/dot_general | solution.py:205
  (125 shorter events, 37.1 us)
Async XLA Ops:
  0.6 1.6 %copy-start = (bf16[2,1440,384]{2,1,0:T(8,128)(2,1)S(1)}, bf16[2,1440,384]{2,1,0:T(8,128)(2,1)}, u32[]{:S(2)}) copy-start(bf16[2,1440,384]{2,1,0:T(8,128)(2,1)} %param.14) | copy-start | bytes 6635524
  0.6 6.5 %copy-start.1 = (s32[32]{0:T(128)S(1)}, s32[32]{0:T(128)}, u32[]{:S(2)}) copy-start(s32[32]{0:T(128)} %param.18) | copy-start | bytes 388
  0.7 33.4 %copy-start.2 = (bf16[2,2,384,384]{3,2,1,0:T(8,128)(2,1)S(1)}, bf16[2,2,384,384]{3,2,1,0:T(8,128)(2,1)}, u32[]{:S(2)}) copy-start(bf16[2,2,384,384]{3,2,1,0:T(8,128)(2,1)} %param.17) | copy-start | bytes 3538948
  4.0 14.1 %collective-permute-start = (f32[1,2,8,384]{3,2,1,0:T(8,128)S(1)}, f32[1,2,8,384]{3,2,1,0:T(8,128)}, u32[]{:S(2)}, u32[]{:S(2)}) collective-permute-start(f32[1,2,8,384]{3,2,1,0:T(8,128)S(1)} %get-tuple-element.37), channel_id=1, source_target_pairs={{0,1},{1,0},{2,3},{3,2},{4,5},{5,4},{6,7},{7,6},{8,9},{9,8},{10,11... | collective-permute-start | bytes 73736 | tf_op jit(solution)/shard_map/ppermute | solution.py:101
  4.5 13.6 %collective-permute-start.1 = (f32[1,2,8,384]{3,2,1,0:T(8,128)S(1)}, f32[1,2,8,384]{3,2,1,0:T(8,128)}, u32[]{:S(2)}, u32[]{:S(2)}) collective-permute-start(f32[1,2,8,384]{3,2,1,0:T(8,128)S(1)} %get-tuple-element.37), channel_id=1, source_target_pairs={{0,2},{1,3},{2,0},{3,1},{4,6},{5,7},{6,4},{7,5},{8,10},{9,11},{10,... | collective-permute-start | bytes 73736 | tf_op jit(solution)/shard_map/ppermute | solution.py:101
  7.0 11.1 %collective-permute-start.2 = (f32[1,2,8,384]{3,2,1,0:T(8,128)S(1)}, f32[1,2,8,384]{3,2,1,0:T(8,128)}, u32[]{:S(2)}, u32[]{:S(2)}) collective-permute-start(f32[1,2,8,384]{3,2,1,0:T(8,128)S(1)} %get-tuple-element.37), channel_id=1, source_target_pairs={{0,3},{1,2},{2,1},{3,0},{4,7},{5,6},{6,5},{7,4},{8,11},{9,10},{10,... | collective-permute-start | bytes 73736 | tf_op jit(solution)/shard_map/ppermute | solution.py:101
  18.9 8.5 %collective-permute-start.3 = (f32[4,2,8,384]{3,2,1,0:T(8,128)S(1)}, f32[4,2,8,384]{3,2,1,0:T(8,128)S(1)}, u32[]{:S(2)}, u32[]{:S(2)}) collective-permute-start(f32[4,2,8,384]{3,2,1,0:T(8,128)S(1)} %pad_maximum_fusion.1), channel_id=1, source_target_pairs={{0,4},{1,5},{2,6},{3,7},{4,0},{5,1},{6,2},{7,3},{8,12},{9,13},{10,... | collective-permute-start | bytes 294920 | tf_op jit(solution)/shard_map/ppermute | solution.py:101
  20.7 10.6 %collective-permute-start.4 = (f32[4,2,8,384]{3,2,1,0:T(8,128)S(1)}, f32[4,2,8,384]{3,2,1,0:T(8,128)S(1)}, u32[]{:S(2)}, u32[]{:S(2)}) collective-permute-start(f32[4,2,8,384]{3,2,1,0:T(8,128)S(1)} %pad_maximum_fusion.1), channel_id=1, source_target_pairs={{0,8},{1,9},{2,10},{3,11},{4,12},{5,13},{6,14},{7,15},{8,0},{9,1},... | collective-permute-start | bytes 294920 | tf_op jit(solution)/shard_map/ppermute | solution.py:101
  23.3 8.7 %collective-permute-start.5 = (f32[4,2,8,384]{3,2,1,0:T(8,128)S(1)}, f32[4,2,8,384]{3,2,1,0:T(8,128)S(1)}, u32[]{:S(2)}, u32[]{:S(2)}) collective-permute-start(f32[4,2,8,384]{3,2,1,0:T(8,128)S(1)} %pad_maximum_fusion.1), channel_id=1, source_target_pairs={{0,12},{1,13},{2,14},{3,15},{4,8},{5,9},{6,10},{7,11},{8,4},{9,5},... | collective-permute-start | bytes 294920 | tf_op jit(solution)/shard_map/ppermute | solution.py:101
  28.0 24.7 %copy-start.4 = (bf16[1440,8,1]{0,1,2:T(8,128)(2,1)S(1)}, bf16[1440,8,1]{0,1,2:T(8,128)(2,1)}, u32[]{:S(2)}) copy-start(bf16[1440,8,1]{0,1,2:T(8,128)(2,1)} %constant.122) | copy-start | bytes 69124
  35.5 5.0 %collective-permute-start.6 = (bf16[1,2,8,384]{3,2,1,0:T(8,128)(2,1)}, bf16[1,2,8,384]{3,2,1,0:T(8,128)(2,1)}, u32[]{:S(2)}, u32[]{:S(2)}) collective-permute-start(bf16[1,2,8,384]{3,2,1,0:T(8,128)(2,1)} %get-tuple-element.26), channel_id=1, source_target_pairs={{0,1},{1,0},{2,3},{3,2},{4,5},{5,4},{6,7},{7,6},{8,9},{9,8},{10,11... | collective-permute-start | bytes 36872 | tf_op jit(solution)/shard_map/ppermute | solution.py:101
  35.5 5.0 %collective-permute-start.7 = (bf16[1,2,8,384]{3,2,1,0:T(8,128)(2,1)}, bf16[1,2,8,384]{3,2,1,0:T(8,128)(2,1)}, u32[]{:S(2)}, u32[]{:S(2)}) collective-permute-start(bf16[1,2,8,384]{3,2,1,0:T(8,128)(2,1)} %get-tuple-element.26), channel_id=1, source_target_pairs={{0,2},{1,3},{2,0},{3,1},{4,6},{5,7},{6,4},{7,5},{8,10},{9,11},{10,... | collective-permute-start | bytes 36872 | tf_op jit(solution)/shard_map/ppermute | solution.py:101
  37.0 3.5 %collective-permute-start.8 = (bf16[1,2,8,384]{3,2,1,0:T(8,128)(2,1)}, bf16[1,2,8,384]{3,2,1,0:T(8,128)(2,1)}, u32[]{:S(2)}, u32[]{:S(2)}) collective-permute-start(bf16[1,2,8,384]{3,2,1,0:T(8,128)(2,1)} %get-tuple-element.26), channel_id=1, source_target_pairs={{0,3},{1,2},{2,1},{3,0},{4,7},{5,6},{6,5},{7,4},{8,11},{9,10},{10,... | collective-permute-start | bytes 36872 | tf_op jit(solution)/shard_map/ppermute | solution.py:101
  41.3 8.4 %collective-permute-start.9 = (bf16[4,2,8,384]{3,2,1,0:T(8,128)(2,1)S(1)}, bf16[4,2,8,384]{3,2,1,0:T(8,128)(2,1)S(1)}, u32[]{:S(2)}, u32[]{:S(2)}) collective-permute-start(bf16[4,2,8,384]{3,2,1,0:T(8,128)(2,1)S(1)} %pad_maximum_fusion.3), channel_id=1, source_target_pairs={{0,4},{1,5},{2,6},{3,7},{4,0},{5,1},{6,2},{7,3},{8,12},{9,13},{10,... | collective-permute-start | bytes 147464 | tf_op jit(solution)/shard_map/ppermute | solution.py:101
  42.5 7.7 %collective-permute-start.10 = (bf16[4,2,8,384]{3,2,1,0:T(8,128)(2,1)S(1)}, bf16[4,2,8,384]{3,2,1,0:T(8,128)(2,1)S(1)}, u32[]{:S(2)}, u32[]{:S(2)}) collective-permute-start(bf16[4,2,8,384]{3,2,1,0:T(8,128)(2,1)S(1)} %pad_maximum_fusion.3), channel_id=1, source_target_pairs={{0,8},{1,9},{2,10},{3,11},{4,12},{5,13},{6,14},{7,15},{8,0},{9,1},... | collective-permute-start | bytes 147464 | tf_op jit(solution)/shard_map/ppermute | solution.py:101
  44.6 6.3 %collective-permute-start.11 = (bf16[4,2,8,384]{3,2,1,0:T(8,128)(2,1)S(1)}, bf16[4,2,8,384]{3,2,1,0:T(8,128)(2,1)S(1)}, u32[]{:S(2)}, u32[]{:S(2)}) collective-permute-start(bf16[4,2,8,384]{3,2,1,0:T(8,128)(2,1)S(1)} %pad_maximum_fusion.3), channel_id=1, source_target_pairs={{0,12},{1,13},{2,14},{3,15},{4,8},{5,9},{6,10},{7,11},{8,4},{9,5},... | collective-permute-start | bytes 147464 | tf_op jit(solution)/shard_map/ppermute | solution.py:101
  59.1 3.7 %collective-permute-start.12 = (f32[1,2,8,384]{3,2,1,0:T(8,128)S(1)}, f32[1,2,8,384]{3,2,1,0:T(8,128)S(1)}, u32[]{:S(2)}, u32[]{:S(2)}) collective-permute-start(f32[1,2,8,384]{3,2,1,0:T(8,128)S(1)} %get-tuple-element.39), channel_id=1, source_target_pairs={{0,1},{1,0},{2,3},{3,2},{4,5},{5,4},{6,7},{7,6},{8,9},{9,8},{10,11... | collective-permute-start | bytes 73736 | tf_op jit(solution)/shard_map/ppermute | solution.py:101
  59.1 3.9 %collective-permute-start.13 = (f32[1,2,8,384]{3,2,1,0:T(8,128)S(1)}, f32[1,2,8,384]{3,2,1,0:T(8,128)S(1)}, u32[]{:S(2)}, u32[]{:S(2)}) collective-permute-start(f32[1,2,8,384]{3,2,1,0:T(8,128)S(1)} %get-tuple-element.39), channel_id=1, source_target_pairs={{0,2},{1,3},{2,0},{3,1},{4,6},{5,7},{6,4},{7,5},{8,10},{9,11},{10,... | collective-permute-start | bytes 73736 | tf_op jit(solution)/shard_map/ppermute | solution.py:101
  60.7 3.3 %collective-permute-start.14 = (f32[1,2,8,384]{3,2,1,0:T(8,128)S(1)}, f32[1,2,8,384]{3,2,1,0:T(8,128)S(1)}, u32[]{:S(2)}, u32[]{:S(2)}) collective-permute-start(f32[1,2,8,384]{3,2,1,0:T(8,128)S(1)} %get-tuple-element.39), channel_id=1, source_target_pairs={{0,3},{1,2},{2,1},{3,0},{4,7},{5,6},{6,5},{7,4},{8,11},{9,10},{10,... | collective-permute-start | bytes 73736 | tf_op jit(solution)/shard_map/ppermute | solution.py:101
  62.4 28.3 %collective-permute-start.24 = (f32[8,24,384]{2,1,0:T(8,128)S(1)}, f32[8,24,384]{2,1,0:T(8,128)S(1)}, u32[]{:S(2)}, u32[]{:S(2)}) collective-permute-start(f32[8,24,384]{2,1,0:T(8,128)S(1)} %select_bitcast_fusion), channel_id=1, source_target_pairs={{0,1},{1,0},{2,3},{3,2},{4,5},{5,4},{6,7},{7,6},{8,9},{9,8},{10,11... | collective-permute-start | bytes 884744 | tf_op jit(solution)/shard_map/ppermute | solution.py:116
  63.9 6.5 %collective-permute-start.15 = (f32[4,2,8,384]{3,2,1,0:T(8,128)S(1)}, f32[4,2,8,384]{3,2,1,0:T(8,128)S(1)}, u32[]{:S(2)}, u32[]{:S(2)}) collective-permute-start(f32[4,2,8,384]{3,2,1,0:T(8,128)S(1)} %pad_maximum_fusion.2), channel_id=1, source_target_pairs={{0,4},{1,5},{2,6},{3,7},{4,0},{5,1},{6,2},{7,3},{8,12},{9,13},{10,... | collective-permute-start | bytes 294920 | tf_op jit(solution)/shard_map/ppermute | solution.py:101
  64.3 10.8 %collective-permute-start.16 = (f32[4,2,8,384]{3,2,1,0:T(8,128)S(1)}, f32[4,2,8,384]{3,2,1,0:T(8,128)S(1)}, u32[]{:S(2)}, u32[]{:S(2)}) collective-permute-start(f32[4,2,8,384]{3,2,1,0:T(8,128)S(1)} %pad_maximum_fusion.2), channel_id=1, source_target_pairs={{0,8},{1,9},{2,10},{3,11},{4,12},{5,13},{6,14},{7,15},{8,0},{9,1},... | collective-permute-start | bytes 294920 | tf_op jit(solution)/shard_map/ppermute | solution.py:101
  67.3 7.9 %collective-permute-start.17 = (f32[4,2,8,384]{3,2,1,0:T(8,128)S(1)}, f32[4,2,8,384]{3,2,1,0:T(8,128)S(1)}, u32[]{:S(2)}, u32[]{:S(2)}) collective-permute-start(f32[4,2,8,384]{3,2,1,0:T(8,128)S(1)} %pad_maximum_fusion.2), channel_id=1, source_target_pairs={{0,12},{1,13},{2,14},{3,15},{4,8},{5,9},{6,10},{7,11},{8,4},{9,5},... | collective-permute-start | bytes 294920 | tf_op jit(solution)/shard_map/ppermute | solution.py:101
  76.8 4.7 %collective-permute-start.18 = (bf16[1,2,8,384]{3,2,1,0:T(8,128)(2,1)S(1)}, bf16[1,2,8,384]{3,2,1,0:T(8,128)(2,1)S(1)}, u32[]{:S(2)}, u32[]{:S(2)}) collective-permute-start(bf16[1,2,8,384]{3,2,1,0:T(8,128)(2,1)S(1)} %get-tuple-element.22), channel_id=1, source_target_pairs={{0,1},{1,0},{2,3},{3,2},{4,5},{5,4},{6,7},{7,6},{8,9},{9,8},{10,11... | collective-permute-start | bytes 36872 | tf_op jit(solution)/shard_map/ppermute | solution.py:101
  76.8 4.7 %collective-permute-start.19 = (bf16[1,2,8,384]{3,2,1,0:T(8,128)(2,1)S(1)}, bf16[1,2,8,384]{3,2,1,0:T(8,128)(2,1)S(1)}, u32[]{:S(2)}, u32[]{:S(2)}) collective-permute-start(bf16[1,2,8,384]{3,2,1,0:T(8,128)(2,1)S(1)} %get-tuple-element.22), channel_id=1, source_target_pairs={{0,2},{1,3},{2,0},{3,1},{4,6},{5,7},{6,4},{7,5},{8,10},{9,11},{10,... | collective-permute-start | bytes 36872 | tf_op jit(solution)/shard_map/ppermute | solution.py:101
  77.7 3.8 %collective-permute-start.20 = (bf16[1,2,8,384]{3,2,1,0:T(8,128)(2,1)S(1)}, bf16[1,2,8,384]{3,2,1,0:T(8,128)(2,1)S(1)}, u32[]{:S(2)}, u32[]{:S(2)}) collective-permute-start(bf16[1,2,8,384]{3,2,1,0:T(8,128)(2,1)S(1)} %get-tuple-element.22), channel_id=1, source_target_pairs={{0,3},{1,2},{2,1},{3,0},{4,7},{5,6},{6,5},{7,4},{8,11},{9,10},{10,... | collective-permute-start | bytes 36872 | tf_op jit(solution)/shard_map/ppermute | solution.py:101
  81.5 4.5 %collective-permute-start.21 = (bf16[4,2,8,384]{3,2,1,0:T(8,128)(2,1)S(1)}, bf16[4,2,8,384]{3,2,1,0:T(8,128)(2,1)S(1)}, u32[]{:S(2)}, u32[]{:S(2)}) collective-permute-start(bf16[4,2,8,384]{3,2,1,0:T(8,128)(2,1)S(1)} %pad_maximum_fusion.4), channel_id=1, source_target_pairs={{0,4},{1,5},{2,6},{3,7},{4,0},{5,1},{6,2},{7,3},{8,12},{9,13},{10,... | collective-permute-start | bytes 147464 | tf_op jit(solution)/shard_map/ppermute | solution.py:101
  83.5 6.6 %collective-permute-start.22 = (bf16[4,2,8,384]{3,2,1,0:T(8,128)(2,1)S(1)}, bf16[4,2,8,384]{3,2,1,0:T(8,128)(2,1)S(1)}, u32[]{:S(2)}, u32[]{:S(2)}) collective-permute-start(bf16[4,2,8,384]{3,2,1,0:T(8,128)(2,1)S(1)} %pad_maximum_fusion.4), channel_id=1, source_target_pairs={{0,8},{1,9},{2,10},{3,11},{4,12},{5,13},{6,14},{7,15},{8,0},{9,1},... | collective-permute-start | bytes 147464 | tf_op jit(solution)/shard_map/ppermute | solution.py:101
  84.7 6.0 %collective-permute-start.23 = (bf16[4,2,8,384]{3,2,1,0:T(8,128)(2,1)S(1)}, bf16[4,2,8,384]{3,2,1,0:T(8,128)(2,1)S(1)}, u32[]{:S(2)}, u32[]{:S(2)}) collective-permute-start(bf16[4,2,8,384]{3,2,1,0:T(8,128)(2,1)S(1)} %pad_maximum_fusion.4), channel_id=1, source_target_pairs={{0,12},{1,13},{2,14},{3,15},{4,8},{5,9},{6,10},{7,11},{8,4},{9,5},... | collective-permute-start | bytes 147464 | tf_op jit(solution)/shard_map/ppermute | solution.py:101
  90.8 5.2 %collective-permute-start.25 = (f32[4,24,384]{2,1,0:T(8,128)S(1)}, f32[4,24,384]{2,1,0:T(8,128)S(1)}, u32[]{:S(2)}, u32[]{:S(2)}) collective-permute-start(f32[4,24,384]{2,1,0:T(8,128)S(1)} %select_bitcast_fusion.1), channel_id=1, source_target_pairs={{0,2},{1,3},{2,0},{3,1},{4,6},{5,7},{6,4},{7,5},{8,10},{9,11},{10,... | collective-permute-start | bytes 442376 | tf_op jit(solution)/shard_map/ppermute | solution.py:116
  96.1 4.4 %collective-permute-start.26 = (f32[2,24,384]{2,1,0:T(8,128)S(1)}, f32[2,24,384]{2,1,0:T(8,128)S(1)}, u32[]{:S(2)}, u32[]{:S(2)}) collective-permute-start(f32[2,24,384]{2,1,0:T(8,128)S(1)} %select_bitcast_fusion.2), channel_id=1, source_target_pairs={{0,4},{1,5},{2,6},{3,7},{4,0},{5,1},{6,2},{7,3},{8,12},{9,13},{10,... | collective-permute-start | bytes 221192 | tf_op jit(solution)/shard_map/ppermute | solution.py:116
  100.5 5.5 %collective-permute-start.27 = (f32[1,24,384]{2,1,0:T(8,128)S(1)}, f32[1,24,384]{2,1,0:T(8,128)S(1)}, u32[]{:S(2)}, u32[]{:S(2)}) collective-permute-start(f32[1,24,384]{2,1,0:T(8,128)S(1)} %select_bitcast_fusion.3), channel_id=1, source_target_pairs={{0,8},{1,9},{2,10},{3,11},{4,12},{5,13},{6,14},{7,15},{8,0},{9,1},... | collective-permute-start | bytes 110600 | tf_op jit(solution)/shard_map/ppermute | solution.py:116
  (2 other events, 3.2 us)

commit v2 on v1

--- a/solution.py
+++ b/solution.py
@@ -89,32 +89,23 @@
     return jax.nn.gelu(values, approximate=True)
 
 
-def xor_gather(x, axis_name, groups):
+def xor_reduce_scatter(part, axis_name, groups, me):
     bits = groups.bit_length() - 1
-    cur = x[None]
+    cur = part
     low = 0
     while low < bits:
         width = min(2, bits - low)
-        parts = [cur]
-        for k in range(1, 1 << width):
+        fan = 1 << width
+        view = cur.reshape((cur.shape[0] // fan, fan) + cur.shape[1:])
+        mine = (me >> low) & (fan - 1)
+        total = lax.dynamic_index_in_dim(view, mine, axis=1, keepdims=False)
+        for k in range(1, fan):
             mask = k << low
-            parts.append(lax.ppermute(cur, axis_name, [(i, i ^ mask) for i in range(groups)]))
-        cur = jnp.concatenate(parts, axis=0)
+            sent = lax.dynamic_index_in_dim(view, jnp.bitwise_xor(mine, k), axis=1, keepdims=False)
+            total = total + lax.ppermute(sent, axis_name, [(i, i ^ mask) for i in range(groups)])
+        cur = total
         low += width
-    return cur
-
-
-def xor_reduce_scatter(part, axis_name, groups, me):
-    bits = groups.bit_length() - 1
-    cur = part.reshape((groups, part.shape[0] // groups) + part.shape[1:])
-    for b in range(bits):
-        pairs = cur.reshape((cur.shape[0] // 2, 2) + cur.shape[1:])
-        bit = (me >> b) & 1
-        keep = jnp.where(bit == 0, pairs[:, 0], pairs[:, 1])
-        send = jnp.where(bit == 0, pairs[:, 1], pairs[:, 0])
-        mask = 1 << b
-        cur = keep + lax.ppermute(send, axis_name, [(i, i ^ mask) for i in range(groups)])
-    return cur.reshape(cur.shape[1:])
+    return cur[0]
 
 
 def complex_apply(coeffs, weights, orders):
@@ -172,28 +163,30 @@
         plm_all = legendre_scan(cosines, sines, degrees, orders)
         quad_all = plm_all * jnp.asarray((math.pi / lat_total * sines).astype(np.float32))[None, None, :]
 
-    row_ids = jnp.arange(lat_total, dtype=jnp.int32)
-    row_cols = jnp.bitwise_xor(me, row_ids // lat_rows) * lat_rows + row_ids % lat_rows
-    slot_ids = jnp.arange(degrees, dtype=jnp.int32)
-    slot_src = jnp.bitwise_xor(me, slot_ids // per_owner) * per_owner + slot_ids % per_owner
-    slot_deg = jnp.take(slot_degree, slot_src, axis=0)
     own_deg = lax.dynamic_slice_in_dim(slot_degree, me * per_owner, per_owner)
-
-    own_quad = jnp.take(jnp.take(quad_all, own_deg, axis=0), row_cols, axis=2)
-    own_plm = jnp.take(jnp.take(plm_all, own_deg, axis=0), row_cols, axis=2)
-    rows_plm = jnp.take(lax.dynamic_slice_in_dim(plm_all, me * lat_rows, lat_rows, axis=2), slot_deg, axis=0)
-    rows_quad = jnp.take(lax.dynamic_slice_in_dim(quad_all, me * lat_rows, lat_rows, axis=2), slot_deg, axis=0)
-
-    def gather(values):
-        out = xor_gather(values, "lat", groups)
-        return out.reshape((-1,) + out.shape[2:])
+    own_quad = jnp.take(quad_all, own_deg, axis=0)
+    own_plm = jnp.take(plm_all, own_deg, axis=0)
+    rows_plm = jnp.take(lax.dynamic_slice_in_dim(plm_all, me * lat_rows, lat_rows, axis=2), slot_degree, axis=0)
+    rows_quad = jnp.take(lax.dynamic_slice_in_dim(quad_all, me * lat_rows, lat_rows, axis=2), slot_degree, axis=0)
+
+    def to_owners(table, values):
+        part = jnp.einsum("sfj,jfc->sfc", table, values, precision=highest)
+        part = part.reshape((groups, per_owner) + part.shape[1:])
+        return xor_reduce_scatter(part, "lat", groups, me)
+
+    def to_rows(table, values, extra=None):
+        part = jnp.einsum("sfj,sfc->jfc", table, values, precision=highest)
+        part = part.reshape((groups, -1))
+        if extra is not None:
+            part = jnp.concatenate([part, extra.reshape((groups, -1))], axis=1)
+        out = xor_reduce_scatter(part, "lat", groups, me)
+        size = lat_rows * 2 * orders * activations.shape[2]
+        return out[:size].reshape((lat_rows, 2 * orders, activations.shape[2])), out[size:]
 
     spectrum = jnp.einsum("jkc,kf->jfc", activations, fourier, preferred_element_type=jnp.float32)
-    all_spectrum = gather(spectrum)
-    coeffs = jnp.einsum("sfj,jfc->sfc", own_quad, all_spectrum, precision=highest).astype(jnp.bfloat16)
+    coeffs = to_owners(rows_quad, spectrum).astype(jnp.bfloat16)
     filtered = complex_apply(coeffs, spectral_weight, orders).astype(jnp.bfloat16)
-    all_filtered = gather(filtered).astype(jnp.float32)
-    grid_modes = jnp.einsum("sfj,sfc->jfc", rows_plm, all_filtered, precision=highest).astype(jnp.bfloat16)
+    grid_modes = to_rows(own_plm, filtered.astype(jnp.float32))[0].astype(jnp.bfloat16)
 
     spatial = jnp.einsum("jfc,kf->jkc", grid_modes, fourier, preferred_element_type=jnp.float32)
     skip_out = jnp.einsum("jkc,cd->jkd", activations, skip_weight, preferred_element_type=jnp.float32)
@@ -201,16 +194,15 @@
     slope_b = pullback(upstream.astype(jnp.float32))[0].astype(jnp.bfloat16)
 
     skip_terms = jnp.einsum("jkc,jkd->cd", activations, slope_b, preferred_element_type=jnp.float32)
-    grad_skip = xor_reduce_scatter(skip_terms, "lat", groups, me) * (1.0 / math.sqrt(lat_total * lon_total))
     through_skip = jnp.einsum("jkd,cd->jkc", slope_b, skip_weight, preferred_element_type=jnp.float32)
 
     mode_grads = jnp.einsum("jkc,kf->jfc", slope_b, fourier, preferred_element_type=jnp.float32)
-    all_mode_grads = gather(mode_grads)
-    coeff_grads = jnp.einsum("sfj,jfc->sfc", own_plm, all_mode_grads, precision=highest).astype(jnp.bfloat16)
+    coeff_grads = to_owners(rows_plm, mode_grads).astype(jnp.bfloat16)
     weight_grads, back_coeffs = complex_adjoint(coeffs, coeff_grads, spectral_weight, orders)
     back_b = back_coeffs.astype(jnp.bfloat16)
-    all_back = gather(back_b).astype(jnp.float32)
-    row_grads = jnp.einsum("sfj,sfc->jfc", rows_quad, all_back, precision=highest).astype(jnp.bfloat16)
+    row_sums, skip_sums = to_rows(own_quad, back_b.astype(jnp.float32), skip_terms)
+    row_grads = row_sums.astype(jnp.bfloat16)
+    grad_skip = skip_sums.reshape((-1, skip_terms.shape[1])) * (1.0 / math.sqrt(lat_total * lon_total))
     through_modes = jnp.einsum("jfc,kf->jkc", row_grads, fourier, preferred_element_type=jnp.float32)
     grad_activations = (upstream.astype(jnp.float32) + through_skip + through_modes).astype(jnp.bfloat16)
     return (grad_activations, weight_grads.astype(jnp.bfloat16), grad_skip)

time: 108 us -> 127 us (1.18)
  local copies, waits for them, and re-layouts: 25.9 us -> 37.3 us
  matrix products: 19 us -> 26.4 us
  waiting for transfers between devices: 21.9 us -> 27.6 us
  starting transfers between devices: 32 us -> 26.9 us
    unnamed x33 -> x28, local copies, waits for them, and re-layouts: 14.2 us -> 5.99 us
    dynamic_slice x1 -> x11, local copies, waits for them, and re-layouts: 1 us -> 8.24 us  [the longest x4 5.2 us: xor_reduce_scatter(): total = lax.dynamic_index_in_dim(view, mine, axis=1, keepdims=False)]
    another operation x0 -> x3, local copies, waits for them, and re-layouts: none -> 5.83 us  [xor_reduce_scatter(): view = cur.reshape((cur.shape[0] // fan, fan) + cur.shape[1:])]
    ppermute x28 -> x24, waiting for transfers between devices: 21.9 us -> 27.6 us  [xor_reduce_scatter(): lax.ppermute(sent, axis_name, [(i, i ^ mask) for i in range(groups)])]
    dot_general x1, matrix products: 0.78 us -> 5.99 us  [local(): jnp.einsum('jfc,kf->jkc', grid_modes, fourier, preferred_element_type=jnp...]
    ppermute x28 -> x24, starting transfers between devices: 32 us -> 26.9 us  [xor_reduce_scatter(): lax.ppermute(sent, axis_name, [(i, i ^ mask) for i in range(groups)])]
    concatenate x4 -> x3, local copies, waits for them, and re-layouts: 1.29 us -> 5.25 us  [to_rows(): part = jnp.concatenate([part, extra.reshape((groups, -1))], axis=1)]
    gather x5 -> x2, local copies, waits for them, and re-layouts: 5.43 us -> 2.9 us  [the longest x1 1.45 us: local(): own_plm = jnp.take(plm_all, own_deg, axis=0)]
  transfers between devices with their start and end apart: 28 -> 24, of which waited for: 9 -> 11; matrix products, arithmetic and copies ran while one was open for 32% -> 15% of each run, Pallas kernels for 0% -> 0%
where the time goes in v2:
time: 127 us; the launch traced here: 126 us
  local copies, waits for them, and re-layouts  37.3 us (29%)
  waiting for transfers between devices  27.6 us (22%)
  starting transfers between devices  26.9 us (21%)
  matrix products  26.4 us (21%)
  other arithmetic  7.11 us (6%)
    ppermute x24, waiting for transfers between devices, xor_reduce_scatter(): lax.ppermute(sent, axis_name, [(i, i ^ mask) for i in range(groups)])  27.6 us
    ppermute x24, starting transfers between devices, xor_reduce_scatter(): lax.ppermute(sent, axis_name, [(i, i ^ mask) for i in range(groups)])  26.9 us
    unnamed x28, local copies, waits for them, and re-layouts  5.99 us
    dot_general x1, matrix products, local(): jnp.einsum('jfc,kf->jkc', grid_modes, fourier, preferred_element_type=jnp...  5.99 us
    another operation x3, local copies, waits for them, and re-layouts, xor_reduce_scatter(): view = cur.reshape((cur.shape[0] // fan, fan) + cur.shape[1:])  5.83 us
    concatenate x3, local copies, waits for them, and re-layouts, to_rows(): part = jnp.concatenate([part, extra.reshape((groups, -1))], axis=1)  5.25 us
    dynamic_slice x4, local copies, waits for them, and re-layouts, xor_reduce_scatter(): total = lax.dynamic_index_in_dim(view, mine, axis=1, keepdims=False)  5.2 us
    dot_general x1, matrix products, local(): jnp.einsum('jkc,jkd->cd', activations, slope_b, preferred_element_type=jn...  3.82 us
  transfers between devices with their start and end apart: 24, of which 11 were waited for; matrix products, arithmetic and copies ran while one was open for 15% of the time, Pallas kernels for 0%

profile of v2, /device:TPU:0, one launch (start us, length us, event | category | flops | bytes accessed | tf_op | source)
XLA Modules:
  0.0 126.3 jit_solution(17513045027118694920)
XLA Ops:
  8.3 2.0 %reshape_reshape.9 = f32[4,4,2,8,384]{4,2,1,0,3:T(2,128)} reshape(f32[32,8,384]{2,0,1:T(8,128)} %convolution_bitcast_fusion.4) | data formatting | bytes 786432 | tf_op jit(solution)/shard_map/reshape;reshape | solution.py:99
  12.1 2.4 %collective-permute-start.2 = (f32[4,2,8,384]{3,2,1,0:T(8,128)}, f32[4,2,8,384]{3,2,1,0:T(8,128)}, u32[]{:S(2)}, u32[]{:S(2)}) collective-permute-start(f32[4,2,8,384]{3,2,1,0:T(8,128)} %bitcast.131), channel_id=1, source_target_pairs={{0,3},{1,2},{2,1},{3,0},{4,7},{5,6},{6,5},{7,4},{8,11},{9,10},{10,... | collective-permute-start | bytes 294920 | tf_op jit(solution)/shard_map/ppermute | solution.py:105
  16.5 1.4 %gather_fusion.3 = f32[2,8,32]{2,1,0:T(8,128)S(1)} fusion(f32[32,8,32]{2,1,0:T(8,128)} %constant.133.clone2.1, s32[1024]{0:T(1024)S(1)} %get-tuple-element.47), kind=kCustom, calls=%fused_computation.3.clone | custom fusion | bytes 4104 | tf_op jit(solution)/shard_map/jit(_take)/gather | solution.py:167
  17.9 1.5 %gather_fusion.1 = f32[2,8,32]{2,1,0:T(8,128)S(1)} fusion(f32[32,8,32]{2,1,0:T(8,128)} %constant.132.clone2.1, s32[1024]{0:T(1024)S(1)} %get-tuple-element.47), kind=kCustom, calls=%fused_computation.1.clone | custom fusion | bytes 4104 | tf_op jit(solution)/shard_map/jit(_take)/gather | solution.py:168
  19.4 1.4 %collective-permute-done.1 = f32[4,2,8,384]{3,2,1,0:T(8,128)} collective-permute-done((f32[4,2,8,384]{3,2,1,0:T(8,128)}, f32[4,2,8,384]{3,2,1,0:T(8,128)}, u32[]{:S(2)}, u32[]{:S(2)}) %collective-permute-start.1) | collective-permute-done | bytes 98336 | tf_op jit(solution)/shard_map/ppermute | solution.py:105
  23.1 3.8 %collective-permute-start.5 = (f32[1,2,8,384]{3,2,1,0:T(8,128)}, f32[1,2,8,384]{3,2,1,0:T(8,128)S(1)}, u32[]{:S(2)}, u32[]{:S(2)}) collective-permute-start(f32[1,2,8,384]{3,2,1,0:T(8,128)} %get-tuple-element.39), channel_id=1, source_target_pairs={{0,12},{1,13},{2,14},{3,15},{4,8},{5,9},{6,10},{7,11},{8,4},{9,5},... | collective-permute-start | bytes 73736 | tf_op jit(solution)/shard_map/ppermute | solution.py:105
  27.6 1.4 %collective-permute-done.5 = f32[1,2,8,384]{3,2,1,0:T(8,128)S(1)} collective-permute-done((f32[1,2,8,384]{3,2,1,0:T(8,128)}, f32[1,2,8,384]{3,2,1,0:T(8,128)S(1)}, u32[]{:S(2)}, u32[]{:S(2)}) %collective-permute-start.5) | collective-permute-done | bytes 24608 | tf_op jit(solution)/shard_map/ppermute | solution.py:105
  28.9 2.7 %collective-permute-done.4 = f32[1,2,8,384]{3,2,1,0:T(8,128)S(1)} collective-permute-done((f32[1,2,8,384]{3,2,1,0:T(8,128)S(1)}, f32[1,2,8,384]{3,2,1,0:T(8,128)S(1)}, u32[]{:S(2)}, u32[]{:S(2)}) %collective-permute-start.4) | collective-permute-done | bytes 24608 | tf_op jit(solution)/shard_map/ppermute | solution.py:105
  34.6 1.9 %reshape_reshape.10 = f32[4,4,6144]{2,1,0:T(4,128)} reshape(f32[32,8,384]{2,1,0:T(8,128)} %copy.26) | data formatting | bytes 786432 | tf_op jit(solution)/shard_map/reshape;reshape | solution.py:99
  36.5 2.1 %constant_dynamic-slice_fusion.21 = (f32[4,1,6144]{2,1,0:T(1,128)S(1)}, f32[4,1,6144]{2,1,0:T(1,128)S(1)}, f32[4,1,6144]{2,1,0:T(1,128)S(1)}, f32[4,1,6144]{2,1,0:T(1,128)S(1)}) fusion(f32[4,4,6144]{2,1,0:T(4,128)} %reshape_reshape.10, s32[]{:T(128)S(6)} %select_n.74, s32[]{:T(128)S(6)} %select_n.77, s32[]{:T(128)S(6)} %select_n.76, s32[]{:T(128)S(6)} %select_n.75), kind=kLoop, calls=%fused_computation.136 | loop fusion | bytes 786448 | tf_op jit(solution)/shard_map/jit(dynamic_index_in_dim)/dynamic_slice | solution.py:101
  38.8 1.5 %collective-permute-start.7 = (f32[4,6144]{1,0:T(4,128)S(1)}, f32[4,6144]{1,0:T(4,128)S(1)}, u32[]{:S(2)}, u32[]{:S(2)}) collective-permute-start(f32[4,6144]{1,0:T(4,128)S(1)} %bitcast.139), channel_id=1, source_target_pairs={{0,2},{1,3},{2,0},{3,1},{4,6},{5,7},{6,4},{7,5},{8,10},{9,11},{10,... | collective-permute-start | bytes 294920 | tf_op jit(solution)/shard_map/ppermute | solution.py:105
  40.8 2.9 %collective-permute-done.8 = f32[4,6144]{1,0:T(4,128)S(1)} collective-permute-done((f32[4,6144]{1,0:T(4,128)S(1)}, f32[4,6144]{1,0:T(4,128)S(1)}, u32[]{:S(2)}, u32[]{:S(2)}) %collective-permute-start.8) | collective-permute-done | bytes 98336 | tf_op jit(solution)/shard_map/ppermute | solution.py:105
  43.7 2.2 %collective-permute-done.7 = f32[4,6144]{1,0:T(4,128)S(1)} collective-permute-done((f32[4,6144]{1,0:T(4,128)S(1)}, f32[4,6144]{1,0:T(4,128)S(1)}, u32[]{:S(2)}, u32[]{:S(2)}) %collective-permute-start.7) | collective-permute-done | bytes 98336 | tf_op jit(solution)/shard_map/ppermute | solution.py:105
  46.7 1.6 %collective-permute-start.11 = (f32[1,6144]{1,0:T(1,128)}, f32[1,6144]{1,0:T(1,128)}, u32[]{:S(2)}, u32[]{:S(2)}) collective-permute-start(f32[1,6144]{1,0:T(1,128)} %get-tuple-element.36), channel_id=1, source_target_pairs={{0,12},{1,13},{2,14},{3,15},{4,8},{5,9},{6,10},{7,11},{8,4},{9,5},... | collective-permute-start | bytes 73736 | tf_op jit(solution)/shard_map/ppermute | solution.py:105
  48.8 2.3 %collective-permute-start.9 = (f32[1,6144]{1,0:T(1,128)}, f32[1,6144]{1,0:T(1,128)}, u32[]{:S(2)}, u32[]{:S(2)}) collective-permute-start(f32[1,6144]{1,0:T(1,128)} %get-tuple-element.35), channel_id=1, source_target_pairs={{0,4},{1,5},{2,6},{3,7},{4,0},{5,1},{6,2},{7,3},{8,12},{9,13},{10,... | collective-permute-start | bytes 73736 | tf_op jit(solution)/shard_map/ppermute | solution.py:105
  51.1 3.5 %fusion.41 = f32[2,1440,384]{2,1,0:T(8,128)} fusion(bf16[2,1440,384]{2,1,0:T(8,128)(2,1)S(1)} %copy-done, bf16[384,384]{1,0:T(8,128)(2,1)S(1)} %copy-done.6), kind=kOutput, calls=%fused_computation.59 | convolution fusion | flops 849346560 | bytes 6930432 | tf_op jit(solution)/shard_map/jkc,cd->jkd/dot_general | solution.py:192
  56.4 6.0 %fusion.6 = bf16[2,1440,384]{2,1,0:T(8,128)(2,1)S(1)} fusion(bf16[2,1440,384]{2,1,0:T(8,128)(2,1)} %param.13, f32[2,1440,384]{2,1,0:T(8,128)} %fusion.41, bf16[2,8,384]{2,1,0:T(8,128)(2,1)S(1)} %convert_element_type.41, bf16[1440,8,1]{0,1,2:T(8,128)(2,1)S(1)} %copy-done.9), kind=kOutput, calls=%fused_computation.15 | convolution fusion | flops 42024960 | bytes 8882688 | tf_op jit(solution)/shard_map/jfc,kf->jkc/dot_general | solution.py:191
  65.4 2.0 %reshape_reshape.11 = f32[4,4,2,8,384]{4,2,1,0,3:T(2,128)} reshape(f32[32,8,384]{2,0,1:T(8,128)} %convolution_bitcast_fusion.2) | data formatting | bytes 786432 | tf_op jit(solution)/shard_map/reshape;reshape | solution.py:99
  70.6 3.0 %collective-permute-done.14 = f32[4,2,8,384]{3,2,1,0:T(8,128)S(1)} collective-permute-done((f32[4,2,8,384]{3,2,1,0:T(8,128)S(1)}, f32[4,2,8,384]{3,2,1,0:T(8,128)S(1)}, u32[]{:S(2)}, u32[]{:S(2)}) %collective-permute-start.14) | collective-permute-done | bytes 98336 | tf_op jit(solution)/shard_map/ppermute | solution.py:105
  75.3 1.6 %collective-permute-start.17 = (f32[1,2,8,384]{3,2,1,0:T(8,128)}, f32[1,2,8,384]{3,2,1,0:T(8,128)}, u32[]{:S(2)}, u32[]{:S(2)}) collective-permute-start(f32[1,2,8,384]{3,2,1,0:T(8,128)} %get-tuple-element.33), channel_id=1, source_target_pairs={{0,12},{1,13},{2,14},{3,15},{4,8},{5,9},{6,10},{7,11},{8,4},{9,5},... | collective-permute-start | bytes 73736 | tf_op jit(solution)/shard_map/ppermute | solution.py:105
  77.3 2.4 %collective-permute-start.15 = (f32[1,2,8,384]{3,2,1,0:T(8,128)}, f32[1,2,8,384]{3,2,1,0:T(8,128)}, u32[]{:S(2)}, u32[]{:S(2)}) collective-permute-start(f32[1,2,8,384]{3,2,1,0:T(8,128)} %get-tuple-element.32), channel_id=1, source_target_pairs={{0,4},{1,5},{2,6},{3,7},{4,0},{5,1},{6,2},{7,3},{8,12},{9,13},{10,... | collective-permute-start | bytes 73736 | tf_op jit(solution)/shard_map/ppermute | solution.py:105
  79.7 3.8 %convolution_bitcast_fusion = f32[384,384]{0,1:T(8,128)} fusion(bf16[2,1440,384]{2,1,0:T(8,128)(2,1)} %copy-done.1, bf16[2,1440,384]{2,1,0:T(8,128)(2,1)S(1)} %copy-done), kind=kOutput, calls=%fused_computation.26 | convolution fusion | flops 849346560 | bytes 5013504 | tf_op jit(solution)/shard_map/jkc,jkd->cd/dot_general | solution.py:196
  83.5 2.2 %copy.34 = f32[384,384]{1,0:T(8,128)} copy(f32[384,384]{0,1:T(8,128)} %convolution_bitcast_fusion) | data formatting | bytes 1179648 | tf_op jit(solution)/shard_map/jkc,jkd->cd/dot_general | solution.py:196
  85.7 2.1 %concatenate.19 = f32[4,4,9216]{2,1,0:T(4,128)} reshape(f32[384,384]{1,0:T(8,128)} %copy.34) | data formatting | bytes 1179648 | tf_op jit(solution)/shard_map/concatenate | solution.py:181
  89.7 1.4 %fusion.76 = f32[2,384,384]{2,1,0:T(8,128)} fusion(bf16[2,8,384]{2,1,0:T(8,128)(2,1)S(1)} %fusion.58, bf16[2,8,384]{2,1,0:T(8,128)(2,1)S(1)} %fusion.57), kind=kOutput, calls=%fused_computation.162 | convolution fusion | flops 2359296 | bytes 1191936 | tf_op jit(solution)/shard_map/smc,smd->scd/dot_general | solution.py:129
  93.0 1.9 %concatenate.18 = f32[4,4,6144]{2,1,0:T(4,128)} reshape(f32[32,8,384]{2,1,0:T(8,128)} %copy.33) | data formatting | bytes 786432 | tf_op jit(solution)/shard_map/concatenate | solution.py:181
  101.0 5.4 %collective-permute-done.20 = f32[4,15360]{1,0:T(4,128)S(1)} collective-permute-done((f32[4,15360]{1,0:T(4,128)S(1)}, f32[4,15360]{1,0:T(4,128)S(1)}, u32[]{:S(2)}, u32[]{:S(2)}) %collective-permute-start.20) | collective-permute-done | bytes 245792 | tf_op jit(solution)/shard_map/ppermute | solution.py:105
  106.4 4.9 %collective-permute-done.19 = f32[4,15360]{1,0:T(4,128)S(1)} collective-permute-done((f32[4,15360]{1,0:T(4,128)S(1)}, f32[4,15360]{1,0:T(4,128)S(1)}, u32[]{:S(2)}, u32[]{:S(2)}) %collective-permute-start.19) | collective-permute-done | bytes 245792 | tf_op jit(solution)/shard_map/ppermute | solution.py:105
  111.6 1.9 %collective-permute-start.23 = (f32[1,15360]{1,0:T(1,128)S(1)}, f32[1,15360]{1,0:T(1,128)S(1)}, u32[]{:S(2)}, u32[]{:S(2)}) collective-permute-start(f32[1,15360]{1,0:T(1,128)S(1)} %get-tuple-element.30), channel_id=1, source_target_pairs={{0,12},{1,13},{2,14},{3,15},{4,8},{5,9},{6,10},{7,11},{8,4},{9,5},... | collective-permute-start | bytes 184328 | tf_op jit(solution)/shard_map/ppermute | solution.py:105
  113.5 2.5 %collective-permute-start.21 = (f32[1,15360]{1,0:T(1,128)S(1)}, f32[1,15360]{1,0:T(1,128)S(1)}, u32[]{:S(2)}, u32[]{:S(2)}) collective-permute-start(f32[1,15360]{1,0:T(1,128)S(1)} %get-tuple-element.29), channel_id=1, source_target_pairs={{0,4},{1,5},{2,6},{3,7},{4,0},{5,1},{6,2},{7,3},{8,12},{9,13},{10,... | collective-permute-start | bytes 184328 | tf_op jit(solution)/shard_map/ppermute | solution.py:105
  118.3 1.8 %collective-permute-done.22 = f32[1,15360]{1,0:T(1,128)S(1)} collective-permute-done((f32[1,15360]{1,0:T(1,128)S(1)}, f32[1,15360]{1,0:T(1,128)S(1)}, u32[]{:S(2)}, u32[]{:S(2)}) %collective-permute-start.22) | collective-permute-done | bytes 61472 | tf_op jit(solution)/shard_map/ppermute | solution.py:105
  122.7 3.0 %fusion.11 = bf16[2,1440,384]{2,1,0:T(8,128)(2,1)} fusion(bf16[2,1440,384]{2,1,0:T(8,128)(2,1)S(1)} %copy-done.5, f32[2,384,1440]{1,2,0:T(8,128)S(1)} %fusion.93, bf16[2,1440,384]{2,1,0:T(8,128)(2,1)S(1)} %copy-done.2, bf16[384,384]{1,0:T(8,128)(2,1)S(1)} %copy-done.7), kind=kOutput, calls=%fused_computation.20 | convolution fusion | flops 853770240 | bytes 11354112 | tf_op jit(solution)/shard_map/jkd,cd->jkc/dot_general | solution.py:197
  (121 shorter events, 44.9 us)
Async XLA Ops:
  0.6 5.3 %copy-start = (bf16[2,1440,384]{2,1,0:T(8,128)(2,1)S(1)}, bf16[2,1440,384]{2,1,0:T(8,128)(2,1)}, u32[]{:S(2)}) copy-start(bf16[2,1440,384]{2,1,0:T(8,128)(2,1)} %param.12) | copy-start | bytes 6635524
  7.0 25.4 %copy-start.3 = (bf16[2,2,384,384]{3,2,1,0:T(8,128)(2,1)S(1)}, bf16[2,2,384,384]{3,2,1,0:T(8,128)(2,1)}, u32[]{:S(2)}) copy-start(bf16[2,2,384,384]{3,2,1,0:T(8,128)(2,1)} %param.15) | copy-start | bytes 3538948
  12.1 7.4 %collective-permute-start.2 = (f32[4,2,8,384]{3,2,1,0:T(8,128)}, f32[4,2,8,384]{3,2,1,0:T(8,128)}, u32[]{:S(2)}, u32[]{:S(2)}) collective-permute-start(f32[4,2,8,384]{3,2,1,0:T(8,128)} %bitcast.131), channel_id=1, source_target_pairs={{0,3},{1,2},{2,1},{3,0},{4,7},{5,6},{6,5},{7,4},{8,11},{9,10},{10,... | collective-permute-start | bytes 294920 | tf_op jit(solution)/shard_map/ppermute | solution.py:105
  15.1 5.7 %collective-permute-start.1 = (f32[4,2,8,384]{3,2,1,0:T(8,128)}, f32[4,2,8,384]{3,2,1,0:T(8,128)}, u32[]{:S(2)}, u32[]{:S(2)}) collective-permute-start(f32[4,2,8,384]{3,2,1,0:T(8,128)} %bitcast.132), channel_id=1, source_target_pairs={{0,2},{1,3},{2,0},{3,1},{4,6},{5,7},{6,4},{7,5},{8,10},{9,11},{10,... | collective-permute-start | bytes 294920 | tf_op jit(solution)/shard_map/ppermute | solution.py:105
  16.4 4.5 %collective-permute-start = (f32[4,2,8,384]{3,2,1,0:T(8,128)}, f32[4,2,8,384]{3,2,1,0:T(8,128)}, u32[]{:S(2)}, u32[]{:S(2)}) collective-permute-start(f32[4,2,8,384]{3,2,1,0:T(8,128)} %bitcast.133), channel_id=1, source_target_pairs={{0,1},{1,0},{2,3},{3,2},{4,5},{5,4},{6,7},{7,6},{8,9},{9,8},{10,11... | collective-permute-start | bytes 294920 | tf_op jit(solution)/shard_map/ppermute | solution.py:105
  23.1 5.8 %collective-permute-start.5 = (f32[1,2,8,384]{3,2,1,0:T(8,128)}, f32[1,2,8,384]{3,2,1,0:T(8,128)S(1)}, u32[]{:S(2)}, u32[]{:S(2)}) collective-permute-start(f32[1,2,8,384]{3,2,1,0:T(8,128)} %get-tuple-element.39), channel_id=1, source_target_pairs={{0,12},{1,13},{2,14},{3,15},{4,8},{5,9},{6,10},{7,11},{8,4},{9,5},... | collective-permute-start | bytes 73736 | tf_op jit(solution)/shard_map/ppermute | solution.py:105
  26.9 4.7 %collective-permute-start.4 = (f32[1,2,8,384]{3,2,1,0:T(8,128)S(1)}, f32[1,2,8,384]{3,2,1,0:T(8,128)S(1)}, u32[]{:S(2)}, u32[]{:S(2)}) collective-permute-start(f32[1,2,8,384]{3,2,1,0:T(8,128)S(1)} %get-tuple-element.40), channel_id=1, source_target_pairs={{0,8},{1,9},{2,10},{3,11},{4,12},{5,13},{6,14},{7,15},{8,0},{9,1},... | collective-permute-start | bytes 73736 | tf_op jit(solution)/shard_map/ppermute | solution.py:105
  26.9 4.7 %collective-permute-start.3 = (f32[1,2,8,384]{3,2,1,0:T(8,128)S(1)}, f32[1,2,8,384]{3,2,1,0:T(8,128)}, u32[]{:S(2)}, u32[]{:S(2)}) collective-permute-start(f32[1,2,8,384]{3,2,1,0:T(8,128)S(1)} %get-tuple-element.38), channel_id=1, source_target_pairs={{0,4},{1,5},{2,6},{3,7},{4,0},{5,1},{6,2},{7,3},{8,12},{9,13},{10,... | collective-permute-start | bytes 73736 | tf_op jit(solution)/shard_map/ppermute | solution.py:105
  36.5 14.6 %copy-start.6 = (bf16[384,384]{1,0:T(8,128)(2,1)S(1)}, bf16[384,384]{1,0:T(8,128)(2,1)}, u32[]{:S(2)}) copy-start(bf16[384,384]{1,0:T(8,128)(2,1)} %param.14) | copy-start | bytes 884740
  38.6 5.1 %collective-permute-start.8 = (f32[4,6144]{1,0:T(4,128)S(1)}, f32[4,6144]{1,0:T(4,128)S(1)}, u32[]{:S(2)}, u32[]{:S(2)}) collective-permute-start(f32[4,6144]{1,0:T(4,128)S(1)} %bitcast.137), channel_id=1, source_target_pairs={{0,3},{1,2},{2,1},{3,0},{4,7},{5,6},{6,5},{7,4},{8,11},{9,10},{10,... | collective-permute-start | bytes 294920 | tf_op jit(solution)/shard_map/ppermute | solution.py:105
  38.8 7.1 %collective-permute-start.7 = (f32[4,6144]{1,0:T(4,128)S(1)}, f32[4,6144]{1,0:T(4,128)S(1)}, u32[]{:S(2)}, u32[]{:S(2)}) collective-permute-start(f32[4,6144]{1,0:T(4,128)S(1)} %bitcast.139), channel_id=1, source_target_pairs={{0,2},{1,3},{2,0},{3,1},{4,6},{5,7},{6,4},{7,5},{8,10},{9,11},{10,... | collective-permute-start | bytes 294920 | tf_op jit(solution)/shard_map/ppermute | solution.py:105
  40.4 5.5 %collective-permute-start.6 = (f32[4,6144]{1,0:T(4,128)S(1)}, f32[4,6144]{1,0:T(4,128)S(1)}, u32[]{:S(2)}, u32[]{:S(2)}) collective-permute-start(f32[4,6144]{1,0:T(4,128)S(1)} %bitcast.141), channel_id=1, source_target_pairs={{0,1},{1,0},{2,3},{3,2},{4,5},{5,4},{6,7},{7,6},{8,9},{9,8},{10,11... | collective-permute-start | bytes 294920 | tf_op jit(solution)/shard_map/ppermute | solution.py:105
  46.7 8.8 %collective-permute-start.11 = (f32[1,6144]{1,0:T(1,128)}, f32[1,6144]{1,0:T(1,128)}, u32[]{:S(2)}, u32[]{:S(2)}) collective-permute-start(f32[1,6144]{1,0:T(1,128)} %get-tuple-element.36), channel_id=1, source_target_pairs={{0,12},{1,13},{2,14},{3,15},{4,8},{5,9},{6,10},{7,11},{8,4},{9,5},... | collective-permute-start | bytes 73736 | tf_op jit(solution)/shard_map/ppermute | solution.py:105
  48.2 7.2 %collective-permute-start.10 = (f32[1,6144]{1,0:T(1,128)}, f32[1,6144]{1,0:T(1,128)}, u32[]{:S(2)}, u32[]{:S(2)}) collective-permute-start(f32[1,6144]{1,0:T(1,128)} %get-tuple-element.37), channel_id=1, source_target_pairs={{0,8},{1,9},{2,10},{3,11},{4,12},{5,13},{6,14},{7,15},{8,0},{9,1},... | collective-permute-start | bytes 73736 | tf_op jit(solution)/shard_map/ppermute | solution.py:105
  48.8 7.5 %copy-start.9 = (bf16[1440,8,1]{0,1,2:T(8,128)(2,1)S(1)}, bf16[1440,8,1]{0,1,2:T(8,128)(2,1)}, u32[]{:S(2)}) copy-start(bf16[1440,8,1]{0,1,2:T(8,128)(2,1)} %constant.137) | copy-start | bytes 69124
  48.8 6.6 %collective-permute-start.9 = (f32[1,6144]{1,0:T(1,128)}, f32[1,6144]{1,0:T(1,128)}, u32[]{:S(2)}, u32[]{:S(2)}) collective-permute-start(f32[1,6144]{1,0:T(1,128)} %get-tuple-element.35), channel_id=1, source_target_pairs={{0,4},{1,5},{2,6},{3,7},{4,0},{5,1},{6,2},{7,3},{8,12},{9,13},{10,... | collective-permute-start | bytes 73736 | tf_op jit(solution)/shard_map/ppermute | solution.py:105
  62.4 1.4 %copy-start.1 = (bf16[2,1440,384]{2,1,0:T(8,128)(2,1)}, bf16[2,1440,384]{2,1,0:T(8,128)(2,1)S(1)}, u32[]{:S(2)}) copy-start(bf16[2,1440,384]{2,1,0:T(8,128)(2,1)S(1)} %fusion.6) | copy-start | bytes 6635524
  68.5 5.1 %collective-permute-start.14 = (f32[4,2,8,384]{3,2,1,0:T(8,128)S(1)}, f32[4,2,8,384]{3,2,1,0:T(8,128)S(1)}, u32[]{:S(2)}, u32[]{:S(2)}) collective-permute-start(f32[4,2,8,384]{3,2,1,0:T(8,128)S(1)} %bitcast.138), channel_id=1, source_target_pairs={{0,3},{1,2},{2,1},{3,0},{4,7},{5,6},{6,5},{7,4},{8,11},{9,10},{10,... | collective-permute-start | bytes 294920 | tf_op jit(solution)/shard_map/ppermute | solution.py:105
  68.7 6.0 %collective-permute-start.13 = (f32[4,2,8,384]{3,2,1,0:T(8,128)S(1)}, f32[4,2,8,384]{3,2,1,0:T(8,128)S(1)}, u32[]{:S(2)}, u32[]{:S(2)}) collective-permute-start(f32[4,2,8,384]{3,2,1,0:T(8,128)S(1)} %bitcast.140), channel_id=1, source_target_pairs={{0,2},{1,3},{2,0},{3,1},{4,6},{5,7},{6,4},{7,5},{8,10},{9,11},{10,... | collective-permute-start | bytes 294920 | tf_op jit(solution)/shard_map/ppermute | solution.py:105
  69.5 5.1 %collective-permute-start.12 = (f32[4,2,8,384]{3,2,1,0:T(8,128)S(1)}, f32[4,2,8,384]{3,2,1,0:T(8,128)S(1)}, u32[]{:S(2)}, u32[]{:S(2)}) collective-permute-start(f32[4,2,8,384]{3,2,1,0:T(8,128)S(1)} %bitcast.142), channel_id=1, source_target_pairs={{0,1},{1,0},{2,3},{3,2},{4,5},{5,4},{6,7},{7,6},{8,9},{9,8},{10,11... | collective-permute-start | bytes 294920 | tf_op jit(solution)/shard_map/ppermute | solution.py:105
  75.3 12.5 %collective-permute-start.17 = (f32[1,2,8,384]{3,2,1,0:T(8,128)}, f32[1,2,8,384]{3,2,1,0:T(8,128)}, u32[]{:S(2)}, u32[]{:S(2)}) collective-permute-start(f32[1,2,8,384]{3,2,1,0:T(8,128)} %get-tuple-element.33), channel_id=1, source_target_pairs={{0,12},{1,13},{2,14},{3,15},{4,8},{5,9},{6,10},{7,11},{8,4},{9,5},... | collective-permute-start | bytes 73736 | tf_op jit(solution)/shard_map/ppermute | solution.py:105
  76.9 10.9 %collective-permute-start.16 = (f32[1,2,8,384]{3,2,1,0:T(8,128)}, f32[1,2,8,384]{3,2,1,0:T(8,128)}, u32[]{:S(2)}, u32[]{:S(2)}) collective-permute-start(f32[1,2,8,384]{3,2,1,0:T(8,128)} %get-tuple-element.34), channel_id=1, source_target_pairs={{0,8},{1,9},{2,10},{3,11},{4,12},{5,13},{6,14},{7,15},{8,0},{9,1},... | collective-permute-start | bytes 73736 | tf_op jit(solution)/shard_map/ppermute | solution.py:105
  77.3 10.6 %collective-permute-start.15 = (f32[1,2,8,384]{3,2,1,0:T(8,128)}, f32[1,2,8,384]{3,2,1,0:T(8,128)}, u32[]{:S(2)}, u32[]{:S(2)}) collective-permute-start(f32[1,2,8,384]{3,2,1,0:T(8,128)} %get-tuple-element.32), channel_id=1, source_target_pairs={{0,4},{1,5},{2,6},{3,7},{4,0},{5,1},{6,2},{7,3},{8,12},{9,13},{10,... | collective-permute-start | bytes 73736 | tf_op jit(solution)/shard_map/ppermute | solution.py:105
  95.9 4.4 %copy-start.4 = (f32[2,384,384]{2,1,0:T(8,128)S(1)}, f32[2,384,384]{2,1,0:T(8,128)}, u32[]{:S(2)}) copy-start(f32[2,384,384]{2,1,0:T(8,128)} %fusion.76) | copy-start | bytes 3538948
  98.1 8.3 %collective-permute-start.20 = (f32[4,15360]{1,0:T(4,128)S(1)}, f32[4,15360]{1,0:T(4,128)S(1)}, u32[]{:S(2)}, u32[]{:S(2)}) collective-permute-start(f32[4,15360]{1,0:T(4,128)S(1)} %bitcast.134), channel_id=1, source_target_pairs={{0,3},{1,2},{2,1},{3,0},{4,7},{5,6},{6,5},{7,4},{8,11},{9,10},{10,... | collective-permute-start | bytes 737288 | tf_op jit(solution)/shard_map/ppermute | solution.py:105
  98.2 13.0 %collective-permute-start.19 = (f32[4,15360]{1,0:T(4,128)S(1)}, f32[4,15360]{1,0:T(4,128)S(1)}, u32[]{:S(2)}, u32[]{:S(2)}) collective-permute-start(f32[4,15360]{1,0:T(4,128)S(1)} %bitcast.135), channel_id=1, source_target_pairs={{0,2},{1,3},{2,0},{3,1},{4,6},{5,7},{6,4},{7,5},{8,10},{9,11},{10,... | collective-permute-start | bytes 737288 | tf_op jit(solution)/shard_map/ppermute | solution.py:105
  99.6 11.7 %collective-permute-start.18 = (f32[4,15360]{1,0:T(4,128)S(1)}, f32[4,15360]{1,0:T(4,128)S(1)}, u32[]{:S(2)}, u32[]{:S(2)}) collective-permute-start(f32[4,15360]{1,0:T(4,128)S(1)} %bitcast.136), channel_id=1, source_target_pairs={{0,1},{1,0},{2,3},{3,2},{4,5},{5,4},{6,7},{7,6},{8,9},{9,8},{10,11... | collective-permute-start | bytes 737288 | tf_op jit(solution)/shard_map/ppermute | solution.py:105
  111.6 6.7 %collective-permute-start.23 = (f32[1,15360]{1,0:T(1,128)S(1)}, f32[1,15360]{1,0:T(1,128)S(1)}, u32[]{:S(2)}, u32[]{:S(2)}) collective-permute-start(f32[1,15360]{1,0:T(1,128)S(1)} %get-tuple-element.30), channel_id=1, source_target_pairs={{0,12},{1,13},{2,14},{3,15},{4,8},{5,9},{6,10},{7,11},{8,4},{9,5},... | collective-permute-start | bytes 184328 | tf_op jit(solution)/shard_map/ppermute | solution.py:105
  113.5 6.6 %collective-permute-start.22 = (f32[1,15360]{1,0:T(1,128)S(1)}, f32[1,15360]{1,0:T(1,128)S(1)}, u32[]{:S(2)}, u32[]{:S(2)}) collective-permute-start(f32[1,15360]{1,0:T(1,128)S(1)} %get-tuple-element.31), channel_id=1, source_target_pairs={{0,8},{1,9},{2,10},{3,11},{4,12},{5,13},{6,14},{7,15},{8,0},{9,1},... | collective-permute-start | bytes 184328 | tf_op jit(solution)/shard_map/ppermute | solution.py:105
  113.5 6.6 %collective-permute-start.21 = (f32[1,15360]{1,0:T(1,128)S(1)}, f32[1,15360]{1,0:T(1,128)S(1)}, u32[]{:S(2)}, u32[]{:S(2)}) collective-permute-start(f32[1,15360]{1,0:T(1,128)S(1)} %get-tuple-element.29), channel_id=1, source_target_pairs={{0,4},{1,5},{2,6},{3,7},{4,0},{5,1},{6,2},{7,3},{8,12},{9,13},{10,... | collective-permute-start | bytes 184328 | tf_op jit(solution)/shard_map/ppermute | solution.py:105
  120.4 1.6 %copy-start.2 = (bf16[2,1440,384]{2,1,0:T(8,128)(2,1)S(1)}, bf16[2,1440,384]{2,1,0:T(8,128)(2,1)}, u32[]{:S(2)}) copy-start(bf16[2,1440,384]{2,1,0:T(8,128)(2,1)} %copy-done.1) | copy-start | bytes 6635524
  120.4 2.3 %copy-start.5 = (bf16[2,1440,384]{2,1,0:T(8,128)(2,1)S(1)}, bf16[2,1440,384]{2,1,0:T(8,128)(2,1)}, u32[]{:S(2)}) copy-start(bf16[2,1440,384]{2,1,0:T(8,128)(2,1)} %param.13) | copy-start | bytes 6635524
  (2 other events, 1.8 us)

commit v3 on v2

--- a/solution.py
+++ b/solution.py
@@ -89,22 +89,54 @@
     return jax.nn.gelu(values, approximate=True)
 
 
-def xor_reduce_scatter(part, axis_name, groups, me):
+def xor_gather_parts(x, axis_name, groups):
     bits = groups.bit_length() - 1
-    cur = part
+    parts = [x[None]]
     low = 0
     while low < bits:
         width = min(2, bits - low)
+        cur = parts[0] if len(parts) == 1 else jnp.concatenate(parts, axis=0)
+        parts = [cur]
+        for k in range(1, 1 << width):
+            mask = k << low
+            parts.append(lax.ppermute(cur, axis_name, [(i, i ^ mask) for i in range(groups)]))
+        low += width
+    return parts
+
+
+def xor_blocks(table, me, groups, axis):
+    bits = groups.bit_length() - 1
+    shape = table.shape
+    size = shape[axis] // groups
+    for b in range(bits):
+        view = table.reshape(shape[:axis] + (groups >> (b + 1), 2, size << b) + shape[axis + 1:])
+        swapped = jnp.flip(view, axis=axis + 1).reshape(shape)
+        table = jnp.where(((me >> b) & 1) == 1, swapped, table)
+    return table
+
+
+def xor_reduce_scatter(part, axis_name, groups, me, high_first):
+    bits = groups.bit_length() - 1
+    rounds = []
+    low = 0
+    while low < bits:
+        rounds.append((low, min(2, bits - low)))
+        low += 2
+    if high_first:
+        rounds = [(bits - low - width, width) for low, width in rounds]
+    cur = part
+    for low, width in rounds:
         fan = 1 << width
-        view = cur.reshape((cur.shape[0] // fan, fan) + cur.shape[1:])
+        rest = cur.shape[1:]
+        axis = 0 if high_first else 1
+        view = cur.reshape(((fan, cur.shape[0] // fan) if high_first else (cur.shape[0] // fan, fan)) + rest)
         mine = (me >> low) & (fan - 1)
-        total = lax.dynamic_index_in_dim(view, mine, axis=1, keepdims=False)
+        total = lax.dynamic_index_in_dim(view, mine, axis=axis, keepdims=False)
         for k in range(1, fan):
             mask = k << low
-            sent = lax.dynamic_index_in_dim(view, jnp.bitwise_xor(mine, k), axis=1, keepdims=False)
+            sent = lax.dynamic_index_in_dim(view, jnp.bitwise_xor(mine, k), axis=axis, keepdims=False)
             total = total + lax.ppermute(sent, axis_name, [(i, i ^ mask) for i in range(groups)])
         cur = total
-        low += width
     return cur[0]
 
 
@@ -164,29 +196,38 @@
         quad_all = plm_all * jnp.asarray((math.pi / lat_total * sines).astype(np.float32))[None, None, :]
 
     own_deg = lax.dynamic_slice_in_dim(slot_degree, me * per_owner, per_owner)
-    own_quad = jnp.take(quad_all, own_deg, axis=0)
-    own_plm = jnp.take(plm_all, own_deg, axis=0)
-    rows_plm = jnp.take(lax.dynamic_slice_in_dim(plm_all, me * lat_rows, lat_rows, axis=2), slot_degree, axis=0)
-    rows_quad = jnp.take(lax.dynamic_slice_in_dim(quad_all, me * lat_rows, lat_rows, axis=2), slot_degree, axis=0)
-
-    def to_owners(table, values):
-        part = jnp.einsum("sfj,jfc->sfc", table, values, precision=highest)
-        part = part.reshape((groups, per_owner) + part.shape[1:])
-        return xor_reduce_scatter(part, "lat", groups, me)
-
-    def to_rows(table, values, extra=None):
-        part = jnp.einsum("sfj,sfc->jfc", table, values, precision=highest)
-        part = part.reshape((groups, -1))
-        if extra is not None:
-            part = jnp.concatenate([part, extra.reshape((groups, -1))], axis=1)
-        out = xor_reduce_scatter(part, "lat", groups, me)
-        size = lat_rows * 2 * orders * activations.shape[2]
-        return out[:size].reshape((lat_rows, 2 * orders, activations.shape[2])), out[size:]
+    own_pick = own_deg[:, None] == jnp.arange(degrees, dtype=jnp.int32)[None, :]
+    slot_pick = slot_degree[:, None] == jnp.arange(degrees, dtype=jnp.int32)[None, :]
+
+    def pick(choice, table):
+        return jnp.sum(jnp.where(choice[:, :, None, None], table[None], 0.0), axis=1)
+
+    own_quad = xor_blocks(pick(own_pick, quad_all), me, groups, axis=2)
+    own_plm = xor_blocks(pick(own_pick, plm_all), me, groups, axis=2)
+    my_rows_plm = lax.dynamic_slice_in_dim(plm_all, me * lat_rows, lat_rows, axis=2)
+    my_rows_quad = lax.dynamic_slice_in_dim(quad_all, me * lat_rows, lat_rows, axis=2)
+    rows_plm = xor_blocks(pick(slot_pick, my_rows_plm), me, groups, axis=0)
+    rows_quad = xor_blocks(pick(slot_pick, my_rows_quad), me, groups, axis=0)
+
+    def gathered_sum(values, table, to_rows):
+        parts = xor_gather_parts(values, "lat", groups)
+        total = None
+        start = 0
+        for part in parts:
+            flat = part.reshape((-1,) + part.shape[2:]).astype(jnp.float32)
+            n = flat.shape[0]
+            if to_rows:
+                piece = jnp.einsum("sfj,sfc->jfc", table[start:start + n], flat, precision=highest)
+            else:
+                piece = jnp.einsum("sfj,jfc->sfc", table[:, :, start:start + n], flat, precision=highest)
+            total = piece if total is None else total + piece
+            start += n
+        return total
 
     spectrum = jnp.einsum("jkc,kf->jfc", activations, fourier, preferred_element_type=jnp.float32)
-    coeffs = to_owners(rows_quad, spectrum).astype(jnp.bfloat16)
+    coeffs = gathered_sum(spectrum, own_quad, False).astype(jnp.bfloat16)
     filtered = complex_apply(coeffs, spectral_weight, orders).astype(jnp.bfloat16)
-    grid_modes = to_rows(own_plm, filtered.astype(jnp.float32))[0].astype(jnp.bfloat16)
+    grid_modes = gathered_sum(filtered, rows_plm, True).astype(jnp.bfloat16)
 
     spatial = jnp.einsum("jfc,kf->jkc", grid_modes, fourier, preferred_element_type=jnp.float32)
     skip_out = jnp.einsum("jkc,cd->jkd", activations, skip_weight, preferred_element_type=jnp.float32)
@@ -194,15 +235,14 @@
     slope_b = pullback(upstream.astype(jnp.float32))[0].astype(jnp.bfloat16)
 
     skip_terms = jnp.einsum("jkc,jkd->cd", activations, slope_b, preferred_element_type=jnp.float32)
+    skip_blocks = skip_terms.reshape((groups, -1) + skip_terms.shape[1:])
+    grad_skip = xor_reduce_scatter(skip_blocks, "lat", groups, me, True) * (1.0 / math.sqrt(lat_total * lon_total))
     through_skip = jnp.einsum("jkd,cd->jkc", slope_b, skip_weight, preferred_element_type=jnp.float32)
 
     mode_grads = jnp.einsum("jkc,kf->jfc", slope_b, fourier, preferred_element_type=jnp.float32)
-    coeff_grads = to_owners(rows_plm, mode_grads).astype(jnp.bfloat16)
+    coeff_grads = gathered_sum(mode_grads, own_plm, False).astype(jnp.bfloat16)
     weight_grads, back_coeffs = complex_adjoint(coeffs, coeff_grads, spectral_weight, orders)
-    back_b = back_coeffs.astype(jnp.bfloat16)
-    row_sums, skip_sums = to_rows(own_quad, back_b.astype(jnp.float32), skip_terms)
-    row_grads = row_sums.astype(jnp.bfloat16)
-    grad_skip = skip_sums.reshape((-1, skip_terms.shape[1])) * (1.0 / math.sqrt(lat_total * lon_total))
+    row_grads = gathered_sum(back_coeffs.astype(jnp.bfloat16), rows_quad, True).astype(jnp.bfloat16)
     through_modes = jnp.einsum("jfc,kf->jkc", row_grads, fourier, preferred_element_type=jnp.float32)
     grad_activations = (upstream.astype(jnp.float32) + through_skip + through_modes).astype(jnp.bfloat16)
     return (grad_activations, weight_grads.astype(jnp.bfloat16), grad_skip)

time: 127 us -> 159 us (1.25); the launches traced: 126 us -> 156 us
  local copies, waits for them, and re-layouts: 37.3 us -> 52.3 us
  other arithmetic: 7.11 us -> 16 us
  starting transfers between devices: 26.9 us -> 32.6 us
    ppermute x24 -> x6, waiting for transfers between devices: 27.6 us -> 0.02 us  [xor_reduce_scatter(): lax.ppermute(sent, axis_name, [(i, i ^ mask) for i in range(groups)])]
    ppermute x0 -> x24, waiting for transfers between devices: none -> 27.4 us  [xor_gather_parts(): lax.ppermute(cur, axis_name, [(i, i ^ mask) for i in range(groups)])]
    ppermute x0 -> x24, starting transfers between devices: none -> 26.2 us  [xor_gather_parts(): lax.ppermute(cur, axis_name, [(i, i ^ mask) for i in range(groups)])]
    reshape x0 -> x24, local copies, waits for them, and re-layouts: none -> 24.8 us  [the longest x22 24.8 us: xor_blocks(): swapped = jnp.flip(view, axis=axis + 1).reshape(shape)]
    ppermute x24 -> x6, starting transfers between devices: 26.9 us -> 6.4 us  [xor_reduce_scatter(): lax.ppermute(sent, axis_name, [(i, i ^ mask) for i in range(groups)])]
    rev x0 -> x32, local copies, waits for them, and re-layouts: none -> 18.3 us  [xor_blocks(): swapped = jnp.flip(view, axis=axis + 1).reshape(shape)]
    select_n x3 -> x15, other arithmetic: 1.6 us -> 11.1 us  [xor_blocks(): table = jnp.where(me >> b & 1 == 1, swapped, table)]
    dynamic_slice x11 -> x2, local copies, waits for them, and re-layouts: 8.24 us -> 0.79 us  [the longest x1 0.72 us: local(): lax.dynamic_slice_in_dim(quad_all, me * lat_rows, lat_rows, axis=2)]
  transfers between devices with their start and end apart: 24 -> 30, of which waited for: 11 -> 8; matrix products, arithmetic and copies ran while one was open for 15% -> 47% of each run, Pallas kernels for 0% -> 0%
where the time goes in v3:
time: 159 us; the launch traced here: 156 us
  local copies, waits for them, and re-layouts  52.3 us (33%)
  starting transfers between devices  32.6 us (21%)
  waiting for transfers between devices  27.4 us (17%)
  matrix products  26.2 us (16%)
  other arithmetic  16 us (10%)
    ppermute x24, waiting for transfers between devices, xor_gather_parts(): lax.ppermute(cur, axis_name, [(i, i ^ mask) for i in range(groups)])  27.4 us
    ppermute x24, starting transfers between devices, xor_gather_parts(): lax.ppermute(cur, axis_name, [(i, i ^ mask) for i in range(groups)])  26.2 us
    reshape x22, local copies, waits for them, and re-layouts, xor_blocks(): swapped = jnp.flip(view, axis=axis + 1).reshape(shape)  24.8 us
    rev x32, local copies, waits for them, and re-layouts, xor_blocks(): swapped = jnp.flip(view, axis=axis + 1).reshape(shape)  18.3 us
    select_n x15, other arithmetic, xor_blocks(): table = jnp.where(me >> b & 1 == 1, swapped, table)  11.1 us
    ppermute x6, starting transfers between devices, xor_reduce_scatter(): lax.ppermute(sent, axis_name, [(i, i ^ mask) for i in range(groups)])  6.4 us
    dot_general x8, matrix products, gathered_sum(): jnp.einsum('sfj,jfc->sfc', table[:, :, start:start + n], flat, precision=...  5.6 us
    unnamed x59, local copies, waits for them, and re-layouts  4.79 us
  transfers between devices with their start and end apart: 30, of which 8 were waited for; matrix products, arithmetic and copies ran while one was open for 47% of the time, Pallas kernels for 0%

profile of v3, /device:TPU:0, one launch (start us, length us, event | category | flops | bytes accessed | tf_op | source)
XLA Modules:
  0.0 155.7 jit_solution(6821359796733696262)
XLA Ops:
  0.7 1.6 %copy-done = bf16[2,1440,384]{2,1,0:T(8,128)(2,1)S(1)} copy-done((bf16[2,1440,384]{2,1,0:T(8,128)(2,1)S(1)}, bf16[2,1440,384]{2,1,0:T(8,128)(2,1)}, u32[]{:S(2)}) %copy-start) | copy-done | bytes 2211864
  2.3 1.7 %convolution_bitcast_fusion.1 = f32[1,2,8,384]{3,2,1,0:T(8,128)} fusion(bf16[1440,8,1]{0,1,2:T(8,128)(2,1)} %constant.63, bf16[2,1440,384]{2,1,0:T(8,128)(2,1)S(1)} %copy-done), kind=kOutput, calls=%fused_computation.38 | convolution fusion | flops 17694720 | bytes 2259456 | tf_op jit(solution)/shard_map/jkc,kf->jfc/dot_general | solution.py:227
  4.0 2.4 %collective-permute-start.2 = (f32[1,2,8,384]{3,2,1,0:T(8,128)}, f32[1,2,8,384]{3,2,1,0:T(8,128)}, u32[]{:S(2)}, u32[]{:S(2)}) collective-permute-start(f32[1,2,8,384]{3,2,1,0:T(8,128)} %convolution_bitcast_fusion.1), channel_id=1, source_target_pairs={{0,3},{1,2},{2,1},{3,0},{4,7},{5,6},{6,5},{7,4},{8,11},{9,10},{10,... | collective-permute-start | bytes 73736 | tf_op jit(solution)/shard_map/ppermute | solution.py:102
  23.8 1.4 bitcast_select_fusion
  26.6 1.4 copy.367
  31.7 1.4 copy.298
  33.1 1.4 copy.296
  36.8 1.4 copy.343
  38.2 1.4 copy.341
  47.0 1.4 copy.370
  52.0 1.4 pad_maximum_fusion.1
  53.4 1.9 %collective-permute-start.3 = (f32[4,2,8,384]{3,2,1,0:T(8,128)}, f32[4,2,8,384]{3,2,1,0:T(8,128)}, u32[]{:S(2)}, u32[]{:S(2)}) collective-permute-start(f32[4,2,8,384]{3,2,1,0:T(8,128)} %pad_maximum_fusion.1), channel_id=1, source_target_pairs={{0,4},{1,5},{2,6},{3,7},{4,0},{5,1},{6,2},{7,3},{8,12},{9,13},{10,... | collective-permute-start | bytes 294920 | tf_op jit(solution)/shard_map/ppermute | solution.py:102
  56.0 1.4 copy.300
  62.2 1.4 reshape.485
  63.6 1.4 copy.304
  65.0 1.4 copy.302
  66.5 2.6 %collective-permute-start.5 = (f32[4,2,8,384]{3,2,1,0:T(8,128)}, f32[4,2,8,384]{3,2,1,0:T(8,128)S(1)}, u32[]{:S(2)}, u32[]{:S(2)}) collective-permute-start(f32[4,2,8,384]{3,2,1,0:T(8,128)} %pad_maximum_fusion.1), channel_id=1, source_target_pairs={{0,12},{1,13},{2,14},{3,15},{4,8},{5,9},{6,10},{7,11},{8,4},{9,5},... | collective-permute-start | bytes 294920 | tf_op jit(solution)/shard_map/ppermute | solution.py:102
  71.6 2.3 %collective-permute-done.5 = f32[4,2,8,384]{3,2,1,0:T(8,128)S(1)} collective-permute-done((f32[4,2,8,384]{3,2,1,0:T(8,128)}, f32[4,2,8,384]{3,2,1,0:T(8,128)S(1)}, u32[]{:S(2)}, u32[]{:S(2)}) %collective-permute-start.5) | collective-permute-done | bytes 98336 | tf_op jit(solution)/shard_map/ppermute | solution.py:102
  74.9 2.9 %collective-permute-done.4 = f32[4,2,8,384]{3,2,1,0:T(8,128)S(1)} collective-permute-done((f32[4,2,8,384]{3,2,1,0:T(8,128)}, f32[4,2,8,384]{3,2,1,0:T(8,128)S(1)}, u32[]{:S(2)}, u32[]{:S(2)}) %collective-permute-start.4) | collective-permute-done | bytes 98336 | tf_op jit(solution)/shard_map/ppermute | solution.py:102
  85.6 1.5 reshape.515
  89.1 3.3 %collective-permute-start.11 = (bf16[4,2,8,384]{3,2,1,0:T(8,128)(2,1)S(1)}, bf16[4,2,8,384]{3,2,1,0:T(8,128)(2,1)S(1)}, u32[]{:S(2)}, u32[]{:S(2)}) collective-permute-start(bf16[4,2,8,384]{3,2,1,0:T(8,128)(2,1)S(1)} %pad_maximum_fusion.3), channel_id=1, source_target_pairs={{0,12},{1,13},{2,14},{3,15},{4,8},{5,9},{6,10},{7,11},{8,4},{9,5},... | collective-permute-start | bytes 147464 | tf_op jit(solution)/shard_map/ppermute | solution.py:102
  96.1 1.8 %collective-permute-done.10 = bf16[4,2,8,384]{3,2,1,0:T(8,128)(2,1)S(1)} collective-permute-done((bf16[4,2,8,384]{3,2,1,0:T(8,128)(2,1)S(1)}, bf16[4,2,8,384]{3,2,1,0:T(8,128)(2,1)S(1)}, u32[]{:S(2)}, u32[]{:S(2)}) %collective-permute-start.10) | collective-permute-done | bytes 49184 | tf_op jit(solution)/shard_map/ppermute | solution.py:102
  100.5 4.4 %fusion.6 = bf16[2,1440,384]{2,1,0:T(8,128)(2,1)S(1)} fusion(bf16[2,1440,384]{2,1,0:T(8,128)(2,1)S(1)} %copy-done.2, f32[2,384,1440]{1,2,0:T(8,128)S(1)} %fusion.88, bf16[2,1440,384]{2,1,0:T(8,128)(2,1)S(1)} %copy-done, bf16[384,384]{1,0:T(8,128)(2,1)S(1)} %copy-done.8), kind=kOutput, calls=%fused_computation.11 | convolution fusion | flops 873676800 | bytes 11354112 | tf_op jit(solution)/shard_map/jkc,cd->jkd/dot_general | solution.py:233
  105.3 1.8 %collective-permute-start.13 = (f32[1,2,8,384]{3,2,1,0:T(8,128)S(1)}, f32[1,2,8,384]{3,2,1,0:T(8,128)S(1)}, u32[]{:S(2)}, u32[]{:S(2)}) collective-permute-start(f32[1,2,8,384]{3,2,1,0:T(8,128)S(1)} %convolution_bitcast_fusion), channel_id=1, source_target_pairs={{0,2},{1,3},{2,0},{3,1},{4,6},{5,7},{6,4},{7,5},{8,10},{9,11},{10,... | collective-permute-start | bytes 73736 | tf_op jit(solution)/shard_map/ppermute | solution.py:102
  109.7 3.2 %collective-permute-start.26 = (f32[4,24,384]{2,1,0:T(8,128)S(1)}, f32[4,24,384]{2,1,0:T(8,128)S(1)}, u32[]{:S(2)}, u32[]{:S(2)}) collective-permute-start(f32[4,24,384]{2,1,0:T(8,128)S(1)} %get-tuple-element.23), channel_id=1, source_target_pairs={{0,12},{1,13},{2,14},{3,15},{4,8},{5,9},{6,10},{7,11},{8,4},{9,5},... | collective-permute-start | bytes 442376 | tf_op jit(solution)/shard_map/ppermute | solution.py:138
  114.1 3.2 %collective-permute-start.17 = (f32[4,2,8,384]{3,2,1,0:T(8,128)S(1)}, f32[4,2,8,384]{3,2,1,0:T(8,128)S(1)}, u32[]{:S(2)}, u32[]{:S(2)}) collective-permute-start(f32[4,2,8,384]{3,2,1,0:T(8,128)S(1)} %pad_maximum_fusion.2), channel_id=1, source_target_pairs={{0,12},{1,13},{2,14},{3,15},{4,8},{5,9},{6,10},{7,11},{8,4},{9,5},... | collective-permute-start | bytes 294920 | tf_op jit(solution)/shard_map/ppermute | solution.py:102
  117.9 10.2 %collective-permute-done.17 = f32[4,2,8,384]{3,2,1,0:T(8,128)S(1)} collective-permute-done((f32[4,2,8,384]{3,2,1,0:T(8,128)S(1)}, f32[4,2,8,384]{3,2,1,0:T(8,128)S(1)}, u32[]{:S(2)}, u32[]{:S(2)}) %collective-permute-start.17) | collective-permute-done | bytes 98336 | tf_op jit(solution)/shard_map/ppermute | solution.py:102
  128.4 6.5 %collective-permute-done.16 = f32[4,2,8,384]{3,2,1,0:T(8,128)S(1)} collective-permute-done((f32[4,2,8,384]{3,2,1,0:T(8,128)S(1)}, f32[4,2,8,384]{3,2,1,0:T(8,128)S(1)}, u32[]{:S(2)}, u32[]{:S(2)}) %collective-permute-start.16) | collective-permute-done | bytes 98336 | tf_op jit(solution)/shard_map/ppermute | solution.py:102
  143.2 2.3 %collective-permute-start.23 = (bf16[4,2,8,384]{3,2,1,0:T(8,128)(2,1)S(1)}, bf16[4,2,8,384]{3,2,1,0:T(8,128)(2,1)S(1)}, u32[]{:S(2)}, u32[]{:S(2)}) collective-permute-start(bf16[4,2,8,384]{3,2,1,0:T(8,128)(2,1)S(1)} %pad_maximum_fusion.4), channel_id=1, source_target_pairs={{0,12},{1,13},{2,14},{3,15},{4,8},{5,9},{6,10},{7,11},{8,4},{9,5},... | collective-permute-start | bytes 147464 | tf_op jit(solution)/shard_map/ppermute | solution.py:102
  145.6 2.1 %collective-permute-start.22 = (bf16[4,2,8,384]{3,2,1,0:T(8,128)(2,1)S(1)}, bf16[4,2,8,384]{3,2,1,0:T(8,128)(2,1)S(1)}, u32[]{:S(2)}, u32[]{:S(2)}) collective-permute-start(bf16[4,2,8,384]{3,2,1,0:T(8,128)(2,1)S(1)} %pad_maximum_fusion.4), channel_id=1, source_target_pairs={{0,8},{1,9},{2,10},{3,11},{4,12},{5,13},{6,14},{7,15},{8,0},{9,1},... | collective-permute-start | bytes 147464 | tf_op jit(solution)/shard_map/ppermute | solution.py:102
  148.3 2.6 %collective-permute-done.21 = bf16[4,2,8,384]{3,2,1,0:T(8,128)(2,1)S(1)} collective-permute-done((bf16[4,2,8,384]{3,2,1,0:T(8,128)(2,1)S(1)}, bf16[4,2,8,384]{3,2,1,0:T(8,128)(2,1)S(1)}, u32[]{:S(2)}, u32[]{:S(2)}) %collective-permute-start.21) | collective-permute-done | bytes 49184 | tf_op jit(solution)/shard_map/ppermute | solution.py:102
  152.8 3.0 %fusion.11 = bf16[2,1440,384]{2,1,0:T(8,128)(2,1)} fusion(bf16[2,1440,384]{2,1,0:T(8,128)(2,1)S(1)} %copy-done.2, f32[2,384,1440]{1,2,0:T(8,128)S(1)} %fusion.86, bf16[2,1440,384]{2,1,0:T(8,128)(2,1)S(1)} %fusion.6, bf16[384,384]{1,0:T(8,128)(2,1)S(1)} %copy-done.8), kind=kOutput, calls=%fused_computation.16 | convolution fusion | flops 853770240 | bytes 11354112 | tf_op jit(solution)/shard_map/jkd,cd->jkc/dot_general | solution.py:240
  (218 shorter events, 75.9 us)
Async XLA Ops:
  4.0 47.9 %collective-permute-start.2 = (f32[1,2,8,384]{3,2,1,0:T(8,128)}, f32[1,2,8,384]{3,2,1,0:T(8,128)}, u32[]{:S(2)}, u32[]{:S(2)}) collective-permute-start(f32[1,2,8,384]{3,2,1,0:T(8,128)} %convolution_bitcast_fusion.1), channel_id=1, source_target_pairs={{0,3},{1,2},{2,1},{3,0},{4,7},{5,6},{6,5},{7,4},{8,11},{9,10},{10,... | collective-permute-start | bytes 73736 | tf_op jit(solution)/shard_map/ppermute | solution.py:102
  6.4 45.5 %collective-permute-start.1 = (f32[1,2,8,384]{3,2,1,0:T(8,128)}, f32[1,2,8,384]{3,2,1,0:T(8,128)}, u32[]{:S(2)}, u32[]{:S(2)}) collective-permute-start(f32[1,2,8,384]{3,2,1,0:T(8,128)} %convolution_bitcast_fusion.1), channel_id=1, source_target_pairs={{0,2},{1,3},{2,0},{3,1},{4,6},{5,7},{6,4},{7,5},{8,10},{9,11},{10,... | collective-permute-start | bytes 73736 | tf_op jit(solution)/shard_map/ppermute | solution.py:102
  7.0 44.9 %collective-permute-start = (f32[1,2,8,384]{3,2,1,0:T(8,128)}, f32[1,2,8,384]{3,2,1,0:T(8,128)}, u32[]{:S(2)}, u32[]{:S(2)}) collective-permute-start(f32[1,2,8,384]{3,2,1,0:T(8,128)} %convolution_bitcast_fusion.1), channel_id=1, source_target_pairs={{0,1},{1,0},{2,3},{3,2},{4,5},{5,4},{6,7},{7,6},{8,9},{9,8},{10,11... | collective-permute-start | bytes 73736 | tf_op jit(solution)/shard_map/ppermute | solution.py:102
  11.9 67.0 %copy-start.1 = (bf16[2,2,384,384]{3,2,1,0:T(8,128)(2,1)S(1)}, bf16[2,2,384,384]{3,2,1,0:T(8,128)(2,1)}, u32[]{:S(2)}) copy-start(bf16[2,2,384,384]{3,2,1,0:T(8,128)(2,1)} %param.11) | copy-start | bytes 3538948
  41.6 46.1 %copy-start.4 = (f32[8,2,2,8,2]{3,2,1,0,4:T(2,128)S(1)}, f32[8,2,2,8,2]{3,2,1,0,4:T(2,128)}, u32[]{:S(2)}) copy-start(f32[8,2,2,8,2]{3,2,1,0,4:T(2,128)} %copy-done.3) | copy-start | bytes 6148
  53.4 15.8 %collective-permute-start.3 = (f32[4,2,8,384]{3,2,1,0:T(8,128)}, f32[4,2,8,384]{3,2,1,0:T(8,128)}, u32[]{:S(2)}, u32[]{:S(2)}) collective-permute-start(f32[4,2,8,384]{3,2,1,0:T(8,128)} %pad_maximum_fusion.1), channel_id=1, source_target_pairs={{0,4},{1,5},{2,6},{3,7},{4,0},{5,1},{6,2},{7,3},{8,12},{9,13},{10,... | collective-permute-start | bytes 294920 | tf_op jit(solution)/shard_map/ppermute | solution.py:102
  66.5 7.4 %collective-permute-start.5 = (f32[4,2,8,384]{3,2,1,0:T(8,128)}, f32[4,2,8,384]{3,2,1,0:T(8,128)S(1)}, u32[]{:S(2)}, u32[]{:S(2)}) collective-permute-start(f32[4,2,8,384]{3,2,1,0:T(8,128)} %pad_maximum_fusion.1), channel_id=1, source_target_pairs={{0,12},{1,13},{2,14},{3,15},{4,8},{5,9},{6,10},{7,11},{8,4},{9,5},... | collective-permute-start | bytes 294920 | tf_op jit(solution)/shard_map/ppermute | solution.py:102
  69.0 8.8 %collective-permute-start.4 = (f32[4,2,8,384]{3,2,1,0:T(8,128)}, f32[4,2,8,384]{3,2,1,0:T(8,128)S(1)}, u32[]{:S(2)}, u32[]{:S(2)}) collective-permute-start(f32[4,2,8,384]{3,2,1,0:T(8,128)} %pad_maximum_fusion.1), channel_id=1, source_target_pairs={{0,8},{1,9},{2,10},{3,11},{4,12},{5,13},{6,14},{7,15},{8,0},{9,1},... | collective-permute-start | bytes 294920 | tf_op jit(solution)/shard_map/ppermute | solution.py:102
  80.3 7.4 %collective-permute-start.8 = (bf16[1,2,8,384]{3,2,1,0:T(8,128)(2,1)}, bf16[1,2,8,384]{3,2,1,0:T(8,128)(2,1)}, u32[]{:S(2)}, u32[]{:S(2)}) collective-permute-start(bf16[1,2,8,384]{3,2,1,0:T(8,128)(2,1)} %pad_maximum_fusion.5), channel_id=1, source_target_pairs={{0,3},{1,2},{2,1},{3,0},{4,7},{5,6},{6,5},{7,4},{8,11},{9,10},{10,... | collective-permute-start | bytes 36872 | tf_op jit(solution)/shard_map/ppermute | solution.py:102
  81.4 6.4 %collective-permute-start.7 = (bf16[1,2,8,384]{3,2,1,0:T(8,128)(2,1)}, bf16[1,2,8,384]{3,2,1,0:T(8,128)(2,1)}, u32[]{:S(2)}, u32[]{:S(2)}) collective-permute-start(bf16[1,2,8,384]{3,2,1,0:T(8,128)(2,1)} %pad_maximum_fusion.5), channel_id=1, source_target_pairs={{0,2},{1,3},{2,0},{3,1},{4,6},{5,7},{6,4},{7,5},{8,10},{9,11},{10,... | collective-permute-start | bytes 36872 | tf_op jit(solution)/shard_map/ppermute | solution.py:102
  82.7 5.1 %collective-permute-start.6 = (bf16[1,2,8,384]{3,2,1,0:T(8,128)(2,1)}, bf16[1,2,8,384]{3,2,1,0:T(8,128)(2,1)}, u32[]{:S(2)}, u32[]{:S(2)}) collective-permute-start(bf16[1,2,8,384]{3,2,1,0:T(8,128)(2,1)} %pad_maximum_fusion.5), channel_id=1, source_target_pairs={{0,1},{1,0},{2,3},{3,2},{4,5},{5,4},{6,7},{7,6},{8,9},{9,8},{10,11... | collective-permute-start | bytes 36872 | tf_op jit(solution)/shard_map/ppermute | solution.py:102
  88.6 4.3 %collective-permute-start.9 = (bf16[4,2,8,384]{3,2,1,0:T(8,128)(2,1)S(1)}, bf16[4,2,8,384]{3,2,1,0:T(8,128)(2,1)S(1)}, u32[]{:S(2)}, u32[]{:S(2)}) collective-permute-start(bf16[4,2,8,384]{3,2,1,0:T(8,128)(2,1)S(1)} %pad_maximum_fusion.3), channel_id=1, source_target_pairs={{0,4},{1,5},{2,6},{3,7},{4,0},{5,1},{6,2},{7,3},{8,12},{9,13},{10,... | collective-permute-start | bytes 147464 | tf_op jit(solution)/shard_map/ppermute | solution.py:102
  89.1 6.0 %collective-permute-start.11 = (bf16[4,2,8,384]{3,2,1,0:T(8,128)(2,1)S(1)}, bf16[4,2,8,384]{3,2,1,0:T(8,128)(2,1)S(1)}, u32[]{:S(2)}, u32[]{:S(2)}) collective-permute-start(bf16[4,2,8,384]{3,2,1,0:T(8,128)(2,1)S(1)} %pad_maximum_fusion.3), channel_id=1, source_target_pairs={{0,12},{1,13},{2,14},{3,15},{4,8},{5,9},{6,10},{7,11},{8,4},{9,5},... | collective-permute-start | bytes 147464 | tf_op jit(solution)/shard_map/ppermute | solution.py:102
  92.4 5.5 %collective-permute-start.10 = (bf16[4,2,8,384]{3,2,1,0:T(8,128)(2,1)S(1)}, bf16[4,2,8,384]{3,2,1,0:T(8,128)(2,1)S(1)}, u32[]{:S(2)}, u32[]{:S(2)}) collective-permute-start(bf16[4,2,8,384]{3,2,1,0:T(8,128)(2,1)S(1)} %pad_maximum_fusion.3), channel_id=1, source_target_pairs={{0,8},{1,9},{2,10},{3,11},{4,12},{5,13},{6,14},{7,15},{8,0},{9,1},... | collective-permute-start | bytes 147464 | tf_op jit(solution)/shard_map/ppermute | solution.py:102
  105.3 3.3 %collective-permute-start.14 = (f32[1,2,8,384]{3,2,1,0:T(8,128)S(1)}, f32[1,2,8,384]{3,2,1,0:T(8,128)S(1)}, u32[]{:S(2)}, u32[]{:S(2)}) collective-permute-start(f32[1,2,8,384]{3,2,1,0:T(8,128)S(1)} %convolution_bitcast_fusion), channel_id=1, source_target_pairs={{0,3},{1,2},{2,1},{3,0},{4,7},{5,6},{6,5},{7,4},{8,11},{9,10},{10,... | collective-permute-start | bytes 73736 | tf_op jit(solution)/shard_map/ppermute | solution.py:102
  105.3 3.9 %collective-permute-start.13 = (f32[1,2,8,384]{3,2,1,0:T(8,128)S(1)}, f32[1,2,8,384]{3,2,1,0:T(8,128)S(1)}, u32[]{:S(2)}, u32[]{:S(2)}) collective-permute-start(f32[1,2,8,384]{3,2,1,0:T(8,128)S(1)} %convolution_bitcast_fusion), channel_id=1, source_target_pairs={{0,2},{1,3},{2,0},{3,1},{4,6},{5,7},{6,4},{7,5},{8,10},{9,11},{10,... | collective-permute-start | bytes 73736 | tf_op jit(solution)/shard_map/ppermute | solution.py:102
  107.2 2.1 %collective-permute-start.12 = (f32[1,2,8,384]{3,2,1,0:T(8,128)S(1)}, f32[1,2,8,384]{3,2,1,0:T(8,128)S(1)}, u32[]{:S(2)}, u32[]{:S(2)}) collective-permute-start(f32[1,2,8,384]{3,2,1,0:T(8,128)S(1)} %convolution_bitcast_fusion), channel_id=1, source_target_pairs={{0,1},{1,0},{2,3},{3,2},{4,5},{5,4},{6,7},{7,6},{8,9},{9,8},{10,11... | collective-permute-start | bytes 73736 | tf_op jit(solution)/shard_map/ppermute | solution.py:102
  109.2 8.1 %collective-permute-start.15 = (f32[4,2,8,384]{3,2,1,0:T(8,128)S(1)}, f32[4,2,8,384]{3,2,1,0:T(8,128)S(1)}, u32[]{:S(2)}, u32[]{:S(2)}) collective-permute-start(f32[4,2,8,384]{3,2,1,0:T(8,128)S(1)} %pad_maximum_fusion.2), channel_id=1, source_target_pairs={{0,4},{1,5},{2,6},{3,7},{4,0},{5,1},{6,2},{7,3},{8,12},{9,13},{10,... | collective-permute-start | bytes 294920 | tf_op jit(solution)/shard_map/ppermute | solution.py:102
  109.7 30.9 %collective-permute-start.26 = (f32[4,24,384]{2,1,0:T(8,128)S(1)}, f32[4,24,384]{2,1,0:T(8,128)S(1)}, u32[]{:S(2)}, u32[]{:S(2)}) collective-permute-start(f32[4,24,384]{2,1,0:T(8,128)S(1)} %get-tuple-element.23), channel_id=1, source_target_pairs={{0,12},{1,13},{2,14},{3,15},{4,8},{5,9},{6,10},{7,11},{8,4},{9,5},... | collective-permute-start | bytes 442376 | tf_op jit(solution)/shard_map/ppermute | solution.py:138
  112.9 28.3 %collective-permute-start.25 = (f32[4,24,384]{2,1,0:T(8,128)S(1)}, f32[4,24,384]{2,1,0:T(8,128)S(1)}, u32[]{:S(2)}, u32[]{:S(2)}) collective-permute-start(f32[4,24,384]{2,1,0:T(8,128)S(1)} %get-tuple-element.24), channel_id=1, source_target_pairs={{0,8},{1,9},{2,10},{3,11},{4,12},{5,13},{6,14},{7,15},{8,0},{9,1},... | collective-permute-start | bytes 442376 | tf_op jit(solution)/shard_map/ppermute | solution.py:138
  112.9 28.3 %collective-permute-start.24 = (f32[4,24,384]{2,1,0:T(8,128)S(1)}, f32[4,24,384]{2,1,0:T(8,128)S(1)}, u32[]{:S(2)}, u32[]{:S(2)}) collective-permute-start(f32[4,24,384]{2,1,0:T(8,128)S(1)} %get-tuple-element.22), channel_id=1, source_target_pairs={{0,4},{1,5},{2,6},{3,7},{4,0},{5,1},{6,2},{7,3},{8,12},{9,13},{10,... | collective-permute-start | bytes 442376 | tf_op jit(solution)/shard_map/ppermute | solution.py:138
  114.1 14.0 %collective-permute-start.17 = (f32[4,2,8,384]{3,2,1,0:T(8,128)S(1)}, f32[4,2,8,384]{3,2,1,0:T(8,128)S(1)}, u32[]{:S(2)}, u32[]{:S(2)}) collective-permute-start(f32[4,2,8,384]{3,2,1,0:T(8,128)S(1)} %pad_maximum_fusion.2), channel_id=1, source_target_pairs={{0,12},{1,13},{2,14},{3,15},{4,8},{5,9},{6,10},{7,11},{8,4},{9,5},... | collective-permute-start | bytes 294920 | tf_op jit(solution)/shard_map/ppermute | solution.py:102
  117.3 17.6 %collective-permute-start.16 = (f32[4,2,8,384]{3,2,1,0:T(8,128)S(1)}, f32[4,2,8,384]{3,2,1,0:T(8,128)S(1)}, u32[]{:S(2)}, u32[]{:S(2)}) collective-permute-start(f32[4,2,8,384]{3,2,1,0:T(8,128)S(1)} %pad_maximum_fusion.2), channel_id=1, source_target_pairs={{0,8},{1,9},{2,10},{3,11},{4,12},{5,13},{6,14},{7,15},{8,0},{9,1},... | collective-permute-start | bytes 294920 | tf_op jit(solution)/shard_map/ppermute | solution.py:102
  136.5 6.5 %collective-permute-start.20 = (bf16[1,2,8,384]{3,2,1,0:T(8,128)(2,1)S(1)}, bf16[1,2,8,384]{3,2,1,0:T(8,128)(2,1)S(1)}, u32[]{:S(2)}, u32[]{:S(2)}) collective-permute-start(bf16[1,2,8,384]{3,2,1,0:T(8,128)(2,1)S(1)} %pad_maximum_fusion.6), channel_id=1, source_target_pairs={{0,3},{1,2},{2,1},{3,0},{4,7},{5,6},{6,5},{7,4},{8,11},{9,10},{10,... | collective-permute-start | bytes 36872 | tf_op jit(solution)/shard_map/ppermute | solution.py:102
  136.5 6.7 %collective-permute-start.19 = (bf16[1,2,8,384]{3,2,1,0:T(8,128)(2,1)S(1)}, bf16[1,2,8,384]{3,2,1,0:T(8,128)(2,1)S(1)}, u32[]{:S(2)}, u32[]{:S(2)}) collective-permute-start(bf16[1,2,8,384]{3,2,1,0:T(8,128)(2,1)S(1)} %pad_maximum_fusion.6), channel_id=1, source_target_pairs={{0,2},{1,3},{2,0},{3,1},{4,6},{5,7},{6,4},{7,5},{8,10},{9,11},{10,... | collective-permute-start | bytes 36872 | tf_op jit(solution)/shard_map/ppermute | solution.py:102
  140.6 2.6 %collective-permute-start.18 = (bf16[1,2,8,384]{3,2,1,0:T(8,128)(2,1)S(1)}, bf16[1,2,8,384]{3,2,1,0:T(8,128)(2,1)S(1)}, u32[]{:S(2)}, u32[]{:S(2)}) collective-permute-start(bf16[1,2,8,384]{3,2,1,0:T(8,128)(2,1)S(1)} %pad_maximum_fusion.6), channel_id=1, source_target_pairs={{0,1},{1,0},{2,3},{3,2},{4,5},{5,4},{6,7},{7,6},{8,9},{9,8},{10,11... | collective-permute-start | bytes 36872 | tf_op jit(solution)/shard_map/ppermute | solution.py:102
  141.3 4.3 %collective-permute-start.29 = (f32[1,24,384]{2,1,0:T(8,128)S(1)}, f32[1,24,384]{2,1,0:T(8,128)S(1)}, u32[]{:S(2)}, u32[]{:S(2)}) collective-permute-start(f32[1,24,384]{2,1,0:T(8,128)S(1)} %get-tuple-element.26), channel_id=1, source_target_pairs={{0,3},{1,2},{2,1},{3,0},{4,7},{5,6},{6,5},{7,4},{8,11},{9,10},{10,... | collective-permute-start | bytes 110600 | tf_op jit(solution)/shard_map/ppermute | solution.py:138
  141.7 6.0 %collective-permute-start.28 = (f32[1,24,384]{2,1,0:T(8,128)S(1)}, f32[1,24,384]{2,1,0:T(8,128)S(1)}, u32[]{:S(2)}, u32[]{:S(2)}) collective-permute-start(f32[1,24,384]{2,1,0:T(8,128)S(1)} %get-tuple-element.27), channel_id=1, source_target_pairs={{0,2},{1,3},{2,0},{3,1},{4,6},{5,7},{6,4},{7,5},{8,10},{9,11},{10,... | collective-permute-start | bytes 110600 | tf_op jit(solution)/shard_map/ppermute | solution.py:138
  143.0 4.7 %collective-permute-start.27 = (f32[1,24,384]{2,1,0:T(8,128)S(1)}, f32[1,24,384]{2,1,0:T(8,128)S(1)}, u32[]{:S(2)}, u32[]{:S(2)}) collective-permute-start(f32[1,24,384]{2,1,0:T(8,128)S(1)} %get-tuple-element.25), channel_id=1, source_target_pairs={{0,1},{1,0},{2,3},{3,2},{4,5},{5,4},{6,7},{7,6},{8,9},{9,8},{10,11... | collective-permute-start | bytes 110600 | tf_op jit(solution)/shard_map/ppermute | solution.py:138
  143.2 8.2 %collective-permute-start.23 = (bf16[4,2,8,384]{3,2,1,0:T(8,128)(2,1)S(1)}, bf16[4,2,8,384]{3,2,1,0:T(8,128)(2,1)S(1)}, u32[]{:S(2)}, u32[]{:S(2)}) collective-permute-start(bf16[4,2,8,384]{3,2,1,0:T(8,128)(2,1)S(1)} %pad_maximum_fusion.4), channel_id=1, source_target_pairs={{0,12},{1,13},{2,14},{3,15},{4,8},{5,9},{6,10},{7,11},{8,4},{9,5},... | collective-permute-start | bytes 147464 | tf_op jit(solution)/shard_map/ppermute | solution.py:102
  145.6 5.4 %collective-permute-start.21 = (bf16[4,2,8,384]{3,2,1,0:T(8,128)(2,1)S(1)}, bf16[4,2,8,384]{3,2,1,0:T(8,128)(2,1)S(1)}, u32[]{:S(2)}, u32[]{:S(2)}) collective-permute-start(bf16[4,2,8,384]{3,2,1,0:T(8,128)(2,1)S(1)} %pad_maximum_fusion.4), channel_id=1, source_target_pairs={{0,4},{1,5},{2,6},{3,7},{4,0},{5,1},{6,2},{7,3},{8,12},{9,13},{10,... | collective-permute-start | bytes 147464 | tf_op jit(solution)/shard_map/ppermute | solution.py:102
  145.6 6.1 %collective-permute-start.22 = (bf16[4,2,8,384]{3,2,1,0:T(8,128)(2,1)S(1)}, bf16[4,2,8,384]{3,2,1,0:T(8,128)(2,1)S(1)}, u32[]{:S(2)}, u32[]{:S(2)}) collective-permute-start(bf16[4,2,8,384]{3,2,1,0:T(8,128)(2,1)S(1)} %pad_maximum_fusion.4), channel_id=1, source_target_pairs={{0,8},{1,9},{2,10},{3,11},{4,12},{5,13},{6,14},{7,15},{8,0},{9,1},... | collective-permute-start | bytes 147464 | tf_op jit(solution)/shard_map/ppermute | solution.py:102
  (27 other events, 276.4 us)

commit v4 on v1

--- a/solution.py
+++ b/solution.py
@@ -106,15 +106,21 @@
 
 def xor_reduce_scatter(part, axis_name, groups, me):
     bits = groups.bit_length() - 1
-    cur = part.reshape((groups, part.shape[0] // groups) + part.shape[1:])
-    for b in range(bits):
-        pairs = cur.reshape((cur.shape[0] // 2, 2) + cur.shape[1:])
-        bit = (me >> b) & 1
-        keep = jnp.where(bit == 0, pairs[:, 0], pairs[:, 1])
-        send = jnp.where(bit == 0, pairs[:, 1], pairs[:, 0])
-        mask = 1 << b
-        cur = keep + lax.ppermute(send, axis_name, [(i, i ^ mask) for i in range(groups)])
-    return cur.reshape(cur.shape[1:])
+    cur = part
+    low = 0
+    while low < bits:
+        width = min(2, bits - low)
+        fan = 1 << width
+        view = cur.reshape((cur.shape[0] // fan, fan) + cur.shape[1:])
+        mine = (me >> low) & (fan - 1)
+        total = lax.dynamic_index_in_dim(view, mine, axis=1, keepdims=False)
+        for k in range(1, fan):
+            mask = k << low
+            sent = lax.dynamic_index_in_dim(view, jnp.bitwise_xor(mine, k), axis=1, keepdims=False)
+            total = total + lax.ppermute(sent, axis_name, [(i, i ^ mask) for i in range(groups)])
+        cur = total
+        low += width
+    return cur[0]
 
 
 def complex_apply(coeffs, weights, orders):
@@ -172,17 +178,20 @@
         plm_all = legendre_scan(cosines, sines, degrees, orders)
         quad_all = plm_all * jnp.asarray((math.pi / lat_total * sines).astype(np.float32))[None, None, :]
 
+    both = jnp.concatenate([quad_all, plm_all], axis=1).transpose(0, 2, 1)
     row_ids = jnp.arange(lat_total, dtype=jnp.int32)
     row_cols = jnp.bitwise_xor(me, row_ids // lat_rows) * lat_rows + row_ids % lat_rows
     slot_ids = jnp.arange(degrees, dtype=jnp.int32)
     slot_src = jnp.bitwise_xor(me, slot_ids // per_owner) * per_owner + slot_ids % per_owner
-    slot_deg = jnp.take(slot_degree, slot_src, axis=0)
     own_deg = lax.dynamic_slice_in_dim(slot_degree, me * per_owner, per_owner)
-
-    own_quad = jnp.take(jnp.take(quad_all, own_deg, axis=0), row_cols, axis=2)
-    own_plm = jnp.take(jnp.take(plm_all, own_deg, axis=0), row_cols, axis=2)
-    rows_plm = jnp.take(lax.dynamic_slice_in_dim(plm_all, me * lat_rows, lat_rows, axis=2), slot_deg, axis=0)
-    rows_quad = jnp.take(lax.dynamic_slice_in_dim(quad_all, me * lat_rows, lat_rows, axis=2), slot_deg, axis=0)
+    own_both = both[own_deg[:, None], row_cols[None, :]]
+    my_rows = me * lat_rows + jnp.arange(lat_rows, dtype=jnp.int32)
+    rows_both = both[jnp.take(slot_degree, slot_src)[:, None], my_rows[None, :]]
+    nf = 2 * orders
+    own_quad = own_both[:, :, :nf].transpose(0, 2, 1)
+    own_plm = own_both[:, :, nf:].transpose(0, 2, 1)
+    rows_quad = rows_both[:, :, :nf].transpose(0, 2, 1)
+    rows_plm = rows_both[:, :, nf:].transpose(0, 2, 1)
 
     def gather(values):
         out = xor_gather(values, "lat", groups)
@@ -201,7 +210,8 @@
     slope_b = pullback(upstream.astype(jnp.float32))[0].astype(jnp.bfloat16)
 
     skip_terms = jnp.einsum("jkc,jkd->cd", activations, slope_b, preferred_element_type=jnp.float32)
-    grad_skip = xor_reduce_scatter(skip_terms, "lat", groups, me) * (1.0 / math.sqrt(lat_total * lon_total))
+    skip_blocks = skip_terms.reshape((groups, -1) + skip_terms.shape[1:])
+    grad_skip = xor_reduce_scatter(skip_blocks, "lat", groups, me) * (1.0 / math.sqrt(lat_total * lon_total))
     through_skip = jnp.einsum("jkd,cd->jkc", slope_b, skip_weight, preferred_element_type=jnp.float32)
 
     mode_grads = jnp.einsum("jkc,kf->jfc", slope_b, fourier, preferred_element_type=jnp.float32)

time: 108 us -> 96.2 us (0.89)
  local copies, waits for them, and re-layouts: 25.9 us -> 20.6 us
  waiting for transfers between devices: 21.9 us -> 18 us
  other arithmetic: 6.82 us -> 3.31 us
  starting transfers between devices: 32 us -> 33.3 us
    ppermute x4 -> x6, waiting for transfers between devices: 6.14 us -> 1.87 us  [xor_reduce_scatter(): lax.ppermute(sent, axis_name, [(i, i ^ mask) for i in range(groups)])]
    select_n x9 -> x1, other arithmetic: 3.03 us -> 0.01 us  [local(): rows_both = both[jnp.take(slot_degree, slot_src)[:, None], my_rows[None, :]]]
    gather x7 -> x3, local copies, waits for them, and re-layouts: 6.65 us -> 3.87 us  [the longest x2 2.28 us: local(): rows_both = both[jnp.take(slot_degree, slot_src)[:, None], my_rows[None, :]]]
    select_n x6 -> x0, local copies, waits for them, and re-layouts: 2.74 us -> none  [the longest x2 0.92 us: local(): own_quad = jnp.take(jnp.take(quad_all, own_deg, axis=0), row_cols, axis=2)]
    transpose x0 -> x3, local copies, waits for them, and re-layouts: none -> 1.56 us  [the longest x1 0.83 us: local(): rows_quad = rows_both[:, :, :nf].transpose(0, 2, 1)]
    ppermute x4 -> x6, starting transfers between devices: 5.44 us -> 6.82 us  [xor_reduce_scatter(): lax.ppermute(sent, axis_name, [(i, i ^ mask) for i in range(groups)])]
    unnamed x33 -> x35, local copies, waits for them, and re-layouts: 14.2 us -> 13.6 us
  transfers between devices with their start and end apart: 28 -> 30, of which waited for: 9 -> 8; matrix products, arithmetic and copies ran while one was open for 32% -> 24% of each run, Pallas kernels for 0% -> 0%
where the time goes in v4:
time: 96.2 us; the launch traced here: 95.5 us
  starting transfers between devices  33.3 us (35%)
  local copies, waits for them, and re-layouts  20.6 us (21%)
  matrix products  19.3 us (20%)
  waiting for transfers between devices  18 us (19%)
  other arithmetic  3.31 us (3%)
  between operations  0.97 us (1%)
    ppermute x24, starting transfers between devices, xor_gather(): lax.ppermute(cur, axis_name, [(i, i ^ mask) for i in range(groups)])  26.5 us
    ppermute x24, waiting for transfers between devices, xor_gather(): lax.ppermute(cur, axis_name, [(i, i ^ mask) for i in range(groups)])  16.1 us
    unnamed x35, local copies, waits for them, and re-layouts  13.6 us
    ppermute x6, starting transfers between devices, xor_reduce_scatter(): lax.ppermute(sent, axis_name, [(i, i ^ mask) for i in range(groups)])  6.82 us
    dot_general x1, matrix products, local(): jnp.einsum('jkc,cd->jkd', activations, skip_weight, preferred_element_typ...  4.41 us
    dot_general x1, matrix products, local(): jnp.einsum('jkd,cd->jkc', slope_b, skip_weight, preferred_element_type=jn...  3.17 us
    gather x2, local copies, waits for them, and re-layouts, local(): rows_both = both[jnp.take(slot_degree, slot_src)[:, None], my_rows[None, :]]  2.28 us
  transfers between devices with their start and end apart: 30, of which 8 were waited for; matrix products, arithmetic and copies ran while one was open for 24% of the time, Pallas kernels for 0%

profile of v4, /device:TPU:0, one launch (start us, length us, event | category | flops | bytes accessed | tf_op | source)
XLA Modules:
  0.0 95.5 jit_solution(5021304995395442697)
XLA Ops:
  0.7 1.6 %copy-done = bf16[2,1440,384]{2,1,0:T(8,128)(2,1)S(1)} copy-done((bf16[2,1440,384]{2,1,0:T(8,128)(2,1)S(1)}, bf16[2,1440,384]{2,1,0:T(8,128)(2,1)}, u32[]{:S(2)}) %copy-start) | copy-done | bytes 2211864
  2.3 1.7 %constant_dynamic-update-slice_fusion.6 = (f32[16,2,8,384]{3,2,1,0:T(8,128)}, f32[1,2,8,384]{3,2,1,0:T(8,128)S(1)}) fusion(bf16[1440,8,1]{0,1,2:T(8,128)(2,1)} %constant.149, bf16[2,1440,384]{2,1,0:T(8,128)(2,1)S(1)} %copy-done), kind=kOutput, calls=%fused_computation.88 | convolution fusion | flops 17694720 | bytes 2284032 | tf_op jit(solution)/shard_map/jkc,kf->jfc/dot_general | solution.py:200
  4.5 2.5 %collective-permute-start.1 = (f32[1,2,8,384]{3,2,1,0:T(8,128)S(1)}, f32[1,2,8,384]{3,2,1,0:T(8,128)}, u32[]{:S(2)}, u32[]{:S(2)}) collective-permute-start(f32[1,2,8,384]{3,2,1,0:T(8,128)S(1)} %get-tuple-element.28), channel_id=1, source_target_pairs={{0,2},{1,3},{2,0},{3,1},{4,6},{5,7},{6,4},{7,5},{8,10},{9,11},{10,... | collective-permute-start | bytes 73736 | tf_op jit(solution)/shard_map/ppermute | solution.py:101
  8.1 1.6 %gather_fusion = f32[64,16]{1,0:T(8,128)S(1)} fusion(f32[32,32,16]{2,1,0:T(8,128)} %constant.122, s32[64]{0:T(128)S(1)} %reshape.205), kind=kCustom, calls=%fused_computation | custom fusion | bytes 8704 | tf_op jit(solution)/shard_map/gather | solution.py:187
  10.0 1.6 %gather_fusion.2 = f32[64,16]{1,0:T(8,128)S(1)} fusion(f32[32,32,16]{2,1,0:T(8,128)} %constant.122, s32[64]{0:T(128)S(1)} %reshape.219), kind=kCustom, calls=%fused_computation.2 | custom fusion | bytes 8704 | tf_op jit(solution)/shard_map/gather | solution.py:189
  12.4 1.8 %collective-permute-start.3 = (f32[4,2,8,384]{3,2,1,0:T(8,128)S(1)}, f32[4,2,8,384]{3,2,1,0:T(8,128)S(1)}, u32[]{:S(2)}, u32[]{:S(2)}) collective-permute-start(f32[4,2,8,384]{3,2,1,0:T(8,128)S(1)} %pad_maximum_fusion.1), channel_id=1, source_target_pairs={{0,4},{1,5},{2,6},{3,7},{4,0},{5,1},{6,2},{7,3},{8,12},{9,13},{10,... | collective-permute-start | bytes 294920 | tf_op jit(solution)/shard_map/ppermute | solution.py:101
  14.2 2.6 %collective-permute-start.4 = (f32[4,2,8,384]{3,2,1,0:T(8,128)S(1)}, f32[4,2,8,384]{3,2,1,0:T(8,128)S(1)}, u32[]{:S(2)}, u32[]{:S(2)}) collective-permute-start(f32[4,2,8,384]{3,2,1,0:T(8,128)S(1)} %pad_maximum_fusion.1), channel_id=1, source_target_pairs={{0,8},{1,9},{2,10},{3,11},{4,12},{5,13},{6,14},{7,15},{8,0},{9,1},... | collective-permute-start | bytes 294920 | tf_op jit(solution)/shard_map/ppermute | solution.py:101
  17.5 1.3 %constant_dynamic-update-slice_fusion.4 = f32[16,2,8,384]{3,2,1,0:T(8,128)} fusion(f32[16,2,8,384]{3,2,1,0:T(8,128)} %constant_dynamic-update-slice_fusion.5, f32[1,2,8,384]{3,2,1,0:T(8,128)} %collective-permute-done.1), kind=kLoop, calls=%fused_computation.86 | loop fusion | bytes 49152
  18.8 1.3 %constant_dynamic-update-slice_fusion.3 = f32[16,2,8,384]{3,2,1,0:T(8,128)} fusion(f32[16,2,8,384]{3,2,1,0:T(8,128)} %constant_dynamic-update-slice_fusion.4, f32[1,2,8,384]{3,2,1,0:T(8,128)} %collective-permute-done.2), kind=kLoop, calls=%fused_computation.85 | loop fusion | bytes 49152
  20.8 4.1 %collective-permute-done.4 = f32[4,2,8,384]{3,2,1,0:T(8,128)S(1)} collective-permute-done((f32[4,2,8,384]{3,2,1,0:T(8,128)S(1)}, f32[4,2,8,384]{3,2,1,0:T(8,128)S(1)}, u32[]{:S(2)}, u32[]{:S(2)}) %collective-permute-start.4) | collective-permute-done | bytes 98336 | tf_op jit(solution)/shard_map/ppermute | solution.py:101
  26.2 1.4 %fusion.16 = bf16[2,8,384]{2,0,1:T(2,128)(2,1)S(1)} fusion(f32[32,8,384]{2,1,0:T(8,128)} %bitcast.119, f32[2,32,8]{1,0,2:T(2,128)S(1)} %copy.62), kind=kOutput, calls=%fused_computation.36 | convolution fusion | flops 2365440 | bytes 407552 | tf_op jit(solution)/shard_map/sfj,jfc->sfc/dot_general | solution.py:202
  29.0 1.5 %collective-permute-start.7 = (bf16[1,2,8,384]{3,2,1,0:T(8,128)(2,1)}, bf16[1,2,8,384]{3,2,1,0:T(8,128)(2,1)}, u32[]{:S(2)}, u32[]{:S(2)}) collective-permute-start(bf16[1,2,8,384]{3,2,1,0:T(8,128)(2,1)} %get-tuple-element.23), channel_id=1, source_target_pairs={{0,2},{1,3},{2,0},{3,1},{4,6},{5,7},{6,4},{7,5},{8,10},{9,11},{10,... | collective-permute-start | bytes 36872 | tf_op jit(solution)/shard_map/ppermute | solution.py:101
  34.7 1.3 %collective-permute-start.9 = (bf16[4,2,8,384]{3,2,1,0:T(8,128)(2,1)S(1)}, bf16[4,2,8,384]{3,2,1,0:T(8,128)(2,1)S(1)}, u32[]{:S(2)}, u32[]{:S(2)}) collective-permute-start(bf16[4,2,8,384]{3,2,1,0:T(8,128)(2,1)S(1)} %pad_maximum_fusion.3), channel_id=1, source_target_pairs={{0,4},{1,5},{2,6},{3,7},{4,0},{5,1},{6,2},{7,3},{8,12},{9,13},{10,... | collective-permute-start | bytes 147464 | tf_op jit(solution)/shard_map/ppermute | solution.py:101
  36.0 2.0 %collective-permute-start.10 = (bf16[4,2,8,384]{3,2,1,0:T(8,128)(2,1)S(1)}, bf16[4,2,8,384]{3,2,1,0:T(8,128)(2,1)S(1)}, u32[]{:S(2)}, u32[]{:S(2)}) collective-permute-start(bf16[4,2,8,384]{3,2,1,0:T(8,128)(2,1)S(1)} %pad_maximum_fusion.3), channel_id=1, source_target_pairs={{0,8},{1,9},{2,10},{3,11},{4,12},{5,13},{6,14},{7,15},{8,0},{9,1},... | collective-permute-start | bytes 147464 | tf_op jit(solution)/shard_map/ppermute | solution.py:101
  39.2 1.3 %constant_dynamic-update-slice_fusion.12 = bf16[16,2,8,384]{3,2,1,0:T(8,128)(2,1)} fusion(bf16[16,2,8,384]{3,2,1,0:T(8,128)(2,1)} %get-tuple-element.24, bf16[1,2,8,384]{3,2,1,0:T(8,128)(2,1)} %collective-permute-done.6), kind=kLoop, calls=%fused_computation.94 | loop fusion | bytes 24576
  40.5 1.3 %constant_dynamic-update-slice_fusion.11 = bf16[16,2,8,384]{3,2,1,0:T(8,128)(2,1)} fusion(bf16[16,2,8,384]{3,2,1,0:T(8,128)(2,1)} %constant_dynamic-update-slice_fusion.12, bf16[1,2,8,384]{3,2,1,0:T(8,128)(2,1)} %collective-permute-done.7), kind=kLoop, calls=%fused_computation.93 | loop fusion | bytes 24576
  41.8 1.3 %constant_dynamic-update-slice_fusion.10 = bf16[16,2,8,384]{3,2,1,0:T(8,128)(2,1)} fusion(bf16[16,2,8,384]{3,2,1,0:T(8,128)(2,1)} %constant_dynamic-update-slice_fusion.11, bf16[1,2,8,384]{3,2,1,0:T(8,128)(2,1)} %collective-permute-done.8), kind=kLoop, calls=%fused_computation.92 | loop fusion | bytes 24576
  47.8 4.4 %fusion.6 = bf16[2,1440,384]{2,1,0:T(8,128)(2,1)S(1)} fusion(bf16[2,1440,384]{2,1,0:T(8,128)(2,1)S(1)} %copy-done.3, f32[2,384,1440]{1,2,0:T(8,128)S(1)} %fusion.57, bf16[2,1440,384]{2,1,0:T(8,128)(2,1)S(1)} %copy-done, bf16[384,384]{1,0:T(8,128)(2,1)S(1)} %copy-done.5), kind=kOutput, calls=%fused_computation.14 | convolution fusion | flops 873676800 | bytes 11354112 | tf_op jit(solution)/shard_map/jkc,cd->jkd/dot_general | solution.py:208
  54.5 1.4 %fusion.98 = f32[384,384,1]{0,1,2:T(8,128)S(1)} fusion(bf16[2,1440,384]{2,1,0:T(8,128)(2,1)S(1)} %fusion.6, bf16[2,1440,384]{2,1,0:T(8,128)(2,1)S(1)} %copy-done), kind=kOutput, calls=%fused_computation.182 | convolution fusion | flops 849346560 | bytes 5013504 | tf_op jit(solution)/shard_map/jkc,jkd->cd/dot_general | solution.py:212
  56.6 1.4 %collective-permute-start.25 = (f32[4,24,384]{2,1,0:T(8,128)S(1)}, f32[4,24,384]{2,1,0:T(8,128)S(1)}, u32[]{:S(2)}, u32[]{:S(2)}) collective-permute-start(f32[4,24,384]{2,1,0:T(8,128)S(1)} %get-tuple-element.11), channel_id=1, source_target_pairs={{0,2},{1,3},{2,0},{3,1},{4,6},{5,7},{6,4},{7,5},{8,10},{9,11},{10,... | collective-permute-start | bytes 442376 | tf_op jit(solution)/shard_map/ppermute | solution.py:120
  58.4 2.9 %collective-permute-start.16 = (f32[4,2,8,384]{3,2,1,0:T(8,128)S(1)}, f32[4,2,8,384]{3,2,1,0:T(8,128)S(1)}, u32[]{:S(2)}, u32[]{:S(2)}) collective-permute-start(f32[4,2,8,384]{3,2,1,0:T(8,128)S(1)} %pad_maximum_fusion.2), channel_id=1, source_target_pairs={{0,8},{1,9},{2,10},{3,11},{4,12},{5,13},{6,14},{7,15},{8,0},{9,1},... | collective-permute-start | bytes 294920 | tf_op jit(solution)/shard_map/ppermute | solution.py:101
  62.5 1.6 %collective-permute-done.15 = f32[4,2,8,384]{3,2,1,0:T(8,128)S(1)} collective-permute-done((f32[4,2,8,384]{3,2,1,0:T(8,128)S(1)}, f32[4,2,8,384]{3,2,1,0:T(8,128)S(1)}, u32[]{:S(2)}, u32[]{:S(2)}) %collective-permute-start.15) | collective-permute-done | bytes 98336 | tf_op jit(solution)/shard_map/ppermute | solution.py:101
  64.1 5.0 %collective-permute-done.16 = f32[4,2,8,384]{3,2,1,0:T(8,128)S(1)} collective-permute-done((f32[4,2,8,384]{3,2,1,0:T(8,128)S(1)}, f32[4,2,8,384]{3,2,1,0:T(8,128)S(1)}, u32[]{:S(2)}, u32[]{:S(2)}) %collective-permute-start.16) | collective-permute-done | bytes 98336 | tf_op jit(solution)/shard_map/ppermute | solution.py:101
  75.8 1.7 %collective-permute-start.21 = (bf16[4,2,8,384]{3,2,1,0:T(8,128)(2,1)S(1)}, bf16[4,2,8,384]{3,2,1,0:T(8,128)(2,1)S(1)}, u32[]{:S(2)}, u32[]{:S(2)}) collective-permute-start(bf16[4,2,8,384]{3,2,1,0:T(8,128)(2,1)S(1)} %pad_maximum_fusion.4), channel_id=1, source_target_pairs={{0,4},{1,5},{2,6},{3,7},{4,0},{5,1},{6,2},{7,3},{8,12},{9,13},{10,... | collective-permute-start | bytes 147464 | tf_op jit(solution)/shard_map/ppermute | solution.py:101
  77.6 1.4 %collective-permute-start.22 = (bf16[4,2,8,384]{3,2,1,0:T(8,128)(2,1)S(1)}, bf16[4,2,8,384]{3,2,1,0:T(8,128)(2,1)S(1)}, u32[]{:S(2)}, u32[]{:S(2)}) collective-permute-start(bf16[4,2,8,384]{3,2,1,0:T(8,128)(2,1)S(1)} %pad_maximum_fusion.4), channel_id=1, source_target_pairs={{0,8},{1,9},{2,10},{3,11},{4,12},{5,13},{6,14},{7,15},{8,0},{9,1},... | collective-permute-start | bytes 147464 | tf_op jit(solution)/shard_map/ppermute | solution.py:101
  79.1 1.4 %collective-permute-start.29 = (f32[1,24,384]{2,1,0:T(8,128)S(1)}, f32[1,24,384]{2,1,0:T(8,128)S(1)}, u32[]{:S(2)}, u32[]{:S(2)}) collective-permute-start(f32[1,24,384]{2,1,0:T(8,128)S(1)} %get-tuple-element.13), channel_id=1, source_target_pairs={{0,12},{1,13},{2,14},{3,15},{4,8},{5,9},{6,10},{7,11},{8,4},{9,5},... | collective-permute-start | bytes 110600 | tf_op jit(solution)/shard_map/ppermute | solution.py:120
  80.5 1.8 %collective-permute-start.28 = (f32[1,24,384]{2,1,0:T(8,128)S(1)}, f32[1,24,384]{2,1,0:T(8,128)S(1)}, u32[]{:S(2)}, u32[]{:S(2)}) collective-permute-start(f32[1,24,384]{2,1,0:T(8,128)S(1)} %get-tuple-element.14), channel_id=1, source_target_pairs={{0,8},{1,9},{2,10},{3,11},{4,12},{5,13},{6,14},{7,15},{8,0},{9,1},... | collective-permute-start | bytes 110600 | tf_op jit(solution)/shard_map/ppermute | solution.py:120
  82.2 1.3 %collective-permute-start.27 = (f32[1,24,384]{2,1,0:T(8,128)S(1)}, f32[1,24,384]{2,1,0:T(8,128)S(1)}, u32[]{:S(2)}, u32[]{:S(2)}) collective-permute-start(f32[1,24,384]{2,1,0:T(8,128)S(1)} %get-tuple-element.12), channel_id=1, source_target_pairs={{0,4},{1,5},{2,6},{3,7},{4,0},{5,1},{6,2},{7,3},{8,12},{9,13},{10,... | collective-permute-start | bytes 110600 | tf_op jit(solution)/shard_map/ppermute | solution.py:120
  83.6 1.8 %collective-permute-done.29 = f32[1,24,384]{2,1,0:T(8,128)S(1)} collective-permute-done((f32[1,24,384]{2,1,0:T(8,128)S(1)}, f32[1,24,384]{2,1,0:T(8,128)S(1)}, u32[]{:S(2)}, u32[]{:S(2)}) %collective-permute-start.29) | collective-permute-done | bytes 36896 | tf_op jit(solution)/shard_map/ppermute | solution.py:120
  85.4 1.2 %collective-permute-start.23 = (bf16[4,2,8,384]{3,2,1,0:T(8,128)(2,1)S(1)}, bf16[4,2,8,384]{3,2,1,0:T(8,128)(2,1)S(1)}, u32[]{:S(2)}, u32[]{:S(2)}) collective-permute-start(bf16[4,2,8,384]{3,2,1,0:T(8,128)(2,1)S(1)} %pad_maximum_fusion.4), channel_id=1, source_target_pairs={{0,12},{1,13},{2,14},{3,15},{4,8},{5,9},{6,10},{7,11},{8,4},{9,5},... | collective-permute-start | bytes 147464 | tf_op jit(solution)/shard_map/ppermute | solution.py:101
  87.3 3.9 %collective-permute-done.23 = bf16[4,2,8,384]{3,2,1,0:T(8,128)(2,1)S(1)} collective-permute-done((bf16[4,2,8,384]{3,2,1,0:T(8,128)(2,1)S(1)}, bf16[4,2,8,384]{3,2,1,0:T(8,128)(2,1)S(1)}, u32[]{:S(2)}, u32[]{:S(2)}) %collective-permute-start.23) | collective-permute-done | bytes 49184 | tf_op jit(solution)/shard_map/ppermute | solution.py:101
  92.3 3.2 %fusion.11 = bf16[2,1440,384]{2,1,0:T(8,128)(2,1)} fusion(bf16[2,1440,384]{2,1,0:T(8,128)(2,1)S(1)} %copy-done.3, f32[2,384,1440]{1,2,0:T(8,128)S(1)} %fusion.60, bf16[2,1440,384]{2,1,0:T(8,128)(2,1)S(1)} %fusion.6, bf16[384,384]{1,0:T(8,128)(2,1)S(1)} %copy-done.5), kind=kOutput, calls=%fused_computation.19 | convolution fusion | flops 853770240 | bytes 11354112 | tf_op jit(solution)/shard_map/jkd,cd->jkc/dot_general | solution.py:215
  (118 shorter events, 29.7 us)
Async XLA Ops:
  0.7 26.9 %copy-start.2 = (bf16[2,2,384,384]{3,2,1,0:T(8,128)(2,1)S(1)}, bf16[2,2,384,384]{3,2,1,0:T(8,128)(2,1)}, u32[]{:S(2)}) copy-start(bf16[2,2,384,384]{3,2,1,0:T(8,128)(2,1)} %param.11) | copy-start | bytes 3538948
  4.0 7.6 %collective-permute-start = (f32[1,2,8,384]{3,2,1,0:T(8,128)S(1)}, f32[1,2,8,384]{3,2,1,0:T(8,128)S(1)}, u32[]{:S(2)}, u32[]{:S(2)}) collective-permute-start(f32[1,2,8,384]{3,2,1,0:T(8,128)S(1)} %get-tuple-element.28), channel_id=1, source_target_pairs={{0,1},{1,0},{2,3},{3,2},{4,5},{5,4},{6,7},{7,6},{8,9},{9,8},{10,11... | collective-permute-start | bytes 73736 | tf_op jit(solution)/shard_map/ppermute | solution.py:101
  4.5 7.2 %collective-permute-start.1 = (f32[1,2,8,384]{3,2,1,0:T(8,128)S(1)}, f32[1,2,8,384]{3,2,1,0:T(8,128)}, u32[]{:S(2)}, u32[]{:S(2)}) collective-permute-start(f32[1,2,8,384]{3,2,1,0:T(8,128)S(1)} %get-tuple-element.28), channel_id=1, source_target_pairs={{0,2},{1,3},{2,0},{3,1},{4,6},{5,7},{6,4},{7,5},{8,10},{9,11},{10,... | collective-permute-start | bytes 73736 | tf_op jit(solution)/shard_map/ppermute | solution.py:101
  7.0 4.7 %collective-permute-start.2 = (f32[1,2,8,384]{3,2,1,0:T(8,128)S(1)}, f32[1,2,8,384]{3,2,1,0:T(8,128)}, u32[]{:S(2)}, u32[]{:S(2)}) collective-permute-start(f32[1,2,8,384]{3,2,1,0:T(8,128)S(1)} %get-tuple-element.28), channel_id=1, source_target_pairs={{0,3},{1,2},{2,1},{3,0},{4,7},{5,6},{6,5},{7,4},{8,11},{9,10},{10,... | collective-permute-start | bytes 73736 | tf_op jit(solution)/shard_map/ppermute | solution.py:101
  12.4 7.7 %collective-permute-start.3 = (f32[4,2,8,384]{3,2,1,0:T(8,128)S(1)}, f32[4,2,8,384]{3,2,1,0:T(8,128)S(1)}, u32[]{:S(2)}, u32[]{:S(2)}) collective-permute-start(f32[4,2,8,384]{3,2,1,0:T(8,128)S(1)} %pad_maximum_fusion.1), channel_id=1, source_target_pairs={{0,4},{1,5},{2,6},{3,7},{4,0},{5,1},{6,2},{7,3},{8,12},{9,13},{10,... | collective-permute-start | bytes 294920 | tf_op jit(solution)/shard_map/ppermute | solution.py:101
  14.2 10.6 %collective-permute-start.4 = (f32[4,2,8,384]{3,2,1,0:T(8,128)S(1)}, f32[4,2,8,384]{3,2,1,0:T(8,128)S(1)}, u32[]{:S(2)}, u32[]{:S(2)}) collective-permute-start(f32[4,2,8,384]{3,2,1,0:T(8,128)S(1)} %pad_maximum_fusion.1), channel_id=1, source_target_pairs={{0,8},{1,9},{2,10},{3,11},{4,12},{5,13},{6,14},{7,15},{8,0},{9,1},... | collective-permute-start | bytes 294920 | tf_op jit(solution)/shard_map/ppermute | solution.py:101
  16.8 8.7 %collective-permute-start.5 = (f32[4,2,8,384]{3,2,1,0:T(8,128)S(1)}, f32[4,2,8,384]{3,2,1,0:T(8,128)S(1)}, u32[]{:S(2)}, u32[]{:S(2)}) collective-permute-start(f32[4,2,8,384]{3,2,1,0:T(8,128)S(1)} %pad_maximum_fusion.1), channel_id=1, source_target_pairs={{0,12},{1,13},{2,14},{3,15},{4,8},{5,9},{6,10},{7,11},{8,4},{9,5},... | collective-permute-start | bytes 294920 | tf_op jit(solution)/shard_map/ppermute | solution.py:101
  20.8 25.3 %copy-start.4 = (bf16[1440,8,1]{0,1,2:T(8,128)(2,1)S(1)}, bf16[1440,8,1]{0,1,2:T(8,128)(2,1)}, u32[]{:S(2)}) copy-start(bf16[1440,8,1]{0,1,2:T(8,128)(2,1)} %constant.149) | copy-start | bytes 69124
  29.0 3.5 %collective-permute-start.6 = (bf16[1,2,8,384]{3,2,1,0:T(8,128)(2,1)}, bf16[1,2,8,384]{3,2,1,0:T(8,128)(2,1)}, u32[]{:S(2)}, u32[]{:S(2)}) collective-permute-start(bf16[1,2,8,384]{3,2,1,0:T(8,128)(2,1)} %get-tuple-element.23), channel_id=1, source_target_pairs={{0,1},{1,0},{2,3},{3,2},{4,5},{5,4},{6,7},{7,6},{8,9},{9,8},{10,11... | collective-permute-start | bytes 36872 | tf_op jit(solution)/shard_map/ppermute | solution.py:101
  29.0 4.0 %collective-permute-start.7 = (bf16[1,2,8,384]{3,2,1,0:T(8,128)(2,1)}, bf16[1,2,8,384]{3,2,1,0:T(8,128)(2,1)}, u32[]{:S(2)}, u32[]{:S(2)}) collective-permute-start(bf16[1,2,8,384]{3,2,1,0:T(8,128)(2,1)} %get-tuple-element.23), channel_id=1, source_target_pairs={{0,2},{1,3},{2,0},{3,1},{4,6},{5,7},{6,4},{7,5},{8,10},{9,11},{10,... | collective-permute-start | bytes 36872 | tf_op jit(solution)/shard_map/ppermute | solution.py:101
  30.5 3.4 %collective-permute-start.8 = (bf16[1,2,8,384]{3,2,1,0:T(8,128)(2,1)}, bf16[1,2,8,384]{3,2,1,0:T(8,128)(2,1)}, u32[]{:S(2)}, u32[]{:S(2)}) collective-permute-start(bf16[1,2,8,384]{3,2,1,0:T(8,128)(2,1)} %get-tuple-element.23), channel_id=1, source_target_pairs={{0,3},{1,2},{2,1},{3,0},{4,7},{5,6},{6,5},{7,4},{8,11},{9,10},{10,... | collective-permute-start | bytes 36872 | tf_op jit(solution)/shard_map/ppermute | solution.py:101
  34.7 8.4 %collective-permute-start.9 = (bf16[4,2,8,384]{3,2,1,0:T(8,128)(2,1)S(1)}, bf16[4,2,8,384]{3,2,1,0:T(8,128)(2,1)S(1)}, u32[]{:S(2)}, u32[]{:S(2)}) collective-permute-start(bf16[4,2,8,384]{3,2,1,0:T(8,128)(2,1)S(1)} %pad_maximum_fusion.3), channel_id=1, source_target_pairs={{0,4},{1,5},{2,6},{3,7},{4,0},{5,1},{6,2},{7,3},{8,12},{9,13},{10,... | collective-permute-start | bytes 147464 | tf_op jit(solution)/shard_map/ppermute | solution.py:101
  36.0 7.7 %collective-permute-start.10 = (bf16[4,2,8,384]{3,2,1,0:T(8,128)(2,1)S(1)}, bf16[4,2,8,384]{3,2,1,0:T(8,128)(2,1)S(1)}, u32[]{:S(2)}, u32[]{:S(2)}) collective-permute-start(bf16[4,2,8,384]{3,2,1,0:T(8,128)(2,1)S(1)} %pad_maximum_fusion.3), channel_id=1, source_target_pairs={{0,8},{1,9},{2,10},{3,11},{4,12},{5,13},{6,14},{7,15},{8,0},{9,1},... | collective-permute-start | bytes 147464 | tf_op jit(solution)/shard_map/ppermute | solution.py:101
  38.0 6.3 %collective-permute-start.11 = (bf16[4,2,8,384]{3,2,1,0:T(8,128)(2,1)S(1)}, bf16[4,2,8,384]{3,2,1,0:T(8,128)(2,1)S(1)}, u32[]{:S(2)}, u32[]{:S(2)}) collective-permute-start(bf16[4,2,8,384]{3,2,1,0:T(8,128)(2,1)S(1)} %pad_maximum_fusion.3), channel_id=1, source_target_pairs={{0,12},{1,13},{2,14},{3,15},{4,8},{5,9},{6,10},{7,11},{8,4},{9,5},... | collective-permute-start | bytes 147464 | tf_op jit(solution)/shard_map/ppermute | solution.py:101
  52.6 5.4 %collective-permute-start.12 = (f32[1,2,8,384]{3,2,1,0:T(8,128)S(1)}, f32[1,2,8,384]{3,2,1,0:T(8,128)S(1)}, u32[]{:S(2)}, u32[]{:S(2)}) collective-permute-start(f32[1,2,8,384]{3,2,1,0:T(8,128)S(1)} %get-tuple-element.30), channel_id=1, source_target_pairs={{0,1},{1,0},{2,3},{3,2},{4,5},{5,4},{6,7},{7,6},{8,9},{9,8},{10,11... | collective-permute-start | bytes 73736 | tf_op jit(solution)/shard_map/ppermute | solution.py:101
  52.6 5.4 %collective-permute-start.13 = (f32[1,2,8,384]{3,2,1,0:T(8,128)S(1)}, f32[1,2,8,384]{3,2,1,0:T(8,128)S(1)}, u32[]{:S(2)}, u32[]{:S(2)}) collective-permute-start(f32[1,2,8,384]{3,2,1,0:T(8,128)S(1)} %get-tuple-element.30), channel_id=1, source_target_pairs={{0,2},{1,3},{2,0},{3,1},{4,6},{5,7},{6,4},{7,5},{8,10},{9,11},{10,... | collective-permute-start | bytes 73736 | tf_op jit(solution)/shard_map/ppermute | solution.py:101
  53.3 4.7 %collective-permute-start.14 = (f32[1,2,8,384]{3,2,1,0:T(8,128)S(1)}, f32[1,2,8,384]{3,2,1,0:T(8,128)S(1)}, u32[]{:S(2)}, u32[]{:S(2)}) collective-permute-start(f32[1,2,8,384]{3,2,1,0:T(8,128)S(1)} %get-tuple-element.30), channel_id=1, source_target_pairs={{0,3},{1,2},{2,1},{3,0},{4,7},{5,6},{6,5},{7,4},{8,11},{9,10},{10,... | collective-permute-start | bytes 73736 | tf_op jit(solution)/shard_map/ppermute | solution.py:101
  56.0 23.0 %collective-permute-start.26 = (f32[4,24,384]{2,1,0:T(8,128)S(1)}, f32[4,24,384]{2,1,0:T(8,128)S(1)}, u32[]{:S(2)}, u32[]{:S(2)}) collective-permute-start(f32[4,24,384]{2,1,0:T(8,128)S(1)} %get-tuple-element.10), channel_id=1, source_target_pairs={{0,3},{1,2},{2,1},{3,0},{4,7},{5,6},{6,5},{7,4},{8,11},{9,10},{10,... | collective-permute-start | bytes 442376 | tf_op jit(solution)/shard_map/ppermute | solution.py:120
  56.6 22.4 %collective-permute-start.25 = (f32[4,24,384]{2,1,0:T(8,128)S(1)}, f32[4,24,384]{2,1,0:T(8,128)S(1)}, u32[]{:S(2)}, u32[]{:S(2)}) collective-permute-start(f32[4,24,384]{2,1,0:T(8,128)S(1)} %get-tuple-element.11), channel_id=1, source_target_pairs={{0,2},{1,3},{2,0},{3,1},{4,6},{5,7},{6,4},{7,5},{8,10},{9,11},{10,... | collective-permute-start | bytes 442376 | tf_op jit(solution)/shard_map/ppermute | solution.py:120
  58.0 6.0 %collective-permute-start.15 = (f32[4,2,8,384]{3,2,1,0:T(8,128)S(1)}, f32[4,2,8,384]{3,2,1,0:T(8,128)S(1)}, u32[]{:S(2)}, u32[]{:S(2)}) collective-permute-start(f32[4,2,8,384]{3,2,1,0:T(8,128)S(1)} %pad_maximum_fusion.2), channel_id=1, source_target_pairs={{0,4},{1,5},{2,6},{3,7},{4,0},{5,1},{6,2},{7,3},{8,12},{9,13},{10,... | collective-permute-start | bytes 294920 | tf_op jit(solution)/shard_map/ppermute | solution.py:101
  58.4 10.7 %collective-permute-start.16 = (f32[4,2,8,384]{3,2,1,0:T(8,128)S(1)}, f32[4,2,8,384]{3,2,1,0:T(8,128)S(1)}, u32[]{:S(2)}, u32[]{:S(2)}) collective-permute-start(f32[4,2,8,384]{3,2,1,0:T(8,128)S(1)} %pad_maximum_fusion.2), channel_id=1, source_target_pairs={{0,8},{1,9},{2,10},{3,11},{4,12},{5,13},{6,14},{7,15},{8,0},{9,1},... | collective-permute-start | bytes 294920 | tf_op jit(solution)/shard_map/ppermute | solution.py:101
  61.3 7.8 %collective-permute-start.17 = (f32[4,2,8,384]{3,2,1,0:T(8,128)S(1)}, f32[4,2,8,384]{3,2,1,0:T(8,128)S(1)}, u32[]{:S(2)}, u32[]{:S(2)}) collective-permute-start(f32[4,2,8,384]{3,2,1,0:T(8,128)S(1)} %pad_maximum_fusion.2), channel_id=1, source_target_pairs={{0,12},{1,13},{2,14},{3,15},{4,8},{5,9},{6,10},{7,11},{8,4},{9,5},... | collective-permute-start | bytes 294920 | tf_op jit(solution)/shard_map/ppermute | solution.py:101
  70.7 4.7 %collective-permute-start.18 = (bf16[1,2,8,384]{3,2,1,0:T(8,128)(2,1)S(1)}, bf16[1,2,8,384]{3,2,1,0:T(8,128)(2,1)S(1)}, u32[]{:S(2)}, u32[]{:S(2)}) collective-permute-start(bf16[1,2,8,384]{3,2,1,0:T(8,128)(2,1)S(1)} %get-tuple-element.19), channel_id=1, source_target_pairs={{0,1},{1,0},{2,3},{3,2},{4,5},{5,4},{6,7},{7,6},{8,9},{9,8},{10,11... | collective-permute-start | bytes 36872 | tf_op jit(solution)/shard_map/ppermute | solution.py:101
  70.8 5.0 %collective-permute-start.19 = (bf16[1,2,8,384]{3,2,1,0:T(8,128)(2,1)S(1)}, bf16[1,2,8,384]{3,2,1,0:T(8,128)(2,1)S(1)}, u32[]{:S(2)}, u32[]{:S(2)}) collective-permute-start(bf16[1,2,8,384]{3,2,1,0:T(8,128)(2,1)S(1)} %get-tuple-element.19), channel_id=1, source_target_pairs={{0,2},{1,3},{2,0},{3,1},{4,6},{5,7},{6,4},{7,5},{8,10},{9,11},{10,... | collective-permute-start | bytes 36872 | tf_op jit(solution)/shard_map/ppermute | solution.py:101
  71.5 4.3 %collective-permute-start.20 = (bf16[1,2,8,384]{3,2,1,0:T(8,128)(2,1)S(1)}, bf16[1,2,8,384]{3,2,1,0:T(8,128)(2,1)S(1)}, u32[]{:S(2)}, u32[]{:S(2)}) collective-permute-start(bf16[1,2,8,384]{3,2,1,0:T(8,128)(2,1)S(1)} %get-tuple-element.19), channel_id=1, source_target_pairs={{0,3},{1,2},{2,1},{3,0},{4,7},{5,6},{6,5},{7,4},{8,11},{9,10},{10,... | collective-permute-start | bytes 36872 | tf_op jit(solution)/shard_map/ppermute | solution.py:101
  75.5 3.6 %collective-permute-start.24 = (f32[4,24,384]{2,1,0:T(8,128)S(1)}, f32[4,24,384]{2,1,0:T(8,128)S(1)}, u32[]{:S(2)}, u32[]{:S(2)}) collective-permute-start(f32[4,24,384]{2,1,0:T(8,128)S(1)} %get-tuple-element.9), channel_id=1, source_target_pairs={{0,1},{1,0},{2,3},{3,2},{4,5},{5,4},{6,7},{7,6},{8,9},{9,8},{10,11... | collective-permute-start | bytes 442376 | tf_op jit(solution)/shard_map/ppermute | solution.py:120
  75.8 11.5 %collective-permute-start.21 = (bf16[4,2,8,384]{3,2,1,0:T(8,128)(2,1)S(1)}, bf16[4,2,8,384]{3,2,1,0:T(8,128)(2,1)S(1)}, u32[]{:S(2)}, u32[]{:S(2)}) collective-permute-start(bf16[4,2,8,384]{3,2,1,0:T(8,128)(2,1)S(1)} %pad_maximum_fusion.4), channel_id=1, source_target_pairs={{0,4},{1,5},{2,6},{3,7},{4,0},{5,1},{6,2},{7,3},{8,12},{9,13},{10,... | collective-permute-start | bytes 147464 | tf_op jit(solution)/shard_map/ppermute | solution.py:101
  77.6 9.8 %collective-permute-start.22 = (bf16[4,2,8,384]{3,2,1,0:T(8,128)(2,1)S(1)}, bf16[4,2,8,384]{3,2,1,0:T(8,128)(2,1)S(1)}, u32[]{:S(2)}, u32[]{:S(2)}) collective-permute-start(bf16[4,2,8,384]{3,2,1,0:T(8,128)(2,1)S(1)} %pad_maximum_fusion.4), channel_id=1, source_target_pairs={{0,8},{1,9},{2,10},{3,11},{4,12},{5,13},{6,14},{7,15},{8,0},{9,1},... | collective-permute-start | bytes 147464 | tf_op jit(solution)/shard_map/ppermute | solution.py:101
  79.1 6.3 %collective-permute-start.29 = (f32[1,24,384]{2,1,0:T(8,128)S(1)}, f32[1,24,384]{2,1,0:T(8,128)S(1)}, u32[]{:S(2)}, u32[]{:S(2)}) collective-permute-start(f32[1,24,384]{2,1,0:T(8,128)S(1)} %get-tuple-element.13), channel_id=1, source_target_pairs={{0,12},{1,13},{2,14},{3,15},{4,8},{5,9},{6,10},{7,11},{8,4},{9,5},... | collective-permute-start | bytes 110600 | tf_op jit(solution)/shard_map/ppermute | solution.py:120
  80.5 6.1 %collective-permute-start.28 = (f32[1,24,384]{2,1,0:T(8,128)S(1)}, f32[1,24,384]{2,1,0:T(8,128)S(1)}, u32[]{:S(2)}, u32[]{:S(2)}) collective-permute-start(f32[1,24,384]{2,1,0:T(8,128)S(1)} %get-tuple-element.14), channel_id=1, source_target_pairs={{0,8},{1,9},{2,10},{3,11},{4,12},{5,13},{6,14},{7,15},{8,0},{9,1},... | collective-permute-start | bytes 110600 | tf_op jit(solution)/shard_map/ppermute | solution.py:120
  82.2 4.4 %collective-permute-start.27 = (f32[1,24,384]{2,1,0:T(8,128)S(1)}, f32[1,24,384]{2,1,0:T(8,128)S(1)}, u32[]{:S(2)}, u32[]{:S(2)}) collective-permute-start(f32[1,24,384]{2,1,0:T(8,128)S(1)} %get-tuple-element.12), channel_id=1, source_target_pairs={{0,4},{1,5},{2,6},{3,7},{4,0},{5,1},{6,2},{7,3},{8,12},{9,13},{10,... | collective-permute-start | bytes 110600 | tf_op jit(solution)/shard_map/ppermute | solution.py:120
  85.4 5.9 %collective-permute-start.23 = (bf16[4,2,8,384]{3,2,1,0:T(8,128)(2,1)S(1)}, bf16[4,2,8,384]{3,2,1,0:T(8,128)(2,1)S(1)}, u32[]{:S(2)}, u32[]{:S(2)}) collective-permute-start(bf16[4,2,8,384]{3,2,1,0:T(8,128)(2,1)S(1)} %pad_maximum_fusion.4), channel_id=1, source_target_pairs={{0,12},{1,13},{2,14},{3,15},{4,8},{5,9},{6,10},{7,11},{8,4},{9,5},... | collective-permute-start | bytes 147464 | tf_op jit(solution)/shard_map/ppermute | solution.py:101
  (4 other events, 11.4 us)

commit v5 on v4

--- a/solution.py
+++ b/solution.py
@@ -123,6 +123,27 @@
     return cur[0]
 
 
+def xor_exchange(values, table, axis_name, groups, me, lo, spec):
+    parts = [values]
+    for k in range(1, 1 << lo):
+        parts.append(lax.ppermute(values, axis_name, [(i, i ^ k) for i in range(groups)]))
+    stacked = jnp.stack(parts).astype(jnp.float32)
+    cur = jnp.einsum(spec, table, stacked, precision=lax.Precision.HIGHEST)
+    hi = groups.bit_length() - 1 - lo
+    b = 0
+    while b < hi:
+        width = min(2, hi - b)
+        fan = 1 << width
+        view = cur.reshape((cur.shape[0] // fan, fan) + cur.shape[1:])
+        total = view[:, 0]
+        for k in range(1, fan):
+            mask = k << (lo + b)
+            total = total + lax.ppermute(view[:, k], axis_name, [(i, i ^ mask) for i in range(groups)])
+        cur = total
+        b += width
+    return cur[0]
+
+
 def complex_apply(coeffs, weights, orders):
     real_in, imag_in = (coeffs[:, :orders], coeffs[:, orders:])
     real_w, imag_w = (weights[:, 0], weights[:, 1])
@@ -178,31 +199,32 @@
         plm_all = legendre_scan(cosines, sines, degrees, orders)
         quad_all = plm_all * jnp.asarray((math.pi / lat_total * sines).astype(np.float32))[None, None, :]
 
+    bits = groups.bit_length() - 1
+    lo = min(2, bits)
     both = jnp.concatenate([quad_all, plm_all], axis=1).transpose(0, 2, 1)
-    row_ids = jnp.arange(lat_total, dtype=jnp.int32)
-    row_cols = jnp.bitwise_xor(me, row_ids // lat_rows) * lat_rows + row_ids % lat_rows
-    slot_ids = jnp.arange(degrees, dtype=jnp.int32)
-    slot_src = jnp.bitwise_xor(me, slot_ids // per_owner) * per_owner + slot_ids % per_owner
-    own_deg = lax.dynamic_slice_in_dim(slot_degree, me * per_owner, per_owner)
-    own_both = both[own_deg[:, None], row_cols[None, :]]
-    my_rows = me * lat_rows + jnp.arange(lat_rows, dtype=jnp.int32)
-    rows_both = both[jnp.take(slot_degree, slot_src)[:, None], my_rows[None, :]]
+    near = jnp.bitwise_xor(me, jnp.arange(1 << lo, dtype=jnp.int32))
+    far = jnp.bitwise_xor(me >> lo, jnp.arange(groups >> lo, dtype=jnp.int32)) * (1 << lo) + (me & ((1 << lo) - 1))
+    slot_r = jnp.arange(per_owner, dtype=jnp.int32)
+    row_r = jnp.arange(lat_rows, dtype=jnp.int32)
+    far_deg = jnp.take(slot_degree, far[:, None] * per_owner + slot_r[None, :])
+    near_rows = near[:, None] * lat_rows + row_r[None, :]
+    own_both = both[far_deg[:, :, None, None], near_rows[None, None, :, :]]
+    near_deg = jnp.take(slot_degree, near[:, None] * per_owner + slot_r[None, :])
+    far_rows = far[:, None] * lat_rows + row_r[None, :]
+    rows_both = both[near_deg[None, :, :, None], far_rows[:, None, None, :]]
     nf = 2 * orders
-    own_quad = own_both[:, :, :nf].transpose(0, 2, 1)
-    own_plm = own_both[:, :, nf:].transpose(0, 2, 1)
-    rows_quad = rows_both[:, :, :nf].transpose(0, 2, 1)
-    rows_plm = rows_both[:, :, nf:].transpose(0, 2, 1)
-
-    def gather(values):
-        out = xor_gather(values, "lat", groups)
-        return out.reshape((-1,) + out.shape[2:])
+    own_quad, own_plm = own_both[..., :nf], own_both[..., nf:]
+    rows_plm, rows_quad = rows_both[..., nf:], rows_both[..., :nf]
+    to_owners = "xskrf,krfc->xsfc"
+    to_rows = "xksrf,ksfc->xrfc"
+
+    def exchange(values, table, spec):
+        return xor_exchange(values, table, "lat", groups, me, lo, spec)
 
     spectrum = jnp.einsum("jkc,kf->jfc", activations, fourier, preferred_element_type=jnp.float32)
-    all_spectrum = gather(spectrum)
-    coeffs = jnp.einsum("sfj,jfc->sfc", own_quad, all_spectrum, precision=highest).astype(jnp.bfloat16)
+    coeffs = exchange(spectrum, own_quad, to_owners).astype(jnp.bfloat16)
     filtered = complex_apply(coeffs, spectral_weight, orders).astype(jnp.bfloat16)
-    all_filtered = gather(filtered).astype(jnp.float32)
-    grid_modes = jnp.einsum("sfj,sfc->jfc", rows_plm, all_filtered, precision=highest).astype(jnp.bfloat16)
+    grid_modes = exchange(filtered, rows_plm, to_rows).astype(jnp.bfloat16)
 
     spatial = jnp.einsum("jfc,kf->jkc", grid_modes, fourier, preferred_element_type=jnp.float32)
     skip_out = jnp.einsum("jkc,cd->jkd", activations, skip_weight, preferred_element_type=jnp.float32)
@@ -215,12 +237,9 @@
     through_skip = jnp.einsum("jkd,cd->jkc", slope_b, skip_weight, preferred_element_type=jnp.float32)
 
     mode_grads = jnp.einsum("jkc,kf->jfc", slope_b, fourier, preferred_element_type=jnp.float32)
-    all_mode_grads = gather(mode_grads)
-    coeff_grads = jnp.einsum("sfj,jfc->sfc", own_plm, all_mode_grads, precision=highest).astype(jnp.bfloat16)
+    coeff_grads = exchange(mode_grads, own_plm, to_owners).astype(jnp.bfloat16)
     weight_grads, back_coeffs = complex_adjoint(coeffs, coeff_grads, spectral_weight, orders)
-    back_b = back_coeffs.astype(jnp.bfloat16)
-    all_back = gather(back_b).astype(jnp.float32)
-    row_grads = jnp.einsum("sfj,sfc->jfc", rows_quad, all_back, precision=highest).astype(jnp.bfloat16)
+    row_grads = exchange(back_coeffs.astype(jnp.bfloat16), rows_quad, to_rows).astype(jnp.bfloat16)
     through_modes = jnp.einsum("jfc,kf->jkc", row_grads, fourier, preferred_element_type=jnp.float32)
     grad_activations = (upstream.astype(jnp.float32) + through_skip + through_modes).astype(jnp.bfloat16)
     return (grad_activations, weight_grads.astype(jnp.bfloat16), grad_skip)

time: 96.2 us -> 86.3 us (0.90)
  waiting for transfers between devices: 18 us -> 12.3 us
  local copies, waits for them, and re-layouts: 20.6 us -> 15.4 us
  matrix products: 19.3 us -> 22.2 us
  starting transfers between devices: 33.3 us -> 31.3 us
    ppermute x24, waiting for transfers between devices: 16.1 us -> 6.66 us  [the longest x12 5.01 us: xor_exchange(): lax.ppermute(view[:, k], axis_name, [(i, i ^ mask) for i in range(groups)])]
    unnamed x35, local copies, waits for them, and re-layouts: 13.6 us -> 8.01 us
    dot_general x1, matrix products: 0.78 us -> 5.99 us  [local(): jnp.einsum('jfc,kf->jkc', grid_modes, fourier, preferred_element_type=jnp...]
    ppermute x6, waiting for transfers between devices: 1.87 us -> 5.65 us  [xor_reduce_scatter(): lax.ppermute(sent, axis_name, [(i, i ^ mask) for i in range(groups)])]
    ppermute x24, starting transfers between devices: 26.5 us -> 24.3 us  [the longest x12 15.2 us: xor_exchange(): lax.ppermute(view[:, k], axis_name, [(i, i ^ mask) for i in range(groups)])]
    slice x1 -> x6, local copies, waits for them, and re-layouts: 0.07 us -> 2.24 us  [the longest x4 0.87 us: xor_exchange(): total = view[:, 0]]
    dot_general x4, matrix products: 3.16 us -> 1.35 us  [xor_exchange(): cur = jnp.einsum(spec, table, stacked, precision=lax.Precision.HIGHEST)]
    dot_general x1, matrix products: 0.78 us -> 2.45 us  [local(): jnp.einsum('jfc,kf->jkc', row_grads, fourier, preferred_element_type=jnp....]
  transfers between devices with their start and end apart: 30 -> 30, of which waited for: 8 -> 8; matrix products, arithmetic and copies ran while one was open for 24% -> 26% of each run, Pallas kernels for 0% -> 0%
where the time goes in v5:
time: 86.3 us; the launch traced here: 85.8 us
  starting transfers between devices  31.3 us (36%)
  matrix products  22.2 us (26%)
  local copies, waits for them, and re-layouts  15.4 us (18%)
  waiting for transfers between devices  12.3 us (14%)
  other arithmetic  3.59 us (4%)
  between operations  1.1 us (1%)
    ppermute x12, starting transfers between devices, xor_exchange(): lax.ppermute(view[:, k], axis_name, [(i, i ^ mask) for i in range(groups)])  15.2 us
    ppermute x12, starting transfers between devices, xor_exchange(): lax.ppermute(values, axis_name, [(i, i ^ k) for i in range(groups)])  9.07 us
    unnamed x35, local copies, waits for them, and re-layouts  8.01 us
    ppermute x6, starting transfers between devices, xor_reduce_scatter(): lax.ppermute(sent, axis_name, [(i, i ^ mask) for i in range(groups)])  6.99 us
    dot_general x1, matrix products, local(): jnp.einsum('jfc,kf->jkc', grid_modes, fourier, preferred_element_type=jnp...  5.99 us
    ppermute x6, waiting for transfers between devices, xor_reduce_scatter(): lax.ppermute(sent, axis_name, [(i, i ^ mask) for i in range(groups)])  5.65 us
    ppermute x12, waiting for transfers between devices, xor_exchange(): lax.ppermute(view[:, k], axis_name, [(i, i ^ mask) for i in range(groups)])  5.01 us
    dot_general x1, matrix products, local(): jnp.einsum('jkc,cd->jkd', activations, skip_weight, preferred_element_typ...  4.51 us
  transfers between devices with their start and end apart: 30, of which 8 were waited for; matrix products, arithmetic and copies ran while one was open for 26% of the time, Pallas kernels for 0%

profile of v5, /device:TPU:0, one launch (start us, length us, event | category | flops | bytes accessed | tf_op | source)
XLA Modules:
  0.0 85.8 jit_solution(8515821842781967258)
XLA Ops:
  0.7 1.6 %copy-done = bf16[2,1440,384]{2,1,0:T(8,128)(2,1)S(1)} copy-done((bf16[2,1440,384]{2,1,0:T(8,128)(2,1)S(1)}, bf16[2,1440,384]{2,1,0:T(8,128)(2,1)}, u32[]{:S(2)}) %copy-start) | copy-done | bytes 2211864
  2.3 1.1 %fusion.102 = f32[8,2,384]{2,0,1:T(8,128)S(1)} fusion(bf16[1440,8,1]{0,1,2:T(8,128)(2,1)} %constant.108, bf16[2,1440,384]{2,1,0:T(8,128)(2,1)S(1)} %copy-done), kind=kOutput, calls=%fused_computation.165 | convolution fusion | flops 17694720 | bytes 2259456 | tf_op jit(solution)/shard_map/jkc,kf->jfc/dot_general | solution.py:224
  3.4 3.0 %collective-permute-start.1 = (f32[2,8,384]{2,1,0:T(8,128)S(1)}, f32[2,8,384]{2,1,0:T(8,128)S(1)}, u32[]{:S(2)}, u32[]{:S(2)}) collective-permute-start(f32[2,8,384]{2,1,0:T(8,128)S(1)} %bitcast.231), channel_id=1, source_target_pairs={{0,2},{1,3},{2,0},{3,1},{4,6},{5,7},{6,4},{7,5},{8,10},{9,11},{10,... | collective-permute-start | bytes 73736 | tf_op jit(solution)/shard_map/ppermute | solution.py:129
  8.6 1.6 %gather_fusion = f32[64,16]{1,0:T(8,128)S(1)} fusion(f32[32,32,16]{2,1,0:T(8,128)} %constant.81, s32[64]{0:T(128)S(1)} %reshape.185), kind=kCustom, calls=%fused_computation.2 | custom fusion | bytes 8704 | tf_op jit(solution)/shard_map/gather | solution.py:211
  14.2 3.1 %collective-permute-start.4 = (f32[1,2,8,384]{3,1,2,0:T(2,128)}, f32[1,2,8,384]{3,1,2,0:T(2,128)S(1)}, u32[]{:S(2)}, u32[]{:S(2)}) collective-permute-start(f32[1,2,8,384]{3,1,2,0:T(2,128)} %bitcast.221), channel_id=1, source_target_pairs={{0,8},{1,9},{2,10},{3,11},{4,12},{5,13},{6,14},{7,15},{8,0},{9,1},... | collective-permute-start | bytes 73736 | tf_op jit(solution)/shard_map/ppermute | solution.py:141
  17.3 1.3 %collective-permute-start.5 = (f32[1,2,8,384]{3,1,2,0:T(2,128)}, f32[1,2,8,384]{3,1,2,0:T(2,128)S(1)}, u32[]{:S(2)}, u32[]{:S(2)}) collective-permute-start(f32[1,2,8,384]{3,1,2,0:T(2,128)} %bitcast.226), channel_id=1, source_target_pairs={{0,12},{1,13},{2,14},{3,15},{4,8},{5,9},{6,10},{7,11},{8,4},{9,5},... | collective-permute-start | bytes 73736 | tf_op jit(solution)/shard_map/ppermute | solution.py:141
  19.1 1.6 %gather_fusion.1 = f32[64,16]{1,0:T(8,128)S(1)} fusion(f32[32,32,16]{2,1,0:T(8,128)} %constant.81, s32[64]{0:T(128)S(1)} %reshape.191), kind=kCustom, calls=%fused_computation.3 | custom fusion | bytes 8704 | tf_op jit(solution)/shard_map/gather | solution.py:214
  20.7 2.5 %collective-permute-done.5 = f32[1,2,8,384]{3,1,2,0:T(2,128)S(1)} collective-permute-done((f32[1,2,8,384]{3,1,2,0:T(2,128)}, f32[1,2,8,384]{3,1,2,0:T(2,128)S(1)}, u32[]{:S(2)}, u32[]{:S(2)}) %collective-permute-start.5) | collective-permute-done | bytes 24608 | tf_op jit(solution)/shard_map/ppermute | solution.py:141
  24.6 1.6 %collective-permute-start.7 = (bf16[2,8,384]{2,1,0:T(8,128)(2,1)}, bf16[2,8,384]{2,1,0:T(8,128)(2,1)S(1)}, u32[]{:S(2)}, u32[]{:S(2)}) collective-permute-start(bf16[2,8,384]{2,1,0:T(8,128)(2,1)} %pad_maximum_fusion.1), channel_id=1, source_target_pairs={{0,2},{1,3},{2,0},{3,1},{4,6},{5,7},{6,4},{7,5},{8,10},{9,11},{10,... | collective-permute-start | bytes 36872 | tf_op jit(solution)/shard_map/ppermute | solution.py:129
  31.4 1.2 %collective-permute-start.10 = (f32[1,2,8,384]{3,1,2,0:T(2,128)}, f32[1,2,8,384]{3,1,2,0:T(2,128)}, u32[]{:S(2)}, u32[]{:S(2)}) collective-permute-start(f32[1,2,8,384]{3,1,2,0:T(2,128)} %bitcast.219), channel_id=1, source_target_pairs={{0,8},{1,9},{2,10},{3,11},{4,12},{5,13},{6,14},{7,15},{8,0},{9,1},... | collective-permute-start | bytes 73736 | tf_op jit(solution)/shard_map/ppermute | solution.py:141
  32.6 0.9 %collective-permute-start.11 = (f32[1,2,8,384]{3,1,2,0:T(2,128)}, f32[1,2,8,384]{3,1,2,0:T(2,128)}, u32[]{:S(2)}, u32[]{:S(2)}) collective-permute-start(f32[1,2,8,384]{3,1,2,0:T(2,128)} %bitcast.225), channel_id=1, source_target_pairs={{0,12},{1,13},{2,14},{3,15},{4,8},{5,9},{6,10},{7,11},{8,4},{9,5},... | collective-permute-start | bytes 73736 | tf_op jit(solution)/shard_map/ppermute | solution.py:141
  33.6 1.3 %collective-permute-start.9 = (f32[1,2,8,384]{3,1,2,0:T(2,128)}, f32[1,2,8,384]{3,1,2,0:T(2,128)}, u32[]{:S(2)}, u32[]{:S(2)}) collective-permute-start(f32[1,2,8,384]{3,1,2,0:T(2,128)} %bitcast.220), channel_id=1, source_target_pairs={{0,4},{1,5},{2,6},{3,7},{4,0},{5,1},{6,2},{7,3},{8,12},{9,13},{10,... | collective-permute-start | bytes 73736 | tf_op jit(solution)/shard_map/ppermute | solution.py:141
  34.9 4.5 %fusion.42 = f32[2,1440,384]{2,1,0:T(8,128)} fusion(bf16[2,1440,384]{2,1,0:T(8,128)(2,1)S(1)} %copy-done, bf16[384,384]{1,0:T(8,128)(2,1)} %param.12), kind=kOutput, calls=%fused_computation.63 | convolution fusion | flops 849346560 | bytes 6930432 | tf_op jit(solution)/shard_map/jkc,cd->jkd/dot_general | solution.py:230
  39.6 0.9 %copy.123 = f32[4,4,2,2,8]{1,0,2,3,4:T(4,128)S(1)} copy(f32[4,4,2,2,8]{4,3,2,1,0:T(2,128)} %get-tuple-element.34) | data formatting | bytes 4096
  41.4 6.0 %fusion.6 = bf16[2,1440,384]{2,1,0:T(8,128)(2,1)S(1)} fusion(bf16[2,1440,384]{2,1,0:T(8,128)(2,1)} %param.11, f32[2,1440,384]{2,1,0:T(8,128)} %fusion.42, bf16[1440,8,1]{0,1,2:T(8,128)(2,1)S(1)} %copy-done.5, bf16[2,8,384]{2,0,1:T(2,128)(2,1)S(1)} %fusion.70), kind=kOutput, calls=%fused_computation.15 | convolution fusion | flops 42024960 | bytes 8882688 | tf_op jit(solution)/shard_map/jfc,kf->jkc/dot_general | solution.py:229
  47.8 1.5 %collective-permute-start.13 = (f32[2,8,384]{2,1,0:T(8,128)S(1)}, f32[2,8,384]{2,1,0:T(8,128)S(1)}, u32[]{:S(2)}, u32[]{:S(2)}) collective-permute-start(f32[2,8,384]{2,1,0:T(8,128)S(1)} %bitcast.235), channel_id=1, source_target_pairs={{0,2},{1,3},{2,0},{3,1},{4,6},{5,7},{6,4},{7,5},{8,10},{9,11},{10,... | collective-permute-start | bytes 73736 | tf_op jit(solution)/shard_map/ppermute | solution.py:129
  50.0 1.5 %fusion.40 = f32[2,1440,384]{2,1,0:T(8,128)S(1)} fusion(bf16[2,1440,384]{2,1,0:T(8,128)(2,1)S(1)} %fusion.6, bf16[384,384]{1,0:T(8,128)(2,1)S(1)} %copy-done.4), kind=kOutput, calls=%fused_computation.61 | convolution fusion | flops 849346560 | bytes 6930432 | tf_op jit(solution)/shard_map/jkd,cd->jkc/dot_general | solution.py:237
  51.5 1.4 %fusion.104 = f32[384,384,1]{0,1,2:T(8,128)S(1)} fusion(bf16[2,1440,384]{2,1,0:T(8,128)(2,1)S(1)} %fusion.6, bf16[2,1440,384]{2,1,0:T(8,128)(2,1)S(1)} %copy-done), kind=kOutput, calls=%fused_computation.167 | convolution fusion | flops 849346560 | bytes 5013504 | tf_op jit(solution)/shard_map/jkc,jkd->cd/dot_general | solution.py:234
  53.5 2.2 %collective-permute-start.16 = (f32[1,2,8,384]{3,1,2,0:T(2,128)S(1)}, f32[1,2,8,384]{3,1,2,0:T(2,128)S(1)}, u32[]{:S(2)}, u32[]{:S(2)}) collective-permute-start(f32[1,2,8,384]{3,1,2,0:T(2,128)S(1)} %bitcast.251), channel_id=1, source_target_pairs={{0,8},{1,9},{2,10},{3,11},{4,12},{5,13},{6,14},{7,15},{8,0},{9,1},... | collective-permute-start | bytes 73736 | tf_op jit(solution)/shard_map/ppermute | solution.py:141
  55.7 0.9 %collective-permute-start.17 = (f32[1,2,8,384]{3,1,2,0:T(2,128)S(1)}, f32[1,2,8,384]{3,1,2,0:T(2,128)S(1)}, u32[]{:S(2)}, u32[]{:S(2)}) collective-permute-start(f32[1,2,8,384]{3,1,2,0:T(2,128)S(1)} %bitcast.249), channel_id=1, source_target_pairs={{0,12},{1,13},{2,14},{3,15},{4,8},{5,9},{6,10},{7,11},{8,4},{9,5},... | collective-permute-start | bytes 73736 | tf_op jit(solution)/shard_map/ppermute | solution.py:141
  57.2 1.6 %collective-permute-start.26 = (f32[4,24,384]{2,1,0:T(8,128)S(1)}, f32[4,24,384]{2,1,0:T(8,128)S(1)}, u32[]{:S(2)}, u32[]{:S(2)}) collective-permute-start(f32[4,24,384]{2,1,0:T(8,128)S(1)} %get-tuple-element.11), channel_id=1, source_target_pairs={{0,3},{1,2},{2,1},{3,0},{4,7},{5,6},{6,5},{7,4},{8,11},{9,10},{10,... | collective-permute-start | bytes 442376 | tf_op jit(solution)/shard_map/ppermute | solution.py:120
  58.8 2.5 %collective-permute-done.17 = f32[1,2,8,384]{3,1,2,0:T(2,128)S(1)} collective-permute-done((f32[1,2,8,384]{3,1,2,0:T(2,128)S(1)}, f32[1,2,8,384]{3,1,2,0:T(2,128)S(1)}, u32[]{:S(2)}, u32[]{:S(2)}) %collective-permute-start.17) | collective-permute-done | bytes 24608 | tf_op jit(solution)/shard_map/ppermute | solution.py:141
  62.6 1.6 %collective-permute-start.19 = (bf16[2,8,384]{2,1,0:T(8,128)(2,1)S(1)}, bf16[2,8,384]{2,1,0:T(8,128)(2,1)S(1)}, u32[]{:S(2)}, u32[]{:S(2)}) collective-permute-start(bf16[2,8,384]{2,1,0:T(8,128)(2,1)S(1)} %pad_maximum_fusion.2), channel_id=1, source_target_pairs={{0,2},{1,3},{2,0},{3,1},{4,6},{5,7},{6,4},{7,5},{8,10},{9,11},{10,... | collective-permute-start | bytes 36872 | tf_op jit(solution)/shard_map/ppermute | solution.py:129
  67.7 1.3 %collective-permute-start.23 = (f32[1,2,8,384]{3,1,2,0:T(2,128)S(1)}, f32[1,2,8,384]{3,1,2,0:T(2,128)S(1)}, u32[]{:S(2)}, u32[]{:S(2)}) collective-permute-start(f32[1,2,8,384]{3,1,2,0:T(2,128)S(1)} %bitcast.250), channel_id=1, source_target_pairs={{0,12},{1,13},{2,14},{3,15},{4,8},{5,9},{6,10},{7,11},{8,4},{9,5},... | collective-permute-start | bytes 73736 | tf_op jit(solution)/shard_map/ppermute | solution.py:141
  69.0 1.4 %collective-permute-start.21 = (f32[1,2,8,384]{3,1,2,0:T(2,128)S(1)}, f32[1,2,8,384]{3,1,2,0:T(2,128)S(1)}, u32[]{:S(2)}, u32[]{:S(2)}) collective-permute-start(f32[1,2,8,384]{3,1,2,0:T(2,128)S(1)} %bitcast.248), channel_id=1, source_target_pairs={{0,4},{1,5},{2,6},{3,7},{4,0},{5,1},{6,2},{7,3},{8,12},{9,13},{10,... | collective-permute-start | bytes 73736 | tf_op jit(solution)/shard_map/ppermute | solution.py:141
  70.6 1.1 %copy.88 = bf16[2,2,384,384]{3,2,1,0:T(8,128)(2,1)} copy(bf16[2,2,384,384]{3,2,0,1:T(8,128)(2,1)S(1)} %pad_maximum_fusion) | data formatting | bytes 2359296
  71.7 1.7 %collective-permute-start.25 = (f32[4,24,384]{2,1,0:T(8,128)S(1)}, f32[4,24,384]{2,1,0:T(8,128)S(1)}, u32[]{:S(2)}, u32[]{:S(2)}) collective-permute-start(f32[4,24,384]{2,1,0:T(8,128)S(1)} %get-tuple-element.12), channel_id=1, source_target_pairs={{0,2},{1,3},{2,0},{3,1},{4,6},{5,7},{6,4},{7,5},{8,10},{9,11},{10,... | collective-permute-start | bytes 442376 | tf_op jit(solution)/shard_map/ppermute | solution.py:120
  73.5 3.5 %collective-permute-done.25 = f32[4,24,384]{2,1,0:T(8,128)S(1)} collective-permute-done((f32[4,24,384]{2,1,0:T(8,128)S(1)}, f32[4,24,384]{2,1,0:T(8,128)S(1)}, u32[]{:S(2)}, u32[]{:S(2)}) %collective-permute-start.25) | collective-permute-done | bytes 147488 | tf_op jit(solution)/shard_map/ppermute | solution.py:120
  77.1 1.0 %collective-permute-start.27 = (f32[1,24,384]{2,1,0:T(8,128)S(1)}, f32[1,24,384]{2,1,0:T(8,128)S(1)}, u32[]{:S(2)}, u32[]{:S(2)}) collective-permute-start(f32[1,24,384]{2,1,0:T(8,128)S(1)} %get-tuple-element.13), channel_id=1, source_target_pairs={{0,4},{1,5},{2,6},{3,7},{4,0},{5,1},{6,2},{7,3},{8,12},{9,13},{10,... | collective-permute-start | bytes 110600 | tf_op jit(solution)/shard_map/ppermute | solution.py:120
  78.1 2.3 %collective-permute-start.29 = (f32[1,24,384]{2,1,0:T(8,128)S(1)}, f32[1,24,384]{2,1,0:T(8,128)S(1)}, u32[]{:S(2)}, u32[]{:S(2)}) collective-permute-start(f32[1,24,384]{2,1,0:T(8,128)S(1)} %get-tuple-element.14), channel_id=1, source_target_pairs={{0,12},{1,13},{2,14},{3,15},{4,8},{5,9},{6,10},{7,11},{8,4},{9,5},... | collective-permute-start | bytes 110600 | tf_op jit(solution)/shard_map/ppermute | solution.py:120
  80.7 2.5 %fusion.11 = bf16[2,1440,384]{2,1,0:T(8,128)(2,1)} fusion(f32[2,1440,384]{2,1,0:T(8,128)S(1)} %fusion.40, bf16[2,1440,384]{2,1,0:T(8,128)(2,1)S(1)} %copy-done.3, bf16[1440,8,1]{0,1,2:T(8,128)(2,1)S(1)} %copy-done.5, bf16[2,8,384]{2,0,1:T(2,128)(2,1)S(1)} %fusion.68), kind=kOutput, calls=%fused_computation.20 | convolution fusion | flops 22118400 | bytes 8882688 | tf_op jit(solution)/shard_map/jfc,kf->jkc/dot_general | solution.py:243
  83.8 1.4 %collective-permute-done.28 = f32[1,24,384]{2,1,0:T(8,128)S(1)} collective-permute-done((f32[1,24,384]{2,1,0:T(8,128)S(1)}, f32[1,24,384]{2,1,0:T(8,128)S(1)}, u32[]{:S(2)}, u32[]{:S(2)}) %collective-permute-start.28) | collective-permute-done | bytes 36896 | tf_op jit(solution)/shard_map/ppermute | solution.py:120
  (128 shorter events, 23.0 us)
Async XLA Ops:
  3.4 7.7 %collective-permute-start.1 = (f32[2,8,384]{2,1,0:T(8,128)S(1)}, f32[2,8,384]{2,1,0:T(8,128)S(1)}, u32[]{:S(2)}, u32[]{:S(2)}) collective-permute-start(f32[2,8,384]{2,1,0:T(8,128)S(1)} %bitcast.231), channel_id=1, source_target_pairs={{0,2},{1,3},{2,0},{3,1},{4,6},{5,7},{6,4},{7,5},{8,10},{9,11},{10,... | collective-permute-start | bytes 73736 | tf_op jit(solution)/shard_map/ppermute | solution.py:129
  6.4 4.8 %collective-permute-start = (f32[2,8,384]{2,1,0:T(8,128)S(1)}, f32[2,8,384]{2,1,0:T(8,128)}, u32[]{:S(2)}, u32[]{:S(2)}) collective-permute-start(f32[2,8,384]{2,1,0:T(8,128)S(1)} %bitcast.232), channel_id=1, source_target_pairs={{0,1},{1,0},{2,3},{3,2},{4,5},{5,4},{6,7},{7,6},{8,9},{9,8},{10,11... | collective-permute-start | bytes 73736 | tf_op jit(solution)/shard_map/ppermute | solution.py:129
  6.4 4.8 %collective-permute-start.2 = (f32[2,8,384]{2,1,0:T(8,128)S(1)}, f32[2,8,384]{2,1,0:T(8,128)}, u32[]{:S(2)}, u32[]{:S(2)}) collective-permute-start(f32[2,8,384]{2,1,0:T(8,128)S(1)} %bitcast.233), channel_id=1, source_target_pairs={{0,3},{1,2},{2,1},{3,0},{4,7},{5,6},{6,5},{7,4},{8,11},{9,10},{10,... | collective-permute-start | bytes 73736 | tf_op jit(solution)/shard_map/ppermute | solution.py:129
  7.4 15.8 %copy-start.2 = (bf16[2,2,384,384]{3,2,1,0:T(8,128)(2,1)S(1)}, bf16[2,2,384,384]{3,2,1,0:T(8,128)(2,1)}, u32[]{:S(2)}) copy-start(bf16[2,2,384,384]{3,2,1,0:T(8,128)(2,1)} %param.13) | copy-start | bytes 3538948
  14.2 6.4 %collective-permute-start.4 = (f32[1,2,8,384]{3,1,2,0:T(2,128)}, f32[1,2,8,384]{3,1,2,0:T(2,128)S(1)}, u32[]{:S(2)}, u32[]{:S(2)}) collective-permute-start(f32[1,2,8,384]{3,1,2,0:T(2,128)} %bitcast.221), channel_id=1, source_target_pairs={{0,8},{1,9},{2,10},{3,11},{4,12},{5,13},{6,14},{7,15},{8,0},{9,1},... | collective-permute-start | bytes 73736 | tf_op jit(solution)/shard_map/ppermute | solution.py:141
  17.3 5.8 %collective-permute-start.5 = (f32[1,2,8,384]{3,1,2,0:T(2,128)}, f32[1,2,8,384]{3,1,2,0:T(2,128)S(1)}, u32[]{:S(2)}, u32[]{:S(2)}) collective-permute-start(f32[1,2,8,384]{3,1,2,0:T(2,128)} %bitcast.226), channel_id=1, source_target_pairs={{0,12},{1,13},{2,14},{3,15},{4,8},{5,9},{6,10},{7,11},{8,4},{9,5},... | collective-permute-start | bytes 73736 | tf_op jit(solution)/shard_map/ppermute | solution.py:141
  18.6 4.5 %collective-permute-start.3 = (f32[1,2,8,384]{3,1,2,0:T(2,128)}, f32[1,2,8,384]{3,1,2,0:T(2,128)S(1)}, u32[]{:S(2)}, u32[]{:S(2)}) collective-permute-start(f32[1,2,8,384]{3,1,2,0:T(2,128)} %bitcast.222), channel_id=1, source_target_pairs={{0,4},{1,5},{2,6},{3,7},{4,0},{5,1},{6,2},{7,3},{8,12},{9,13},{10,... | collective-permute-start | bytes 73736 | tf_op jit(solution)/shard_map/ppermute | solution.py:141
  24.6 3.4 %collective-permute-start.8 = (bf16[2,8,384]{2,1,0:T(8,128)(2,1)}, bf16[2,8,384]{2,1,0:T(8,128)(2,1)S(1)}, u32[]{:S(2)}, u32[]{:S(2)}) collective-permute-start(bf16[2,8,384]{2,1,0:T(8,128)(2,1)} %pad_maximum_fusion.1), channel_id=1, source_target_pairs={{0,3},{1,2},{2,1},{3,0},{4,7},{5,6},{6,5},{7,4},{8,11},{9,10},{10,... | collective-permute-start | bytes 36872 | tf_op jit(solution)/shard_map/ppermute | solution.py:129
  24.6 3.9 %collective-permute-start.7 = (bf16[2,8,384]{2,1,0:T(8,128)(2,1)}, bf16[2,8,384]{2,1,0:T(8,128)(2,1)S(1)}, u32[]{:S(2)}, u32[]{:S(2)}) collective-permute-start(bf16[2,8,384]{2,1,0:T(8,128)(2,1)} %pad_maximum_fusion.1), channel_id=1, source_target_pairs={{0,2},{1,3},{2,0},{3,1},{4,6},{5,7},{6,4},{7,5},{8,10},{9,11},{10,... | collective-permute-start | bytes 36872 | tf_op jit(solution)/shard_map/ppermute | solution.py:129
  26.2 2.4 %collective-permute-start.6 = (bf16[2,8,384]{2,1,0:T(8,128)(2,1)}, bf16[2,8,384]{2,1,0:T(8,128)(2,1)S(1)}, u32[]{:S(2)}, u32[]{:S(2)}) collective-permute-start(bf16[2,8,384]{2,1,0:T(8,128)(2,1)} %pad_maximum_fusion.1), channel_id=1, source_target_pairs={{0,1},{1,0},{2,3},{3,2},{4,5},{5,4},{6,7},{7,6},{8,9},{9,8},{10,11... | collective-permute-start | bytes 36872 | tf_op jit(solution)/shard_map/ppermute | solution.py:129
  31.4 9.1 %collective-permute-start.10 = (f32[1,2,8,384]{3,1,2,0:T(2,128)}, f32[1,2,8,384]{3,1,2,0:T(2,128)}, u32[]{:S(2)}, u32[]{:S(2)}) collective-permute-start(f32[1,2,8,384]{3,1,2,0:T(2,128)} %bitcast.219), channel_id=1, source_target_pairs={{0,8},{1,9},{2,10},{3,11},{4,12},{5,13},{6,14},{7,15},{8,0},{9,1},... | collective-permute-start | bytes 73736 | tf_op jit(solution)/shard_map/ppermute | solution.py:141
  32.6 7.9 %collective-permute-start.11 = (f32[1,2,8,384]{3,1,2,0:T(2,128)}, f32[1,2,8,384]{3,1,2,0:T(2,128)}, u32[]{:S(2)}, u32[]{:S(2)}) collective-permute-start(f32[1,2,8,384]{3,1,2,0:T(2,128)} %bitcast.225), channel_id=1, source_target_pairs={{0,12},{1,13},{2,14},{3,15},{4,8},{5,9},{6,10},{7,11},{8,4},{9,5},... | collective-permute-start | bytes 73736 | tf_op jit(solution)/shard_map/ppermute | solution.py:141
  33.6 7.0 %collective-permute-start.9 = (f32[1,2,8,384]{3,1,2,0:T(2,128)}, f32[1,2,8,384]{3,1,2,0:T(2,128)}, u32[]{:S(2)}, u32[]{:S(2)}) collective-permute-start(f32[1,2,8,384]{3,1,2,0:T(2,128)} %bitcast.220), channel_id=1, source_target_pairs={{0,4},{1,5},{2,6},{3,7},{4,0},{5,1},{6,2},{7,3},{8,12},{9,13},{10,... | collective-permute-start | bytes 73736 | tf_op jit(solution)/shard_map/ppermute | solution.py:141
  47.8 5.1 %collective-permute-start.13 = (f32[2,8,384]{2,1,0:T(8,128)S(1)}, f32[2,8,384]{2,1,0:T(8,128)S(1)}, u32[]{:S(2)}, u32[]{:S(2)}) collective-permute-start(f32[2,8,384]{2,1,0:T(8,128)S(1)} %bitcast.235), channel_id=1, source_target_pairs={{0,2},{1,3},{2,0},{3,1},{4,6},{5,7},{6,4},{7,5},{8,10},{9,11},{10,... | collective-permute-start | bytes 73736 | tf_op jit(solution)/shard_map/ppermute | solution.py:129
  49.3 3.6 %collective-permute-start.12 = (f32[2,8,384]{2,1,0:T(8,128)S(1)}, f32[2,8,384]{2,1,0:T(8,128)S(1)}, u32[]{:S(2)}, u32[]{:S(2)}) collective-permute-start(f32[2,8,384]{2,1,0:T(8,128)S(1)} %bitcast.236), channel_id=1, source_target_pairs={{0,1},{1,0},{2,3},{3,2},{4,5},{5,4},{6,7},{7,6},{8,9},{9,8},{10,11... | collective-permute-start | bytes 73736 | tf_op jit(solution)/shard_map/ppermute | solution.py:129
  49.3 3.6 %collective-permute-start.14 = (f32[2,8,384]{2,1,0:T(8,128)S(1)}, f32[2,8,384]{2,1,0:T(8,128)S(1)}, u32[]{:S(2)}, u32[]{:S(2)}) collective-permute-start(f32[2,8,384]{2,1,0:T(8,128)S(1)} %bitcast.237), channel_id=1, source_target_pairs={{0,3},{1,2},{2,1},{3,0},{4,7},{5,6},{6,5},{7,4},{8,11},{9,10},{10,... | collective-permute-start | bytes 73736 | tf_op jit(solution)/shard_map/ppermute | solution.py:129
  52.9 11.6 %copy-start.7 = (bf16[2,4,384]{2,0,1:T(2,128)(2,1)S(1)}, bf16[2,4,384]{2,0,1:T(2,128)(2,1)}, u32[]{:S(2)}) copy-start(bf16[2,4,384]{2,0,1:T(2,128)(2,1)} %copy-done.6) | copy-start | bytes 18436
  53.5 5.3 %collective-permute-start.16 = (f32[1,2,8,384]{3,1,2,0:T(2,128)S(1)}, f32[1,2,8,384]{3,1,2,0:T(2,128)S(1)}, u32[]{:S(2)}, u32[]{:S(2)}) collective-permute-start(f32[1,2,8,384]{3,1,2,0:T(2,128)S(1)} %bitcast.251), channel_id=1, source_target_pairs={{0,8},{1,9},{2,10},{3,11},{4,12},{5,13},{6,14},{7,15},{8,0},{9,1},... | collective-permute-start | bytes 73736 | tf_op jit(solution)/shard_map/ppermute | solution.py:141
  55.7 5.6 %collective-permute-start.17 = (f32[1,2,8,384]{3,1,2,0:T(2,128)S(1)}, f32[1,2,8,384]{3,1,2,0:T(2,128)S(1)}, u32[]{:S(2)}, u32[]{:S(2)}) collective-permute-start(f32[1,2,8,384]{3,1,2,0:T(2,128)S(1)} %bitcast.249), channel_id=1, source_target_pairs={{0,12},{1,13},{2,14},{3,15},{4,8},{5,9},{6,10},{7,11},{8,4},{9,5},... | collective-permute-start | bytes 73736 | tf_op jit(solution)/shard_map/ppermute | solution.py:141
  56.6 4.7 %collective-permute-start.15 = (f32[1,2,8,384]{3,1,2,0:T(2,128)S(1)}, f32[1,2,8,384]{3,1,2,0:T(2,128)S(1)}, u32[]{:S(2)}, u32[]{:S(2)}) collective-permute-start(f32[1,2,8,384]{3,1,2,0:T(2,128)S(1)} %bitcast.247), channel_id=1, source_target_pairs={{0,4},{1,5},{2,6},{3,7},{4,0},{5,1},{6,2},{7,3},{8,12},{9,13},{10,... | collective-permute-start | bytes 73736 | tf_op jit(solution)/shard_map/ppermute | solution.py:141
  57.1 16.4 %collective-permute-start.24 = (f32[4,24,384]{2,1,0:T(8,128)S(1)}, f32[4,24,384]{2,1,0:T(8,128)S(1)}, u32[]{:S(2)}, u32[]{:S(2)}) collective-permute-start(f32[4,24,384]{2,1,0:T(8,128)S(1)} %get-tuple-element.10), channel_id=1, source_target_pairs={{0,1},{1,0},{2,3},{3,2},{4,5},{5,4},{6,7},{7,6},{8,9},{9,8},{10,11... | collective-permute-start | bytes 442376 | tf_op jit(solution)/shard_map/ppermute | solution.py:120
  57.2 16.3 %collective-permute-start.26 = (f32[4,24,384]{2,1,0:T(8,128)S(1)}, f32[4,24,384]{2,1,0:T(8,128)S(1)}, u32[]{:S(2)}, u32[]{:S(2)}) collective-permute-start(f32[4,24,384]{2,1,0:T(8,128)S(1)} %get-tuple-element.11), channel_id=1, source_target_pairs={{0,3},{1,2},{2,1},{3,0},{4,7},{5,6},{6,5},{7,4},{8,11},{9,10},{10,... | collective-permute-start | bytes 442376 | tf_op jit(solution)/shard_map/ppermute | solution.py:120
  62.6 3.5 %collective-permute-start.20 = (bf16[2,8,384]{2,1,0:T(8,128)(2,1)S(1)}, bf16[2,8,384]{2,1,0:T(8,128)(2,1)S(1)}, u32[]{:S(2)}, u32[]{:S(2)}) collective-permute-start(bf16[2,8,384]{2,1,0:T(8,128)(2,1)S(1)} %pad_maximum_fusion.2), channel_id=1, source_target_pairs={{0,3},{1,2},{2,1},{3,0},{4,7},{5,6},{6,5},{7,4},{8,11},{9,10},{10,... | collective-permute-start | bytes 36872 | tf_op jit(solution)/shard_map/ppermute | solution.py:129
  62.6 3.8 %collective-permute-start.19 = (bf16[2,8,384]{2,1,0:T(8,128)(2,1)S(1)}, bf16[2,8,384]{2,1,0:T(8,128)(2,1)S(1)}, u32[]{:S(2)}, u32[]{:S(2)}) collective-permute-start(bf16[2,8,384]{2,1,0:T(8,128)(2,1)S(1)} %pad_maximum_fusion.2), channel_id=1, source_target_pairs={{0,2},{1,3},{2,0},{3,1},{4,6},{5,7},{6,4},{7,5},{8,10},{9,11},{10,... | collective-permute-start | bytes 36872 | tf_op jit(solution)/shard_map/ppermute | solution.py:129
  64.2 2.2 %collective-permute-start.18 = (bf16[2,8,384]{2,1,0:T(8,128)(2,1)S(1)}, bf16[2,8,384]{2,1,0:T(8,128)(2,1)S(1)}, u32[]{:S(2)}, u32[]{:S(2)}) collective-permute-start(bf16[2,8,384]{2,1,0:T(8,128)(2,1)S(1)} %pad_maximum_fusion.2), channel_id=1, source_target_pairs={{0,1},{1,0},{2,3},{3,2},{4,5},{5,4},{6,7},{7,6},{8,9},{9,8},{10,11... | collective-permute-start | bytes 36872 | tf_op jit(solution)/shard_map/ppermute | solution.py:129
  66.9 4.8 %collective-permute-start.22 = (f32[1,2,8,384]{3,1,2,0:T(2,128)S(1)}, f32[1,2,8,384]{3,1,2,0:T(2,128)S(1)}, u32[]{:S(2)}, u32[]{:S(2)}) collective-permute-start(f32[1,2,8,384]{3,1,2,0:T(2,128)S(1)} %bitcast.252), channel_id=1, source_target_pairs={{0,8},{1,9},{2,10},{3,11},{4,12},{5,13},{6,14},{7,15},{8,0},{9,1},... | collective-permute-start | bytes 73736 | tf_op jit(solution)/shard_map/ppermute | solution.py:141
  67.7 5.7 %collective-permute-start.23 = (f32[1,2,8,384]{3,1,2,0:T(2,128)S(1)}, f32[1,2,8,384]{3,1,2,0:T(2,128)S(1)}, u32[]{:S(2)}, u32[]{:S(2)}) collective-permute-start(f32[1,2,8,384]{3,1,2,0:T(2,128)S(1)} %bitcast.250), channel_id=1, source_target_pairs={{0,12},{1,13},{2,14},{3,15},{4,8},{5,9},{6,10},{7,11},{8,4},{9,5},... | collective-permute-start | bytes 73736 | tf_op jit(solution)/shard_map/ppermute | solution.py:141
  69.0 4.4 %collective-permute-start.21 = (f32[1,2,8,384]{3,1,2,0:T(2,128)S(1)}, f32[1,2,8,384]{3,1,2,0:T(2,128)S(1)}, u32[]{:S(2)}, u32[]{:S(2)}) collective-permute-start(f32[1,2,8,384]{3,1,2,0:T(2,128)S(1)} %bitcast.248), channel_id=1, source_target_pairs={{0,4},{1,5},{2,6},{3,7},{4,0},{5,1},{6,2},{7,3},{8,12},{9,13},{10,... | collective-permute-start | bytes 73736 | tf_op jit(solution)/shard_map/ppermute | solution.py:141
  71.7 5.3 %collective-permute-start.25 = (f32[4,24,384]{2,1,0:T(8,128)S(1)}, f32[4,24,384]{2,1,0:T(8,128)S(1)}, u32[]{:S(2)}, u32[]{:S(2)}) collective-permute-start(f32[4,24,384]{2,1,0:T(8,128)S(1)} %get-tuple-element.12), channel_id=1, source_target_pairs={{0,2},{1,3},{2,0},{3,1},{4,6},{5,7},{6,4},{7,5},{8,10},{9,11},{10,... | collective-permute-start | bytes 442376 | tf_op jit(solution)/shard_map/ppermute | solution.py:120
  77.1 6.0 %collective-permute-start.27 = (f32[1,24,384]{2,1,0:T(8,128)S(1)}, f32[1,24,384]{2,1,0:T(8,128)S(1)}, u32[]{:S(2)}, u32[]{:S(2)}) collective-permute-start(f32[1,24,384]{2,1,0:T(8,128)S(1)} %get-tuple-element.13), channel_id=1, source_target_pairs={{0,4},{1,5},{2,6},{3,7},{4,0},{5,1},{6,2},{7,3},{8,12},{9,13},{10,... | collective-permute-start | bytes 110600 | tf_op jit(solution)/shard_map/ppermute | solution.py:120
  78.1 5.8 %collective-permute-start.29 = (f32[1,24,384]{2,1,0:T(8,128)S(1)}, f32[1,24,384]{2,1,0:T(8,128)S(1)}, u32[]{:S(2)}, u32[]{:S(2)}) collective-permute-start(f32[1,24,384]{2,1,0:T(8,128)S(1)} %get-tuple-element.14), channel_id=1, source_target_pairs={{0,12},{1,13},{2,14},{3,15},{4,8},{5,9},{6,10},{7,11},{8,4},{9,5},... | collective-permute-start | bytes 110600 | tf_op jit(solution)/shard_map/ppermute | solution.py:120
  80.4 4.9 %collective-permute-start.28 = (f32[1,24,384]{2,1,0:T(8,128)S(1)}, f32[1,24,384]{2,1,0:T(8,128)S(1)}, u32[]{:S(2)}, u32[]{:S(2)}) collective-permute-start(f32[1,24,384]{2,1,0:T(8,128)S(1)} %get-tuple-element.15), channel_id=1, source_target_pairs={{0,8},{1,9},{2,10},{3,11},{4,12},{5,13},{6,14},{7,15},{8,0},{9,1},... | collective-permute-start | bytes 110600 | tf_op jit(solution)/shard_map/ppermute | solution.py:120
  (7 other events, 38.1 us)

commit v6 on v5

--- a/solution.py
+++ b/solution.py
@@ -123,12 +123,28 @@
     return cur[0]
 
 
-def xor_exchange(values, table, axis_name, groups, me, lo, spec):
-    parts = [values]
-    for k in range(1, 1 << lo):
-        parts.append(lax.ppermute(values, axis_name, [(i, i ^ k) for i in range(groups)]))
+def xor_exchange(values, table, axis_name, groups, me, lo, spec, extra=None):
+    fan_lo = 1 << lo
+    size = values.size
+    if extra is not None:
+        extra_view = extra.reshape((extra.shape[0] // fan_lo, fan_lo, -1))
+        extra_sum = extra_view[:, 0]
+    parts = [values.astype(jnp.float32) if extra is not None else values]
+    for k in range(1, fan_lo):
+        pairs = [(i, i ^ k) for i in range(groups)]
+        if extra is None:
+            parts.append(lax.ppermute(values, axis_name, pairs))
+        else:
+            message = jnp.concatenate([values.astype(jnp.float32).reshape(-1), extra_view[:, k].reshape(-1)])
+            moved = lax.ppermute(message, axis_name, pairs)
+            parts.append(moved[:size].reshape(values.shape))
+            extra_sum = extra_sum + moved[size:].reshape(extra_sum.shape)
     stacked = jnp.stack(parts).astype(jnp.float32)
     cur = jnp.einsum(spec, table, stacked, precision=lax.Precision.HIGHEST)
+    out_shape = cur.shape[1:]
+    cur = cur.reshape((cur.shape[0], -1))
+    if extra is not None:
+        cur = jnp.concatenate([cur, extra_sum], axis=1)
     hi = groups.bit_length() - 1 - lo
     b = 0
     while b < hi:
@@ -141,7 +157,8 @@
             total = total + lax.ppermute(view[:, k], axis_name, [(i, i ^ mask) for i in range(groups)])
         cur = total
         b += width
-    return cur[0]
+    n = math.prod(out_shape)
+    return cur[0, :n].reshape(out_shape), cur[0, n:]
 
 
 def complex_apply(coeffs, weights, orders):
@@ -218,13 +235,13 @@
     to_owners = "xskrf,krfc->xsfc"
     to_rows = "xksrf,ksfc->xrfc"
 
-    def exchange(values, table, spec):
-        return xor_exchange(values, table, "lat", groups, me, lo, spec)
+    def exchange(values, table, spec, extra=None):
+        return xor_exchange(values, table, "lat", groups, me, lo, spec, extra)
 
     spectrum = jnp.einsum("jkc,kf->jfc", activations, fourier, preferred_element_type=jnp.float32)
-    coeffs = exchange(spectrum, own_quad, to_owners).astype(jnp.bfloat16)
+    coeffs = exchange(spectrum, own_quad, to_owners)[0].astype(jnp.bfloat16)
     filtered = complex_apply(coeffs, spectral_weight, orders).astype(jnp.bfloat16)
-    grid_modes = exchange(filtered, rows_plm, to_rows).astype(jnp.bfloat16)
+    grid_modes = exchange(filtered, rows_plm, to_rows)[0].astype(jnp.bfloat16)
 
     spatial = jnp.einsum("jfc,kf->jkc", grid_modes, fourier, preferred_element_type=jnp.float32)
     skip_out = jnp.einsum("jkc,cd->jkd", activations, skip_weight, preferred_element_type=jnp.float32)
@@ -233,13 +250,15 @@
 
     skip_terms = jnp.einsum("jkc,jkd->cd", activations, slope_b, preferred_element_type=jnp.float32)
     skip_blocks = skip_terms.reshape((groups, -1) + skip_terms.shape[1:])
-    grad_skip = xor_reduce_scatter(skip_blocks, "lat", groups, me) * (1.0 / math.sqrt(lat_total * lon_total))
+    skip_rel = jnp.take(skip_blocks, jnp.bitwise_xor(me, jnp.arange(groups, dtype=jnp.int32)), axis=0)
     through_skip = jnp.einsum("jkd,cd->jkc", slope_b, skip_weight, preferred_element_type=jnp.float32)
 
     mode_grads = jnp.einsum("jkc,kf->jfc", slope_b, fourier, preferred_element_type=jnp.float32)
-    coeff_grads = exchange(mode_grads, own_plm, to_owners).astype(jnp.bfloat16)
+    coeff_grads = exchange(mode_grads, own_plm, to_owners)[0].astype(jnp.bfloat16)
     weight_grads, back_coeffs = complex_adjoint(coeffs, coeff_grads, spectral_weight, orders)
-    row_grads = exchange(back_coeffs.astype(jnp.bfloat16), rows_quad, to_rows).astype(jnp.bfloat16)
+    row_sums, skip_sums = exchange(back_coeffs.astype(jnp.bfloat16), rows_quad, to_rows, skip_rel)
+    row_grads = row_sums.astype(jnp.bfloat16)
+    grad_skip = skip_sums.reshape(skip_blocks.shape[1:]) * (1.0 / math.sqrt(lat_total * lon_total))
     through_modes = jnp.einsum("jfc,kf->jkc", row_grads, fourier, preferred_element_type=jnp.float32)
     grad_activations = (upstream.astype(jnp.float32) + through_skip + through_modes).astype(jnp.bfloat16)
     return (grad_activations, weight_grads.astype(jnp.bfloat16), grad_skip)

time: 86.3 us -> 115 us (1.33); the launches traced: 85.8 us -> 113 us
  local copies, waits for them, and re-layouts: 15.4 us -> 34.1 us
  other arithmetic: 3.59 us -> 12.5 us
  matrix products: 22.2 us -> 28.7 us
  starting transfers between devices: 31.3 us -> 26.5 us
  waiting for transfers between devices: 12.3 us -> 10.3 us
    ppermute x18 -> x12, starting transfers between devices: 16.1 us -> 8.69 us  [the longest x9 6.83 us: xor_exchange(): parts.append(lax.ppermute(values, axis_name, pairs))]
    slice x6 -> x11, local copies, waits for them, and re-layouts: 0.9 us -> 7.96 us  [the longest x1 3.18 us: xor_exchange(): extra_sum = extra_view[:, 0]]
    dot_general x4, matrix products: 1.5 us -> 6.5 us  [outer_sum(): jnp.einsum('smc,smd->scd', operand_a, operand_b, preferred_element_type=j...]
    gather x0 -> x2, local copies, waits for them, and re-layouts: none -> 4.73 us  [local(): jnp.take(skip_blocks, jnp.bitwise_xor(me, jnp.arange(groups, dtype=jnp.in...]
    another operation x0 -> x3, local copies, waits for them, and re-layouts: none -> 2.78 us  [xor_exchange(): view = cur.reshape((cur.shape[0] // fan, fan) + cur.shape[1:])]
    select_n x0 -> x3, other arithmetic: none -> 2.68 us  [the longest x2 2.6 us: local(): jnp.take(skip_blocks, jnp.bitwise_xor(me, jnp.arange(groups, dtype=jnp.in...]
    ppermute x12, starting transfers between devices: 15.2 us -> 17.9 us  [xor_exchange(): lax.ppermute(view[:, k], axis_name, [(i, i ^ mask) for i in range(groups)])]
    ppermute x18 -> x12, waiting for transfers between devices: 7.29 us -> 4.98 us  [the longest x3 3.51 us: xor_exchange(): moved = lax.ppermute(message, axis_name, pairs)]
  transfers between devices with their start and end apart: 30 -> 24, of which waited for: 8 -> 7; matrix products, arithmetic and copies ran while one was open for 26% -> 31% of each run, Pallas kernels for 0% -> 0%
where the time goes in v6:
time: 115 us; the launch traced here: 113 us
  local copies, waits for them, and re-layouts  34.1 us (30%)
  matrix products  28.7 us (25%)
  starting transfers between devices  26.5 us (23%)
  other arithmetic  12.5 us (11%)
  waiting for transfers between devices  10.3 us (9%)
    ppermute x12, starting transfers between devices, xor_exchange(): lax.ppermute(view[:, k], axis_name, [(i, i ^ mask) for i in range(groups)])  17.9 us
    unnamed x42, local copies, waits for them, and re-layouts  9.07 us
    ppermute x9, starting transfers between devices, xor_exchange(): parts.append(lax.ppermute(values, axis_name, pairs))  6.83 us
    dot_general x4, matrix products, outer_sum(): jnp.einsum('smc,smd->scd', operand_a, operand_b, preferred_element_type=j...  6.5 us
    dot_general x1, matrix products, local(): jnp.einsum('jfc,kf->jkc', grid_modes, fourier, preferred_element_type=jnp...  5.99 us
    ppermute x12, waiting for transfers between devices, xor_exchange(): lax.ppermute(view[:, k], axis_name, [(i, i ^ mask) for i in range(groups)])  5.3 us
    gather x2, local copies, waits for them, and re-layouts, local(): jnp.take(skip_blocks, jnp.bitwise_xor(me, jnp.arange(groups, dtype=jnp.in...  4.73 us
    dot_general x1, matrix products, local(): jnp.einsum('jkc,cd->jkd', activations, skip_weight, preferred_element_typ...  4.58 us
  transfers between devices with their start and end apart: 24, of which 7 were waited for; matrix products, arithmetic and copies ran while one was open for 31% of the time, Pallas kernels for 0%

profile of v6, /device:TPU:0, one launch (start us, length us, event | category | flops | bytes accessed | tf_op | source)
XLA Modules:
  0.0 113.3 jit_solution(11917467016445752851)
XLA Ops:
  0.7 1.6 %copy-done = bf16[2,1440,384]{2,1,0:T(8,128)(2,1)S(1)} copy-done((bf16[2,1440,384]{2,1,0:T(8,128)(2,1)S(1)}, bf16[2,1440,384]{2,1,0:T(8,128)(2,1)}, u32[]{:S(2)}) %copy-start) | copy-done | bytes 2211864
  3.4 2.4 %collective-permute-start.2 = (f32[2,8,384]{2,1,0:T(8,128)S(1)}, f32[2,8,384]{2,1,0:T(8,128)S(1)}, u32[]{:S(2)}, u32[]{:S(2)}) collective-permute-start(f32[2,8,384]{2,1,0:T(8,128)S(1)} %bitcast.206), channel_id=1, source_target_pairs={{0,3},{1,2},{2,1},{3,0},{4,7},{5,6},{6,5},{7,4},{8,11},{9,10},{10,... | collective-permute-start | bytes 73736 | tf_op jit(solution)/shard_map/ppermute | solution.py:136
  10.2 4.6 %fusion.41 = f32[2,1440,384]{2,1,0:T(8,128)} fusion(bf16[2,1440,384]{2,1,0:T(8,128)(2,1)S(1)} %copy-done, bf16[384,384]{1,0:T(8,128)(2,1)} %param.12), kind=kOutput, calls=%fused_computation.66 | convolution fusion | flops 849346560 | bytes 6930432 | tf_op jit(solution)/shard_map/jkc,cd->jkd/dot_general | solution.py:247
  15.0 1.6 %gather_fusion.1 = f32[64,16]{1,0:T(8,128)S(1)} fusion(f32[32,32,16]{2,1,0:T(8,128)} %constant.74, s32[64]{0:T(128)S(1)} %reshape.250), kind=kCustom, calls=%fused_computation.3 | custom fusion | bytes 8704 | tf_op jit(solution)/shard_map/gather | solution.py:231
  20.3 3.9 %collective-permute-start.5 = (f32[1,6144]{1,0:T(1,128)S(1)}, f32[1,6144]{1,0:T(1,128)S(1)}, u32[]{:S(2)}, u32[]{:S(2)}) collective-permute-start(f32[1,6144]{1,0:T(1,128)S(1)} %get-tuple-element.24), channel_id=1, source_target_pairs={{0,12},{1,13},{2,14},{3,15},{4,8},{5,9},{6,10},{7,11},{8,4},{9,5},... | collective-permute-start | bytes 73736 | tf_op jit(solution)/shard_map/ppermute | solution.py:157
  26.0 2.9 %collective-permute-done.4 = f32[1,6144]{1,0:T(1,128)S(1)} collective-permute-done((f32[1,6144]{1,0:T(1,128)S(1)}, f32[1,6144]{1,0:T(1,128)S(1)}, u32[]{:S(2)}, u32[]{:S(2)}) %collective-permute-start.4) | collective-permute-done | bytes 24608 | tf_op jit(solution)/shard_map/ppermute | solution.py:157
  30.6 1.5 %collective-permute-start.7 = (bf16[2,8,384]{2,1,0:T(8,128)(2,1)}, bf16[2,8,384]{2,1,0:T(8,128)(2,1)}, u32[]{:S(2)}, u32[]{:S(2)}) collective-permute-start(bf16[2,8,384]{2,1,0:T(8,128)(2,1)} %pad_maximum_fusion.4), channel_id=1, source_target_pairs={{0,2},{1,3},{2,0},{3,1},{4,6},{5,7},{6,4},{7,5},{8,10},{9,11},{10,... | collective-permute-start | bytes 36872 | tf_op jit(solution)/shard_map/ppermute | solution.py:136
  37.9 1.5 %collective-permute-start.11 = (f32[1,6144]{1,0:T(1,128)}, f32[1,6144]{1,0:T(1,128)S(1)}, u32[]{:S(2)}, u32[]{:S(2)}) collective-permute-start(f32[1,6144]{1,0:T(1,128)} %get-tuple-element.21), channel_id=1, source_target_pairs={{0,12},{1,13},{2,14},{3,15},{4,8},{5,9},{6,10},{7,11},{8,4},{9,5},... | collective-permute-start | bytes 73736 | tf_op jit(solution)/shard_map/ppermute | solution.py:157
  39.9 2.5 %collective-permute-start.9 = (f32[1,6144]{1,0:T(1,128)}, f32[1,6144]{1,0:T(1,128)}, u32[]{:S(2)}, u32[]{:S(2)}) collective-permute-start(f32[1,6144]{1,0:T(1,128)} %get-tuple-element.20), channel_id=1, source_target_pairs={{0,4},{1,5},{2,6},{3,7},{4,0},{5,1},{6,2},{7,3},{8,12},{9,13},{10,... | collective-permute-start | bytes 73736 | tf_op jit(solution)/shard_map/ppermute | solution.py:157
  42.4 1.5 %copy.54 = f32[4,2,4,2,8]{2,0,3,1,4:T(4,128)} copy(f32[4,2,4,2,8]{4,3,2,1,0:T(2,128)} %get-tuple-element.29) | data formatting | bytes 4096
  43.9 1.6 %copy.55 = f32[4,4,2,2,8]{1,0,2,3,4:T(4,128)} copy(f32[4,4,2,2,8]{4,3,2,1,0:T(2,128)} %get-tuple-element.26) | data formatting | bytes 4096
  47.0 6.0 %fusion.6 = bf16[2,1440,384]{2,1,0:T(8,128)(2,1)S(1)} fusion(bf16[2,1440,384]{2,1,0:T(8,128)(2,1)} %param.11, f32[2,1440,384]{2,1,0:T(8,128)} %fusion.41, bf16[2,8,384]{2,1,0:T(8,128)(2,1)S(1)} %convert_element_type.75, bf16[1440,8,1]{0,1,2:T(8,128)(2,1)S(1)} %copy-done.12), kind=kOutput, calls=%fused_computation.16 | convolution fusion | flops 42024960 | bytes 8882688 | tf_op jit(solution)/shard_map/jfc,kf->jkc/dot_general | solution.py:246
  53.4 1.5 %collective-permute-start.13 = (f32[2,8,384]{2,1,0:T(8,128)S(1)}, f32[2,8,384]{2,1,0:T(8,128)S(1)}, u32[]{:S(2)}, u32[]{:S(2)}) collective-permute-start(f32[2,8,384]{2,1,0:T(8,128)S(1)} %bitcast.211), channel_id=1, source_target_pairs={{0,2},{1,3},{2,0},{3,1},{4,6},{5,7},{6,4},{7,5},{8,10},{9,11},{10,... | collective-permute-start | bytes 73736 | tf_op jit(solution)/shard_map/ppermute | solution.py:136
  55.3 2.2 %fusion.91 = f32[384,384,1]{0,1,2:T(8,128)} fusion(bf16[2,1440,384]{2,1,0:T(8,128)(2,1)S(1)} %fusion.6, bf16[2,1440,384]{2,1,0:T(8,128)(2,1)S(1)} %copy-done), kind=kOutput, calls=%fused_computation.164 | convolution fusion | flops 849346560 | bytes 5013504 | tf_op jit(solution)/shard_map/jkc,jkd->cd/dot_general | solution.py:251
  57.5 2.6 %gather_fusion.2 = f32[16,24,384]{2,1,0:T(8,128)} fusion(f32[16,24,384]{2,1,0:T(8,128)} %bitcast.201, s32[1024]{0:T(1024)} %pad_clamp_fusion), kind=kCustom, calls=%fused_computation.4 | custom fusion | bytes 1179712 | tf_op jit(solution)/shard_map/jit(_take)/gather | solution.py:253
  60.1 2.1 %gather.18 = f32[4,4,9216]{2,1,0:T(4,128)} reshape(f32[16,24,384]{2,1,0:T(8,128)} %gather_fusion.2) | data formatting | bytes 1179648 | tf_op jit(solution)/shard_map/jit(_take)/gather | solution.py:253
  62.2 2.1 %broadcast_select_fusion = f32[4,4,9216]{2,1,0:T(4,128)} fusion(f32[4,4,9216]{2,1,0:T(4,128)} %gather.18, pred[4,4]{1,0:T(4,128)(4,1)S(1)} %compare_and_fusion), kind=kLoop, calls=%fused_computation.68 | loop fusion | flops 147456 | bytes 1179664 | tf_op jit(solution)/shard_map/jit(_take)/select_n | solution.py:253
  67.1 1.5 %collective-permute-start.17 = (f32[1,6144]{1,0:T(1,128)S(1)}, f32[1,6144]{1,0:T(1,128)S(1)}, u32[]{:S(2)}, u32[]{:S(2)}) collective-permute-start(f32[1,6144]{1,0:T(1,128)S(1)} %get-tuple-element.18), channel_id=1, source_target_pairs={{0,12},{1,13},{2,14},{3,15},{4,8},{5,9},{6,10},{7,11},{8,4},{9,5},... | collective-permute-start | bytes 73736 | tf_op jit(solution)/shard_map/ppermute | solution.py:157
  69.1 2.5 %collective-permute-start.15 = (f32[1,6144]{1,0:T(1,128)S(1)}, f32[1,6144]{1,0:T(1,128)S(1)}, u32[]{:S(2)}, u32[]{:S(2)}) collective-permute-start(f32[1,6144]{1,0:T(1,128)S(1)} %get-tuple-element.17), channel_id=1, source_target_pairs={{0,4},{1,5},{2,6},{3,7},{4,0},{5,1},{6,2},{7,3},{8,12},{9,13},{10,... | collective-permute-start | bytes 73736 | tf_op jit(solution)/shard_map/ppermute | solution.py:157
  71.6 3.2 %fusion.86 = (f32[4,1,9216]{2,1,0:T(1,128)}, f32[4,1,9216]{2,1,0:T(1,128)}, f32[4,1,9216]{2,1,0:T(1,128)}, f32[4,1,9216]{2,1,0:T(1,128)}) fusion(f32[4,4,9216]{2,1,0:T(4,128)} %broadcast_select_fusion), kind=kLoop, calls=%fused_computation.159 | loop fusion | bytes 1179648 | tf_op jit(solution)/shard_map/slice | solution.py:131
  75.4 1.4 %fusion.67 = f32[2,384,384]{2,1,0:T(8,128)} fusion(bf16[2,8,384]{2,1,0:T(8,128)(2,1)S(1)} %convert_element_type.78, bf16[2,8,384]{2,1,0:T(8,128)(2,1)S(1)} %convert_element_type.73), kind=kOutput, calls=%fused_computation.138 | convolution fusion | flops 2359296 | bytes 1191936 | tf_op jit(solution)/shard_map/smc,smd->scd/dot_general | solution.py:182
  76.9 1.4 %fusion.73 = f32[2,384,384]{2,1,0:T(8,128)} fusion(bf16[2,8,384]{2,1,0:T(8,128)(2,1)S(1)} %convert_element_type.78, bf16[2,8,384]{2,1,0:T(8,128)(2,1)S(1)} %convert_element_type.73), kind=kOutput, calls=%fused_computation.144 | convolution fusion | flops 2359296 | bytes 1191936 | tf_op jit(solution)/shard_map/smc,smd->scd/dot_general | solution.py:182
  78.9 1.9 %pad_maximum_fusion.3 = (f32[43008]{0:T(1024)}, f32[43008]{0:T(1024)}, f32[43008]{0:T(1024)S(1)}) fusion(f32[6144]{0:T(1024)S(1)} %reshape.227, f32[36864]{0:T(1024)} %bitcast.200, f32[36864]{0:T(1024)} %bitcast.199, f32[36864]{0:T(1024)} %bitcast.198), kind=kLoop, calls=%fused_computation.64 | loop fusion | flops 129024 | bytes 983040 | tf_op jit(solution)/shard_map/concatenate | solution.py:138
  81.0 1.3 %collective-permute-start.19 = (f32[43008]{0:T(1024)}, f32[43008]{0:T(1024)}, u32[]{:S(2)}, u32[]{:S(2)}) collective-permute-start(f32[43008]{0:T(1024)} %get-tuple-element.31), channel_id=1, source_target_pairs={{0,2},{1,3},{2,0},{3,1},{4,6},{5,7},{6,4},{7,5},{8,10},{9,11},{10,... | collective-permute-start | bytes 516104 | tf_op jit(solution)/shard_map/ppermute | solution.py:139
  82.6 2.5 %fusion.14 = bf16[2,1,384,384]{3,2,0,1:T(8,128)(2,1)} fusion(f32[2,384,384]{2,1,0:T(8,128)} %fusion.67, bf16[2,8,384]{2,1,0:T(8,128)(2,1)S(1)} %convert_element_type.78, bf16[2,8,384]{2,1,0:T(8,128)(2,1)S(1)} %convert_element_type.73), kind=kOutput, calls=%fused_computation.27 | convolution fusion | flops 2949120 | bytes 1781760 | tf_op jit(solution)/shard_map/smc,smd->scd/dot_general | solution.py:182
  88.2 3.0 %collective-permute-done.19 = f32[43008]{0:T(1024)} collective-permute-done((f32[43008]{0:T(1024)}, f32[43008]{0:T(1024)}, u32[]{:S(2)}, u32[]{:S(2)}) %collective-permute-start.19) | collective-permute-done | bytes 172064 | tf_op jit(solution)/shard_map/ppermute | solution.py:139
  96.9 1.2 %convolution_bitcast_fusion = f32[4,2,8,384]{3,0,1,2:T(4,128)S(1)} fusion(f32[4,4,2,2,8]{1,0,2,3,4:T(4,128)} %copy.55, f32[4,2,8,384,1]{3,2,1,0,4:T(8,128)S(1)} %maximum_bitcast_fusion.3), kind=kOutput, calls=%fused_computation.30 | convolution fusion | flops 2359296 | bytes 198656 | tf_op jit(solution)/shard_map/xksrf,ksfc->xrfc/dot_general | solution.py:143
  98.5 1.5 %collective-permute-start.23 = (f32[1,15360]{1,0:T(1,128)S(1)}, f32[1,15360]{1,0:T(1,128)S(1)}, u32[]{:S(2)}, u32[]{:S(2)}) collective-permute-start(f32[1,15360]{1,0:T(1,128)S(1)} %get-tuple-element.15), channel_id=1, source_target_pairs={{0,12},{1,13},{2,14},{3,15},{4,8},{5,9},{6,10},{7,11},{8,4},{9,5},... | collective-permute-start | bytes 184328 | tf_op jit(solution)/shard_map/ppermute | solution.py:157
  100.6 2.3 %collective-permute-start.21 = (f32[1,15360]{1,0:T(1,128)S(1)}, f32[1,15360]{1,0:T(1,128)S(1)}, u32[]{:S(2)}, u32[]{:S(2)}) collective-permute-start(f32[1,15360]{1,0:T(1,128)S(1)} %get-tuple-element.14), channel_id=1, source_target_pairs={{0,4},{1,5},{2,6},{3,7},{4,0},{5,1},{6,2},{7,3},{8,12},{9,13},{10,... | collective-permute-start | bytes 184328 | tf_op jit(solution)/shard_map/ppermute | solution.py:157
  102.9 1.2 %pad_maximum_fusion = bf16[2,2,384,384]{3,2,0,1:T(8,128)(2,1)S(1)} fusion(bf16[2,1,384,384]{3,2,0,1:T(8,128)(2,1)} %fusion.14, bf16[2,1,384,384]{3,2,0,1:T(8,128)(2,1)S(1)} %copy-done.6), kind=kLoop, calls=%fused_computation.29 | loop fusion | flops 589824 | bytes 2359296 | tf_op jit(solution)/shard_map/stack | solution.py:192
  105.3 1.7 %collective-permute-done.22 = f32[1,15360]{1,0:T(1,128)S(1)} collective-permute-done((f32[1,15360]{1,0:T(1,128)S(1)}, f32[1,15360]{1,0:T(1,128)S(1)}, u32[]{:S(2)}, u32[]{:S(2)}) %collective-permute-start.22) | collective-permute-done | bytes 61472 | tf_op jit(solution)/shard_map/ppermute | solution.py:157
  109.7 3.0 %fusion.11 = bf16[2,1440,384]{2,1,0:T(8,128)(2,1)} fusion(bf16[2,1440,384]{2,1,0:T(8,128)(2,1)S(1)} %copy-done.7, f32[2,384,1440]{1,2,0:T(8,128)S(1)} %fusion.92, bf16[2,1440,384]{2,1,0:T(8,128)(2,1)S(1)} %copy-done.4, bf16[384,384]{1,0:T(8,128)(2,1)S(1)} %copy-done.8), kind=kOutput, calls=%fused_computation.21 | convolution fusion | flops 853770240 | bytes 11354112 | tf_op jit(solution)/shard_map/jkd,cd->jkc/dot_general | solution.py:254
  (155 shorter events, 40.5 us)
Async XLA Ops:
  0.6 6.0 %copy-start.1 = (s32[32]{0:T(128)S(1)}, s32[32]{0:T(128)}, u32[]{:S(2)}) copy-start(s32[32]{0:T(128)} %param.14) | copy-start | bytes 388
  3.4 14.1 %collective-permute-start.2 = (f32[2,8,384]{2,1,0:T(8,128)S(1)}, f32[2,8,384]{2,1,0:T(8,128)S(1)}, u32[]{:S(2)}, u32[]{:S(2)}) collective-permute-start(f32[2,8,384]{2,1,0:T(8,128)S(1)} %bitcast.206), channel_id=1, source_target_pairs={{0,3},{1,2},{2,1},{3,0},{4,7},{5,6},{6,5},{7,4},{8,11},{9,10},{10,... | collective-permute-start | bytes 73736 | tf_op jit(solution)/shard_map/ppermute | solution.py:136
  5.8 11.7 %collective-permute-start.1 = (f32[2,8,384]{2,1,0:T(8,128)S(1)}, f32[2,8,384]{2,1,0:T(8,128)}, u32[]{:S(2)}, u32[]{:S(2)}) collective-permute-start(f32[2,8,384]{2,1,0:T(8,128)S(1)} %bitcast.207), channel_id=1, source_target_pairs={{0,2},{1,3},{2,0},{3,1},{4,6},{5,7},{6,4},{7,5},{8,10},{9,11},{10,... | collective-permute-start | bytes 73736 | tf_op jit(solution)/shard_map/ppermute | solution.py:136
  6.4 11.1 %collective-permute-start = (f32[2,8,384]{2,1,0:T(8,128)S(1)}, f32[2,8,384]{2,1,0:T(8,128)}, u32[]{:S(2)}, u32[]{:S(2)}) collective-permute-start(f32[2,8,384]{2,1,0:T(8,128)S(1)} %bitcast.208), channel_id=1, source_target_pairs={{0,1},{1,0},{2,3},{3,2},{4,5},{5,4},{6,7},{7,6},{8,9},{9,8},{10,11... | collective-permute-start | bytes 73736 | tf_op jit(solution)/shard_map/ppermute | solution.py:136
  10.2 18.9 %copy-start.2 = (bf16[2,2,384,384]{3,2,1,0:T(8,128)(2,1)S(1)}, bf16[2,2,384,384]{3,2,1,0:T(8,128)(2,1)}, u32[]{:S(2)}) copy-start(bf16[2,2,384,384]{3,2,1,0:T(8,128)(2,1)} %param.13) | copy-start | bytes 3538948
  18.7 28.3 %copy-start.12 = (bf16[1440,8,1]{0,1,2:T(8,128)(2,1)S(1)}, bf16[1440,8,1]{0,1,2:T(8,128)(2,1)}, u32[]{:S(2)}) copy-start(bf16[1440,8,1]{0,1,2:T(8,128)(2,1)} %constant.101) | copy-start | bytes 69124
  20.3 5.7 %collective-permute-start.5 = (f32[1,6144]{1,0:T(1,128)S(1)}, f32[1,6144]{1,0:T(1,128)S(1)}, u32[]{:S(2)}, u32[]{:S(2)}) collective-permute-start(f32[1,6144]{1,0:T(1,128)S(1)} %get-tuple-element.24), channel_id=1, source_target_pairs={{0,12},{1,13},{2,14},{3,15},{4,8},{5,9},{6,10},{7,11},{8,4},{9,5},... | collective-permute-start | bytes 73736 | tf_op jit(solution)/shard_map/ppermute | solution.py:157
  24.2 4.7 %collective-permute-start.4 = (f32[1,6144]{1,0:T(1,128)S(1)}, f32[1,6144]{1,0:T(1,128)S(1)}, u32[]{:S(2)}, u32[]{:S(2)}) collective-permute-start(f32[1,6144]{1,0:T(1,128)S(1)} %get-tuple-element.25), channel_id=1, source_target_pairs={{0,8},{1,9},{2,10},{3,11},{4,12},{5,13},{6,14},{7,15},{8,0},{9,1},... | collective-permute-start | bytes 73736 | tf_op jit(solution)/shard_map/ppermute | solution.py:157
  24.2 4.7 %collective-permute-start.3 = (f32[1,6144]{1,0:T(1,128)S(1)}, f32[1,6144]{1,0:T(1,128)S(1)}, u32[]{:S(2)}, u32[]{:S(2)}) collective-permute-start(f32[1,6144]{1,0:T(1,128)S(1)} %get-tuple-element.23), channel_id=1, source_target_pairs={{0,4},{1,5},{2,6},{3,7},{4,0},{5,1},{6,2},{7,3},{8,12},{9,13},{10,... | collective-permute-start | bytes 73736 | tf_op jit(solution)/shard_map/ppermute | solution.py:157
  30.5 3.4 %collective-permute-start.8 = (bf16[2,8,384]{2,1,0:T(8,128)(2,1)}, bf16[2,8,384]{2,1,0:T(8,128)(2,1)S(1)}, u32[]{:S(2)}, u32[]{:S(2)}) collective-permute-start(bf16[2,8,384]{2,1,0:T(8,128)(2,1)} %pad_maximum_fusion.4), channel_id=1, source_target_pairs={{0,3},{1,2},{2,1},{3,0},{4,7},{5,6},{6,5},{7,4},{8,11},{9,10},{10,... | collective-permute-start | bytes 36872 | tf_op jit(solution)/shard_map/ppermute | solution.py:136
  30.6 4.0 %collective-permute-start.7 = (bf16[2,8,384]{2,1,0:T(8,128)(2,1)}, bf16[2,8,384]{2,1,0:T(8,128)(2,1)}, u32[]{:S(2)}, u32[]{:S(2)}) collective-permute-start(bf16[2,8,384]{2,1,0:T(8,128)(2,1)} %pad_maximum_fusion.4), channel_id=1, source_target_pairs={{0,2},{1,3},{2,0},{3,1},{4,6},{5,7},{6,4},{7,5},{8,10},{9,11},{10,... | collective-permute-start | bytes 36872 | tf_op jit(solution)/shard_map/ppermute | solution.py:136
  32.1 2.5 %collective-permute-start.6 = (bf16[2,8,384]{2,1,0:T(8,128)(2,1)}, bf16[2,8,384]{2,1,0:T(8,128)(2,1)}, u32[]{:S(2)}, u32[]{:S(2)}) collective-permute-start(bf16[2,8,384]{2,1,0:T(8,128)(2,1)} %pad_maximum_fusion.4), channel_id=1, source_target_pairs={{0,1},{1,0},{2,3},{3,2},{4,5},{5,4},{6,7},{7,6},{8,9},{9,8},{10,11... | collective-permute-start | bytes 36872 | tf_op jit(solution)/shard_map/ppermute | solution.py:136
  37.9 7.5 %collective-permute-start.11 = (f32[1,6144]{1,0:T(1,128)}, f32[1,6144]{1,0:T(1,128)S(1)}, u32[]{:S(2)}, u32[]{:S(2)}) collective-permute-start(f32[1,6144]{1,0:T(1,128)} %get-tuple-element.21), channel_id=1, source_target_pairs={{0,12},{1,13},{2,14},{3,15},{4,8},{5,9},{6,10},{7,11},{8,4},{9,5},... | collective-permute-start | bytes 73736 | tf_op jit(solution)/shard_map/ppermute | solution.py:157
  39.4 6.0 %collective-permute-start.10 = (f32[1,6144]{1,0:T(1,128)}, f32[1,6144]{1,0:T(1,128)}, u32[]{:S(2)}, u32[]{:S(2)}) collective-permute-start(f32[1,6144]{1,0:T(1,128)} %get-tuple-element.22), channel_id=1, source_target_pairs={{0,8},{1,9},{2,10},{3,11},{4,12},{5,13},{6,14},{7,15},{8,0},{9,1},... | collective-permute-start | bytes 73736 | tf_op jit(solution)/shard_map/ppermute | solution.py:157
  39.9 6.2 %collective-permute-start.9 = (f32[1,6144]{1,0:T(1,128)}, f32[1,6144]{1,0:T(1,128)}, u32[]{:S(2)}, u32[]{:S(2)}) collective-permute-start(f32[1,6144]{1,0:T(1,128)} %get-tuple-element.20), channel_id=1, source_target_pairs={{0,4},{1,5},{2,6},{3,7},{4,0},{5,1},{6,2},{7,3},{8,12},{9,13},{10,... | collective-permute-start | bytes 73736 | tf_op jit(solution)/shard_map/ppermute | solution.py:157
  53.4 10.9 %collective-permute-start.14 = (f32[2,8,384]{2,1,0:T(8,128)S(1)}, f32[2,8,384]{2,1,0:T(8,128)S(1)}, u32[]{:S(2)}, u32[]{:S(2)}) collective-permute-start(f32[2,8,384]{2,1,0:T(8,128)S(1)} %bitcast.210), channel_id=1, source_target_pairs={{0,3},{1,2},{2,1},{3,0},{4,7},{5,6},{6,5},{7,4},{8,11},{9,10},{10,... | collective-permute-start | bytes 73736 | tf_op jit(solution)/shard_map/ppermute | solution.py:136
  53.4 10.9 %collective-permute-start.13 = (f32[2,8,384]{2,1,0:T(8,128)S(1)}, f32[2,8,384]{2,1,0:T(8,128)S(1)}, u32[]{:S(2)}, u32[]{:S(2)}) collective-permute-start(f32[2,8,384]{2,1,0:T(8,128)S(1)} %bitcast.211), channel_id=1, source_target_pairs={{0,2},{1,3},{2,0},{3,1},{4,6},{5,7},{6,4},{7,5},{8,10},{9,11},{10,... | collective-permute-start | bytes 73736 | tf_op jit(solution)/shard_map/ppermute | solution.py:136
  54.9 9.4 %collective-permute-start.12 = (f32[2,8,384]{2,1,0:T(8,128)S(1)}, f32[2,8,384]{2,1,0:T(8,128)}, u32[]{:S(2)}, u32[]{:S(2)}) collective-permute-start(f32[2,8,384]{2,1,0:T(8,128)S(1)} %bitcast.212), channel_id=1, source_target_pairs={{0,1},{1,0},{2,3},{3,2},{4,5},{5,4},{6,7},{7,6},{8,9},{9,8},{10,11... | collective-permute-start | bytes 73736 | tf_op jit(solution)/shard_map/ppermute | solution.py:136
  57.5 7.6 %copy-start.11 = (f32[4,2,4,2,8]{2,0,3,1,4:T(4,128)S(1)}, f32[4,2,4,2,8]{2,0,3,1,4:T(4,128)}, u32[]{:S(2)}) copy-start(f32[4,2,4,2,8]{2,0,3,1,4:T(4,128)} %copy.54) | copy-start | bytes 6148
  67.1 7.6 %collective-permute-start.17 = (f32[1,6144]{1,0:T(1,128)S(1)}, f32[1,6144]{1,0:T(1,128)S(1)}, u32[]{:S(2)}, u32[]{:S(2)}) collective-permute-start(f32[1,6144]{1,0:T(1,128)S(1)} %get-tuple-element.18), channel_id=1, source_target_pairs={{0,12},{1,13},{2,14},{3,15},{4,8},{5,9},{6,10},{7,11},{8,4},{9,5},... | collective-permute-start | bytes 73736 | tf_op jit(solution)/shard_map/ppermute | solution.py:157
  68.7 6.1 %collective-permute-start.16 = (f32[1,6144]{1,0:T(1,128)S(1)}, f32[1,6144]{1,0:T(1,128)S(1)}, u32[]{:S(2)}, u32[]{:S(2)}) collective-permute-start(f32[1,6144]{1,0:T(1,128)S(1)} %get-tuple-element.19), channel_id=1, source_target_pairs={{0,8},{1,9},{2,10},{3,11},{4,12},{5,13},{6,14},{7,15},{8,0},{9,1},... | collective-permute-start | bytes 73736 | tf_op jit(solution)/shard_map/ppermute | solution.py:157
  69.1 5.7 %collective-permute-start.15 = (f32[1,6144]{1,0:T(1,128)S(1)}, f32[1,6144]{1,0:T(1,128)S(1)}, u32[]{:S(2)}, u32[]{:S(2)}) collective-permute-start(f32[1,6144]{1,0:T(1,128)S(1)} %get-tuple-element.17), channel_id=1, source_target_pairs={{0,4},{1,5},{2,6},{3,7},{4,0},{5,1},{6,2},{7,3},{8,12},{9,13},{10,... | collective-permute-start | bytes 73736 | tf_op jit(solution)/shard_map/ppermute | solution.py:157
  78.8 7.0 %copy-start.5 = (f32[2,384,384]{2,1,0:T(8,128)S(1)}, f32[2,384,384]{2,1,0:T(8,128)}, u32[]{:S(2)}) copy-start(f32[2,384,384]{2,1,0:T(8,128)} %fusion.73) | copy-start | bytes 3538948
  80.8 6.7 %collective-permute-start.20 = (f32[43008]{0:T(1024)S(1)}, f32[43008]{0:T(1024)S(1)}, u32[]{:S(2)}, u32[]{:S(2)}) collective-permute-start(f32[43008]{0:T(1024)S(1)} %get-tuple-element.32), channel_id=1, source_target_pairs={{0,3},{1,2},{2,1},{3,0},{4,7},{5,6},{6,5},{7,4},{8,11},{9,10},{10,... | collective-permute-start | bytes 516104 | tf_op jit(solution)/shard_map/ppermute | solution.py:139
  81.0 10.2 %collective-permute-start.19 = (f32[43008]{0:T(1024)}, f32[43008]{0:T(1024)}, u32[]{:S(2)}, u32[]{:S(2)}) collective-permute-start(f32[43008]{0:T(1024)} %get-tuple-element.31), channel_id=1, source_target_pairs={{0,2},{1,3},{2,0},{3,1},{4,6},{5,7},{6,4},{7,5},{8,10},{9,11},{10,... | collective-permute-start | bytes 516104 | tf_op jit(solution)/shard_map/ppermute | solution.py:139
  82.2 9.9 %collective-permute-start.18 = (f32[43008]{0:T(1024)}, f32[43008]{0:T(1024)}, u32[]{:S(2)}, u32[]{:S(2)}) collective-permute-start(f32[43008]{0:T(1024)} %get-tuple-element.30), channel_id=1, source_target_pairs={{0,1},{1,0},{2,3},{3,2},{4,5},{5,4},{6,7},{7,6},{8,9},{9,8},{10,11... | collective-permute-start | bytes 516104 | tf_op jit(solution)/shard_map/ppermute | solution.py:139
  86.9 11.2 %copy-start.9 = (f32[4,1,9216]{2,1,0:T(1,128)S(1)}, f32[4,1,9216]{2,1,0:T(1,128)}, u32[]{:S(2)}) copy-start(f32[4,1,9216]{2,1,0:T(1,128)} %get-tuple-element.10) | copy-start | bytes 442372
  96.0 6.9 %copy-start.6 = (bf16[2,1,384,384]{3,2,0,1:T(8,128)(2,1)S(1)}, bf16[2,1,384,384]{3,2,0,1:T(8,128)(2,1)}, u32[]{:S(2)}) copy-start(bf16[2,1,384,384]{3,2,0,1:T(8,128)(2,1)} %fusion.15) | copy-start | bytes 1769476
  98.5 6.8 %collective-permute-start.23 = (f32[1,15360]{1,0:T(1,128)S(1)}, f32[1,15360]{1,0:T(1,128)S(1)}, u32[]{:S(2)}, u32[]{:S(2)}) collective-permute-start(f32[1,15360]{1,0:T(1,128)S(1)} %get-tuple-element.15), channel_id=1, source_target_pairs={{0,12},{1,13},{2,14},{3,15},{4,8},{5,9},{6,10},{7,11},{8,4},{9,5},... | collective-permute-start | bytes 184328 | tf_op jit(solution)/shard_map/ppermute | solution.py:157
  100.0 7.0 %collective-permute-start.22 = (f32[1,15360]{1,0:T(1,128)S(1)}, f32[1,15360]{1,0:T(1,128)S(1)}, u32[]{:S(2)}, u32[]{:S(2)}) collective-permute-start(f32[1,15360]{1,0:T(1,128)S(1)} %get-tuple-element.16), channel_id=1, source_target_pairs={{0,8},{1,9},{2,10},{3,11},{4,12},{5,13},{6,14},{7,15},{8,0},{9,1},... | collective-permute-start | bytes 184328 | tf_op jit(solution)/shard_map/ppermute | solution.py:157
  100.6 6.7 %copy-start.13 = (bf16[1440,8,1]{0,1,2:T(8,128)(2,1)S(1)}, bf16[1440,8,1]{0,1,2:T(8,128)(2,1)}, u32[]{:S(2)}) copy-start(bf16[1440,8,1]{0,1,2:T(8,128)(2,1)} %constant.101) | copy-start | bytes 69124
  100.6 6.4 %collective-permute-start.21 = (f32[1,15360]{1,0:T(1,128)S(1)}, f32[1,15360]{1,0:T(1,128)S(1)}, u32[]{:S(2)}, u32[]{:S(2)}) collective-permute-start(f32[1,15360]{1,0:T(1,128)S(1)} %get-tuple-element.14), channel_id=1, source_target_pairs={{0,4},{1,5},{2,6},{3,7},{4,0},{5,1},{6,2},{7,3},{8,12},{9,13},{10,... | collective-permute-start | bytes 184328 | tf_op jit(solution)/shard_map/ppermute | solution.py:157
  (10 other events, 25.0 us)

commit v7 on v5

--- a/solution.py
+++ b/solution.py
@@ -128,9 +128,20 @@
     for k in range(1, 1 << lo):
         parts.append(lax.ppermute(values, axis_name, [(i, i ^ k) for i in range(groups)]))
     stacked = jnp.stack(parts).astype(jnp.float32)
-    cur = jnp.einsum(spec, table, stacked, precision=lax.Precision.HIGHEST)
     hi = groups.bit_length() - 1 - lo
-    b = 0
+    if hi == 0:
+        return jnp.einsum(spec, table, stacked, precision=lax.Precision.HIGHEST)[0]
+    width = min(2, hi)
+    fan = 1 << width
+    tables = table.reshape((table.shape[0] // fan, fan) + table.shape[1:])
+    cur = None
+    for k in range(fan):
+        piece = jnp.einsum(spec, tables[:, k], stacked, precision=lax.Precision.HIGHEST)
+        if k > 0:
+            mask = k << lo
+            piece = lax.ppermute(piece, axis_name, [(i, i ^ mask) for i in range(groups)])
+        cur = piece if cur is None else cur + piece
+    b = width
     while b < hi:
         width = min(2, hi - b)
         fan = 1 << width

time: 86.3 us -> 105 us (1.22)
  matrix products: 22.2 us -> 35.2 us
  local copies, waits for them, and re-layouts: 15.4 us -> 23.4 us
  waiting for transfers between devices: 12.3 us -> 8.41 us
    another operation x0 -> x20, local copies, waits for them, and re-layouts: none -> 14.2 us
    dot_general x4 -> x16, matrix products: 1.35 us -> 14.2 us  [xor_exchange(): jnp.einsum(spec, tables[:, k], stacked, precision=lax.Precision.HIGHEST)]
    ppermute x6, waiting for transfers between devices: 5.65 us -> 0.75 us  [xor_reduce_scatter(): lax.ppermute(sent, axis_name, [(i, i ^ mask) for i in range(groups)])]
    unnamed x35 -> x39, local copies, waits for them, and re-layouts: 8.01 us -> 4 us
    ppermute x12, waiting for transfers between devices: 5.01 us -> 7.63 us  [xor_exchange(): lax.ppermute(piece, axis_name, [(i, i ^ mask) for i in range(groups)])]
    slice x6 -> x0, local copies, waits for them, and re-layouts: 2.24 us -> none  [the longest x4 0.87 us: xor_exchange(): total = view[:, 0]]
    ppermute x12, waiting for transfers between devices: 1.65 us -> 0.03 us  [xor_exchange(): lax.ppermute(values, axis_name, [(i, i ^ k) for i in range(groups)])]
    reshape x0 -> x2, local copies, waits for them, and re-layouts: none -> 1.44 us  [xor_exchange(): tables = table.reshape((table.shape[0] // fan, fan) + table.shape[1:])]
  transfers between devices with their start and end apart: 30 -> 30, of which waited for: 8 -> 5; matrix products, arithmetic and copies ran while one was open for 26% -> 34% of each run, Pallas kernels for 0% -> 0%
where the time goes in v7:
time: 105 us; the launch traced here: 104 us
  matrix products  35.2 us (34%)
  starting transfers between devices  32.3 us (31%)
  local copies, waits for them, and re-layouts  23.4 us (22%)
  waiting for transfers between devices  8.41 us (8%)
  other arithmetic  3.43 us (3%)
  between operations  1.17 us (1%)
    ppermute x12, starting transfers between devices, xor_exchange(): lax.ppermute(piece, axis_name, [(i, i ^ mask) for i in range(groups)])  16.4 us
    dot_general x16, matrix products, xor_exchange(): jnp.einsum(spec, tables[:, k], stacked, precision=lax.Precision.HIGHEST)  14.2 us
    another operation x20, local copies, waits for them, and re-layouts  14.2 us
    ppermute x12, starting transfers between devices, xor_exchange(): lax.ppermute(values, axis_name, [(i, i ^ k) for i in range(groups)])  9.1 us
    ppermute x12, waiting for transfers between devices, xor_exchange(): lax.ppermute(piece, axis_name, [(i, i ^ mask) for i in range(groups)])  7.63 us
    ppermute x6, starting transfers between devices, xor_reduce_scatter(): lax.ppermute(sent, axis_name, [(i, i ^ mask) for i in range(groups)])  6.84 us
    dot_general x1, matrix products, local(): jnp.einsum('jfc,kf->jkc', grid_modes, fourier, preferred_element_type=jnp...  5.99 us
    dot_general x1, matrix products, local(): jnp.einsum('jkc,cd->jkd', activations, skip_weight, preferred_element_typ...  4.59 us
  transfers between devices with their start and end apart: 30, of which 5 were waited for; matrix products, arithmetic and copies ran while one was open for 34% of the time, Pallas kernels for 0%

profile of v7, /device:TPU:0, one launch (start us, length us, event | category | flops | bytes accessed | tf_op | source)
XLA Modules:
  0.0 103.9 jit_solution(660430801579196016)
XLA Ops:
  0.7 1.6 %copy-done = bf16[2,1440,384]{2,1,0:T(8,128)(2,1)S(1)} copy-done((bf16[2,1440,384]{2,1,0:T(8,128)(2,1)S(1)}, bf16[2,1440,384]{2,1,0:T(8,128)(2,1)}, u32[]{:S(2)}) %copy-start) | copy-done | bytes 2211864
  3.4 3.0 %collective-permute-start.1 = (f32[2,8,384]{2,1,0:T(8,128)S(1)}, f32[2,8,384]{2,1,0:T(8,128)S(1)}, u32[]{:S(2)}, u32[]{:S(2)}) collective-permute-start(f32[2,8,384]{2,1,0:T(8,128)S(1)} %bitcast.299), channel_id=1, source_target_pairs={{0,2},{1,3},{2,0},{3,1},{4,6},{5,7},{6,4},{7,5},{8,10},{9,11},{10,... | collective-permute-start | bytes 73736 | tf_op jit(solution)/shard_map/ppermute | solution.py:129
  12.1 4.6 %fusion.62 = f32[2,1440,384]{2,1,0:T(8,128)} fusion(bf16[2,1440,384]{2,1,0:T(8,128)(2,1)S(1)} %copy-done, bf16[384,384]{1,0:T(8,128)(2,1)} %param.12), kind=kOutput, calls=%fused_computation.95 | convolution fusion | flops 849346560 | bytes 6930432 | tf_op jit(solution)/shard_map/jkc,cd->jkd/dot_general | solution.py:241
  20.8 1.6 %convolution_bitcast_fusion.14 = f32[1,2,8,384]{3,1,2,0:T(2,128)} fusion(f32[2,4,2,8]{1,0,2,3:T(2,128)} %copy.67, f32[4,2,8,384]{3,2,1,0:T(8,128)S(1)} %pad_maximum_fusion.1), kind=kOutput, calls=%fused_computation.52 | convolution fusion | flops 589824 | bytes 123392 | tf_op jit(solution)/shard_map/xskrf,krfc->xsfc/dot_general | solution.py:139
  22.4 1.6 %convolution_bitcast_fusion.13 = f32[1,2,8,384]{3,1,2,0:T(2,128)} fusion(f32[2,4,2,8]{1,0,2,3:T(2,128)} %copy.69, f32[4,2,8,384]{3,2,1,0:T(8,128)S(1)} %pad_maximum_fusion.1), kind=kOutput, calls=%fused_computation.51 | convolution fusion | flops 589824 | bytes 123392 | tf_op jit(solution)/shard_map/xskrf,krfc->xsfc/dot_general | solution.py:139
  24.1 1.7 %convolution_bitcast_fusion.12 = f32[1,2,8,384]{3,1,2,0:T(2,128)} fusion(f32[2,4,2,8]{1,0,2,3:T(2,128)} %copy.71, f32[4,2,8,384]{3,2,1,0:T(8,128)S(1)} %pad_maximum_fusion.1), kind=kOutput, calls=%fused_computation.50 | convolution fusion | flops 589824 | bytes 123392 | tf_op jit(solution)/shard_map/xskrf,krfc->xsfc/dot_general | solution.py:139
  25.7 4.0 %collective-permute-start.5 = (f32[1,2,8,384]{3,1,2,0:T(2,128)}, f32[1,2,8,384]{3,1,2,0:T(2,128)}, u32[]{:S(2)}, u32[]{:S(2)}) collective-permute-start(f32[1,2,8,384]{3,1,2,0:T(2,128)} %convolution_bitcast_fusion.12), channel_id=1, source_target_pairs={{0,12},{1,13},{2,14},{3,15},{4,8},{5,9},{6,10},{7,11},{8,4},{9,5},... | collective-permute-start | bytes 73736 | tf_op jit(solution)/shard_map/ppermute | solution.py:142
  30.3 1.4 %slice_bitcast_fusion.11 = (f32[2,4,2,8]{3,2,1,0:T(2,128)}, f32[2,4,2,8]{3,2,1,0:T(2,128)}, f32[2,4,2,8]{3,2,1,0:T(2,128)}, f32[2,4,2,8]{3,2,1,0:T(2,128)S(1)}) fusion(f32[1,4,2,4,2,8]{5,4,3,2,1,0:T(2,128)} %get-tuple-element.24), kind=kLoop, calls=%fused_computation.139 | loop fusion | bytes 4096 | tf_op jit(solution)/shard_map/reshape.37
  31.7 1.4 %copy.65 = f32[2,4,2,8]{1,0,2,3:T(2,128)} copy(f32[2,4,2,8]{3,2,1,0:T(2,128)} %get-tuple-element.32) | data formatting | bytes 1024 | tf_op jit(solution)/shard_map/reshape.12
  33.1 1.7 %collective-permute-done.4 = f32[1,2,8,384]{3,1,2,0:T(2,128)} collective-permute-done((f32[1,2,8,384]{3,1,2,0:T(2,128)}, f32[1,2,8,384]{3,1,2,0:T(2,128)}, u32[]{:S(2)}, u32[]{:S(2)}) %collective-permute-start.4) | collective-permute-done | bytes 24608 | tf_op jit(solution)/shard_map/ppermute | solution.py:142
  37.4 1.6 %collective-permute-start.7 = (bf16[2,8,384]{2,1,0:T(8,128)(2,1)}, bf16[2,8,384]{2,1,0:T(8,128)(2,1)S(1)}, u32[]{:S(2)}, u32[]{:S(2)}) collective-permute-start(bf16[2,8,384]{2,1,0:T(8,128)(2,1)} %pad_maximum_fusion.5), channel_id=1, source_target_pairs={{0,2},{1,3},{2,0},{3,1},{4,6},{5,7},{6,4},{7,5},{8,10},{9,11},{10,... | collective-permute-start | bytes 36872 | tf_op jit(solution)/shard_map/ppermute | solution.py:129
  43.3 1.6 %convolution_bitcast_fusion.10 = f32[1,2,8,384]{3,1,2,0:T(2,128)} fusion(f32[4,2,2,8]{0,2,1,3:T(2,128)} %copy.81, bf16[4,2,8,384]{3,2,1,0:T(8,128)(2,1)S(1)} %pad_maximum_fusion.3), kind=kOutput, calls=%fused_computation.45 | convolution fusion | flops 589824 | bytes 74240 | tf_op jit(solution)/shard_map/xksrf,ksfc->xrfc/dot_general | solution.py:139
  44.9 1.6 %convolution_bitcast_fusion.9 = f32[1,2,8,384]{3,1,2,0:T(2,128)} fusion(f32[4,2,2,8]{0,2,1,3:T(2,128)} %copy.83, bf16[4,2,8,384]{3,2,1,0:T(8,128)(2,1)S(1)} %pad_maximum_fusion.3), kind=kOutput, calls=%fused_computation.44 | convolution fusion | flops 589824 | bytes 74240 | tf_op jit(solution)/shard_map/xksrf,ksfc->xrfc/dot_general | solution.py:139
  46.5 1.6 %convolution_bitcast_fusion.8 = f32[1,2,8,384]{3,1,2,0:T(2,128)} fusion(f32[4,2,2,8]{0,2,1,3:T(2,128)} %copy.85, bf16[4,2,8,384]{3,2,1,0:T(8,128)(2,1)S(1)} %pad_maximum_fusion.3), kind=kOutput, calls=%fused_computation.43 | convolution fusion | flops 589824 | bytes 74240 | tf_op jit(solution)/shard_map/xksrf,ksfc->xrfc/dot_general | solution.py:139
  48.1 2.1 %collective-permute-start.11 = (f32[1,2,8,384]{3,1,2,0:T(2,128)}, f32[1,2,8,384]{3,1,2,0:T(2,128)}, u32[]{:S(2)}, u32[]{:S(2)}) collective-permute-start(f32[1,2,8,384]{3,1,2,0:T(2,128)} %convolution_bitcast_fusion.8), channel_id=1, source_target_pairs={{0,12},{1,13},{2,14},{3,15},{4,8},{5,9},{6,10},{7,11},{8,4},{9,5},... | collective-permute-start | bytes 73736 | tf_op jit(solution)/shard_map/ppermute | solution.py:142
  50.3 2.3 %collective-permute-start.9 = (f32[1,2,8,384]{3,1,2,0:T(2,128)}, f32[1,2,8,384]{3,1,2,0:T(2,128)}, u32[]{:S(2)}, u32[]{:S(2)}) collective-permute-start(f32[1,2,8,384]{3,1,2,0:T(2,128)} %convolution_bitcast_fusion.10), channel_id=1, source_target_pairs={{0,4},{1,5},{2,6},{3,7},{4,0},{5,1},{6,2},{7,3},{8,12},{9,13},{10,... | collective-permute-start | bytes 73736 | tf_op jit(solution)/shard_map/ppermute | solution.py:142
  53.1 1.4 %copy.88 = f32[2,4,2,8]{1,0,2,3:T(2,128)} copy(f32[2,4,2,8]{3,2,1,0:T(2,128)} %get-tuple-element.20) | data formatting | bytes 1024 | tf_op jit(solution)/shard_map/reshape.37
  55.6 1.4 %copy.106 = f32[4,2,2,8]{0,2,1,3:T(2,128)} copy(f32[4,2,2,8]{3,2,1,0:T(2,128)} %get-tuple-element.17) | data formatting | bytes 1024 | tf_op jit(solution)/shard_map/reshape.51
  59.8 6.0 %fusion.6 = bf16[2,1440,384]{2,1,0:T(8,128)(2,1)S(1)} fusion(bf16[2,1440,384]{2,1,0:T(8,128)(2,1)} %param.11, f32[2,1440,384]{2,1,0:T(8,128)} %fusion.62, bf16[1440,8,1]{0,1,2:T(8,128)(2,1)S(1)} %copy-done.6, bf16[2,8,384]{2,0,1:T(2,128)(2,1)S(1)} %fusion.34), kind=kOutput, calls=%fused_computation.15 | convolution fusion | flops 42024960 | bytes 8882688 | tf_op jit(solution)/shard_map/jfc,kf->jkc/dot_general | solution.py:240
  66.2 1.5 %collective-permute-start.13 = (f32[2,8,384]{2,1,0:T(8,128)S(1)}, f32[2,8,384]{2,1,0:T(8,128)S(1)}, u32[]{:S(2)}, u32[]{:S(2)}) collective-permute-start(f32[2,8,384]{2,1,0:T(8,128)S(1)} %bitcast.303), channel_id=1, source_target_pairs={{0,2},{1,3},{2,0},{3,1},{4,6},{5,7},{6,4},{7,5},{8,10},{9,11},{10,... | collective-permute-start | bytes 73736 | tf_op jit(solution)/shard_map/ppermute | solution.py:129
  68.3 1.5 %fusion.60 = f32[2,1440,384]{2,1,0:T(8,128)S(1)} fusion(bf16[2,1440,384]{2,1,0:T(8,128)(2,1)S(1)} %fusion.6, bf16[384,384]{1,0:T(8,128)(2,1)S(1)} %copy-done.4), kind=kOutput, calls=%fused_computation.93 | convolution fusion | flops 849346560 | bytes 6930432 | tf_op jit(solution)/shard_map/jkd,cd->jkc/dot_general | solution.py:248
  69.9 1.4 %fusion.110 = f32[384,384,1]{0,1,2:T(8,128)S(1)} fusion(bf16[2,1440,384]{2,1,0:T(8,128)(2,1)S(1)} %fusion.6, bf16[2,1440,384]{2,1,0:T(8,128)(2,1)S(1)} %copy-done), kind=kOutput, calls=%fused_computation.189 | convolution fusion | flops 849346560 | bytes 5013504 | tf_op jit(solution)/shard_map/jkc,jkd->cd/dot_general | solution.py:245
  72.3 2.2 %collective-permute-start.17 = (f32[1,2,8,384]{3,1,2,0:T(2,128)S(1)}, f32[1,2,8,384]{3,1,2,0:T(2,128)S(1)}, u32[]{:S(2)}, u32[]{:S(2)}) collective-permute-start(f32[1,2,8,384]{3,1,2,0:T(2,128)S(1)} %convolution_bitcast_fusion.4), channel_id=1, source_target_pairs={{0,12},{1,13},{2,14},{3,15},{4,8},{5,9},{6,10},{7,11},{8,4},{9,5},... | collective-permute-start | bytes 73736 | tf_op jit(solution)/shard_map/ppermute | solution.py:142
  74.5 2.3 %collective-permute-start.15 = (f32[1,2,8,384]{3,1,2,0:T(2,128)S(1)}, f32[1,2,8,384]{3,1,2,0:T(2,128)S(1)}, u32[]{:S(2)}, u32[]{:S(2)}) collective-permute-start(f32[1,2,8,384]{3,1,2,0:T(2,128)S(1)} %convolution_bitcast_fusion.6), channel_id=1, source_target_pairs={{0,4},{1,5},{2,6},{3,7},{4,0},{5,1},{6,2},{7,3},{8,12},{9,13},{10,... | collective-permute-start | bytes 73736 | tf_op jit(solution)/shard_map/ppermute | solution.py:142
  76.9 1.6 %collective-permute-start.26 = (f32[4,24,384]{2,1,0:T(8,128)S(1)}, f32[4,24,384]{2,1,0:T(8,128)S(1)}, u32[]{:S(2)}, u32[]{:S(2)}) collective-permute-start(f32[4,24,384]{2,1,0:T(8,128)S(1)} %get-tuple-element.11), channel_id=1, source_target_pairs={{0,3},{1,2},{2,1},{3,0},{4,7},{5,6},{6,5},{7,4},{8,11},{9,10},{10,... | collective-permute-start | bytes 442376 | tf_op jit(solution)/shard_map/ppermute | solution.py:120
  84.2 1.6 %collective-permute-start.25 = (f32[4,24,384]{2,1,0:T(8,128)S(1)}, f32[4,24,384]{2,1,0:T(8,128)S(1)}, u32[]{:S(2)}, u32[]{:S(2)}) collective-permute-start(f32[4,24,384]{2,1,0:T(8,128)S(1)} %get-tuple-element.12), channel_id=1, source_target_pairs={{0,2},{1,3},{2,0},{3,1},{4,6},{5,7},{6,4},{7,5},{8,10},{9,11},{10,... | collective-permute-start | bytes 442376 | tf_op jit(solution)/shard_map/ppermute | solution.py:120
  86.4 1.8 %collective-permute-start.23 = (f32[1,2,8,384]{3,1,2,0:T(2,128)S(1)}, f32[1,2,8,384]{3,1,2,0:T(2,128)S(1)}, u32[]{:S(2)}, u32[]{:S(2)}) collective-permute-start(f32[1,2,8,384]{3,1,2,0:T(2,128)S(1)} %convolution_bitcast_fusion), channel_id=1, source_target_pairs={{0,12},{1,13},{2,14},{3,15},{4,8},{5,9},{6,10},{7,11},{8,4},{9,5},... | collective-permute-start | bytes 73736 | tf_op jit(solution)/shard_map/ppermute | solution.py:142
  89.6 2.7 %collective-permute-done.23 = f32[1,2,8,384]{3,1,2,0:T(2,128)S(1)} collective-permute-done((f32[1,2,8,384]{3,1,2,0:T(2,128)S(1)}, f32[1,2,8,384]{3,1,2,0:T(2,128)S(1)}, u32[]{:S(2)}, u32[]{:S(2)}) %collective-permute-start.23) | collective-permute-done | bytes 24608 | tf_op jit(solution)/shard_map/ppermute | solution.py:142
  93.6 2.5 %collective-permute-done.21 = f32[1,2,8,384]{3,1,2,0:T(2,128)S(1)} collective-permute-done((f32[1,2,8,384]{3,1,2,0:T(2,128)S(1)}, f32[1,2,8,384]{3,1,2,0:T(2,128)S(1)}, u32[]{:S(2)}, u32[]{:S(2)}) %collective-permute-start.21) | collective-permute-done | bytes 24608 | tf_op jit(solution)/shard_map/ppermute | solution.py:142
  96.6 1.8 %collective-permute-start.29 = (f32[1,24,384]{2,1,0:T(8,128)S(1)}, f32[1,24,384]{2,1,0:T(8,128)S(1)}, u32[]{:S(2)}, u32[]{:S(2)}) collective-permute-start(f32[1,24,384]{2,1,0:T(8,128)S(1)} %get-tuple-element.14), channel_id=1, source_target_pairs={{0,12},{1,13},{2,14},{3,15},{4,8},{5,9},{6,10},{7,11},{8,4},{9,5},... | collective-permute-start | bytes 110600 | tf_op jit(solution)/shard_map/ppermute | solution.py:120
  98.4 1.7 %collective-permute-start.28 = (f32[1,24,384]{2,1,0:T(8,128)S(1)}, f32[1,24,384]{2,1,0:T(8,128)S(1)}, u32[]{:S(2)}, u32[]{:S(2)}) collective-permute-start(f32[1,24,384]{2,1,0:T(8,128)S(1)} %get-tuple-element.15), channel_id=1, source_target_pairs={{0,8},{1,9},{2,10},{3,11},{4,12},{5,13},{6,14},{7,15},{8,0},{9,1},... | collective-permute-start | bytes 110600 | tf_op jit(solution)/shard_map/ppermute | solution.py:120
  100.0 2.5 %fusion.11 = bf16[2,1440,384]{2,1,0:T(8,128)(2,1)} fusion(f32[2,1440,384]{2,1,0:T(8,128)S(1)} %fusion.60, bf16[2,1440,384]{2,1,0:T(8,128)(2,1)S(1)} %copy-done.3, bf16[1440,8,1]{0,1,2:T(8,128)(2,1)S(1)} %copy-done.6, bf16[2,8,384]{2,0,1:T(2,128)(2,1)S(1)} %fusion.32), kind=kOutput, calls=%fused_computation.20 | convolution fusion | flops 22118400 | bytes 8882688 | tf_op jit(solution)/shard_map/jfc,kf->jkc/dot_general | solution.py:254
  (156 shorter events, 35.5 us)
Async XLA Ops:
  3.4 16.0 %collective-permute-start.1 = (f32[2,8,384]{2,1,0:T(8,128)S(1)}, f32[2,8,384]{2,1,0:T(8,128)S(1)}, u32[]{:S(2)}, u32[]{:S(2)}) collective-permute-start(f32[2,8,384]{2,1,0:T(8,128)S(1)} %bitcast.299), channel_id=1, source_target_pairs={{0,2},{1,3},{2,0},{3,1},{4,6},{5,7},{6,4},{7,5},{8,10},{9,11},{10,... | collective-permute-start | bytes 73736 | tf_op jit(solution)/shard_map/ppermute | solution.py:129
  6.4 13.0 %collective-permute-start = (f32[2,8,384]{2,1,0:T(8,128)S(1)}, f32[2,8,384]{2,1,0:T(8,128)S(1)}, u32[]{:S(2)}, u32[]{:S(2)}) collective-permute-start(f32[2,8,384]{2,1,0:T(8,128)S(1)} %bitcast.300), channel_id=1, source_target_pairs={{0,1},{1,0},{2,3},{3,2},{4,5},{5,4},{6,7},{7,6},{8,9},{9,8},{10,11... | collective-permute-start | bytes 73736 | tf_op jit(solution)/shard_map/ppermute | solution.py:129
  6.4 13.0 %collective-permute-start.2 = (f32[2,8,384]{2,1,0:T(8,128)S(1)}, f32[2,8,384]{2,1,0:T(8,128)S(1)}, u32[]{:S(2)}, u32[]{:S(2)}) collective-permute-start(f32[2,8,384]{2,1,0:T(8,128)S(1)} %bitcast.301), channel_id=1, source_target_pairs={{0,3},{1,2},{2,1},{3,0},{4,7},{5,6},{6,5},{7,4},{8,11},{9,10},{10,... | collective-permute-start | bytes 73736 | tf_op jit(solution)/shard_map/ppermute | solution.py:129
  12.1 23.9 %copy-start.2 = (bf16[2,2,384,384]{3,2,1,0:T(8,128)(2,1)S(1)}, bf16[2,2,384,384]{3,2,1,0:T(8,128)(2,1)}, u32[]{:S(2)}) copy-start(bf16[2,2,384,384]{3,2,1,0:T(8,128)(2,1)} %param.13) | copy-start | bytes 3538948
  24.1 35.7 %copy-start.6 = (bf16[1440,8,1]{0,1,2:T(8,128)(2,1)S(1)}, bf16[1440,8,1]{0,1,2:T(8,128)(2,1)}, u32[]{:S(2)}) copy-start(bf16[1440,8,1]{0,1,2:T(8,128)(2,1)} %constant.108) | copy-start | bytes 69124
  25.7 7.4 %collective-permute-start.5 = (f32[1,2,8,384]{3,1,2,0:T(2,128)}, f32[1,2,8,384]{3,1,2,0:T(2,128)}, u32[]{:S(2)}, u32[]{:S(2)}) collective-permute-start(f32[1,2,8,384]{3,1,2,0:T(2,128)} %convolution_bitcast_fusion.12), channel_id=1, source_target_pairs={{0,12},{1,13},{2,14},{3,15},{4,8},{5,9},{6,10},{7,11},{8,4},{9,5},... | collective-permute-start | bytes 73736 | tf_op jit(solution)/shard_map/ppermute | solution.py:142
  29.8 5.0 %collective-permute-start.4 = (f32[1,2,8,384]{3,1,2,0:T(2,128)}, f32[1,2,8,384]{3,1,2,0:T(2,128)}, u32[]{:S(2)}, u32[]{:S(2)}) collective-permute-start(f32[1,2,8,384]{3,1,2,0:T(2,128)} %convolution_bitcast_fusion.13), channel_id=1, source_target_pairs={{0,8},{1,9},{2,10},{3,11},{4,12},{5,13},{6,14},{7,15},{8,0},{9,1},... | collective-permute-start | bytes 73736 | tf_op jit(solution)/shard_map/ppermute | solution.py:142
  29.8 5.0 %collective-permute-start.3 = (f32[1,2,8,384]{3,1,2,0:T(2,128)}, f32[1,2,8,384]{3,1,2,0:T(2,128)}, u32[]{:S(2)}, u32[]{:S(2)}) collective-permute-start(f32[1,2,8,384]{3,1,2,0:T(2,128)} %convolution_bitcast_fusion.14), channel_id=1, source_target_pairs={{0,4},{1,5},{2,6},{3,7},{4,0},{5,1},{6,2},{7,3},{8,12},{9,13},{10,... | collective-permute-start | bytes 73736 | tf_op jit(solution)/shard_map/ppermute | solution.py:142
  37.4 4.6 %collective-permute-start.8 = (bf16[2,8,384]{2,1,0:T(8,128)(2,1)}, bf16[2,8,384]{2,1,0:T(8,128)(2,1)S(1)}, u32[]{:S(2)}, u32[]{:S(2)}) collective-permute-start(bf16[2,8,384]{2,1,0:T(8,128)(2,1)} %pad_maximum_fusion.5), channel_id=1, source_target_pairs={{0,3},{1,2},{2,1},{3,0},{4,7},{5,6},{6,5},{7,4},{8,11},{9,10},{10,... | collective-permute-start | bytes 36872 | tf_op jit(solution)/shard_map/ppermute | solution.py:129
  37.4 4.6 %collective-permute-start.7 = (bf16[2,8,384]{2,1,0:T(8,128)(2,1)}, bf16[2,8,384]{2,1,0:T(8,128)(2,1)S(1)}, u32[]{:S(2)}, u32[]{:S(2)}) collective-permute-start(bf16[2,8,384]{2,1,0:T(8,128)(2,1)} %pad_maximum_fusion.5), channel_id=1, source_target_pairs={{0,2},{1,3},{2,0},{3,1},{4,6},{5,7},{6,4},{7,5},{8,10},{9,11},{10,... | collective-permute-start | bytes 36872 | tf_op jit(solution)/shard_map/ppermute | solution.py:129
  39.0 3.0 %collective-permute-start.6 = (bf16[2,8,384]{2,1,0:T(8,128)(2,1)}, bf16[2,8,384]{2,1,0:T(8,128)(2,1)}, u32[]{:S(2)}, u32[]{:S(2)}) collective-permute-start(bf16[2,8,384]{2,1,0:T(8,128)(2,1)} %pad_maximum_fusion.5), channel_id=1, source_target_pairs={{0,1},{1,0},{2,3},{3,2},{4,5},{5,4},{6,7},{7,6},{8,9},{9,8},{10,11... | collective-permute-start | bytes 36872 | tf_op jit(solution)/shard_map/ppermute | solution.py:129
  48.1 10.5 %collective-permute-start.11 = (f32[1,2,8,384]{3,1,2,0:T(2,128)}, f32[1,2,8,384]{3,1,2,0:T(2,128)}, u32[]{:S(2)}, u32[]{:S(2)}) collective-permute-start(f32[1,2,8,384]{3,1,2,0:T(2,128)} %convolution_bitcast_fusion.8), channel_id=1, source_target_pairs={{0,12},{1,13},{2,14},{3,15},{4,8},{5,9},{6,10},{7,11},{8,4},{9,5},... | collective-permute-start | bytes 73736 | tf_op jit(solution)/shard_map/ppermute | solution.py:142
  50.3 8.4 %collective-permute-start.10 = (f32[1,2,8,384]{3,1,2,0:T(2,128)}, f32[1,2,8,384]{3,1,2,0:T(2,128)}, u32[]{:S(2)}, u32[]{:S(2)}) collective-permute-start(f32[1,2,8,384]{3,1,2,0:T(2,128)} %convolution_bitcast_fusion.9), channel_id=1, source_target_pairs={{0,8},{1,9},{2,10},{3,11},{4,12},{5,13},{6,14},{7,15},{8,0},{9,1},... | collective-permute-start | bytes 73736 | tf_op jit(solution)/shard_map/ppermute | solution.py:142
  50.3 8.4 %collective-permute-start.9 = (f32[1,2,8,384]{3,1,2,0:T(2,128)}, f32[1,2,8,384]{3,1,2,0:T(2,128)}, u32[]{:S(2)}, u32[]{:S(2)}) collective-permute-start(f32[1,2,8,384]{3,1,2,0:T(2,128)} %convolution_bitcast_fusion.10), channel_id=1, source_target_pairs={{0,4},{1,5},{2,6},{3,7},{4,0},{5,1},{6,2},{7,3},{8,12},{9,13},{10,... | collective-permute-start | bytes 73736 | tf_op jit(solution)/shard_map/ppermute | solution.py:142
  66.2 5.1 %collective-permute-start.13 = (f32[2,8,384]{2,1,0:T(8,128)S(1)}, f32[2,8,384]{2,1,0:T(8,128)S(1)}, u32[]{:S(2)}, u32[]{:S(2)}) collective-permute-start(f32[2,8,384]{2,1,0:T(8,128)S(1)} %bitcast.303), channel_id=1, source_target_pairs={{0,2},{1,3},{2,0},{3,1},{4,6},{5,7},{6,4},{7,5},{8,10},{9,11},{10,... | collective-permute-start | bytes 73736 | tf_op jit(solution)/shard_map/ppermute | solution.py:129
  67.7 3.6 %collective-permute-start.12 = (f32[2,8,384]{2,1,0:T(8,128)S(1)}, f32[2,8,384]{2,1,0:T(8,128)S(1)}, u32[]{:S(2)}, u32[]{:S(2)}) collective-permute-start(f32[2,8,384]{2,1,0:T(8,128)S(1)} %bitcast.304), channel_id=1, source_target_pairs={{0,1},{1,0},{2,3},{3,2},{4,5},{5,4},{6,7},{7,6},{8,9},{9,8},{10,11... | collective-permute-start | bytes 73736 | tf_op jit(solution)/shard_map/ppermute | solution.py:129
  67.7 3.6 %collective-permute-start.14 = (f32[2,8,384]{2,1,0:T(8,128)S(1)}, f32[2,8,384]{2,1,0:T(8,128)S(1)}, u32[]{:S(2)}, u32[]{:S(2)}) collective-permute-start(f32[2,8,384]{2,1,0:T(8,128)S(1)} %bitcast.305), channel_id=1, source_target_pairs={{0,3},{1,2},{2,1},{3,0},{4,7},{5,6},{6,5},{7,4},{8,11},{9,10},{10,... | collective-permute-start | bytes 73736 | tf_op jit(solution)/shard_map/ppermute | solution.py:129
  72.3 6.2 %collective-permute-start.17 = (f32[1,2,8,384]{3,1,2,0:T(2,128)S(1)}, f32[1,2,8,384]{3,1,2,0:T(2,128)S(1)}, u32[]{:S(2)}, u32[]{:S(2)}) collective-permute-start(f32[1,2,8,384]{3,1,2,0:T(2,128)S(1)} %convolution_bitcast_fusion.4), channel_id=1, source_target_pairs={{0,12},{1,13},{2,14},{3,15},{4,8},{5,9},{6,10},{7,11},{8,4},{9,5},... | collective-permute-start | bytes 73736 | tf_op jit(solution)/shard_map/ppermute | solution.py:142
  74.5 4.7 %collective-permute-start.16 = (f32[1,2,8,384]{3,1,2,0:T(2,128)S(1)}, f32[1,2,8,384]{3,1,2,0:T(2,128)S(1)}, u32[]{:S(2)}, u32[]{:S(2)}) collective-permute-start(f32[1,2,8,384]{3,1,2,0:T(2,128)S(1)} %convolution_bitcast_fusion.5), channel_id=1, source_target_pairs={{0,8},{1,9},{2,10},{3,11},{4,12},{5,13},{6,14},{7,15},{8,0},{9,1},... | collective-permute-start | bytes 73736 | tf_op jit(solution)/shard_map/ppermute | solution.py:142
  74.5 4.7 %collective-permute-start.15 = (f32[1,2,8,384]{3,1,2,0:T(2,128)S(1)}, f32[1,2,8,384]{3,1,2,0:T(2,128)S(1)}, u32[]{:S(2)}, u32[]{:S(2)}) collective-permute-start(f32[1,2,8,384]{3,1,2,0:T(2,128)S(1)} %convolution_bitcast_fusion.6), channel_id=1, source_target_pairs={{0,4},{1,5},{2,6},{3,7},{4,0},{5,1},{6,2},{7,3},{8,12},{9,13},{10,... | collective-permute-start | bytes 73736 | tf_op jit(solution)/shard_map/ppermute | solution.py:142
  76.8 19.6 %collective-permute-start.24 = (f32[4,24,384]{2,1,0:T(8,128)S(1)}, f32[4,24,384]{2,1,0:T(8,128)S(1)}, u32[]{:S(2)}, u32[]{:S(2)}) collective-permute-start(f32[4,24,384]{2,1,0:T(8,128)S(1)} %get-tuple-element.10), channel_id=1, source_target_pairs={{0,1},{1,0},{2,3},{3,2},{4,5},{5,4},{6,7},{7,6},{8,9},{9,8},{10,11... | collective-permute-start | bytes 442376 | tf_op jit(solution)/shard_map/ppermute | solution.py:120
  76.9 19.5 %collective-permute-start.26 = (f32[4,24,384]{2,1,0:T(8,128)S(1)}, f32[4,24,384]{2,1,0:T(8,128)S(1)}, u32[]{:S(2)}, u32[]{:S(2)}) collective-permute-start(f32[4,24,384]{2,1,0:T(8,128)S(1)} %get-tuple-element.11), channel_id=1, source_target_pairs={{0,3},{1,2},{2,1},{3,0},{4,7},{5,6},{6,5},{7,4},{8,11},{9,10},{10,... | collective-permute-start | bytes 442376 | tf_op jit(solution)/shard_map/ppermute | solution.py:120
  80.7 3.5 %collective-permute-start.20 = (bf16[2,8,384]{2,1,0:T(8,128)(2,1)S(1)}, bf16[2,8,384]{2,1,0:T(8,128)(2,1)S(1)}, u32[]{:S(2)}, u32[]{:S(2)}) collective-permute-start(bf16[2,8,384]{2,1,0:T(8,128)(2,1)S(1)} %pad_maximum_fusion.6), channel_id=1, source_target_pairs={{0,3},{1,2},{2,1},{3,0},{4,7},{5,6},{6,5},{7,4},{8,11},{9,10},{10,... | collective-permute-start | bytes 36872 | tf_op jit(solution)/shard_map/ppermute | solution.py:129
  81.1 4.7 %collective-permute-start.19 = (bf16[2,8,384]{2,1,0:T(8,128)(2,1)S(1)}, bf16[2,8,384]{2,1,0:T(8,128)(2,1)S(1)}, u32[]{:S(2)}, u32[]{:S(2)}) collective-permute-start(bf16[2,8,384]{2,1,0:T(8,128)(2,1)S(1)} %pad_maximum_fusion.6), channel_id=1, source_target_pairs={{0,2},{1,3},{2,0},{3,1},{4,6},{5,7},{6,4},{7,5},{8,10},{9,11},{10,... | collective-permute-start | bytes 36872 | tf_op jit(solution)/shard_map/ppermute | solution.py:129
  82.4 3.4 %collective-permute-start.18 = (bf16[2,8,384]{2,1,0:T(8,128)(2,1)S(1)}, bf16[2,8,384]{2,1,0:T(8,128)(2,1)S(1)}, u32[]{:S(2)}, u32[]{:S(2)}) collective-permute-start(bf16[2,8,384]{2,1,0:T(8,128)(2,1)S(1)} %pad_maximum_fusion.6), channel_id=1, source_target_pairs={{0,1},{1,0},{2,3},{3,2},{4,5},{5,4},{6,7},{7,6},{8,9},{9,8},{10,11... | collective-permute-start | bytes 36872 | tf_op jit(solution)/shard_map/ppermute | solution.py:129
  84.2 12.2 %collective-permute-start.25 = (f32[4,24,384]{2,1,0:T(8,128)S(1)}, f32[4,24,384]{2,1,0:T(8,128)S(1)}, u32[]{:S(2)}, u32[]{:S(2)}) collective-permute-start(f32[4,24,384]{2,1,0:T(8,128)S(1)} %get-tuple-element.12), channel_id=1, source_target_pairs={{0,2},{1,3},{2,0},{3,1},{4,6},{5,7},{6,4},{7,5},{8,10},{9,11},{10,... | collective-permute-start | bytes 442376 | tf_op jit(solution)/shard_map/ppermute | solution.py:120
  86.4 5.9 %collective-permute-start.23 = (f32[1,2,8,384]{3,1,2,0:T(2,128)S(1)}, f32[1,2,8,384]{3,1,2,0:T(2,128)S(1)}, u32[]{:S(2)}, u32[]{:S(2)}) collective-permute-start(f32[1,2,8,384]{3,1,2,0:T(2,128)S(1)} %convolution_bitcast_fusion), channel_id=1, source_target_pairs={{0,12},{1,13},{2,14},{3,15},{4,8},{5,9},{6,10},{7,11},{8,4},{9,5},... | collective-permute-start | bytes 73736 | tf_op jit(solution)/shard_map/ppermute | solution.py:142
  88.5 5.1 %collective-permute-start.22 = (f32[1,2,8,384]{3,1,2,0:T(2,128)S(1)}, f32[1,2,8,384]{3,1,2,0:T(2,128)S(1)}, u32[]{:S(2)}, u32[]{:S(2)}) collective-permute-start(f32[1,2,8,384]{3,1,2,0:T(2,128)S(1)} %convolution_bitcast_fusion.1), channel_id=1, source_target_pairs={{0,8},{1,9},{2,10},{3,11},{4,12},{5,13},{6,14},{7,15},{8,0},{9,1},... | collective-permute-start | bytes 73736 | tf_op jit(solution)/shard_map/ppermute | solution.py:142
  92.3 3.8 %collective-permute-start.21 = (f32[1,2,8,384]{3,1,2,0:T(2,128)S(1)}, f32[1,2,8,384]{3,1,2,0:T(2,128)S(1)}, u32[]{:S(2)}, u32[]{:S(2)}) collective-permute-start(f32[1,2,8,384]{3,1,2,0:T(2,128)S(1)} %convolution_bitcast_fusion.2), channel_id=1, source_target_pairs={{0,4},{1,5},{2,6},{3,7},{4,0},{5,1},{6,2},{7,3},{8,12},{9,13},{10,... | collective-permute-start | bytes 73736 | tf_op jit(solution)/shard_map/ppermute | solution.py:142
  96.5 6.0 %collective-permute-start.27 = (f32[1,24,384]{2,1,0:T(8,128)S(1)}, f32[1,24,384]{2,1,0:T(8,128)S(1)}, u32[]{:S(2)}, u32[]{:S(2)}) collective-permute-start(f32[1,24,384]{2,1,0:T(8,128)S(1)} %get-tuple-element.13), channel_id=1, source_target_pairs={{0,4},{1,5},{2,6},{3,7},{4,0},{5,1},{6,2},{7,3},{8,12},{9,13},{10,... | collective-permute-start | bytes 110600 | tf_op jit(solution)/shard_map/ppermute | solution.py:120
  96.6 5.9 %collective-permute-start.29 = (f32[1,24,384]{2,1,0:T(8,128)S(1)}, f32[1,24,384]{2,1,0:T(8,128)S(1)}, u32[]{:S(2)}, u32[]{:S(2)}) collective-permute-start(f32[1,24,384]{2,1,0:T(8,128)S(1)} %get-tuple-element.14), channel_id=1, source_target_pairs={{0,12},{1,13},{2,14},{3,15},{4,8},{5,9},{6,10},{7,11},{8,4},{9,5},... | collective-permute-start | bytes 110600 | tf_op jit(solution)/shard_map/ppermute | solution.py:120
  98.4 4.9 %collective-permute-start.28 = (f32[1,24,384]{2,1,0:T(8,128)S(1)}, f32[1,24,384]{2,1,0:T(8,128)S(1)}, u32[]{:S(2)}, u32[]{:S(2)}) collective-permute-start(f32[1,24,384]{2,1,0:T(8,128)S(1)} %get-tuple-element.15), channel_id=1, source_target_pairs={{0,8},{1,9},{2,10},{3,11},{4,12},{5,13},{6,14},{7,15},{8,0},{9,1},... | collective-permute-start | bytes 110600 | tf_op jit(solution)/shard_map/ppermute | solution.py:120
  (17 other events, 95.9 us)

commit v8 on v5

--- a/solution.py
+++ b/solution.py
@@ -104,12 +104,12 @@
     return cur
 
 
-def xor_reduce_scatter(part, axis_name, groups, me):
+def xor_reduce_scatter(part, axis_name, groups, me, step=2):
     bits = groups.bit_length() - 1
     cur = part
     low = 0
     while low < bits:
-        width = min(2, bits - low)
+        width = min(step, bits - low)
         fan = 1 << width
         view = cur.reshape((cur.shape[0] // fan, fan) + cur.shape[1:])
         mine = (me >> low) & (fan - 1)
@@ -233,7 +233,7 @@
 
     skip_terms = jnp.einsum("jkc,jkd->cd", activations, slope_b, preferred_element_type=jnp.float32)
     skip_blocks = skip_terms.reshape((groups, -1) + skip_terms.shape[1:])
-    grad_skip = xor_reduce_scatter(skip_blocks, "lat", groups, me) * (1.0 / math.sqrt(lat_total * lon_total))
+    grad_skip = xor_reduce_scatter(skip_blocks, "lat", groups, me, 1) * (1.0 / math.sqrt(lat_total * lon_total))
     through_skip = jnp.einsum("jkd,cd->jkc", slope_b, skip_weight, preferred_element_type=jnp.float32)
 
     mode_grads = jnp.einsum("jkc,kf->jfc", slope_b, fourier, preferred_element_type=jnp.float32)

time: 86.3 us -> 84.3 us (0.977)
  starting transfers between devices: 31.3 us -> 27 us
  waiting for transfers between devices: 12.3 us -> 14.5 us
    ppermute x6 -> x4, starting transfers between devices: 6.99 us -> 2.73 us  [xor_reduce_scatter(): lax.ppermute(sent, axis_name, [(i, i ^ mask) for i in range(groups)])]
    ppermute x12, waiting for transfers between devices: 5.01 us -> 8.7 us  [xor_exchange(): lax.ppermute(view[:, k], axis_name, [(i, i ^ mask) for i in range(groups)])]
    ppermute x6 -> x4, waiting for transfers between devices: 5.65 us -> 4.5 us  [xor_reduce_scatter(): lax.ppermute(sent, axis_name, [(i, i ^ mask) for i in range(groups)])]
  transfers between devices with their start and end apart: 30 -> 28, of which waited for: 8 -> 10; matrix products, arithmetic and copies ran while one was open for 26% -> 27% of each run, Pallas kernels for 0% -> 0%
where the time goes in v8:
time: 84.3 us; the launch traced here: 83.8 us
  starting transfers between devices  27 us (32%)
  matrix products  22.2 us (26%)
  local copies, waits for them, and re-layouts  15.4 us (18%)
  waiting for transfers between devices  14.5 us (17%)
  other arithmetic  3.61 us (4%)
  between operations  1.11 us (1%)
    ppermute x12, starting transfers between devices, xor_exchange(): lax.ppermute(view[:, k], axis_name, [(i, i ^ mask) for i in range(groups)])  15.2 us
    ppermute x12, starting transfers between devices, xor_exchange(): lax.ppermute(values, axis_name, [(i, i ^ k) for i in range(groups)])  9.07 us
    ppermute x12, waiting for transfers between devices, xor_exchange(): lax.ppermute(view[:, k], axis_name, [(i, i ^ mask) for i in range(groups)])  8.7 us
    unnamed x35, local copies, waits for them, and re-layouts  8 us
    dot_general x1, matrix products, local(): jnp.einsum('jfc,kf->jkc', grid_modes, fourier, preferred_element_type=jnp...  5.99 us
    dot_general x1, matrix products, local(): jnp.einsum('jkc,cd->jkd', activations, skip_weight, preferred_element_typ...  4.51 us
    ppermute x4, waiting for transfers between devices, xor_reduce_scatter(): lax.ppermute(sent, axis_name, [(i, i ^ mask) for i in range(groups)])  4.5 us
    ppermute x4, starting transfers between devices, xor_reduce_scatter(): lax.ppermute(sent, axis_name, [(i, i ^ mask) for i in range(groups)])  2.73 us
  transfers between devices with their start and end apart: 28, of which 10 were waited for; matrix products, arithmetic and copies ran while one was open for 27% of the time, Pallas kernels for 0%

profile of v8, /device:TPU:0, one launch (start us, length us, event | category | flops | bytes accessed | tf_op | source)
XLA Modules:
  0.0 83.8 jit_solution(3468311639955269138)
XLA Ops:
  0.7 1.6 %copy-done = bf16[2,1440,384]{2,1,0:T(8,128)(2,1)S(1)} copy-done((bf16[2,1440,384]{2,1,0:T(8,128)(2,1)S(1)}, bf16[2,1440,384]{2,1,0:T(8,128)(2,1)}, u32[]{:S(2)}) %copy-start) | copy-done | bytes 2211864
  2.3 1.1 %fusion.100 = f32[8,2,384]{2,0,1:T(8,128)S(1)} fusion(bf16[1440,8,1]{0,1,2:T(8,128)(2,1)} %constant.112, bf16[2,1440,384]{2,1,0:T(8,128)(2,1)S(1)} %copy-done), kind=kOutput, calls=%fused_computation.163 | convolution fusion | flops 17694720 | bytes 2259456 | tf_op jit(solution)/shard_map/jkc,kf->jfc/dot_general | solution.py:224
  3.4 3.0 %collective-permute-start.1 = (f32[2,8,384]{2,1,0:T(8,128)S(1)}, f32[2,8,384]{2,1,0:T(8,128)S(1)}, u32[]{:S(2)}, u32[]{:S(2)}) collective-permute-start(f32[2,8,384]{2,1,0:T(8,128)S(1)} %bitcast.237), channel_id=1, source_target_pairs={{0,2},{1,3},{2,0},{3,1},{4,6},{5,7},{6,4},{7,5},{8,10},{9,11},{10,... | collective-permute-start | bytes 73736 | tf_op jit(solution)/shard_map/ppermute | solution.py:129
  8.6 1.6 %gather_fusion = f32[64,16]{1,0:T(8,128)S(1)} fusion(f32[32,32,16]{2,1,0:T(8,128)} %constant.85, s32[64]{0:T(128)S(1)} %reshape.189), kind=kCustom, calls=%fused_computation.2 | custom fusion | bytes 8704 | tf_op jit(solution)/shard_map/gather | solution.py:211
  14.2 3.1 %collective-permute-start.4 = (f32[1,2,8,384]{3,1,2,0:T(2,128)}, f32[1,2,8,384]{3,1,2,0:T(2,128)S(1)}, u32[]{:S(2)}, u32[]{:S(2)}) collective-permute-start(f32[1,2,8,384]{3,1,2,0:T(2,128)} %bitcast.223), channel_id=1, source_target_pairs={{0,8},{1,9},{2,10},{3,11},{4,12},{5,13},{6,14},{7,15},{8,0},{9,1},... | collective-permute-start | bytes 73736 | tf_op jit(solution)/shard_map/ppermute | solution.py:141
  17.3 1.3 %collective-permute-start.5 = (f32[1,2,8,384]{3,1,2,0:T(2,128)}, f32[1,2,8,384]{3,1,2,0:T(2,128)S(1)}, u32[]{:S(2)}, u32[]{:S(2)}) collective-permute-start(f32[1,2,8,384]{3,1,2,0:T(2,128)} %bitcast.228), channel_id=1, source_target_pairs={{0,12},{1,13},{2,14},{3,15},{4,8},{5,9},{6,10},{7,11},{8,4},{9,5},... | collective-permute-start | bytes 73736 | tf_op jit(solution)/shard_map/ppermute | solution.py:141
  19.1 1.6 %gather_fusion.1 = f32[64,16]{1,0:T(8,128)S(1)} fusion(f32[32,32,16]{2,1,0:T(8,128)} %constant.85, s32[64]{0:T(128)S(1)} %reshape.195), kind=kCustom, calls=%fused_computation.3 | custom fusion | bytes 8704 | tf_op jit(solution)/shard_map/gather | solution.py:214
  20.7 2.5 %collective-permute-done.5 = f32[1,2,8,384]{3,1,2,0:T(2,128)S(1)} collective-permute-done((f32[1,2,8,384]{3,1,2,0:T(2,128)}, f32[1,2,8,384]{3,1,2,0:T(2,128)S(1)}, u32[]{:S(2)}, u32[]{:S(2)}) %collective-permute-start.5) | collective-permute-done | bytes 24608 | tf_op jit(solution)/shard_map/ppermute | solution.py:141
  24.6 1.6 %collective-permute-start.7 = (bf16[2,8,384]{2,1,0:T(8,128)(2,1)}, bf16[2,8,384]{2,1,0:T(8,128)(2,1)S(1)}, u32[]{:S(2)}, u32[]{:S(2)}) collective-permute-start(bf16[2,8,384]{2,1,0:T(8,128)(2,1)} %pad_maximum_fusion.1), channel_id=1, source_target_pairs={{0,2},{1,3},{2,0},{3,1},{4,6},{5,7},{6,4},{7,5},{8,10},{9,11},{10,... | collective-permute-start | bytes 36872 | tf_op jit(solution)/shard_map/ppermute | solution.py:129
  31.4 1.2 %collective-permute-start.10 = (f32[1,2,8,384]{3,1,2,0:T(2,128)}, f32[1,2,8,384]{3,1,2,0:T(2,128)}, u32[]{:S(2)}, u32[]{:S(2)}) collective-permute-start(f32[1,2,8,384]{3,1,2,0:T(2,128)} %bitcast.221), channel_id=1, source_target_pairs={{0,8},{1,9},{2,10},{3,11},{4,12},{5,13},{6,14},{7,15},{8,0},{9,1},... | collective-permute-start | bytes 73736 | tf_op jit(solution)/shard_map/ppermute | solution.py:141
  32.6 0.9 %collective-permute-start.11 = (f32[1,2,8,384]{3,1,2,0:T(2,128)}, f32[1,2,8,384]{3,1,2,0:T(2,128)}, u32[]{:S(2)}, u32[]{:S(2)}) collective-permute-start(f32[1,2,8,384]{3,1,2,0:T(2,128)} %bitcast.227), channel_id=1, source_target_pairs={{0,12},{1,13},{2,14},{3,15},{4,8},{5,9},{6,10},{7,11},{8,4},{9,5},... | collective-permute-start | bytes 73736 | tf_op jit(solution)/shard_map/ppermute | solution.py:141
  33.6 1.3 %collective-permute-start.9 = (f32[1,2,8,384]{3,1,2,0:T(2,128)}, f32[1,2,8,384]{3,1,2,0:T(2,128)}, u32[]{:S(2)}, u32[]{:S(2)}) collective-permute-start(f32[1,2,8,384]{3,1,2,0:T(2,128)} %bitcast.222), channel_id=1, source_target_pairs={{0,4},{1,5},{2,6},{3,7},{4,0},{5,1},{6,2},{7,3},{8,12},{9,13},{10,... | collective-permute-start | bytes 73736 | tf_op jit(solution)/shard_map/ppermute | solution.py:141
  34.9 4.5 %fusion.42 = f32[2,1440,384]{2,1,0:T(8,128)} fusion(bf16[2,1440,384]{2,1,0:T(8,128)(2,1)S(1)} %copy-done, bf16[384,384]{1,0:T(8,128)(2,1)} %param.12), kind=kOutput, calls=%fused_computation.64 | convolution fusion | flops 849346560 | bytes 6930432 | tf_op jit(solution)/shard_map/jkc,cd->jkd/dot_general | solution.py:230
  39.6 0.9 %copy.164 = f32[4,4,2,2,8]{1,0,2,3,4:T(4,128)S(1)} copy(f32[4,4,2,2,8]{4,3,2,1,0:T(2,128)} %get-tuple-element.31) | data formatting | bytes 4096
  41.4 6.0 %fusion.6 = bf16[2,1440,384]{2,1,0:T(8,128)(2,1)S(1)} fusion(bf16[2,1440,384]{2,1,0:T(8,128)(2,1)} %param.11, f32[2,1440,384]{2,1,0:T(8,128)} %fusion.42, bf16[1440,8,1]{0,1,2:T(8,128)(2,1)S(1)} %copy-done.5, bf16[2,8,384]{2,0,1:T(2,128)(2,1)S(1)} %fusion.68), kind=kOutput, calls=%fused_computation.15 | convolution fusion | flops 42024960 | bytes 8882688 | tf_op jit(solution)/shard_map/jfc,kf->jkc/dot_general | solution.py:229
  47.8 1.5 %collective-permute-start.13 = (f32[2,8,384]{2,1,0:T(8,128)S(1)}, f32[2,8,384]{2,1,0:T(8,128)S(1)}, u32[]{:S(2)}, u32[]{:S(2)}) collective-permute-start(f32[2,8,384]{2,1,0:T(8,128)S(1)} %bitcast.241), channel_id=1, source_target_pairs={{0,2},{1,3},{2,0},{3,1},{4,6},{5,7},{6,4},{7,5},{8,10},{9,11},{10,... | collective-permute-start | bytes 73736 | tf_op jit(solution)/shard_map/ppermute | solution.py:129
  49.9 1.5 %fusion.40 = f32[2,1440,384]{2,1,0:T(8,128)S(1)} fusion(bf16[2,1440,384]{2,1,0:T(8,128)(2,1)S(1)} %fusion.6, bf16[384,384]{1,0:T(8,128)(2,1)S(1)} %copy-done.4), kind=kOutput, calls=%fused_computation.62 | convolution fusion | flops 849346560 | bytes 6930432 | tf_op jit(solution)/shard_map/jkd,cd->jkc/dot_general | solution.py:237
  51.5 1.4 %fusion.102 = f32[384,384,1]{0,1,2:T(8,128)S(1)} fusion(bf16[2,1440,384]{2,1,0:T(8,128)(2,1)S(1)} %fusion.6, bf16[2,1440,384]{2,1,0:T(8,128)(2,1)S(1)} %copy-done), kind=kOutput, calls=%fused_computation.165 | convolution fusion | flops 849346560 | bytes 5013504 | tf_op jit(solution)/shard_map/jkc,jkd->cd/dot_general | solution.py:234
  53.5 2.2 %collective-permute-start.16 = (f32[1,2,8,384]{3,1,2,0:T(2,128)S(1)}, f32[1,2,8,384]{3,1,2,0:T(2,128)S(1)}, u32[]{:S(2)}, u32[]{:S(2)}) collective-permute-start(f32[1,2,8,384]{3,1,2,0:T(2,128)S(1)} %bitcast.258), channel_id=1, source_target_pairs={{0,8},{1,9},{2,10},{3,11},{4,12},{5,13},{6,14},{7,15},{8,0},{9,1},... | collective-permute-start | bytes 73736 | tf_op jit(solution)/shard_map/ppermute | solution.py:141
  55.7 0.9 %collective-permute-start.17 = (f32[1,2,8,384]{3,1,2,0:T(2,128)S(1)}, f32[1,2,8,384]{3,1,2,0:T(2,128)S(1)}, u32[]{:S(2)}, u32[]{:S(2)}) collective-permute-start(f32[1,2,8,384]{3,1,2,0:T(2,128)S(1)} %bitcast.257), channel_id=1, source_target_pairs={{0,12},{1,13},{2,14},{3,15},{4,8},{5,9},{6,10},{7,11},{8,4},{9,5},... | collective-permute-start | bytes 73736 | tf_op jit(solution)/shard_map/ppermute | solution.py:141
  57.1 1.6 %collective-permute-done.16 = f32[1,2,8,384]{3,1,2,0:T(2,128)S(1)} collective-permute-done((f32[1,2,8,384]{3,1,2,0:T(2,128)S(1)}, f32[1,2,8,384]{3,1,2,0:T(2,128)S(1)}, u32[]{:S(2)}, u32[]{:S(2)}) %collective-permute-start.16) | collective-permute-done | bytes 24608 | tf_op jit(solution)/shard_map/ppermute | solution.py:141
  58.8 2.5 %collective-permute-done.17 = f32[1,2,8,384]{3,1,2,0:T(2,128)S(1)} collective-permute-done((f32[1,2,8,384]{3,1,2,0:T(2,128)S(1)}, f32[1,2,8,384]{3,1,2,0:T(2,128)S(1)}, u32[]{:S(2)}, u32[]{:S(2)}) %collective-permute-start.17) | collective-permute-done | bytes 24608 | tf_op jit(solution)/shard_map/ppermute | solution.py:141
  62.6 1.6 %collective-permute-start.19 = (bf16[2,8,384]{2,1,0:T(8,128)(2,1)S(1)}, bf16[2,8,384]{2,1,0:T(8,128)(2,1)S(1)}, u32[]{:S(2)}, u32[]{:S(2)}) collective-permute-start(bf16[2,8,384]{2,1,0:T(8,128)(2,1)S(1)} %pad_maximum_fusion.2), channel_id=1, source_target_pairs={{0,2},{1,3},{2,0},{3,1},{4,6},{5,7},{6,4},{7,5},{8,10},{9,11},{10,... | collective-permute-start | bytes 36872 | tf_op jit(solution)/shard_map/ppermute | solution.py:129
  66.1 1.1 %copy.129 = bf16[2,2,384,384]{3,2,1,0:T(8,128)(2,1)} copy(bf16[2,2,384,384]{3,2,0,1:T(8,128)(2,1)S(1)} %pad_maximum_fusion) | data formatting | bytes 2359296
  67.7 1.6 %collective-permute-start.25 = (f32[4,24,384]{2,1,0:T(8,128)S(1)}, f32[4,24,384]{2,1,0:T(8,128)S(1)}, u32[]{:S(2)}, u32[]{:S(2)}) collective-permute-start(f32[4,24,384]{2,1,0:T(8,128)S(1)} %dynamic-slice_bitcast_fusion.1), channel_id=1, source_target_pairs={{0,2},{1,3},{2,0},{3,1},{4,6},{5,7},{6,4},{7,5},{8,10},{9,11},{10,... | collective-permute-start | bytes 442376 | tf_op jit(solution)/shard_map/ppermute | solution.py:120
  70.3 1.3 %collective-permute-start.23 = (f32[1,2,8,384]{3,1,2,0:T(2,128)S(1)}, f32[1,2,8,384]{3,1,2,0:T(2,128)S(1)}, u32[]{:S(2)}, u32[]{:S(2)}) collective-permute-start(f32[1,2,8,384]{3,1,2,0:T(2,128)S(1)} %bitcast.254), channel_id=1, source_target_pairs={{0,12},{1,13},{2,14},{3,15},{4,8},{5,9},{6,10},{7,11},{8,4},{9,5},... | collective-permute-start | bytes 73736 | tf_op jit(solution)/shard_map/ppermute | solution.py:141
  71.6 1.4 %collective-permute-start.21 = (f32[1,2,8,384]{3,1,2,0:T(2,128)S(1)}, f32[1,2,8,384]{3,1,2,0:T(2,128)S(1)}, u32[]{:S(2)}, u32[]{:S(2)}) collective-permute-start(f32[1,2,8,384]{3,1,2,0:T(2,128)S(1)} %bitcast.253), channel_id=1, source_target_pairs={{0,4},{1,5},{2,6},{3,7},{4,0},{5,1},{6,2},{7,3},{8,12},{9,13},{10,... | collective-permute-start | bytes 73736 | tf_op jit(solution)/shard_map/ppermute | solution.py:141
  74.2 1.7 %collective-permute-done.23 = f32[1,2,8,384]{3,1,2,0:T(2,128)S(1)} collective-permute-done((f32[1,2,8,384]{3,1,2,0:T(2,128)S(1)}, f32[1,2,8,384]{3,1,2,0:T(2,128)S(1)}, u32[]{:S(2)}, u32[]{:S(2)}) %collective-permute-start.23) | collective-permute-done | bytes 24608 | tf_op jit(solution)/shard_map/ppermute | solution.py:141
  76.0 2.3 %collective-permute-done.26 = f32[2,24,384]{2,1,0:T(8,128)S(1)} collective-permute-done((f32[2,24,384]{2,1,0:T(8,128)S(1)}, f32[2,24,384]{2,1,0:T(8,128)S(1)}, u32[]{:S(2)}, u32[]{:S(2)}) %collective-permute-start.26) | collective-permute-done | bytes 73760 | tf_op jit(solution)/shard_map/ppermute | solution.py:120
  78.2 1.0 %collective-permute-start.27 = (f32[1,24,384]{2,1,0:T(8,128)S(1)}, f32[1,24,384]{2,1,0:T(8,128)S(1)}, u32[]{:S(2)}, u32[]{:S(2)}) collective-permute-start(f32[1,24,384]{2,1,0:T(8,128)S(1)} %constant_dynamic-slice_fusion), channel_id=1, source_target_pairs={{0,8},{1,9},{2,10},{3,11},{4,12},{5,13},{6,14},{7,15},{8,0},{9,1},... | collective-permute-start | bytes 110600 | tf_op jit(solution)/shard_map/ppermute | solution.py:120
  79.3 2.5 %fusion.11 = bf16[2,1440,384]{2,1,0:T(8,128)(2,1)} fusion(f32[2,1440,384]{2,1,0:T(8,128)S(1)} %fusion.40, bf16[2,1440,384]{2,1,0:T(8,128)(2,1)S(1)} %copy-done.3, bf16[1440,8,1]{0,1,2:T(8,128)(2,1)S(1)} %copy-done.5, bf16[2,8,384]{2,0,1:T(2,128)(2,1)S(1)} %fusion.66), kind=kOutput, calls=%fused_computation.20 | convolution fusion | flops 22118400 | bytes 8882688 | tf_op jit(solution)/shard_map/jfc,kf->jkc/dot_general | solution.py:243
  81.7 1.5 %collective-permute-done.27 = f32[1,24,384]{2,1,0:T(8,128)S(1)} collective-permute-done((f32[1,24,384]{2,1,0:T(8,128)S(1)}, f32[1,24,384]{2,1,0:T(8,128)S(1)}, u32[]{:S(2)}, u32[]{:S(2)}) %collective-permute-start.27) | collective-permute-done | bytes 36896 | tf_op jit(solution)/shard_map/ppermute | solution.py:120
  (128 shorter events, 22.8 us)
Async XLA Ops:
  3.4 7.7 %collective-permute-start.1 = (f32[2,8,384]{2,1,0:T(8,128)S(1)}, f32[2,8,384]{2,1,0:T(8,128)S(1)}, u32[]{:S(2)}, u32[]{:S(2)}) collective-permute-start(f32[2,8,384]{2,1,0:T(8,128)S(1)} %bitcast.237), channel_id=1, source_target_pairs={{0,2},{1,3},{2,0},{3,1},{4,6},{5,7},{6,4},{7,5},{8,10},{9,11},{10,... | collective-permute-start | bytes 73736 | tf_op jit(solution)/shard_map/ppermute | solution.py:129
  6.4 4.8 %collective-permute-start = (f32[2,8,384]{2,1,0:T(8,128)S(1)}, f32[2,8,384]{2,1,0:T(8,128)}, u32[]{:S(2)}, u32[]{:S(2)}) collective-permute-start(f32[2,8,384]{2,1,0:T(8,128)S(1)} %bitcast.238), channel_id=1, source_target_pairs={{0,1},{1,0},{2,3},{3,2},{4,5},{5,4},{6,7},{7,6},{8,9},{9,8},{10,11... | collective-permute-start | bytes 73736 | tf_op jit(solution)/shard_map/ppermute | solution.py:129
  6.4 4.8 %collective-permute-start.2 = (f32[2,8,384]{2,1,0:T(8,128)S(1)}, f32[2,8,384]{2,1,0:T(8,128)}, u32[]{:S(2)}, u32[]{:S(2)}) collective-permute-start(f32[2,8,384]{2,1,0:T(8,128)S(1)} %bitcast.239), channel_id=1, source_target_pairs={{0,3},{1,2},{2,1},{3,0},{4,7},{5,6},{6,5},{7,4},{8,11},{9,10},{10,... | collective-permute-start | bytes 73736 | tf_op jit(solution)/shard_map/ppermute | solution.py:129
  7.4 15.8 %copy-start.2 = (bf16[2,2,384,384]{3,2,1,0:T(8,128)(2,1)S(1)}, bf16[2,2,384,384]{3,2,1,0:T(8,128)(2,1)}, u32[]{:S(2)}) copy-start(bf16[2,2,384,384]{3,2,1,0:T(8,128)(2,1)} %param.13) | copy-start | bytes 3538948
  14.2 6.4 %collective-permute-start.4 = (f32[1,2,8,384]{3,1,2,0:T(2,128)}, f32[1,2,8,384]{3,1,2,0:T(2,128)S(1)}, u32[]{:S(2)}, u32[]{:S(2)}) collective-permute-start(f32[1,2,8,384]{3,1,2,0:T(2,128)} %bitcast.223), channel_id=1, source_target_pairs={{0,8},{1,9},{2,10},{3,11},{4,12},{5,13},{6,14},{7,15},{8,0},{9,1},... | collective-permute-start | bytes 73736 | tf_op jit(solution)/shard_map/ppermute | solution.py:141
  17.3 5.8 %collective-permute-start.5 = (f32[1,2,8,384]{3,1,2,0:T(2,128)}, f32[1,2,8,384]{3,1,2,0:T(2,128)S(1)}, u32[]{:S(2)}, u32[]{:S(2)}) collective-permute-start(f32[1,2,8,384]{3,1,2,0:T(2,128)} %bitcast.228), channel_id=1, source_target_pairs={{0,12},{1,13},{2,14},{3,15},{4,8},{5,9},{6,10},{7,11},{8,4},{9,5},... | collective-permute-start | bytes 73736 | tf_op jit(solution)/shard_map/ppermute | solution.py:141
  18.6 4.5 %collective-permute-start.3 = (f32[1,2,8,384]{3,1,2,0:T(2,128)}, f32[1,2,8,384]{3,1,2,0:T(2,128)S(1)}, u32[]{:S(2)}, u32[]{:S(2)}) collective-permute-start(f32[1,2,8,384]{3,1,2,0:T(2,128)} %bitcast.224), channel_id=1, source_target_pairs={{0,4},{1,5},{2,6},{3,7},{4,0},{5,1},{6,2},{7,3},{8,12},{9,13},{10,... | collective-permute-start | bytes 73736 | tf_op jit(solution)/shard_map/ppermute | solution.py:141
  24.6 3.4 %collective-permute-start.8 = (bf16[2,8,384]{2,1,0:T(8,128)(2,1)}, bf16[2,8,384]{2,1,0:T(8,128)(2,1)S(1)}, u32[]{:S(2)}, u32[]{:S(2)}) collective-permute-start(bf16[2,8,384]{2,1,0:T(8,128)(2,1)} %pad_maximum_fusion.1), channel_id=1, source_target_pairs={{0,3},{1,2},{2,1},{3,0},{4,7},{5,6},{6,5},{7,4},{8,11},{9,10},{10,... | collective-permute-start | bytes 36872 | tf_op jit(solution)/shard_map/ppermute | solution.py:129
  24.6 3.9 %collective-permute-start.7 = (bf16[2,8,384]{2,1,0:T(8,128)(2,1)}, bf16[2,8,384]{2,1,0:T(8,128)(2,1)S(1)}, u32[]{:S(2)}, u32[]{:S(2)}) collective-permute-start(bf16[2,8,384]{2,1,0:T(8,128)(2,1)} %pad_maximum_fusion.1), channel_id=1, source_target_pairs={{0,2},{1,3},{2,0},{3,1},{4,6},{5,7},{6,4},{7,5},{8,10},{9,11},{10,... | collective-permute-start | bytes 36872 | tf_op jit(solution)/shard_map/ppermute | solution.py:129
  26.2 2.4 %collective-permute-start.6 = (bf16[2,8,384]{2,1,0:T(8,128)(2,1)}, bf16[2,8,384]{2,1,0:T(8,128)(2,1)S(1)}, u32[]{:S(2)}, u32[]{:S(2)}) collective-permute-start(bf16[2,8,384]{2,1,0:T(8,128)(2,1)} %pad_maximum_fusion.1), channel_id=1, source_target_pairs={{0,1},{1,0},{2,3},{3,2},{4,5},{5,4},{6,7},{7,6},{8,9},{9,8},{10,11... | collective-permute-start | bytes 36872 | tf_op jit(solution)/shard_map/ppermute | solution.py:129
  31.4 9.1 %collective-permute-start.10 = (f32[1,2,8,384]{3,1,2,0:T(2,128)}, f32[1,2,8,384]{3,1,2,0:T(2,128)}, u32[]{:S(2)}, u32[]{:S(2)}) collective-permute-start(f32[1,2,8,384]{3,1,2,0:T(2,128)} %bitcast.221), channel_id=1, source_target_pairs={{0,8},{1,9},{2,10},{3,11},{4,12},{5,13},{6,14},{7,15},{8,0},{9,1},... | collective-permute-start | bytes 73736 | tf_op jit(solution)/shard_map/ppermute | solution.py:141
  32.6 7.9 %collective-permute-start.11 = (f32[1,2,8,384]{3,1,2,0:T(2,128)}, f32[1,2,8,384]{3,1,2,0:T(2,128)}, u32[]{:S(2)}, u32[]{:S(2)}) collective-permute-start(f32[1,2,8,384]{3,1,2,0:T(2,128)} %bitcast.227), channel_id=1, source_target_pairs={{0,12},{1,13},{2,14},{3,15},{4,8},{5,9},{6,10},{7,11},{8,4},{9,5},... | collective-permute-start | bytes 73736 | tf_op jit(solution)/shard_map/ppermute | solution.py:141
  33.6 7.8 %copy-start.5 = (bf16[1440,8,1]{0,1,2:T(8,128)(2,1)S(1)}, bf16[1440,8,1]{0,1,2:T(8,128)(2,1)}, u32[]{:S(2)}) copy-start(bf16[1440,8,1]{0,1,2:T(8,128)(2,1)} %constant.112) | copy-start | bytes 69124
  33.6 7.0 %collective-permute-start.9 = (f32[1,2,8,384]{3,1,2,0:T(2,128)}, f32[1,2,8,384]{3,1,2,0:T(2,128)}, u32[]{:S(2)}, u32[]{:S(2)}) collective-permute-start(f32[1,2,8,384]{3,1,2,0:T(2,128)} %bitcast.222), channel_id=1, source_target_pairs={{0,4},{1,5},{2,6},{3,7},{4,0},{5,1},{6,2},{7,3},{8,12},{9,13},{10,... | collective-permute-start | bytes 73736 | tf_op jit(solution)/shard_map/ppermute | solution.py:141
  47.8 5.1 %collective-permute-start.13 = (f32[2,8,384]{2,1,0:T(8,128)S(1)}, f32[2,8,384]{2,1,0:T(8,128)S(1)}, u32[]{:S(2)}, u32[]{:S(2)}) collective-permute-start(f32[2,8,384]{2,1,0:T(8,128)S(1)} %bitcast.241), channel_id=1, source_target_pairs={{0,2},{1,3},{2,0},{3,1},{4,6},{5,7},{6,4},{7,5},{8,10},{9,11},{10,... | collective-permute-start | bytes 73736 | tf_op jit(solution)/shard_map/ppermute | solution.py:129
  49.3 3.6 %collective-permute-start.12 = (f32[2,8,384]{2,1,0:T(8,128)S(1)}, f32[2,8,384]{2,1,0:T(8,128)S(1)}, u32[]{:S(2)}, u32[]{:S(2)}) collective-permute-start(f32[2,8,384]{2,1,0:T(8,128)S(1)} %bitcast.242), channel_id=1, source_target_pairs={{0,1},{1,0},{2,3},{3,2},{4,5},{5,4},{6,7},{7,6},{8,9},{9,8},{10,11... | collective-permute-start | bytes 73736 | tf_op jit(solution)/shard_map/ppermute | solution.py:129
  49.3 3.6 %collective-permute-start.14 = (f32[2,8,384]{2,1,0:T(8,128)S(1)}, f32[2,8,384]{2,1,0:T(8,128)S(1)}, u32[]{:S(2)}, u32[]{:S(2)}) collective-permute-start(f32[2,8,384]{2,1,0:T(8,128)S(1)} %bitcast.243), channel_id=1, source_target_pairs={{0,3},{1,2},{2,1},{3,0},{4,7},{5,6},{6,5},{7,4},{8,11},{9,10},{10,... | collective-permute-start | bytes 73736 | tf_op jit(solution)/shard_map/ppermute | solution.py:129
  52.9 11.6 %copy-start.7 = (bf16[2,4,384]{2,0,1:T(2,128)(2,1)S(1)}, bf16[2,4,384]{2,0,1:T(2,128)(2,1)}, u32[]{:S(2)}) copy-start(bf16[2,4,384]{2,0,1:T(2,128)(2,1)} %copy-done.6) | copy-start | bytes 18436
  53.5 5.3 %collective-permute-start.16 = (f32[1,2,8,384]{3,1,2,0:T(2,128)S(1)}, f32[1,2,8,384]{3,1,2,0:T(2,128)S(1)}, u32[]{:S(2)}, u32[]{:S(2)}) collective-permute-start(f32[1,2,8,384]{3,1,2,0:T(2,128)S(1)} %bitcast.258), channel_id=1, source_target_pairs={{0,8},{1,9},{2,10},{3,11},{4,12},{5,13},{6,14},{7,15},{8,0},{9,1},... | collective-permute-start | bytes 73736 | tf_op jit(solution)/shard_map/ppermute | solution.py:141
  55.7 5.6 %collective-permute-start.17 = (f32[1,2,8,384]{3,1,2,0:T(2,128)S(1)}, f32[1,2,8,384]{3,1,2,0:T(2,128)S(1)}, u32[]{:S(2)}, u32[]{:S(2)}) collective-permute-start(f32[1,2,8,384]{3,1,2,0:T(2,128)S(1)} %bitcast.257), channel_id=1, source_target_pairs={{0,12},{1,13},{2,14},{3,15},{4,8},{5,9},{6,10},{7,11},{8,4},{9,5},... | collective-permute-start | bytes 73736 | tf_op jit(solution)/shard_map/ppermute | solution.py:141
  56.6 4.7 %collective-permute-start.15 = (f32[1,2,8,384]{3,1,2,0:T(2,128)S(1)}, f32[1,2,8,384]{3,1,2,0:T(2,128)S(1)}, u32[]{:S(2)}, u32[]{:S(2)}) collective-permute-start(f32[1,2,8,384]{3,1,2,0:T(2,128)S(1)} %bitcast.255), channel_id=1, source_target_pairs={{0,4},{1,5},{2,6},{3,7},{4,0},{5,1},{6,2},{7,3},{8,12},{9,13},{10,... | collective-permute-start | bytes 73736 | tf_op jit(solution)/shard_map/ppermute | solution.py:141
  57.1 10.5 %collective-permute-start.24 = (f32[8,24,384]{2,1,0:T(8,128)S(1)}, f32[8,24,384]{2,1,0:T(8,128)S(1)}, u32[]{:S(2)}, u32[]{:S(2)}) collective-permute-start(f32[8,24,384]{2,1,0:T(8,128)S(1)} %dynamic-slice_bitcast_fusion), channel_id=1, source_target_pairs={{0,1},{1,0},{2,3},{3,2},{4,5},{5,4},{6,7},{7,6},{8,9},{9,8},{10,11... | collective-permute-start | bytes 884744 | tf_op jit(solution)/shard_map/ppermute | solution.py:120
  62.5 4.7 %collective-permute-start.20 = (bf16[2,8,384]{2,1,0:T(8,128)(2,1)S(1)}, bf16[2,8,384]{2,1,0:T(8,128)(2,1)S(1)}, u32[]{:S(2)}, u32[]{:S(2)}) collective-permute-start(bf16[2,8,384]{2,1,0:T(8,128)(2,1)S(1)} %pad_maximum_fusion.2), channel_id=1, source_target_pairs={{0,3},{1,2},{2,1},{3,0},{4,7},{5,6},{6,5},{7,4},{8,11},{9,10},{10,... | collective-permute-start | bytes 36872 | tf_op jit(solution)/shard_map/ppermute | solution.py:129
  62.6 4.7 %collective-permute-start.19 = (bf16[2,8,384]{2,1,0:T(8,128)(2,1)S(1)}, bf16[2,8,384]{2,1,0:T(8,128)(2,1)S(1)}, u32[]{:S(2)}, u32[]{:S(2)}) collective-permute-start(bf16[2,8,384]{2,1,0:T(8,128)(2,1)S(1)} %pad_maximum_fusion.2), channel_id=1, source_target_pairs={{0,2},{1,3},{2,0},{3,1},{4,6},{5,7},{6,4},{7,5},{8,10},{9,11},{10,... | collective-permute-start | bytes 36872 | tf_op jit(solution)/shard_map/ppermute | solution.py:129
  64.2 3.1 %collective-permute-start.18 = (bf16[2,8,384]{2,1,0:T(8,128)(2,1)S(1)}, bf16[2,8,384]{2,1,0:T(8,128)(2,1)S(1)}, u32[]{:S(2)}, u32[]{:S(2)}) collective-permute-start(bf16[2,8,384]{2,1,0:T(8,128)(2,1)S(1)} %pad_maximum_fusion.2), channel_id=1, source_target_pairs={{0,1},{1,0},{2,3},{3,2},{4,5},{5,4},{6,7},{7,6},{8,9},{9,8},{10,11... | collective-permute-start | bytes 36872 | tf_op jit(solution)/shard_map/ppermute | solution.py:129
  66.1 13.1 %copy-start.3 = (bf16[2,1440,384]{2,1,0:T(8,128)(2,1)S(1)}, bf16[2,1440,384]{2,1,0:T(8,128)(2,1)}, u32[]{:S(2)}) copy-start(bf16[2,1440,384]{2,1,0:T(8,128)(2,1)} %param.11) | copy-start | bytes 6635524
  67.7 6.1 %collective-permute-start.25 = (f32[4,24,384]{2,1,0:T(8,128)S(1)}, f32[4,24,384]{2,1,0:T(8,128)S(1)}, u32[]{:S(2)}, u32[]{:S(2)}) collective-permute-start(f32[4,24,384]{2,1,0:T(8,128)S(1)} %dynamic-slice_bitcast_fusion.1), channel_id=1, source_target_pairs={{0,2},{1,3},{2,0},{3,1},{4,6},{5,7},{6,4},{7,5},{8,10},{9,11},{10,... | collective-permute-start | bytes 442376 | tf_op jit(solution)/shard_map/ppermute | solution.py:120
  69.4 4.8 %collective-permute-start.22 = (f32[1,2,8,384]{3,1,2,0:T(2,128)S(1)}, f32[1,2,8,384]{3,1,2,0:T(2,128)S(1)}, u32[]{:S(2)}, u32[]{:S(2)}) collective-permute-start(f32[1,2,8,384]{3,1,2,0:T(2,128)S(1)} %bitcast.256), channel_id=1, source_target_pairs={{0,8},{1,9},{2,10},{3,11},{4,12},{5,13},{6,14},{7,15},{8,0},{9,1},... | collective-permute-start | bytes 73736 | tf_op jit(solution)/shard_map/ppermute | solution.py:141
  70.3 5.6 %collective-permute-start.23 = (f32[1,2,8,384]{3,1,2,0:T(2,128)S(1)}, f32[1,2,8,384]{3,1,2,0:T(2,128)S(1)}, u32[]{:S(2)}, u32[]{:S(2)}) collective-permute-start(f32[1,2,8,384]{3,1,2,0:T(2,128)S(1)} %bitcast.254), channel_id=1, source_target_pairs={{0,12},{1,13},{2,14},{3,15},{4,8},{5,9},{6,10},{7,11},{8,4},{9,5},... | collective-permute-start | bytes 73736 | tf_op jit(solution)/shard_map/ppermute | solution.py:141
  71.6 4.4 %collective-permute-start.21 = (f32[1,2,8,384]{3,1,2,0:T(2,128)S(1)}, f32[1,2,8,384]{3,1,2,0:T(2,128)S(1)}, u32[]{:S(2)}, u32[]{:S(2)}) collective-permute-start(f32[1,2,8,384]{3,1,2,0:T(2,128)S(1)} %bitcast.253), channel_id=1, source_target_pairs={{0,4},{1,5},{2,6},{3,7},{4,0},{5,1},{6,2},{7,3},{8,12},{9,13},{10,... | collective-permute-start | bytes 73736 | tf_op jit(solution)/shard_map/ppermute | solution.py:141
  73.8 4.4 %collective-permute-start.26 = (f32[2,24,384]{2,1,0:T(8,128)S(1)}, f32[2,24,384]{2,1,0:T(8,128)S(1)}, u32[]{:S(2)}, u32[]{:S(2)}) collective-permute-start(f32[2,24,384]{2,1,0:T(8,128)S(1)} %dynamic-slice_bitcast_fusion.2), channel_id=1, source_target_pairs={{0,4},{1,5},{2,6},{3,7},{4,0},{5,1},{6,2},{7,3},{8,12},{9,13},{10,... | collective-permute-start | bytes 221192 | tf_op jit(solution)/shard_map/ppermute | solution.py:120
  78.2 4.9 %collective-permute-start.27 = (f32[1,24,384]{2,1,0:T(8,128)S(1)}, f32[1,24,384]{2,1,0:T(8,128)S(1)}, u32[]{:S(2)}, u32[]{:S(2)}) collective-permute-start(f32[1,24,384]{2,1,0:T(8,128)S(1)} %constant_dynamic-slice_fusion), channel_id=1, source_target_pairs={{0,8},{1,9},{2,10},{3,11},{4,12},{5,13},{6,14},{7,15},{8,0},{9,1},... | collective-permute-start | bytes 110600 | tf_op jit(solution)/shard_map/ppermute | solution.py:120
  (5 other events, 20.1 us)

commit v9 on v8

--- a/solution.py
+++ b/solution.py
@@ -104,7 +104,7 @@
     return cur
 
 
-def xor_reduce_scatter(part, axis_name, groups, me, step=2):
+def xor_reduce_scatter(part, axis_name, groups, me, step=2, narrow=0):
     bits = groups.bit_length() - 1
     cur = part
     low = 0
@@ -117,7 +117,10 @@
         for k in range(1, fan):
             mask = k << low
             sent = lax.dynamic_index_in_dim(view, jnp.bitwise_xor(mine, k), axis=1, keepdims=False)
-            total = total + lax.ppermute(sent, axis_name, [(i, i ^ mask) for i in range(groups)])
+            if low < narrow:
+                sent = sent.astype(jnp.bfloat16)
+            moved = lax.ppermute(sent, axis_name, [(i, i ^ mask) for i in range(groups)])
+            total = total + moved.astype(jnp.float32)
         cur = total
         low += width
     return cur[0]
@@ -233,7 +236,7 @@
 
     skip_terms = jnp.einsum("jkc,jkd->cd", activations, slope_b, preferred_element_type=jnp.float32)
     skip_blocks = skip_terms.reshape((groups, -1) + skip_terms.shape[1:])
-    grad_skip = xor_reduce_scatter(skip_blocks, "lat", groups, me, 1) * (1.0 / math.sqrt(lat_total * lon_total))
+    grad_skip = xor_reduce_scatter(skip_blocks, "lat", groups, me, 1, 2) * (1.0 / math.sqrt(lat_total * lon_total))
     through_skip = jnp.einsum("jkd,cd->jkc", slope_b, skip_weight, preferred_element_type=jnp.float32)
 
     mode_grads = jnp.einsum("jkc,kf->jfc", slope_b, fourier, preferred_element_type=jnp.float32)

time: 84.3 us -> 83.9 us (level)
  waiting for transfers between devices: 14.5 us -> 12.7 us
  starting transfers between devices: 27 us -> 28.5 us
    ppermute x4, waiting for transfers between devices: 4.5 us -> 2.34 us  [xor_reduce_scatter(): lax.ppermute(sent, axis_name, [(i, i ^ mask) for i in range(groups)])]
    ppermute x4, starting transfers between devices: 2.73 us -> 4.17 us  [xor_reduce_scatter(): lax.ppermute(sent, axis_name, [(i, i ^ mask) for i in range(groups)])]
  transfers between devices with their start and end apart: 28 -> 28, of which waited for: 10 -> 9; matrix products, arithmetic and copies ran while one was open for 27% -> 27% of each run, Pallas kernels for 0% -> 0%
where the time goes in v9:
time: 83.9 us; the launch traced here: 83.4 us
  starting transfers between devices  28.5 us (34%)
  matrix products  22.2 us (26%)
  local copies, waits for them, and re-layouts  15.4 us (18%)
  waiting for transfers between devices  12.7 us (15%)
  other arithmetic  3.61 us (4%)
  between operations  1.11 us (1%)
    ppermute x12, starting transfers between devices, xor_exchange(): lax.ppermute(view[:, k], axis_name, [(i, i ^ mask) for i in range(groups)])  15.2 us
    ppermute x12, starting transfers between devices, xor_exchange(): lax.ppermute(values, axis_name, [(i, i ^ k) for i in range(groups)])  9.07 us
    ppermute x12, waiting for transfers between devices, xor_exchange(): lax.ppermute(view[:, k], axis_name, [(i, i ^ mask) for i in range(groups)])  9.05 us
    unnamed x35, local copies, waits for them, and re-layouts  8 us
    dot_general x1, matrix products, local(): jnp.einsum('jfc,kf->jkc', grid_modes, fourier, preferred_element_type=jnp...  5.99 us
    dot_general x1, matrix products, local(): jnp.einsum('jkc,cd->jkd', activations, skip_weight, preferred_element_typ...  4.51 us
    ppermute x4, starting transfers between devices, xor_reduce_scatter(): lax.ppermute(sent, axis_name, [(i, i ^ mask) for i in range(groups)])  4.17 us
    dot_general x1, matrix products, local(): jnp.einsum('jfc,kf->jkc', row_grads, fourier, preferred_element_type=jnp....  2.45 us
  transfers between devices with their start and end apart: 28, of which 9 were waited for; matrix products, arithmetic and copies ran while one was open for 27% of the time, Pallas kernels for 0%

profile of v9, /device:TPU:0, one launch (start us, length us, event | category | flops | bytes accessed | tf_op | source)
XLA Modules:
  0.0 83.4 jit_solution(15894426540063070474)
XLA Ops:
  0.7 1.6 %copy-done = bf16[2,1440,384]{2,1,0:T(8,128)(2,1)S(1)} copy-done((bf16[2,1440,384]{2,1,0:T(8,128)(2,1)S(1)}, bf16[2,1440,384]{2,1,0:T(8,128)(2,1)}, u32[]{:S(2)}) %copy-start) | copy-done | bytes 2211864
  2.3 1.1 %fusion.102 = f32[8,2,384]{2,0,1:T(8,128)S(1)} fusion(bf16[1440,8,1]{0,1,2:T(8,128)(2,1)} %constant.112, bf16[2,1440,384]{2,1,0:T(8,128)(2,1)S(1)} %copy-done), kind=kOutput, calls=%fused_computation.165 | convolution fusion | flops 17694720 | bytes 2259456 | tf_op jit(solution)/shard_map/jkc,kf->jfc/dot_general | solution.py:227
  3.4 3.0 %collective-permute-start.1 = (f32[2,8,384]{2,1,0:T(8,128)S(1)}, f32[2,8,384]{2,1,0:T(8,128)S(1)}, u32[]{:S(2)}, u32[]{:S(2)}) collective-permute-start(f32[2,8,384]{2,1,0:T(8,128)S(1)} %bitcast.241), channel_id=1, source_target_pairs={{0,2},{1,3},{2,0},{3,1},{4,6},{5,7},{6,4},{7,5},{8,10},{9,11},{10,... | collective-permute-start | bytes 73736 | tf_op jit(solution)/shard_map/ppermute | solution.py:132
  8.6 1.6 %gather_fusion = f32[64,16]{1,0:T(8,128)S(1)} fusion(f32[32,32,16]{2,1,0:T(8,128)} %constant.85, s32[64]{0:T(128)S(1)} %reshape.191), kind=kCustom, calls=%fused_computation.2 | custom fusion | bytes 8704 | tf_op jit(solution)/shard_map/gather | solution.py:214
  14.2 3.1 %collective-permute-start.4 = (f32[1,2,8,384]{3,1,2,0:T(2,128)}, f32[1,2,8,384]{3,1,2,0:T(2,128)S(1)}, u32[]{:S(2)}, u32[]{:S(2)}) collective-permute-start(f32[1,2,8,384]{3,1,2,0:T(2,128)} %bitcast.227), channel_id=1, source_target_pairs={{0,8},{1,9},{2,10},{3,11},{4,12},{5,13},{6,14},{7,15},{8,0},{9,1},... | collective-permute-start | bytes 73736 | tf_op jit(solution)/shard_map/ppermute | solution.py:144
  17.3 1.3 %collective-permute-start.5 = (f32[1,2,8,384]{3,1,2,0:T(2,128)}, f32[1,2,8,384]{3,1,2,0:T(2,128)S(1)}, u32[]{:S(2)}, u32[]{:S(2)}) collective-permute-start(f32[1,2,8,384]{3,1,2,0:T(2,128)} %bitcast.232), channel_id=1, source_target_pairs={{0,12},{1,13},{2,14},{3,15},{4,8},{5,9},{6,10},{7,11},{8,4},{9,5},... | collective-permute-start | bytes 73736 | tf_op jit(solution)/shard_map/ppermute | solution.py:144
  19.1 1.6 %gather_fusion.1 = f32[64,16]{1,0:T(8,128)S(1)} fusion(f32[32,32,16]{2,1,0:T(8,128)} %constant.85, s32[64]{0:T(128)S(1)} %reshape.197), kind=kCustom, calls=%fused_computation.3 | custom fusion | bytes 8704 | tf_op jit(solution)/shard_map/gather | solution.py:217
  20.7 2.5 %collective-permute-done.5 = f32[1,2,8,384]{3,1,2,0:T(2,128)S(1)} collective-permute-done((f32[1,2,8,384]{3,1,2,0:T(2,128)}, f32[1,2,8,384]{3,1,2,0:T(2,128)S(1)}, u32[]{:S(2)}, u32[]{:S(2)}) %collective-permute-start.5) | collective-permute-done | bytes 24608 | tf_op jit(solution)/shard_map/ppermute | solution.py:144
  24.6 1.6 %collective-permute-start.7 = (bf16[2,8,384]{2,1,0:T(8,128)(2,1)}, bf16[2,8,384]{2,1,0:T(8,128)(2,1)S(1)}, u32[]{:S(2)}, u32[]{:S(2)}) collective-permute-start(bf16[2,8,384]{2,1,0:T(8,128)(2,1)} %pad_maximum_fusion.1), channel_id=1, source_target_pairs={{0,2},{1,3},{2,0},{3,1},{4,6},{5,7},{6,4},{7,5},{8,10},{9,11},{10,... | collective-permute-start | bytes 36872 | tf_op jit(solution)/shard_map/ppermute | solution.py:132
  31.4 1.2 %collective-permute-start.10 = (f32[1,2,8,384]{3,1,2,0:T(2,128)}, f32[1,2,8,384]{3,1,2,0:T(2,128)}, u32[]{:S(2)}, u32[]{:S(2)}) collective-permute-start(f32[1,2,8,384]{3,1,2,0:T(2,128)} %bitcast.225), channel_id=1, source_target_pairs={{0,8},{1,9},{2,10},{3,11},{4,12},{5,13},{6,14},{7,15},{8,0},{9,1},... | collective-permute-start | bytes 73736 | tf_op jit(solution)/shard_map/ppermute | solution.py:144
  32.6 0.9 %collective-permute-start.11 = (f32[1,2,8,384]{3,1,2,0:T(2,128)}, f32[1,2,8,384]{3,1,2,0:T(2,128)}, u32[]{:S(2)}, u32[]{:S(2)}) collective-permute-start(f32[1,2,8,384]{3,1,2,0:T(2,128)} %bitcast.231), channel_id=1, source_target_pairs={{0,12},{1,13},{2,14},{3,15},{4,8},{5,9},{6,10},{7,11},{8,4},{9,5},... | collective-permute-start | bytes 73736 | tf_op jit(solution)/shard_map/ppermute | solution.py:144
  33.6 1.3 %collective-permute-start.9 = (f32[1,2,8,384]{3,1,2,0:T(2,128)}, f32[1,2,8,384]{3,1,2,0:T(2,128)}, u32[]{:S(2)}, u32[]{:S(2)}) collective-permute-start(f32[1,2,8,384]{3,1,2,0:T(2,128)} %bitcast.226), channel_id=1, source_target_pairs={{0,4},{1,5},{2,6},{3,7},{4,0},{5,1},{6,2},{7,3},{8,12},{9,13},{10,... | collective-permute-start | bytes 73736 | tf_op jit(solution)/shard_map/ppermute | solution.py:144
  34.9 4.5 %fusion.42 = f32[2,1440,384]{2,1,0:T(8,128)} fusion(bf16[2,1440,384]{2,1,0:T(8,128)(2,1)S(1)} %copy-done, bf16[384,384]{1,0:T(8,128)(2,1)} %param.12), kind=kOutput, calls=%fused_computation.65 | convolution fusion | flops 849346560 | bytes 6930432 | tf_op jit(solution)/shard_map/jkc,cd->jkd/dot_general | solution.py:233
  39.6 0.9 %copy.165 = f32[4,4,2,2,8]{1,0,2,3,4:T(4,128)S(1)} copy(f32[4,4,2,2,8]{4,3,2,1,0:T(2,128)} %get-tuple-element.31) | data formatting | bytes 4096
  41.4 6.0 %fusion.6 = bf16[2,1440,384]{2,1,0:T(8,128)(2,1)S(1)} fusion(bf16[2,1440,384]{2,1,0:T(8,128)(2,1)} %param.11, f32[2,1440,384]{2,1,0:T(8,128)} %fusion.42, bf16[1440,8,1]{0,1,2:T(8,128)(2,1)S(1)} %copy-done.5, bf16[2,8,384]{2,0,1:T(2,128)(2,1)S(1)} %fusion.70), kind=kOutput, calls=%fused_computation.15 | convolution fusion | flops 42024960 | bytes 8882688 | tf_op jit(solution)/shard_map/jfc,kf->jkc/dot_general | solution.py:232
  47.8 1.5 %collective-permute-start.13 = (f32[2,8,384]{2,1,0:T(8,128)S(1)}, f32[2,8,384]{2,1,0:T(8,128)S(1)}, u32[]{:S(2)}, u32[]{:S(2)}) collective-permute-start(f32[2,8,384]{2,1,0:T(8,128)S(1)} %bitcast.245), channel_id=1, source_target_pairs={{0,2},{1,3},{2,0},{3,1},{4,6},{5,7},{6,4},{7,5},{8,10},{9,11},{10,... | collective-permute-start | bytes 73736 | tf_op jit(solution)/shard_map/ppermute | solution.py:132
  49.9 1.5 %fusion.40 = f32[2,1440,384]{2,1,0:T(8,128)S(1)} fusion(bf16[2,1440,384]{2,1,0:T(8,128)(2,1)S(1)} %fusion.6, bf16[384,384]{1,0:T(8,128)(2,1)S(1)} %copy-done.4), kind=kOutput, calls=%fused_computation.63 | convolution fusion | flops 849346560 | bytes 6930432 | tf_op jit(solution)/shard_map/jkd,cd->jkc/dot_general | solution.py:240
  51.5 1.4 %fusion.104 = f32[384,384,1]{0,1,2:T(8,128)S(1)} fusion(bf16[2,1440,384]{2,1,0:T(8,128)(2,1)S(1)} %fusion.6, bf16[2,1440,384]{2,1,0:T(8,128)(2,1)S(1)} %copy-done), kind=kOutput, calls=%fused_computation.167 | convolution fusion | flops 849346560 | bytes 5013504 | tf_op jit(solution)/shard_map/jkc,jkd->cd/dot_general | solution.py:237
  53.5 2.2 %collective-permute-start.16 = (f32[1,2,8,384]{3,1,2,0:T(2,128)S(1)}, f32[1,2,8,384]{3,1,2,0:T(2,128)S(1)}, u32[]{:S(2)}, u32[]{:S(2)}) collective-permute-start(f32[1,2,8,384]{3,1,2,0:T(2,128)S(1)} %bitcast.262), channel_id=1, source_target_pairs={{0,8},{1,9},{2,10},{3,11},{4,12},{5,13},{6,14},{7,15},{8,0},{9,1},... | collective-permute-start | bytes 73736 | tf_op jit(solution)/shard_map/ppermute | solution.py:144
  55.7 0.9 %collective-permute-start.17 = (f32[1,2,8,384]{3,1,2,0:T(2,128)S(1)}, f32[1,2,8,384]{3,1,2,0:T(2,128)S(1)}, u32[]{:S(2)}, u32[]{:S(2)}) collective-permute-start(f32[1,2,8,384]{3,1,2,0:T(2,128)S(1)} %bitcast.261), channel_id=1, source_target_pairs={{0,12},{1,13},{2,14},{3,15},{4,8},{5,9},{6,10},{7,11},{8,4},{9,5},... | collective-permute-start | bytes 73736 | tf_op jit(solution)/shard_map/ppermute | solution.py:144
  57.1 1.7 %collective-permute-done.16 = f32[1,2,8,384]{3,1,2,0:T(2,128)S(1)} collective-permute-done((f32[1,2,8,384]{3,1,2,0:T(2,128)S(1)}, f32[1,2,8,384]{3,1,2,0:T(2,128)S(1)}, u32[]{:S(2)}, u32[]{:S(2)}) %collective-permute-start.16) | collective-permute-done | bytes 24608 | tf_op jit(solution)/shard_map/ppermute | solution.py:144
  58.8 2.5 %collective-permute-done.17 = f32[1,2,8,384]{3,1,2,0:T(2,128)S(1)} collective-permute-done((f32[1,2,8,384]{3,1,2,0:T(2,128)S(1)}, f32[1,2,8,384]{3,1,2,0:T(2,128)S(1)}, u32[]{:S(2)}, u32[]{:S(2)}) %collective-permute-start.17) | collective-permute-done | bytes 24608 | tf_op jit(solution)/shard_map/ppermute | solution.py:144
  62.6 1.6 %collective-permute-start.19 = (bf16[2,8,384]{2,1,0:T(8,128)(2,1)S(1)}, bf16[2,8,384]{2,1,0:T(8,128)(2,1)S(1)}, u32[]{:S(2)}, u32[]{:S(2)}) collective-permute-start(bf16[2,8,384]{2,1,0:T(8,128)(2,1)S(1)} %pad_maximum_fusion.2), channel_id=1, source_target_pairs={{0,2},{1,3},{2,0},{3,1},{4,6},{5,7},{6,4},{7,5},{8,10},{9,11},{10,... | collective-permute-start | bytes 36872 | tf_op jit(solution)/shard_map/ppermute | solution.py:132
  66.1 1.1 %copy.130 = bf16[2,2,384,384]{3,2,1,0:T(8,128)(2,1)} copy(bf16[2,2,384,384]{3,2,0,1:T(8,128)(2,1)S(1)} %pad_maximum_fusion) | data formatting | bytes 2359296
  67.7 1.6 %collective-permute-start.25 = (bf16[4,24,384]{2,1,0:T(8,128)(2,1)S(1)}, bf16[4,24,384]{2,1,0:T(8,128)(2,1)S(1)}, u32[]{:S(2)}, u32[]{:S(2)}) collective-permute-start(bf16[4,24,384]{2,1,0:T(8,128)(2,1)S(1)} %fusion.47), channel_id=1, source_target_pairs={{0,2},{1,3},{2,0},{3,1},{4,6},{5,7},{6,4},{7,5},{8,10},{9,11},{10,... | collective-permute-start | bytes 221192 | tf_op jit(solution)/shard_map/ppermute | solution.py:122
  70.3 1.3 %collective-permute-start.23 = (f32[1,2,8,384]{3,1,2,0:T(2,128)S(1)}, f32[1,2,8,384]{3,1,2,0:T(2,128)S(1)}, u32[]{:S(2)}, u32[]{:S(2)}) collective-permute-start(f32[1,2,8,384]{3,1,2,0:T(2,128)S(1)} %bitcast.258), channel_id=1, source_target_pairs={{0,12},{1,13},{2,14},{3,15},{4,8},{5,9},{6,10},{7,11},{8,4},{9,5},... | collective-permute-start | bytes 73736 | tf_op jit(solution)/shard_map/ppermute | solution.py:144
  71.6 1.4 %collective-permute-start.21 = (f32[1,2,8,384]{3,1,2,0:T(2,128)S(1)}, f32[1,2,8,384]{3,1,2,0:T(2,128)S(1)}, u32[]{:S(2)}, u32[]{:S(2)}) collective-permute-start(f32[1,2,8,384]{3,1,2,0:T(2,128)S(1)} %bitcast.257), channel_id=1, source_target_pairs={{0,4},{1,5},{2,6},{3,7},{4,0},{5,1},{6,2},{7,3},{8,12},{9,13},{10,... | collective-permute-start | bytes 73736 | tf_op jit(solution)/shard_map/ppermute | solution.py:144
  74.2 1.9 %collective-permute-done.23 = f32[1,2,8,384]{3,1,2,0:T(2,128)S(1)} collective-permute-done((f32[1,2,8,384]{3,1,2,0:T(2,128)S(1)}, f32[1,2,8,384]{3,1,2,0:T(2,128)S(1)}, u32[]{:S(2)}, u32[]{:S(2)}) %collective-permute-start.23) | collective-permute-done | bytes 24608 | tf_op jit(solution)/shard_map/ppermute | solution.py:144
  76.2 1.3 %collective-permute-done.26 = f32[2,24,384]{2,1,0:T(8,128)S(1)} collective-permute-done((f32[2,24,384]{2,1,0:T(8,128)S(1)}, f32[2,24,384]{2,1,0:T(8,128)S(1)}, u32[]{:S(2)}, u32[]{:S(2)}) %collective-permute-start.26) | collective-permute-done | bytes 73760 | tf_op jit(solution)/shard_map/ppermute | solution.py:122
  77.5 1.8 %collective-permute-start.27 = (f32[1,24,384]{2,1,0:T(8,128)S(1)}, f32[1,24,384]{2,1,0:T(8,128)S(1)}, u32[]{:S(2)}, u32[]{:S(2)}) collective-permute-start(f32[1,24,384]{2,1,0:T(8,128)S(1)} %constant_dynamic-slice_fusion), channel_id=1, source_target_pairs={{0,8},{1,9},{2,10},{3,11},{4,12},{5,13},{6,14},{7,15},{8,0},{9,1},... | collective-permute-start | bytes 110600 | tf_op jit(solution)/shard_map/ppermute | solution.py:122
  79.3 2.5 %fusion.11 = bf16[2,1440,384]{2,1,0:T(8,128)(2,1)} fusion(f32[2,1440,384]{2,1,0:T(8,128)S(1)} %fusion.40, bf16[2,1440,384]{2,1,0:T(8,128)(2,1)S(1)} %copy-done.3, bf16[1440,8,1]{0,1,2:T(8,128)(2,1)S(1)} %copy-done.5, bf16[2,8,384]{2,0,1:T(2,128)(2,1)S(1)} %fusion.68), kind=kOutput, calls=%fused_computation.20 | convolution fusion | flops 22118400 | bytes 8882688 | tf_op jit(solution)/shard_map/jfc,kf->jkc/dot_general | solution.py:246
  81.7 1.1 %collective-permute-done.27 = f32[1,24,384]{2,1,0:T(8,128)S(1)} collective-permute-done((f32[1,24,384]{2,1,0:T(8,128)S(1)}, f32[1,24,384]{2,1,0:T(8,128)S(1)}, u32[]{:S(2)}, u32[]{:S(2)}) %collective-permute-start.27) | collective-permute-done | bytes 36896 | tf_op jit(solution)/shard_map/ppermute | solution.py:122
  (128 shorter events, 22.8 us)
Async XLA Ops:
  3.4 7.7 %collective-permute-start.1 = (f32[2,8,384]{2,1,0:T(8,128)S(1)}, f32[2,8,384]{2,1,0:T(8,128)S(1)}, u32[]{:S(2)}, u32[]{:S(2)}) collective-permute-start(f32[2,8,384]{2,1,0:T(8,128)S(1)} %bitcast.241), channel_id=1, source_target_pairs={{0,2},{1,3},{2,0},{3,1},{4,6},{5,7},{6,4},{7,5},{8,10},{9,11},{10,... | collective-permute-start | bytes 73736 | tf_op jit(solution)/shard_map/ppermute | solution.py:132
  6.4 4.8 %collective-permute-start = (f32[2,8,384]{2,1,0:T(8,128)S(1)}, f32[2,8,384]{2,1,0:T(8,128)}, u32[]{:S(2)}, u32[]{:S(2)}) collective-permute-start(f32[2,8,384]{2,1,0:T(8,128)S(1)} %bitcast.242), channel_id=1, source_target_pairs={{0,1},{1,0},{2,3},{3,2},{4,5},{5,4},{6,7},{7,6},{8,9},{9,8},{10,11... | collective-permute-start | bytes 73736 | tf_op jit(solution)/shard_map/ppermute | solution.py:132
  6.4 4.8 %collective-permute-start.2 = (f32[2,8,384]{2,1,0:T(8,128)S(1)}, f32[2,8,384]{2,1,0:T(8,128)}, u32[]{:S(2)}, u32[]{:S(2)}) collective-permute-start(f32[2,8,384]{2,1,0:T(8,128)S(1)} %bitcast.243), channel_id=1, source_target_pairs={{0,3},{1,2},{2,1},{3,0},{4,7},{5,6},{6,5},{7,4},{8,11},{9,10},{10,... | collective-permute-start | bytes 73736 | tf_op jit(solution)/shard_map/ppermute | solution.py:132
  7.4 15.8 %copy-start.2 = (bf16[2,2,384,384]{3,2,1,0:T(8,128)(2,1)S(1)}, bf16[2,2,384,384]{3,2,1,0:T(8,128)(2,1)}, u32[]{:S(2)}) copy-start(bf16[2,2,384,384]{3,2,1,0:T(8,128)(2,1)} %param.13) | copy-start | bytes 3538948
  14.2 6.4 %collective-permute-start.4 = (f32[1,2,8,384]{3,1,2,0:T(2,128)}, f32[1,2,8,384]{3,1,2,0:T(2,128)S(1)}, u32[]{:S(2)}, u32[]{:S(2)}) collective-permute-start(f32[1,2,8,384]{3,1,2,0:T(2,128)} %bitcast.227), channel_id=1, source_target_pairs={{0,8},{1,9},{2,10},{3,11},{4,12},{5,13},{6,14},{7,15},{8,0},{9,1},... | collective-permute-start | bytes 73736 | tf_op jit(solution)/shard_map/ppermute | solution.py:144
  17.3 5.8 %collective-permute-start.5 = (f32[1,2,8,384]{3,1,2,0:T(2,128)}, f32[1,2,8,384]{3,1,2,0:T(2,128)S(1)}, u32[]{:S(2)}, u32[]{:S(2)}) collective-permute-start(f32[1,2,8,384]{3,1,2,0:T(2,128)} %bitcast.232), channel_id=1, source_target_pairs={{0,12},{1,13},{2,14},{3,15},{4,8},{5,9},{6,10},{7,11},{8,4},{9,5},... | collective-permute-start | bytes 73736 | tf_op jit(solution)/shard_map/ppermute | solution.py:144
  18.6 4.5 %collective-permute-start.3 = (f32[1,2,8,384]{3,1,2,0:T(2,128)}, f32[1,2,8,384]{3,1,2,0:T(2,128)S(1)}, u32[]{:S(2)}, u32[]{:S(2)}) collective-permute-start(f32[1,2,8,384]{3,1,2,0:T(2,128)} %bitcast.228), channel_id=1, source_target_pairs={{0,4},{1,5},{2,6},{3,7},{4,0},{5,1},{6,2},{7,3},{8,12},{9,13},{10,... | collective-permute-start | bytes 73736 | tf_op jit(solution)/shard_map/ppermute | solution.py:144
  24.6 3.4 %collective-permute-start.8 = (bf16[2,8,384]{2,1,0:T(8,128)(2,1)}, bf16[2,8,384]{2,1,0:T(8,128)(2,1)S(1)}, u32[]{:S(2)}, u32[]{:S(2)}) collective-permute-start(bf16[2,8,384]{2,1,0:T(8,128)(2,1)} %pad_maximum_fusion.1), channel_id=1, source_target_pairs={{0,3},{1,2},{2,1},{3,0},{4,7},{5,6},{6,5},{7,4},{8,11},{9,10},{10,... | collective-permute-start | bytes 36872 | tf_op jit(solution)/shard_map/ppermute | solution.py:132
  24.6 3.9 %collective-permute-start.7 = (bf16[2,8,384]{2,1,0:T(8,128)(2,1)}, bf16[2,8,384]{2,1,0:T(8,128)(2,1)S(1)}, u32[]{:S(2)}, u32[]{:S(2)}) collective-permute-start(bf16[2,8,384]{2,1,0:T(8,128)(2,1)} %pad_maximum_fusion.1), channel_id=1, source_target_pairs={{0,2},{1,3},{2,0},{3,1},{4,6},{5,7},{6,4},{7,5},{8,10},{9,11},{10,... | collective-permute-start | bytes 36872 | tf_op jit(solution)/shard_map/ppermute | solution.py:132
  26.2 2.4 %collective-permute-start.6 = (bf16[2,8,384]{2,1,0:T(8,128)(2,1)}, bf16[2,8,384]{2,1,0:T(8,128)(2,1)S(1)}, u32[]{:S(2)}, u32[]{:S(2)}) collective-permute-start(bf16[2,8,384]{2,1,0:T(8,128)(2,1)} %pad_maximum_fusion.1), channel_id=1, source_target_pairs={{0,1},{1,0},{2,3},{3,2},{4,5},{5,4},{6,7},{7,6},{8,9},{9,8},{10,11... | collective-permute-start | bytes 36872 | tf_op jit(solution)/shard_map/ppermute | solution.py:132
  31.4 9.1 %collective-permute-start.10 = (f32[1,2,8,384]{3,1,2,0:T(2,128)}, f32[1,2,8,384]{3,1,2,0:T(2,128)}, u32[]{:S(2)}, u32[]{:S(2)}) collective-permute-start(f32[1,2,8,384]{3,1,2,0:T(2,128)} %bitcast.225), channel_id=1, source_target_pairs={{0,8},{1,9},{2,10},{3,11},{4,12},{5,13},{6,14},{7,15},{8,0},{9,1},... | collective-permute-start | bytes 73736 | tf_op jit(solution)/shard_map/ppermute | solution.py:144
  32.6 7.9 %collective-permute-start.11 = (f32[1,2,8,384]{3,1,2,0:T(2,128)}, f32[1,2,8,384]{3,1,2,0:T(2,128)}, u32[]{:S(2)}, u32[]{:S(2)}) collective-permute-start(f32[1,2,8,384]{3,1,2,0:T(2,128)} %bitcast.231), channel_id=1, source_target_pairs={{0,12},{1,13},{2,14},{3,15},{4,8},{5,9},{6,10},{7,11},{8,4},{9,5},... | collective-permute-start | bytes 73736 | tf_op jit(solution)/shard_map/ppermute | solution.py:144
  33.6 7.8 %copy-start.5 = (bf16[1440,8,1]{0,1,2:T(8,128)(2,1)S(1)}, bf16[1440,8,1]{0,1,2:T(8,128)(2,1)}, u32[]{:S(2)}) copy-start(bf16[1440,8,1]{0,1,2:T(8,128)(2,1)} %constant.112) | copy-start | bytes 69124
  33.6 7.0 %collective-permute-start.9 = (f32[1,2,8,384]{3,1,2,0:T(2,128)}, f32[1,2,8,384]{3,1,2,0:T(2,128)}, u32[]{:S(2)}, u32[]{:S(2)}) collective-permute-start(f32[1,2,8,384]{3,1,2,0:T(2,128)} %bitcast.226), channel_id=1, source_target_pairs={{0,4},{1,5},{2,6},{3,7},{4,0},{5,1},{6,2},{7,3},{8,12},{9,13},{10,... | collective-permute-start | bytes 73736 | tf_op jit(solution)/shard_map/ppermute | solution.py:144
  47.8 5.1 %collective-permute-start.13 = (f32[2,8,384]{2,1,0:T(8,128)S(1)}, f32[2,8,384]{2,1,0:T(8,128)S(1)}, u32[]{:S(2)}, u32[]{:S(2)}) collective-permute-start(f32[2,8,384]{2,1,0:T(8,128)S(1)} %bitcast.245), channel_id=1, source_target_pairs={{0,2},{1,3},{2,0},{3,1},{4,6},{5,7},{6,4},{7,5},{8,10},{9,11},{10,... | collective-permute-start | bytes 73736 | tf_op jit(solution)/shard_map/ppermute | solution.py:132
  49.3 3.6 %collective-permute-start.12 = (f32[2,8,384]{2,1,0:T(8,128)S(1)}, f32[2,8,384]{2,1,0:T(8,128)S(1)}, u32[]{:S(2)}, u32[]{:S(2)}) collective-permute-start(f32[2,8,384]{2,1,0:T(8,128)S(1)} %bitcast.246), channel_id=1, source_target_pairs={{0,1},{1,0},{2,3},{3,2},{4,5},{5,4},{6,7},{7,6},{8,9},{9,8},{10,11... | collective-permute-start | bytes 73736 | tf_op jit(solution)/shard_map/ppermute | solution.py:132
  49.3 3.6 %collective-permute-start.14 = (f32[2,8,384]{2,1,0:T(8,128)S(1)}, f32[2,8,384]{2,1,0:T(8,128)S(1)}, u32[]{:S(2)}, u32[]{:S(2)}) collective-permute-start(f32[2,8,384]{2,1,0:T(8,128)S(1)} %bitcast.247), channel_id=1, source_target_pairs={{0,3},{1,2},{2,1},{3,0},{4,7},{5,6},{6,5},{7,4},{8,11},{9,10},{10,... | collective-permute-start | bytes 73736 | tf_op jit(solution)/shard_map/ppermute | solution.py:132
  52.9 11.6 %copy-start.7 = (bf16[2,4,384]{2,0,1:T(2,128)(2,1)S(1)}, bf16[2,4,384]{2,0,1:T(2,128)(2,1)}, u32[]{:S(2)}) copy-start(bf16[2,4,384]{2,0,1:T(2,128)(2,1)} %copy-done.6) | copy-start | bytes 18436
  53.5 5.3 %collective-permute-start.16 = (f32[1,2,8,384]{3,1,2,0:T(2,128)S(1)}, f32[1,2,8,384]{3,1,2,0:T(2,128)S(1)}, u32[]{:S(2)}, u32[]{:S(2)}) collective-permute-start(f32[1,2,8,384]{3,1,2,0:T(2,128)S(1)} %bitcast.262), channel_id=1, source_target_pairs={{0,8},{1,9},{2,10},{3,11},{4,12},{5,13},{6,14},{7,15},{8,0},{9,1},... | collective-permute-start | bytes 73736 | tf_op jit(solution)/shard_map/ppermute | solution.py:144
  55.7 5.6 %collective-permute-start.17 = (f32[1,2,8,384]{3,1,2,0:T(2,128)S(1)}, f32[1,2,8,384]{3,1,2,0:T(2,128)S(1)}, u32[]{:S(2)}, u32[]{:S(2)}) collective-permute-start(f32[1,2,8,384]{3,1,2,0:T(2,128)S(1)} %bitcast.261), channel_id=1, source_target_pairs={{0,12},{1,13},{2,14},{3,15},{4,8},{5,9},{6,10},{7,11},{8,4},{9,5},... | collective-permute-start | bytes 73736 | tf_op jit(solution)/shard_map/ppermute | solution.py:144
  56.6 4.7 %collective-permute-start.15 = (f32[1,2,8,384]{3,1,2,0:T(2,128)S(1)}, f32[1,2,8,384]{3,1,2,0:T(2,128)S(1)}, u32[]{:S(2)}, u32[]{:S(2)}) collective-permute-start(f32[1,2,8,384]{3,1,2,0:T(2,128)S(1)} %bitcast.259), channel_id=1, source_target_pairs={{0,4},{1,5},{2,6},{3,7},{4,0},{5,1},{6,2},{7,3},{8,12},{9,13},{10,... | collective-permute-start | bytes 73736 | tf_op jit(solution)/shard_map/ppermute | solution.py:144
  57.1 10.5 %collective-permute-start.24 = (bf16[8,24,384]{2,1,0:T(8,128)(2,1)S(1)}, bf16[8,24,384]{2,1,0:T(8,128)(2,1)S(1)}, u32[]{:S(2)}, u32[]{:S(2)}) collective-permute-start(bf16[8,24,384]{2,1,0:T(8,128)(2,1)S(1)} %fusion.44), channel_id=1, source_target_pairs={{0,1},{1,0},{2,3},{3,2},{4,5},{5,4},{6,7},{7,6},{8,9},{9,8},{10,11... | collective-permute-start | bytes 442376 | tf_op jit(solution)/shard_map/ppermute | solution.py:122
  62.5 4.7 %collective-permute-start.20 = (bf16[2,8,384]{2,1,0:T(8,128)(2,1)S(1)}, bf16[2,8,384]{2,1,0:T(8,128)(2,1)S(1)}, u32[]{:S(2)}, u32[]{:S(2)}) collective-permute-start(bf16[2,8,384]{2,1,0:T(8,128)(2,1)S(1)} %pad_maximum_fusion.2), channel_id=1, source_target_pairs={{0,3},{1,2},{2,1},{3,0},{4,7},{5,6},{6,5},{7,4},{8,11},{9,10},{10,... | collective-permute-start | bytes 36872 | tf_op jit(solution)/shard_map/ppermute | solution.py:132
  62.6 4.7 %collective-permute-start.19 = (bf16[2,8,384]{2,1,0:T(8,128)(2,1)S(1)}, bf16[2,8,384]{2,1,0:T(8,128)(2,1)S(1)}, u32[]{:S(2)}, u32[]{:S(2)}) collective-permute-start(bf16[2,8,384]{2,1,0:T(8,128)(2,1)S(1)} %pad_maximum_fusion.2), channel_id=1, source_target_pairs={{0,2},{1,3},{2,0},{3,1},{4,6},{5,7},{6,4},{7,5},{8,10},{9,11},{10,... | collective-permute-start | bytes 36872 | tf_op jit(solution)/shard_map/ppermute | solution.py:132
  64.2 3.1 %collective-permute-start.18 = (bf16[2,8,384]{2,1,0:T(8,128)(2,1)S(1)}, bf16[2,8,384]{2,1,0:T(8,128)(2,1)S(1)}, u32[]{:S(2)}, u32[]{:S(2)}) collective-permute-start(bf16[2,8,384]{2,1,0:T(8,128)(2,1)S(1)} %pad_maximum_fusion.2), channel_id=1, source_target_pairs={{0,1},{1,0},{2,3},{3,2},{4,5},{5,4},{6,7},{7,6},{8,9},{9,8},{10,11... | collective-permute-start | bytes 36872 | tf_op jit(solution)/shard_map/ppermute | solution.py:132
  66.1 13.1 %copy-start.3 = (bf16[2,1440,384]{2,1,0:T(8,128)(2,1)S(1)}, bf16[2,1440,384]{2,1,0:T(8,128)(2,1)}, u32[]{:S(2)}) copy-start(bf16[2,1440,384]{2,1,0:T(8,128)(2,1)} %param.11) | copy-start | bytes 6635524
  67.7 5.3 %collective-permute-start.25 = (bf16[4,24,384]{2,1,0:T(8,128)(2,1)S(1)}, bf16[4,24,384]{2,1,0:T(8,128)(2,1)S(1)}, u32[]{:S(2)}, u32[]{:S(2)}) collective-permute-start(bf16[4,24,384]{2,1,0:T(8,128)(2,1)S(1)} %fusion.47), channel_id=1, source_target_pairs={{0,2},{1,3},{2,0},{3,1},{4,6},{5,7},{6,4},{7,5},{8,10},{9,11},{10,... | collective-permute-start | bytes 221192 | tf_op jit(solution)/shard_map/ppermute | solution.py:122
  69.4 4.8 %collective-permute-start.22 = (f32[1,2,8,384]{3,1,2,0:T(2,128)S(1)}, f32[1,2,8,384]{3,1,2,0:T(2,128)S(1)}, u32[]{:S(2)}, u32[]{:S(2)}) collective-permute-start(f32[1,2,8,384]{3,1,2,0:T(2,128)S(1)} %bitcast.260), channel_id=1, source_target_pairs={{0,8},{1,9},{2,10},{3,11},{4,12},{5,13},{6,14},{7,15},{8,0},{9,1},... | collective-permute-start | bytes 73736 | tf_op jit(solution)/shard_map/ppermute | solution.py:144
  70.3 5.8 %collective-permute-start.23 = (f32[1,2,8,384]{3,1,2,0:T(2,128)S(1)}, f32[1,2,8,384]{3,1,2,0:T(2,128)S(1)}, u32[]{:S(2)}, u32[]{:S(2)}) collective-permute-start(f32[1,2,8,384]{3,1,2,0:T(2,128)S(1)} %bitcast.258), channel_id=1, source_target_pairs={{0,12},{1,13},{2,14},{3,15},{4,8},{5,9},{6,10},{7,11},{8,4},{9,5},... | collective-permute-start | bytes 73736 | tf_op jit(solution)/shard_map/ppermute | solution.py:144
  71.6 4.6 %collective-permute-start.21 = (f32[1,2,8,384]{3,1,2,0:T(2,128)S(1)}, f32[1,2,8,384]{3,1,2,0:T(2,128)S(1)}, u32[]{:S(2)}, u32[]{:S(2)}) collective-permute-start(f32[1,2,8,384]{3,1,2,0:T(2,128)S(1)} %bitcast.257), channel_id=1, source_target_pairs={{0,4},{1,5},{2,6},{3,7},{4,0},{5,1},{6,2},{7,3},{8,12},{9,13},{10,... | collective-permute-start | bytes 73736 | tf_op jit(solution)/shard_map/ppermute | solution.py:144
  73.0 4.4 %collective-permute-start.26 = (f32[2,24,384]{2,1,0:T(8,128)S(1)}, f32[2,24,384]{2,1,0:T(8,128)S(1)}, u32[]{:S(2)}, u32[]{:S(2)}) collective-permute-start(f32[2,24,384]{2,1,0:T(8,128)S(1)} %dynamic-slice_bitcast_fusion), channel_id=1, source_target_pairs={{0,4},{1,5},{2,6},{3,7},{4,0},{5,1},{6,2},{7,3},{8,12},{9,13},{10,... | collective-permute-start | bytes 221192 | tf_op jit(solution)/shard_map/ppermute | solution.py:122
  77.5 5.3 %collective-permute-start.27 = (f32[1,24,384]{2,1,0:T(8,128)S(1)}, f32[1,24,384]{2,1,0:T(8,128)S(1)}, u32[]{:S(2)}, u32[]{:S(2)}) collective-permute-start(f32[1,24,384]{2,1,0:T(8,128)S(1)} %constant_dynamic-slice_fusion), channel_id=1, source_target_pairs={{0,8},{1,9},{2,10},{3,11},{4,12},{5,13},{6,14},{7,15},{8,0},{9,1},... | collective-permute-start | bytes 110600 | tf_op jit(solution)/shard_map/ppermute | solution.py:122
  (5 other events, 20.1 us)

commit v10 on v8

--- a/solution.py
+++ b/solution.py
@@ -123,7 +123,16 @@
     return cur[0]
 
 
-def xor_exchange(values, table, axis_name, groups, me, lo, spec):
+def halve_round(cur, axis_name, groups, me, low):
+    view = cur.reshape((cur.shape[0] // 2, 2) + cur.shape[1:])
+    bit = (me >> low) & 1
+    total = lax.dynamic_index_in_dim(view, bit, axis=1, keepdims=False)
+    sent = lax.dynamic_index_in_dim(view, 1 - bit, axis=1, keepdims=False)
+    mask = 1 << low
+    return total + lax.ppermute(sent, axis_name, [(i, i ^ mask) for i in range(groups)])
+
+
+def xor_exchange(values, table, axis_name, groups, me, lo, spec, side=None):
     parts = [values]
     for k in range(1, 1 << lo):
         parts.append(lax.ppermute(values, axis_name, [(i, i ^ k) for i in range(groups)]))
@@ -132,6 +141,10 @@
     hi = groups.bit_length() - 1 - lo
     b = 0
     while b < hi:
+        if side is not None and side[1] < side[2]:
+            blocks, low, bits = side
+            cur, blocks = lax.optimization_barrier((cur, blocks))
+            side = (halve_round(blocks, axis_name, groups, me, low), low + 1, bits)
         width = min(2, hi - b)
         fan = 1 << width
         view = cur.reshape((cur.shape[0] // fan, fan) + cur.shape[1:])
@@ -141,7 +154,7 @@
             total = total + lax.ppermute(view[:, k], axis_name, [(i, i ^ mask) for i in range(groups)])
         cur = total
         b += width
-    return cur[0]
+    return cur[0], side
 
 
 def complex_apply(coeffs, weights, orders):
@@ -219,7 +232,7 @@
     to_rows = "xksrf,ksfc->xrfc"
 
     def exchange(values, table, spec):
-        return xor_exchange(values, table, "lat", groups, me, lo, spec)
+        return xor_exchange(values, table, "lat", groups, me, lo, spec)[0]
 
     spectrum = jnp.einsum("jkc,kf->jfc", activations, fourier, preferred_element_type=jnp.float32)
     coeffs = exchange(spectrum, own_quad, to_owners).astype(jnp.bfloat16)
@@ -233,13 +246,23 @@
 
     skip_terms = jnp.einsum("jkc,jkd->cd", activations, slope_b, preferred_element_type=jnp.float32)
     skip_blocks = skip_terms.reshape((groups, -1) + skip_terms.shape[1:])
-    grad_skip = xor_reduce_scatter(skip_blocks, "lat", groups, me, 1) * (1.0 / math.sqrt(lat_total * lon_total))
+    skip_side = (halve_round(skip_blocks, "lat", groups, me, 0), 1, bits) if bits > 0 else (skip_blocks, 0, 0)
     through_skip = jnp.einsum("jkd,cd->jkc", slope_b, skip_weight, preferred_element_type=jnp.float32)
 
     mode_grads = jnp.einsum("jkc,kf->jfc", slope_b, fourier, preferred_element_type=jnp.float32)
     coeff_grads = exchange(mode_grads, own_plm, to_owners).astype(jnp.bfloat16)
     weight_grads, back_coeffs = complex_adjoint(coeffs, coeff_grads, spectral_weight, orders)
-    row_grads = exchange(back_coeffs.astype(jnp.bfloat16), rows_quad, to_rows).astype(jnp.bfloat16)
+    back_b = back_coeffs.astype(jnp.bfloat16)
+    if skip_side[1] < skip_side[2]:
+        back_b, held = lax.optimization_barrier((back_b, skip_side[0]))
+        skip_side = (halve_round(held, "lat", groups, me, skip_side[1]), skip_side[1] + 1, bits)
+    row_sums, skip_side = xor_exchange(back_b, rows_quad, "lat", groups, me, lo, to_rows, skip_side)
+    row_grads = row_sums.astype(jnp.bfloat16)
+    skip_sum, low = skip_side[0], skip_side[1]
+    while low < bits:
+        skip_sum = halve_round(skip_sum, "lat", groups, me, low)
+        low += 1
+    grad_skip = skip_sum[0] * (1.0 / math.sqrt(lat_total * lon_total))
     through_modes = jnp.einsum("jfc,kf->jkc", row_grads, fourier, preferred_element_type=jnp.float32)
     grad_activations = (upstream.astype(jnp.float32) + through_skip + through_modes).astype(jnp.bfloat16)
     return (grad_activations, weight_grads.astype(jnp.bfloat16), grad_skip)

time: 84.3 us -> 89.4 us (1.060)
  starting transfers between devices: 27 us -> 30 us
  waiting for transfers between devices: 14.5 us -> 16.5 us
    ppermute x4, waiting for transfers between devices: 4.5 us -> 7.28 us  [halve_round(): lax.ppermute(sent, axis_name, [(i, i ^ mask) for i in range(groups)])]
    ppermute x12, starting transfers between devices: 15.2 us -> 17.9 us  [xor_exchange(): lax.ppermute(view[:, k], axis_name, [(i, i ^ mask) for i in range(groups)])]
    ppermute x12, waiting for transfers between devices: 8.7 us -> 6.26 us  [xor_exchange(): lax.ppermute(view[:, k], axis_name, [(i, i ^ mask) for i in range(groups)])]
    ppermute x12, waiting for transfers between devices: 1.27 us -> 2.95 us  [xor_exchange(): lax.ppermute(values, axis_name, [(i, i ^ k) for i in range(groups)])]
    unnamed x35 -> x33, local copies, waits for them, and re-layouts: 8 us -> 8.03 us
  transfers between devices with their start and end apart: 28 -> 28, of which waited for: 10 -> 14; matrix products, arithmetic and copies ran while one was open for 27% -> 26% of each run, Pallas kernels for 0% -> 0%
where the time goes in v10:
time: 89.4 us; the launch traced here: 88.9 us
  starting transfers between devices  30 us (34%)
  matrix products  22.2 us (25%)
  waiting for transfers between devices  16.5 us (18%)
  local copies, waits for them, and re-layouts  14.8 us (17%)
  other arithmetic  4.39 us (5%)
  between operations  1.04 us (1%)
    ppermute x12, starting transfers between devices, xor_exchange(): lax.ppermute(view[:, k], axis_name, [(i, i ^ mask) for i in range(groups)])  17.9 us
    ppermute x12, starting transfers between devices, xor_exchange(): lax.ppermute(values, axis_name, [(i, i ^ k) for i in range(groups)])  8.76 us
    unnamed x33, local copies, waits for them, and re-layouts  8.03 us
    ppermute x4, waiting for transfers between devices, halve_round(): lax.ppermute(sent, axis_name, [(i, i ^ mask) for i in range(groups)])  7.28 us
    ppermute x12, waiting for transfers between devices, xor_exchange(): lax.ppermute(view[:, k], axis_name, [(i, i ^ mask) for i in range(groups)])  6.26 us
    dot_general x1, matrix products, local(): jnp.einsum('jfc,kf->jkc', grid_modes, fourier, preferred_element_type=jnp...  5.99 us
    dot_general x1, matrix products, local(): jnp.einsum('jkc,cd->jkd', activations, skip_weight, preferred_element_typ...  4.52 us
    ppermute x4, starting transfers between devices, halve_round(): lax.ppermute(sent, axis_name, [(i, i ^ mask) for i in range(groups)])  3.27 us
  transfers between devices with their start and end apart: 28, of which 14 were waited for; matrix products, arithmetic and copies ran while one was open for 26% of the time, Pallas kernels for 0%

profile of v10, /device:TPU:0, one launch (start us, length us, event | category | flops | bytes accessed | tf_op | source)
XLA Modules:
  0.0 88.9 jit_solution(9032056273184830076)
XLA Ops:
  0.7 1.6 %copy-done = bf16[2,1440,384]{2,1,0:T(8,128)(2,1)S(1)} copy-done((bf16[2,1440,384]{2,1,0:T(8,128)(2,1)S(1)}, bf16[2,1440,384]{2,1,0:T(8,128)(2,1)}, u32[]{:S(2)}) %copy-start) | copy-done | bytes 2211864
  2.3 1.1 %fusion.100 = f32[8,2,384]{2,0,1:T(8,128)S(1)} fusion(bf16[1440,8,1]{0,1,2:T(8,128)(2,1)} %constant.116, bf16[2,1440,384]{2,1,0:T(8,128)(2,1)S(1)} %copy-done), kind=kOutput, calls=%fused_computation.163 | convolution fusion | flops 17694720 | bytes 2259456 | tf_op jit(solution)/shard_map/jkc,kf->jfc/dot_general | solution.py:237
  3.4 2.4 %collective-permute-start.2 = (f32[2,8,384]{2,1,0:T(8,128)S(1)}, f32[2,8,384]{2,1,0:T(8,128)S(1)}, u32[]{:S(2)}, u32[]{:S(2)}) collective-permute-start(f32[2,8,384]{2,1,0:T(8,128)S(1)} %bitcast.236), channel_id=1, source_target_pairs={{0,3},{1,2},{2,1},{3,0},{4,7},{5,6},{6,5},{7,4},{8,11},{9,10},{10,... | collective-permute-start | bytes 73736 | tf_op jit(solution)/shard_map/ppermute | solution.py:138
  8.6 1.6 %gather_fusion = f32[64,16]{1,0:T(8,128)S(1)} fusion(f32[32,32,16]{2,1,0:T(8,128)} %constant.89, s32[64]{0:T(128)S(1)} %reshape.158), kind=kCustom, calls=%fused_computation.2 | custom fusion | bytes 8704 | tf_op jit(solution)/shard_map/gather | solution.py:224
  13.0 3.8 %collective-permute-start.5 = (f32[1,2,8,384]{3,1,2,0:T(2,128)}, f32[1,2,8,384]{3,1,2,0:T(2,128)S(1)}, u32[]{:S(2)}, u32[]{:S(2)}) collective-permute-start(f32[1,2,8,384]{3,1,2,0:T(2,128)} %bitcast.226), channel_id=1, source_target_pairs={{0,12},{1,13},{2,14},{3,15},{4,8},{5,9},{6,10},{7,11},{8,4},{9,5},... | collective-permute-start | bytes 73736 | tf_op jit(solution)/shard_map/ppermute | solution.py:154
  18.8 1.6 %gather_fusion.1 = f32[64,16]{1,0:T(8,128)S(1)} fusion(f32[32,32,16]{2,1,0:T(8,128)} %constant.89, s32[64]{0:T(128)S(1)} %reshape.164), kind=kCustom, calls=%fused_computation.3 | custom fusion | bytes 8704 | tf_op jit(solution)/shard_map/gather | solution.py:227
  20.4 2.0 %collective-permute-done.4 = f32[1,2,8,384]{3,1,2,0:T(2,128)S(1)} collective-permute-done((f32[1,2,8,384]{3,1,2,0:T(2,128)}, f32[1,2,8,384]{3,1,2,0:T(2,128)S(1)}, u32[]{:S(2)}, u32[]{:S(2)}) %collective-permute-start.4) | collective-permute-done | bytes 24608 | tf_op jit(solution)/shard_map/ppermute | solution.py:154
  23.9 1.5 %collective-permute-start.7 = (bf16[2,8,384]{2,1,0:T(8,128)(2,1)}, bf16[2,8,384]{2,1,0:T(8,128)(2,1)}, u32[]{:S(2)}, u32[]{:S(2)}) collective-permute-start(bf16[2,8,384]{2,1,0:T(8,128)(2,1)} %pad_maximum_fusion.1), channel_id=1, source_target_pairs={{0,2},{1,3},{2,0},{3,1},{4,6},{5,7},{6,4},{7,5},{8,10},{9,11},{10,... | collective-permute-start | bytes 36872 | tf_op jit(solution)/shard_map/ppermute | solution.py:138
  26.0 1.4 %collective-permute-done.8 = bf16[2,8,384]{2,1,0:T(8,128)(2,1)} collective-permute-done((bf16[2,8,384]{2,1,0:T(8,128)(2,1)}, bf16[2,8,384]{2,1,0:T(8,128)(2,1)}, u32[]{:S(2)}, u32[]{:S(2)}) %collective-permute-start.8) | collective-permute-done | bytes 12320 | tf_op jit(solution)/shard_map/ppermute | solution.py:138
  30.3 2.2 %collective-permute-start.11 = (f32[1,2,8,384]{3,1,2,0:T(2,128)}, f32[1,2,8,384]{3,1,2,0:T(2,128)}, u32[]{:S(2)}, u32[]{:S(2)}) collective-permute-start(f32[1,2,8,384]{3,1,2,0:T(2,128)} %bitcast.225), channel_id=1, source_target_pairs={{0,12},{1,13},{2,14},{3,15},{4,8},{5,9},{6,10},{7,11},{8,4},{9,5},... | collective-permute-start | bytes 73736 | tf_op jit(solution)/shard_map/ppermute | solution.py:154
  34.1 1.8 %collective-permute-start.9 = (f32[1,2,8,384]{3,1,2,0:T(2,128)}, f32[1,2,8,384]{3,1,2,0:T(2,128)}, u32[]{:S(2)}, u32[]{:S(2)}) collective-permute-start(f32[1,2,8,384]{3,1,2,0:T(2,128)} %bitcast.220), channel_id=1, source_target_pairs={{0,4},{1,5},{2,6},{3,7},{4,0},{5,1},{6,2},{7,3},{8,12},{9,13},{10,... | collective-permute-start | bytes 73736 | tf_op jit(solution)/shard_map/ppermute | solution.py:154
  35.9 4.5 %fusion.42 = f32[2,1440,384]{2,1,0:T(8,128)} fusion(bf16[2,1440,384]{2,1,0:T(8,128)(2,1)S(1)} %copy-done, bf16[384,384]{1,0:T(8,128)(2,1)} %param.12), kind=kOutput, calls=%fused_computation.64 | convolution fusion | flops 849346560 | bytes 6930432 | tf_op jit(solution)/shard_map/jkc,cd->jkd/dot_general | solution.py:243
  42.4 6.0 %fusion.6 = bf16[2,1440,384]{2,1,0:T(8,128)(2,1)S(1)} fusion(bf16[2,1440,384]{2,1,0:T(8,128)(2,1)} %param.11, f32[2,1440,384]{2,1,0:T(8,128)} %fusion.42, bf16[1440,8,1]{0,1,2:T(8,128)(2,1)S(1)} %copy-done.5, bf16[2,8,384]{2,0,1:T(2,128)(2,1)S(1)} %fusion.68), kind=kOutput, calls=%fused_computation.15 | convolution fusion | flops 42024960 | bytes 8882688 | tf_op jit(solution)/shard_map/jfc,kf->jkc/dot_general | solution.py:242
  48.4 1.5 %fusion.40 = f32[2,1440,384]{2,1,0:T(8,128)S(1)} fusion(bf16[2,1440,384]{2,1,0:T(8,128)(2,1)S(1)} %fusion.6, bf16[384,384]{1,0:T(8,128)(2,1)S(1)} %copy-done.4), kind=kOutput, calls=%fused_computation.62 | convolution fusion | flops 849346560 | bytes 6930432 | tf_op jit(solution)/shard_map/jkd,cd->jkc/dot_general | solution.py:250
  50.4 1.5 %collective-permute-start.13 = (f32[2,8,384]{2,1,0:T(8,128)S(1)}, f32[2,8,384]{2,1,0:T(8,128)S(1)}, u32[]{:S(2)}, u32[]{:S(2)}) collective-permute-start(f32[2,8,384]{2,1,0:T(8,128)S(1)} %bitcast.241), channel_id=1, source_target_pairs={{0,2},{1,3},{2,0},{3,1},{4,6},{5,7},{6,4},{7,5},{8,10},{9,11},{10,... | collective-permute-start | bytes 73736 | tf_op jit(solution)/shard_map/ppermute | solution.py:138
  52.2 1.4 %fusion.102 = f32[384,384,1]{0,1,2:T(8,128)S(1)} fusion(bf16[2,1440,384]{2,1,0:T(8,128)(2,1)S(1)} %fusion.6, bf16[2,1440,384]{2,1,0:T(8,128)(2,1)S(1)} %copy-done), kind=kOutput, calls=%fused_computation.165 | convolution fusion | flops 849346560 | bytes 5013504 | tf_op jit(solution)/shard_map/jkc,jkd->cd/dot_general | solution.py:247
  54.8 2.3 %collective-permute-start.17 = (f32[1,2,8,384]{3,1,2,0:T(2,128)S(1)}, f32[1,2,8,384]{3,1,2,0:T(2,128)S(1)}, u32[]{:S(2)}, u32[]{:S(2)}) collective-permute-start(f32[1,2,8,384]{3,1,2,0:T(2,128)S(1)} %bitcast.251), channel_id=1, source_target_pairs={{0,12},{1,13},{2,14},{3,15},{4,8},{5,9},{6,10},{7,11},{8,4},{9,5},... | collective-permute-start | bytes 73736 | tf_op jit(solution)/shard_map/ppermute | solution.py:154
  57.1 2.2 %collective-permute-start.15 = (f32[1,2,8,384]{3,1,2,0:T(2,128)S(1)}, f32[1,2,8,384]{3,1,2,0:T(2,128)S(1)}, u32[]{:S(2)}, u32[]{:S(2)}) collective-permute-start(f32[1,2,8,384]{3,1,2,0:T(2,128)S(1)} %bitcast.255), channel_id=1, source_target_pairs={{0,4},{1,5},{2,6},{3,7},{4,0},{5,1},{6,2},{7,3},{8,12},{9,13},{10,... | collective-permute-start | bytes 73736 | tf_op jit(solution)/shard_map/ppermute | solution.py:154
  59.5 1.2 %collective-permute-done.17 = f32[1,2,8,384]{3,1,2,0:T(2,128)S(1)} collective-permute-done((f32[1,2,8,384]{3,1,2,0:T(2,128)S(1)}, f32[1,2,8,384]{3,1,2,0:T(2,128)S(1)}, u32[]{:S(2)}, u32[]{:S(2)}) %collective-permute-start.17) | collective-permute-done | bytes 24608 | tf_op jit(solution)/shard_map/ppermute | solution.py:154
  60.7 1.1 %collective-permute-done.16 = f32[1,2,8,384]{3,1,2,0:T(2,128)S(1)} collective-permute-done((f32[1,2,8,384]{3,1,2,0:T(2,128)S(1)}, f32[1,2,8,384]{3,1,2,0:T(2,128)S(1)}, u32[]{:S(2)}, u32[]{:S(2)}) %collective-permute-start.16) | collective-permute-done | bytes 24608 | tf_op jit(solution)/shard_map/ppermute | solution.py:154
  64.4 1.1 %copy.129 = bf16[2,2,384,384]{3,2,1,0:T(8,128)(2,1)} copy(bf16[2,2,384,384]{3,2,0,1:T(8,128)(2,1)S(1)} %pad_maximum_fusion) | data formatting | bytes 2359296
  66.0 1.5 %collective-permute-start.20 = (bf16[2,8,384]{2,1,0:T(8,128)(2,1)S(1)}, bf16[2,8,384]{2,1,0:T(8,128)(2,1)S(1)}, u32[]{:S(2)}, u32[]{:S(2)}) collective-permute-start(bf16[2,8,384]{2,1,0:T(8,128)(2,1)S(1)} %pad_maximum_fusion.2), channel_id=1, source_target_pairs={{0,2},{1,3},{2,0},{3,1},{4,6},{5,7},{6,4},{7,5},{8,10},{9,11},{10,... | collective-permute-start | bytes 36872 | tf_op jit(solution)/shard_map/ppermute | solution.py:138
  67.9 1.5 %collective-permute-start.22 = (f32[4,24,384]{2,1,0:T(8,128)S(1)}, f32[4,24,384]{2,1,0:T(8,128)S(1)}, u32[]{:S(2)}, u32[]{:S(2)}) collective-permute-start(f32[4,24,384]{2,1,0:T(8,128)S(1)} %dynamic-slice_bitcast_fusion.1), channel_id=1, source_target_pairs={{0,2},{1,3},{2,0},{3,1},{4,6},{5,7},{6,4},{7,5},{8,10},{9,11},{10,... | collective-permute-start | bytes 442376 | tf_op jit(solution)/shard_map/ppermute | solution.py:132
  70.1 3.8 %collective-permute-done.22 = f32[4,24,384]{2,1,0:T(8,128)S(1)} collective-permute-done((f32[4,24,384]{2,1,0:T(8,128)S(1)}, f32[4,24,384]{2,1,0:T(8,128)S(1)}, u32[]{:S(2)}, u32[]{:S(2)}) %collective-permute-start.22) | collective-permute-done | bytes 147488 | tf_op jit(solution)/shard_map/ppermute | solution.py:132
  74.0 2.0 %collective-permute-start.25 = (f32[1,2,8,384]{3,1,2,0:T(2,128)S(1)}, f32[1,2,8,384]{3,1,2,0:T(2,128)S(1)}, u32[]{:S(2)}, u32[]{:S(2)}) collective-permute-start(f32[1,2,8,384]{3,1,2,0:T(2,128)S(1)} %bitcast.252), channel_id=1, source_target_pairs={{0,12},{1,13},{2,14},{3,15},{4,8},{5,9},{6,10},{7,11},{8,4},{9,5},... | collective-permute-start | bytes 73736 | tf_op jit(solution)/shard_map/ppermute | solution.py:154
  76.0 1.0 %collective-permute-start.24 = (f32[1,2,8,384]{3,1,2,0:T(2,128)S(1)}, f32[1,2,8,384]{3,1,2,0:T(2,128)S(1)}, u32[]{:S(2)}, u32[]{:S(2)}) collective-permute-start(f32[1,2,8,384]{3,1,2,0:T(2,128)S(1)} %bitcast.254), channel_id=1, source_target_pairs={{0,8},{1,9},{2,10},{3,11},{4,12},{5,13},{6,14},{7,15},{8,0},{9,1},... | collective-permute-start | bytes 73736 | tf_op jit(solution)/shard_map/ppermute | solution.py:154
  77.0 1.6 %collective-permute-start.23 = (f32[1,2,8,384]{3,1,2,0:T(2,128)S(1)}, f32[1,2,8,384]{3,1,2,0:T(2,128)S(1)}, u32[]{:S(2)}, u32[]{:S(2)}) collective-permute-start(f32[1,2,8,384]{3,1,2,0:T(2,128)S(1)} %bitcast.256), channel_id=1, source_target_pairs={{0,4},{1,5},{2,6},{3,7},{4,0},{5,1},{6,2},{7,3},{8,12},{9,13},{10,... | collective-permute-start | bytes 73736 | tf_op jit(solution)/shard_map/ppermute | solution.py:154
  79.7 1.3 %collective-permute-done.24 = f32[1,2,8,384]{3,1,2,0:T(2,128)S(1)} collective-permute-done((f32[1,2,8,384]{3,1,2,0:T(2,128)S(1)}, f32[1,2,8,384]{3,1,2,0:T(2,128)S(1)}, u32[]{:S(2)}, u32[]{:S(2)}) %collective-permute-start.24) | collective-permute-done | bytes 24608 | tf_op jit(solution)/shard_map/ppermute | solution.py:154
  81.1 1.9 %collective-permute-done.26 = f32[2,24,384]{2,1,0:T(8,128)S(1)} collective-permute-done((f32[2,24,384]{2,1,0:T(8,128)S(1)}, f32[2,24,384]{2,1,0:T(8,128)S(1)}, u32[]{:S(2)}, u32[]{:S(2)}) %collective-permute-start.26) | collective-permute-done | bytes 73760 | tf_op jit(solution)/shard_map/ppermute | solution.py:132
  83.0 1.2 %collective-permute-start.27 = (f32[1,24,384]{2,1,0:T(8,128)S(1)}, f32[1,24,384]{2,1,0:T(8,128)S(1)}, u32[]{:S(2)}, u32[]{:S(2)}) collective-permute-start(f32[1,24,384]{2,1,0:T(8,128)S(1)} %constant_dynamic-slice_fusion), channel_id=1, source_target_pairs={{0,8},{1,9},{2,10},{3,11},{4,12},{5,13},{6,14},{7,15},{8,0},{9,1},... | collective-permute-start | bytes 110600 | tf_op jit(solution)/shard_map/ppermute | solution.py:132
  84.2 2.5 %fusion.11 = bf16[2,1440,384]{2,1,0:T(8,128)(2,1)} fusion(f32[2,1440,384]{2,1,0:T(8,128)S(1)} %fusion.40, bf16[2,1440,384]{2,1,0:T(8,128)(2,1)S(1)} %copy-done.3, bf16[1440,8,1]{0,1,2:T(8,128)(2,1)S(1)} %copy-done.5, bf16[2,8,384]{2,0,1:T(2,128)(2,1)S(1)} %fusion.66), kind=kOutput, calls=%fused_computation.20 | convolution fusion | flops 22118400 | bytes 8882688 | tf_op jit(solution)/shard_map/jfc,kf->jkc/dot_general | solution.py:266
  86.6 1.6 %collective-permute-done.27 = f32[1,24,384]{2,1,0:T(8,128)S(1)} collective-permute-done((f32[1,24,384]{2,1,0:T(8,128)S(1)}, f32[1,24,384]{2,1,0:T(8,128)S(1)}, u32[]{:S(2)}, u32[]{:S(2)}) %collective-permute-start.27) | collective-permute-done | bytes 36896 | tf_op jit(solution)/shard_map/ppermute | solution.py:132
  (126 shorter events, 24.1 us)
Async XLA Ops:
  3.4 7.7 %collective-permute-start.2 = (f32[2,8,384]{2,1,0:T(8,128)S(1)}, f32[2,8,384]{2,1,0:T(8,128)S(1)}, u32[]{:S(2)}, u32[]{:S(2)}) collective-permute-start(f32[2,8,384]{2,1,0:T(8,128)S(1)} %bitcast.236), channel_id=1, source_target_pairs={{0,3},{1,2},{2,1},{3,0},{4,7},{5,6},{6,5},{7,4},{8,11},{9,10},{10,... | collective-permute-start | bytes 73736 | tf_op jit(solution)/shard_map/ppermute | solution.py:138
  5.8 5.3 %collective-permute-start.1 = (f32[2,8,384]{2,1,0:T(8,128)S(1)}, f32[2,8,384]{2,1,0:T(8,128)}, u32[]{:S(2)}, u32[]{:S(2)}) collective-permute-start(f32[2,8,384]{2,1,0:T(8,128)S(1)} %bitcast.237), channel_id=1, source_target_pairs={{0,2},{1,3},{2,0},{3,1},{4,6},{5,7},{6,4},{7,5},{8,10},{9,11},{10,... | collective-permute-start | bytes 73736 | tf_op jit(solution)/shard_map/ppermute | solution.py:138
  6.4 4.7 %collective-permute-start = (f32[2,8,384]{2,1,0:T(8,128)S(1)}, f32[2,8,384]{2,1,0:T(8,128)}, u32[]{:S(2)}, u32[]{:S(2)}) collective-permute-start(f32[2,8,384]{2,1,0:T(8,128)S(1)} %bitcast.238), channel_id=1, source_target_pairs={{0,1},{1,0},{2,3},{3,2},{4,5},{5,4},{6,7},{7,6},{8,9},{9,8},{10,11... | collective-permute-start | bytes 73736 | tf_op jit(solution)/shard_map/ppermute | solution.py:138
  7.3 15.1 %copy-start.2 = (bf16[2,2,384,384]{3,2,1,0:T(8,128)(2,1)S(1)}, bf16[2,2,384,384]{3,2,1,0:T(8,128)(2,1)}, u32[]{:S(2)}) copy-start(bf16[2,2,384,384]{3,2,1,0:T(8,128)(2,1)} %param.13) | copy-start | bytes 3538948
  13.0 7.4 %collective-permute-start.5 = (f32[1,2,8,384]{3,1,2,0:T(2,128)}, f32[1,2,8,384]{3,1,2,0:T(2,128)S(1)}, u32[]{:S(2)}, u32[]{:S(2)}) collective-permute-start(f32[1,2,8,384]{3,1,2,0:T(2,128)} %bitcast.226), channel_id=1, source_target_pairs={{0,12},{1,13},{2,14},{3,15},{4,8},{5,9},{6,10},{7,11},{8,4},{9,5},... | collective-permute-start | bytes 73736 | tf_op jit(solution)/shard_map/ppermute | solution.py:154
  17.4 4.9 %collective-permute-start.4 = (f32[1,2,8,384]{3,1,2,0:T(2,128)}, f32[1,2,8,384]{3,1,2,0:T(2,128)S(1)}, u32[]{:S(2)}, u32[]{:S(2)}) collective-permute-start(f32[1,2,8,384]{3,1,2,0:T(2,128)} %bitcast.221), channel_id=1, source_target_pairs={{0,8},{1,9},{2,10},{3,11},{4,12},{5,13},{6,14},{7,15},{8,0},{9,1},... | collective-permute-start | bytes 73736 | tf_op jit(solution)/shard_map/ppermute | solution.py:154
  18.0 4.3 %collective-permute-start.3 = (f32[1,2,8,384]{3,1,2,0:T(2,128)}, f32[1,2,8,384]{3,1,2,0:T(2,128)S(1)}, u32[]{:S(2)}, u32[]{:S(2)}) collective-permute-start(f32[1,2,8,384]{3,1,2,0:T(2,128)} %bitcast.222), channel_id=1, source_target_pairs={{0,4},{1,5},{2,6},{3,7},{4,0},{5,1},{6,2},{7,3},{8,12},{9,13},{10,... | collective-permute-start | bytes 73736 | tf_op jit(solution)/shard_map/ppermute | solution.py:154
  23.8 3.5 %collective-permute-start.8 = (bf16[2,8,384]{2,1,0:T(8,128)(2,1)}, bf16[2,8,384]{2,1,0:T(8,128)(2,1)}, u32[]{:S(2)}, u32[]{:S(2)}) collective-permute-start(bf16[2,8,384]{2,1,0:T(8,128)(2,1)} %pad_maximum_fusion.1), channel_id=1, source_target_pairs={{0,3},{1,2},{2,1},{3,0},{4,7},{5,6},{6,5},{7,4},{8,11},{9,10},{10,... | collective-permute-start | bytes 36872 | tf_op jit(solution)/shard_map/ppermute | solution.py:138
  23.9 4.0 %collective-permute-start.7 = (bf16[2,8,384]{2,1,0:T(8,128)(2,1)}, bf16[2,8,384]{2,1,0:T(8,128)(2,1)}, u32[]{:S(2)}, u32[]{:S(2)}) collective-permute-start(bf16[2,8,384]{2,1,0:T(8,128)(2,1)} %pad_maximum_fusion.1), channel_id=1, source_target_pairs={{0,2},{1,3},{2,0},{3,1},{4,6},{5,7},{6,4},{7,5},{8,10},{9,11},{10,... | collective-permute-start | bytes 36872 | tf_op jit(solution)/shard_map/ppermute | solution.py:138
  25.4 2.5 %collective-permute-start.6 = (bf16[2,8,384]{2,1,0:T(8,128)(2,1)}, bf16[2,8,384]{2,1,0:T(8,128)(2,1)}, u32[]{:S(2)}, u32[]{:S(2)}) collective-permute-start(bf16[2,8,384]{2,1,0:T(8,128)(2,1)} %pad_maximum_fusion.1), channel_id=1, source_target_pairs={{0,1},{1,0},{2,3},{3,2},{4,5},{5,4},{6,7},{7,6},{8,9},{9,8},{10,11... | collective-permute-start | bytes 36872 | tf_op jit(solution)/shard_map/ppermute | solution.py:138
  30.3 11.3 %collective-permute-start.11 = (f32[1,2,8,384]{3,1,2,0:T(2,128)}, f32[1,2,8,384]{3,1,2,0:T(2,128)}, u32[]{:S(2)}, u32[]{:S(2)}) collective-permute-start(f32[1,2,8,384]{3,1,2,0:T(2,128)} %bitcast.225), channel_id=1, source_target_pairs={{0,12},{1,13},{2,14},{3,15},{4,8},{5,9},{6,10},{7,11},{8,4},{9,5},... | collective-permute-start | bytes 73736 | tf_op jit(solution)/shard_map/ppermute | solution.py:154
  33.1 8.4 %collective-permute-start.10 = (f32[1,2,8,384]{3,1,2,0:T(2,128)}, f32[1,2,8,384]{3,1,2,0:T(2,128)}, u32[]{:S(2)}, u32[]{:S(2)}) collective-permute-start(f32[1,2,8,384]{3,1,2,0:T(2,128)} %bitcast.219), channel_id=1, source_target_pairs={{0,8},{1,9},{2,10},{3,11},{4,12},{5,13},{6,14},{7,15},{8,0},{9,1},... | collective-permute-start | bytes 73736 | tf_op jit(solution)/shard_map/ppermute | solution.py:154
  34.1 8.3 %copy-start.5 = (bf16[1440,8,1]{0,1,2:T(8,128)(2,1)S(1)}, bf16[1440,8,1]{0,1,2:T(8,128)(2,1)}, u32[]{:S(2)}) copy-start(bf16[1440,8,1]{0,1,2:T(8,128)(2,1)} %constant.116) | copy-start | bytes 69124
  34.1 7.4 %collective-permute-start.9 = (f32[1,2,8,384]{3,1,2,0:T(2,128)}, f32[1,2,8,384]{3,1,2,0:T(2,128)}, u32[]{:S(2)}, u32[]{:S(2)}) collective-permute-start(f32[1,2,8,384]{3,1,2,0:T(2,128)} %bitcast.220), channel_id=1, source_target_pairs={{0,4},{1,5},{2,6},{3,7},{4,0},{5,1},{6,2},{7,3},{8,12},{9,13},{10,... | collective-permute-start | bytes 73736 | tf_op jit(solution)/shard_map/ppermute | solution.py:154
  50.3 11.8 %copy-start.7 = (bf16[2,4,384]{2,0,1:T(2,128)(2,1)S(1)}, bf16[2,4,384]{2,0,1:T(2,128)(2,1)}, u32[]{:S(2)}) copy-start(bf16[2,4,384]{2,0,1:T(2,128)(2,1)} %copy-done.6) | copy-start | bytes 18436
  50.3 3.5 %collective-permute-start.14 = (f32[2,8,384]{2,1,0:T(8,128)S(1)}, f32[2,8,384]{2,1,0:T(8,128)S(1)}, u32[]{:S(2)}, u32[]{:S(2)}) collective-permute-start(f32[2,8,384]{2,1,0:T(8,128)S(1)} %bitcast.240), channel_id=1, source_target_pairs={{0,3},{1,2},{2,1},{3,0},{4,7},{5,6},{6,5},{7,4},{8,11},{9,10},{10,... | collective-permute-start | bytes 73736 | tf_op jit(solution)/shard_map/ppermute | solution.py:138
  50.4 3.9 %collective-permute-start.13 = (f32[2,8,384]{2,1,0:T(8,128)S(1)}, f32[2,8,384]{2,1,0:T(8,128)S(1)}, u32[]{:S(2)}, u32[]{:S(2)}) collective-permute-start(f32[2,8,384]{2,1,0:T(8,128)S(1)} %bitcast.241), channel_id=1, source_target_pairs={{0,2},{1,3},{2,0},{3,1},{4,6},{5,7},{6,4},{7,5},{8,10},{9,11},{10,... | collective-permute-start | bytes 73736 | tf_op jit(solution)/shard_map/ppermute | solution.py:138
  51.9 2.3 %collective-permute-start.12 = (f32[2,8,384]{2,1,0:T(8,128)S(1)}, f32[2,8,384]{2,1,0:T(8,128)S(1)}, u32[]{:S(2)}, u32[]{:S(2)}) collective-permute-start(f32[2,8,384]{2,1,0:T(8,128)S(1)} %bitcast.242), channel_id=1, source_target_pairs={{0,1},{1,0},{2,3},{3,2},{4,5},{5,4},{6,7},{7,6},{8,9},{9,8},{10,11... | collective-permute-start | bytes 73736 | tf_op jit(solution)/shard_map/ppermute | solution.py:138
  54.8 5.9 %collective-permute-start.17 = (f32[1,2,8,384]{3,1,2,0:T(2,128)S(1)}, f32[1,2,8,384]{3,1,2,0:T(2,128)S(1)}, u32[]{:S(2)}, u32[]{:S(2)}) collective-permute-start(f32[1,2,8,384]{3,1,2,0:T(2,128)S(1)} %bitcast.251), channel_id=1, source_target_pairs={{0,12},{1,13},{2,14},{3,15},{4,8},{5,9},{6,10},{7,11},{8,4},{9,5},... | collective-permute-start | bytes 73736 | tf_op jit(solution)/shard_map/ppermute | solution.py:154
  57.0 4.8 %collective-permute-start.16 = (f32[1,2,8,384]{3,1,2,0:T(2,128)S(1)}, f32[1,2,8,384]{3,1,2,0:T(2,128)S(1)}, u32[]{:S(2)}, u32[]{:S(2)}) collective-permute-start(f32[1,2,8,384]{3,1,2,0:T(2,128)S(1)} %bitcast.253), channel_id=1, source_target_pairs={{0,8},{1,9},{2,10},{3,11},{4,12},{5,13},{6,14},{7,15},{8,0},{9,1},... | collective-permute-start | bytes 73736 | tf_op jit(solution)/shard_map/ppermute | solution.py:154
  57.1 4.7 %collective-permute-start.15 = (f32[1,2,8,384]{3,1,2,0:T(2,128)S(1)}, f32[1,2,8,384]{3,1,2,0:T(2,128)S(1)}, u32[]{:S(2)}, u32[]{:S(2)}) collective-permute-start(f32[1,2,8,384]{3,1,2,0:T(2,128)S(1)} %bitcast.255), channel_id=1, source_target_pairs={{0,4},{1,5},{2,6},{3,7},{4,0},{5,1},{6,2},{7,3},{8,12},{9,13},{10,... | collective-permute-start | bytes 73736 | tf_op jit(solution)/shard_map/ppermute | solution.py:154
  59.4 6.4 %collective-permute-start.18 = (f32[8,24,384]{2,1,0:T(8,128)S(1)}, f32[8,24,384]{2,1,0:T(8,128)S(1)}, u32[]{:S(2)}, u32[]{:S(2)}) collective-permute-start(f32[8,24,384]{2,1,0:T(8,128)S(1)} %dynamic-slice_bitcast_fusion), channel_id=1, source_target_pairs={{0,1},{1,0},{2,3},{3,2},{4,5},{5,4},{6,7},{7,6},{8,9},{9,8},{10,11... | collective-permute-start | bytes 884744 | tf_op jit(solution)/shard_map/ppermute | solution.py:132
  65.6 18.6 %copy-start.3 = (bf16[2,1440,384]{2,1,0:T(8,128)(2,1)S(1)}, bf16[2,1440,384]{2,1,0:T(8,128)(2,1)}, u32[]{:S(2)}) copy-start(bf16[2,1440,384]{2,1,0:T(8,128)(2,1)} %param.11) | copy-start | bytes 6635524
  65.9 3.5 %collective-permute-start.21 = (bf16[2,8,384]{2,1,0:T(8,128)(2,1)S(1)}, bf16[2,8,384]{2,1,0:T(8,128)(2,1)S(1)}, u32[]{:S(2)}, u32[]{:S(2)}) collective-permute-start(bf16[2,8,384]{2,1,0:T(8,128)(2,1)S(1)} %pad_maximum_fusion.2), channel_id=1, source_target_pairs={{0,3},{1,2},{2,1},{3,0},{4,7},{5,6},{6,5},{7,4},{8,11},{9,10},{10,... | collective-permute-start | bytes 36872 | tf_op jit(solution)/shard_map/ppermute | solution.py:138
  66.0 3.8 %collective-permute-start.20 = (bf16[2,8,384]{2,1,0:T(8,128)(2,1)S(1)}, bf16[2,8,384]{2,1,0:T(8,128)(2,1)S(1)}, u32[]{:S(2)}, u32[]{:S(2)}) collective-permute-start(bf16[2,8,384]{2,1,0:T(8,128)(2,1)S(1)} %pad_maximum_fusion.2), channel_id=1, source_target_pairs={{0,2},{1,3},{2,0},{3,1},{4,6},{5,7},{6,4},{7,5},{8,10},{9,11},{10,... | collective-permute-start | bytes 36872 | tf_op jit(solution)/shard_map/ppermute | solution.py:138
  67.5 2.2 %collective-permute-start.19 = (bf16[2,8,384]{2,1,0:T(8,128)(2,1)S(1)}, bf16[2,8,384]{2,1,0:T(8,128)(2,1)S(1)}, u32[]{:S(2)}, u32[]{:S(2)}) collective-permute-start(bf16[2,8,384]{2,1,0:T(8,128)(2,1)S(1)} %pad_maximum_fusion.2), channel_id=1, source_target_pairs={{0,1},{1,0},{2,3},{3,2},{4,5},{5,4},{6,7},{7,6},{8,9},{9,8},{10,11... | collective-permute-start | bytes 36872 | tf_op jit(solution)/shard_map/ppermute | solution.py:138
  67.9 6.0 %collective-permute-start.22 = (f32[4,24,384]{2,1,0:T(8,128)S(1)}, f32[4,24,384]{2,1,0:T(8,128)S(1)}, u32[]{:S(2)}, u32[]{:S(2)}) collective-permute-start(f32[4,24,384]{2,1,0:T(8,128)S(1)} %dynamic-slice_bitcast_fusion.1), channel_id=1, source_target_pairs={{0,2},{1,3},{2,0},{3,1},{4,6},{5,7},{6,4},{7,5},{8,10},{9,11},{10,... | collective-permute-start | bytes 442376 | tf_op jit(solution)/shard_map/ppermute | solution.py:132
  74.0 5.7 %collective-permute-start.25 = (f32[1,2,8,384]{3,1,2,0:T(2,128)S(1)}, f32[1,2,8,384]{3,1,2,0:T(2,128)S(1)}, u32[]{:S(2)}, u32[]{:S(2)}) collective-permute-start(f32[1,2,8,384]{3,1,2,0:T(2,128)S(1)} %bitcast.252), channel_id=1, source_target_pairs={{0,12},{1,13},{2,14},{3,15},{4,8},{5,9},{6,10},{7,11},{8,4},{9,5},... | collective-permute-start | bytes 73736 | tf_op jit(solution)/shard_map/ppermute | solution.py:154
  76.0 5.0 %collective-permute-start.24 = (f32[1,2,8,384]{3,1,2,0:T(2,128)S(1)}, f32[1,2,8,384]{3,1,2,0:T(2,128)S(1)}, u32[]{:S(2)}, u32[]{:S(2)}) collective-permute-start(f32[1,2,8,384]{3,1,2,0:T(2,128)S(1)} %bitcast.254), channel_id=1, source_target_pairs={{0,8},{1,9},{2,10},{3,11},{4,12},{5,13},{6,14},{7,15},{8,0},{9,1},... | collective-permute-start | bytes 73736 | tf_op jit(solution)/shard_map/ppermute | solution.py:154
  77.0 4.0 %collective-permute-start.23 = (f32[1,2,8,384]{3,1,2,0:T(2,128)S(1)}, f32[1,2,8,384]{3,1,2,0:T(2,128)S(1)}, u32[]{:S(2)}, u32[]{:S(2)}) collective-permute-start(f32[1,2,8,384]{3,1,2,0:T(2,128)S(1)} %bitcast.256), channel_id=1, source_target_pairs={{0,4},{1,5},{2,6},{3,7},{4,0},{5,1},{6,2},{7,3},{8,12},{9,13},{10,... | collective-permute-start | bytes 73736 | tf_op jit(solution)/shard_map/ppermute | solution.py:154
  78.6 4.4 %collective-permute-start.26 = (f32[2,24,384]{2,1,0:T(8,128)S(1)}, f32[2,24,384]{2,1,0:T(8,128)S(1)}, u32[]{:S(2)}, u32[]{:S(2)}) collective-permute-start(f32[2,24,384]{2,1,0:T(8,128)S(1)} %dynamic-slice_bitcast_fusion.2), channel_id=1, source_target_pairs={{0,4},{1,5},{2,6},{3,7},{4,0},{5,1},{6,2},{7,3},{8,12},{9,13},{10,... | collective-permute-start | bytes 221192 | tf_op jit(solution)/shard_map/ppermute | solution.py:132
  83.0 5.3 %collective-permute-start.27 = (f32[1,24,384]{2,1,0:T(8,128)S(1)}, f32[1,24,384]{2,1,0:T(8,128)S(1)}, u32[]{:S(2)}, u32[]{:S(2)}) collective-permute-start(f32[1,24,384]{2,1,0:T(8,128)S(1)} %constant_dynamic-slice_fusion), channel_id=1, source_target_pairs={{0,8},{1,9},{2,10},{3,11},{4,12},{5,13},{6,14},{7,15},{8,0},{9,1},... | collective-permute-start | bytes 110600 | tf_op jit(solution)/shard_map/ppermute | solution.py:132
  (4 other events, 17.1 us)

commit v11 on v8

--- a/solution.py
+++ b/solution.py
@@ -109,7 +109,7 @@
     cur = part
     low = 0
     while low < bits:
-        width = min(step, bits - low)
+        width = min(step if low < 2 else 2, bits - low)
         fan = 1 << width
         view = cur.reshape((cur.shape[0] // fan, fan) + cur.shape[1:])
         mine = (me >> low) & (fan - 1)

time: 84.3 us -> 85.9 us (1.019)
  starting transfers between devices: 27 us -> 29.5 us
  waiting for transfers between devices: 14.5 us -> 13.6 us
    ppermute x4 -> x5, starting transfers between devices: 2.73 us -> 5.22 us  [xor_reduce_scatter(): lax.ppermute(sent, axis_name, [(i, i ^ mask) for i in range(groups)])]
    ppermute x4 -> x5, waiting for transfers between devices: 4.5 us -> 4.4 us  [xor_reduce_scatter(): lax.ppermute(sent, axis_name, [(i, i ^ mask) for i in range(groups)])]
  transfers between devices with their start and end apart: 28 -> 29, of which waited for: 10 -> 9; matrix products, arithmetic and copies ran while one was open for 27% -> 27% of each run, Pallas kernels for 0% -> 0%
where the time goes in v11:
time: 85.9 us; the launch traced here: 85.4 us
  starting transfers between devices  29.5 us (34%)
  matrix products  22.2 us (26%)
  local copies, waits for them, and re-layouts  15.4 us (18%)
  waiting for transfers between devices  13.6 us (16%)
  other arithmetic  3.61 us (4%)
  between operations  1.1 us (1%)
    ppermute x12, starting transfers between devices, xor_exchange(): lax.ppermute(view[:, k], axis_name, [(i, i ^ mask) for i in range(groups)])  15.2 us
    ppermute x12, starting transfers between devices, xor_exchange(): lax.ppermute(values, axis_name, [(i, i ^ k) for i in range(groups)])  9.07 us
    unnamed x35, local copies, waits for them, and re-layouts  8.01 us
    ppermute x12, waiting for transfers between devices, xor_exchange(): lax.ppermute(view[:, k], axis_name, [(i, i ^ mask) for i in range(groups)])  7.95 us
    dot_general x1, matrix products, local(): jnp.einsum('jfc,kf->jkc', grid_modes, fourier, preferred_element_type=jnp...  5.99 us
    ppermute x5, starting transfers between devices, xor_reduce_scatter(): lax.ppermute(sent, axis_name, [(i, i ^ mask) for i in range(groups)])  5.22 us
    dot_general x1, matrix products, local(): jnp.einsum('jkc,cd->jkd', activations, skip_weight, preferred_element_typ...  4.52 us
    ppermute x5, waiting for transfers between devices, xor_reduce_scatter(): lax.ppermute(sent, axis_name, [(i, i ^ mask) for i in range(groups)])  4.4 us
  transfers between devices with their start and end apart: 29, of which 9 were waited for; matrix products, arithmetic and copies ran while one was open for 27% of the time, Pallas kernels for 0%

profile of v11, /device:TPU:0, one launch (start us, length us, event | category | flops | bytes accessed | tf_op | source)
XLA Modules:
  0.0 85.4 jit_solution(18049595706891628965)
XLA Ops:
  0.7 1.6 %copy-done = bf16[2,1440,384]{2,1,0:T(8,128)(2,1)S(1)} copy-done((bf16[2,1440,384]{2,1,0:T(8,128)(2,1)S(1)}, bf16[2,1440,384]{2,1,0:T(8,128)(2,1)}, u32[]{:S(2)}) %copy-start) | copy-done | bytes 2211864
  2.3 1.1 %fusion.100 = f32[8,2,384]{2,0,1:T(8,128)S(1)} fusion(bf16[1440,8,1]{0,1,2:T(8,128)(2,1)} %constant.110, bf16[2,1440,384]{2,1,0:T(8,128)(2,1)S(1)} %copy-done), kind=kOutput, calls=%fused_computation.163 | convolution fusion | flops 17694720 | bytes 2259456 | tf_op jit(solution)/shard_map/jkc,kf->jfc/dot_general | solution.py:224
  3.4 3.0 %collective-permute-start.1 = (f32[2,8,384]{2,1,0:T(8,128)S(1)}, f32[2,8,384]{2,1,0:T(8,128)S(1)}, u32[]{:S(2)}, u32[]{:S(2)}) collective-permute-start(f32[2,8,384]{2,1,0:T(8,128)S(1)} %bitcast.230), channel_id=1, source_target_pairs={{0,2},{1,3},{2,0},{3,1},{4,6},{5,7},{6,4},{7,5},{8,10},{9,11},{10,... | collective-permute-start | bytes 73736 | tf_op jit(solution)/shard_map/ppermute | solution.py:129
  8.6 1.6 %gather_fusion = f32[64,16]{1,0:T(8,128)S(1)} fusion(f32[32,32,16]{2,1,0:T(8,128)} %constant.83, s32[64]{0:T(128)S(1)} %reshape.189), kind=kCustom, calls=%fused_computation.2 | custom fusion | bytes 8704 | tf_op jit(solution)/shard_map/gather | solution.py:211
  14.2 3.1 %collective-permute-start.4 = (f32[1,2,8,384]{3,1,2,0:T(2,128)}, f32[1,2,8,384]{3,1,2,0:T(2,128)S(1)}, u32[]{:S(2)}, u32[]{:S(2)}) collective-permute-start(f32[1,2,8,384]{3,1,2,0:T(2,128)} %bitcast.218), channel_id=1, source_target_pairs={{0,8},{1,9},{2,10},{3,11},{4,12},{5,13},{6,14},{7,15},{8,0},{9,1},... | collective-permute-start | bytes 73736 | tf_op jit(solution)/shard_map/ppermute | solution.py:141
  17.3 1.3 %collective-permute-start.5 = (f32[1,2,8,384]{3,1,2,0:T(2,128)}, f32[1,2,8,384]{3,1,2,0:T(2,128)S(1)}, u32[]{:S(2)}, u32[]{:S(2)}) collective-permute-start(f32[1,2,8,384]{3,1,2,0:T(2,128)} %bitcast.223), channel_id=1, source_target_pairs={{0,12},{1,13},{2,14},{3,15},{4,8},{5,9},{6,10},{7,11},{8,4},{9,5},... | collective-permute-start | bytes 73736 | tf_op jit(solution)/shard_map/ppermute | solution.py:141
  19.1 1.6 %gather_fusion.1 = f32[64,16]{1,0:T(8,128)S(1)} fusion(f32[32,32,16]{2,1,0:T(8,128)} %constant.83, s32[64]{0:T(128)S(1)} %reshape.195), kind=kCustom, calls=%fused_computation.3 | custom fusion | bytes 8704 | tf_op jit(solution)/shard_map/gather | solution.py:214
  20.7 2.5 %collective-permute-done.5 = f32[1,2,8,384]{3,1,2,0:T(2,128)S(1)} collective-permute-done((f32[1,2,8,384]{3,1,2,0:T(2,128)}, f32[1,2,8,384]{3,1,2,0:T(2,128)S(1)}, u32[]{:S(2)}, u32[]{:S(2)}) %collective-permute-start.5) | collective-permute-done | bytes 24608 | tf_op jit(solution)/shard_map/ppermute | solution.py:141
  24.6 1.6 %collective-permute-start.7 = (bf16[2,8,384]{2,1,0:T(8,128)(2,1)}, bf16[2,8,384]{2,1,0:T(8,128)(2,1)S(1)}, u32[]{:S(2)}, u32[]{:S(2)}) collective-permute-start(bf16[2,8,384]{2,1,0:T(8,128)(2,1)} %pad_maximum_fusion.1), channel_id=1, source_target_pairs={{0,2},{1,3},{2,0},{3,1},{4,6},{5,7},{6,4},{7,5},{8,10},{9,11},{10,... | collective-permute-start | bytes 36872 | tf_op jit(solution)/shard_map/ppermute | solution.py:129
  31.4 1.2 %collective-permute-start.10 = (f32[1,2,8,384]{3,1,2,0:T(2,128)}, f32[1,2,8,384]{3,1,2,0:T(2,128)}, u32[]{:S(2)}, u32[]{:S(2)}) collective-permute-start(f32[1,2,8,384]{3,1,2,0:T(2,128)} %bitcast.216), channel_id=1, source_target_pairs={{0,8},{1,9},{2,10},{3,11},{4,12},{5,13},{6,14},{7,15},{8,0},{9,1},... | collective-permute-start | bytes 73736 | tf_op jit(solution)/shard_map/ppermute | solution.py:141
  32.6 0.9 %collective-permute-start.11 = (f32[1,2,8,384]{3,1,2,0:T(2,128)}, f32[1,2,8,384]{3,1,2,0:T(2,128)}, u32[]{:S(2)}, u32[]{:S(2)}) collective-permute-start(f32[1,2,8,384]{3,1,2,0:T(2,128)} %bitcast.222), channel_id=1, source_target_pairs={{0,12},{1,13},{2,14},{3,15},{4,8},{5,9},{6,10},{7,11},{8,4},{9,5},... | collective-permute-start | bytes 73736 | tf_op jit(solution)/shard_map/ppermute | solution.py:141
  33.6 1.3 %collective-permute-start.9 = (f32[1,2,8,384]{3,1,2,0:T(2,128)}, f32[1,2,8,384]{3,1,2,0:T(2,128)}, u32[]{:S(2)}, u32[]{:S(2)}) collective-permute-start(f32[1,2,8,384]{3,1,2,0:T(2,128)} %bitcast.217), channel_id=1, source_target_pairs={{0,4},{1,5},{2,6},{3,7},{4,0},{5,1},{6,2},{7,3},{8,12},{9,13},{10,... | collective-permute-start | bytes 73736 | tf_op jit(solution)/shard_map/ppermute | solution.py:141
  34.9 4.5 %fusion.42 = f32[2,1440,384]{2,1,0:T(8,128)} fusion(bf16[2,1440,384]{2,1,0:T(8,128)(2,1)S(1)} %copy-done, bf16[384,384]{1,0:T(8,128)(2,1)} %param.12), kind=kOutput, calls=%fused_computation.64 | convolution fusion | flops 849346560 | bytes 6930432 | tf_op jit(solution)/shard_map/jkc,cd->jkd/dot_general | solution.py:230
  41.4 6.0 %fusion.6 = bf16[2,1440,384]{2,1,0:T(8,128)(2,1)S(1)} fusion(bf16[2,1440,384]{2,1,0:T(8,128)(2,1)} %param.11, f32[2,1440,384]{2,1,0:T(8,128)} %fusion.42, bf16[1440,8,1]{0,1,2:T(8,128)(2,1)S(1)} %copy-done.5, bf16[2,8,384]{2,0,1:T(2,128)(2,1)S(1)} %fusion.68), kind=kOutput, calls=%fused_computation.15 | convolution fusion | flops 42024960 | bytes 8882688 | tf_op jit(solution)/shard_map/jfc,kf->jkc/dot_general | solution.py:229
  47.8 1.5 %collective-permute-start.13 = (f32[2,8,384]{2,1,0:T(8,128)S(1)}, f32[2,8,384]{2,1,0:T(8,128)S(1)}, u32[]{:S(2)}, u32[]{:S(2)}) collective-permute-start(f32[2,8,384]{2,1,0:T(8,128)S(1)} %bitcast.234), channel_id=1, source_target_pairs={{0,2},{1,3},{2,0},{3,1},{4,6},{5,7},{6,4},{7,5},{8,10},{9,11},{10,... | collective-permute-start | bytes 73736 | tf_op jit(solution)/shard_map/ppermute | solution.py:129
  50.0 1.5 %fusion.40 = f32[2,1440,384]{2,1,0:T(8,128)S(1)} fusion(bf16[2,1440,384]{2,1,0:T(8,128)(2,1)S(1)} %fusion.6, bf16[384,384]{1,0:T(8,128)(2,1)S(1)} %copy-done.4), kind=kOutput, calls=%fused_computation.62 | convolution fusion | flops 849346560 | bytes 6930432 | tf_op jit(solution)/shard_map/jkd,cd->jkc/dot_general | solution.py:237
  51.5 1.4 %fusion.102 = f32[384,384,1]{0,1,2:T(8,128)S(1)} fusion(bf16[2,1440,384]{2,1,0:T(8,128)(2,1)S(1)} %fusion.6, bf16[2,1440,384]{2,1,0:T(8,128)(2,1)S(1)} %copy-done), kind=kOutput, calls=%fused_computation.165 | convolution fusion | flops 849346560 | bytes 5013504 | tf_op jit(solution)/shard_map/jkc,jkd->cd/dot_general | solution.py:234
  53.5 2.2 %collective-permute-start.16 = (f32[1,2,8,384]{3,1,2,0:T(2,128)S(1)}, f32[1,2,8,384]{3,1,2,0:T(2,128)S(1)}, u32[]{:S(2)}, u32[]{:S(2)}) collective-permute-start(f32[1,2,8,384]{3,1,2,0:T(2,128)S(1)} %bitcast.251), channel_id=1, source_target_pairs={{0,8},{1,9},{2,10},{3,11},{4,12},{5,13},{6,14},{7,15},{8,0},{9,1},... | collective-permute-start | bytes 73736 | tf_op jit(solution)/shard_map/ppermute | solution.py:141
  55.7 0.9 %collective-permute-start.17 = (f32[1,2,8,384]{3,1,2,0:T(2,128)S(1)}, f32[1,2,8,384]{3,1,2,0:T(2,128)S(1)}, u32[]{:S(2)}, u32[]{:S(2)}) collective-permute-start(f32[1,2,8,384]{3,1,2,0:T(2,128)S(1)} %bitcast.250), channel_id=1, source_target_pairs={{0,12},{1,13},{2,14},{3,15},{4,8},{5,9},{6,10},{7,11},{8,4},{9,5},... | collective-permute-start | bytes 73736 | tf_op jit(solution)/shard_map/ppermute | solution.py:141
  57.2 1.6 %collective-permute-done.16 = f32[1,2,8,384]{3,1,2,0:T(2,128)S(1)} collective-permute-done((f32[1,2,8,384]{3,1,2,0:T(2,128)S(1)}, f32[1,2,8,384]{3,1,2,0:T(2,128)S(1)}, u32[]{:S(2)}, u32[]{:S(2)}) %collective-permute-start.16) | collective-permute-done | bytes 24608 | tf_op jit(solution)/shard_map/ppermute | solution.py:141
  58.8 2.5 %collective-permute-done.17 = f32[1,2,8,384]{3,1,2,0:T(2,128)S(1)} collective-permute-done((f32[1,2,8,384]{3,1,2,0:T(2,128)S(1)}, f32[1,2,8,384]{3,1,2,0:T(2,128)S(1)}, u32[]{:S(2)}, u32[]{:S(2)}) %collective-permute-start.17) | collective-permute-done | bytes 24608 | tf_op jit(solution)/shard_map/ppermute | solution.py:141
  62.6 1.6 %collective-permute-start.19 = (bf16[2,8,384]{2,1,0:T(8,128)(2,1)S(1)}, bf16[2,8,384]{2,1,0:T(8,128)(2,1)S(1)}, u32[]{:S(2)}, u32[]{:S(2)}) collective-permute-start(bf16[2,8,384]{2,1,0:T(8,128)(2,1)S(1)} %pad_maximum_fusion.2), channel_id=1, source_target_pairs={{0,2},{1,3},{2,0},{3,1},{4,6},{5,7},{6,4},{7,5},{8,10},{9,11},{10,... | collective-permute-start | bytes 36872 | tf_op jit(solution)/shard_map/ppermute | solution.py:129
  66.2 1.1 %copy.88 = bf16[2,2,384,384]{3,2,1,0:T(8,128)(2,1)} copy(bf16[2,2,384,384]{3,2,0,1:T(8,128)(2,1)S(1)} %pad_maximum_fusion) | data formatting | bytes 2359296
  68.7 1.3 %collective-permute-start.23 = (f32[1,2,8,384]{3,1,2,0:T(2,128)S(1)}, f32[1,2,8,384]{3,1,2,0:T(2,128)S(1)}, u32[]{:S(2)}, u32[]{:S(2)}) collective-permute-start(f32[1,2,8,384]{3,1,2,0:T(2,128)S(1)} %bitcast.247), channel_id=1, source_target_pairs={{0,12},{1,13},{2,14},{3,15},{4,8},{5,9},{6,10},{7,11},{8,4},{9,5},... | collective-permute-start | bytes 73736 | tf_op jit(solution)/shard_map/ppermute | solution.py:141
  69.9 1.4 %collective-permute-start.21 = (f32[1,2,8,384]{3,1,2,0:T(2,128)S(1)}, f32[1,2,8,384]{3,1,2,0:T(2,128)S(1)}, u32[]{:S(2)}, u32[]{:S(2)}) collective-permute-start(f32[1,2,8,384]{3,1,2,0:T(2,128)S(1)} %bitcast.246), channel_id=1, source_target_pairs={{0,4},{1,5},{2,6},{3,7},{4,0},{5,1},{6,2},{7,3},{8,12},{9,13},{10,... | collective-permute-start | bytes 73736 | tf_op jit(solution)/shard_map/ppermute | solution.py:141
  71.4 1.6 %collective-permute-start.25 = (f32[4,24,384]{2,1,0:T(8,128)S(1)}, f32[4,24,384]{2,1,0:T(8,128)S(1)}, u32[]{:S(2)}, u32[]{:S(2)}) collective-permute-start(f32[4,24,384]{2,1,0:T(8,128)S(1)} %dynamic-slice_bitcast_fusion.1), channel_id=1, source_target_pairs={{0,2},{1,3},{2,0},{3,1},{4,6},{5,7},{6,4},{7,5},{8,10},{9,11},{10,... | collective-permute-start | bytes 442376 | tf_op jit(solution)/shard_map/ppermute | solution.py:120
  73.0 1.3 %collective-permute-done.23 = f32[1,2,8,384]{3,1,2,0:T(2,128)S(1)} collective-permute-done((f32[1,2,8,384]{3,1,2,0:T(2,128)S(1)}, f32[1,2,8,384]{3,1,2,0:T(2,128)S(1)}, u32[]{:S(2)}, u32[]{:S(2)}) %collective-permute-start.23) | collective-permute-done | bytes 24608 | tf_op jit(solution)/shard_map/ppermute | solution.py:141
  74.3 2.3 %collective-permute-done.25 = f32[4,24,384]{2,1,0:T(8,128)S(1)} collective-permute-done((f32[4,24,384]{2,1,0:T(8,128)S(1)}, f32[4,24,384]{2,1,0:T(8,128)S(1)}, u32[]{:S(2)}, u32[]{:S(2)}) %collective-permute-start.25) | collective-permute-done | bytes 147488 | tf_op jit(solution)/shard_map/ppermute | solution.py:120
  76.7 1.0 %collective-permute-start.26 = (f32[1,24,384]{2,1,0:T(8,128)S(1)}, f32[1,24,384]{2,1,0:T(8,128)S(1)}, u32[]{:S(2)}, u32[]{:S(2)}) collective-permute-start(f32[1,24,384]{2,1,0:T(8,128)S(1)} %get-tuple-element.10), channel_id=1, source_target_pairs={{0,4},{1,5},{2,6},{3,7},{4,0},{5,1},{6,2},{7,3},{8,12},{9,13},{10,... | collective-permute-start | bytes 110600 | tf_op jit(solution)/shard_map/ppermute | solution.py:120
  77.7 2.3 %collective-permute-start.28 = (f32[1,24,384]{2,1,0:T(8,128)S(1)}, f32[1,24,384]{2,1,0:T(8,128)S(1)}, u32[]{:S(2)}, u32[]{:S(2)}) collective-permute-start(f32[1,24,384]{2,1,0:T(8,128)S(1)} %get-tuple-element.11), channel_id=1, source_target_pairs={{0,12},{1,13},{2,14},{3,15},{4,8},{5,9},{6,10},{7,11},{8,4},{9,5},... | collective-permute-start | bytes 110600 | tf_op jit(solution)/shard_map/ppermute | solution.py:120
  80.2 2.5 %fusion.11 = bf16[2,1440,384]{2,1,0:T(8,128)(2,1)} fusion(f32[2,1440,384]{2,1,0:T(8,128)S(1)} %fusion.40, bf16[2,1440,384]{2,1,0:T(8,128)(2,1)S(1)} %copy-done.3, bf16[1440,8,1]{0,1,2:T(8,128)(2,1)S(1)} %copy-done.5, bf16[2,8,384]{2,0,1:T(2,128)(2,1)S(1)} %fusion.66), kind=kOutput, calls=%fused_computation.20 | convolution fusion | flops 22118400 | bytes 8882688 | tf_op jit(solution)/shard_map/jfc,kf->jkc/dot_general | solution.py:243
  83.4 1.4 %collective-permute-done.27 = f32[1,24,384]{2,1,0:T(8,128)S(1)} collective-permute-done((f32[1,24,384]{2,1,0:T(8,128)S(1)}, f32[1,24,384]{2,1,0:T(8,128)S(1)}, u32[]{:S(2)}, u32[]{:S(2)}) %collective-permute-start.27) | collective-permute-done | bytes 36896 | tf_op jit(solution)/shard_map/ppermute | solution.py:120
  (128 shorter events, 23.6 us)
Async XLA Ops:
  3.4 7.7 %collective-permute-start.1 = (f32[2,8,384]{2,1,0:T(8,128)S(1)}, f32[2,8,384]{2,1,0:T(8,128)S(1)}, u32[]{:S(2)}, u32[]{:S(2)}) collective-permute-start(f32[2,8,384]{2,1,0:T(8,128)S(1)} %bitcast.230), channel_id=1, source_target_pairs={{0,2},{1,3},{2,0},{3,1},{4,6},{5,7},{6,4},{7,5},{8,10},{9,11},{10,... | collective-permute-start | bytes 73736 | tf_op jit(solution)/shard_map/ppermute | solution.py:129
  6.4 4.8 %collective-permute-start = (f32[2,8,384]{2,1,0:T(8,128)S(1)}, f32[2,8,384]{2,1,0:T(8,128)}, u32[]{:S(2)}, u32[]{:S(2)}) collective-permute-start(f32[2,8,384]{2,1,0:T(8,128)S(1)} %bitcast.231), channel_id=1, source_target_pairs={{0,1},{1,0},{2,3},{3,2},{4,5},{5,4},{6,7},{7,6},{8,9},{9,8},{10,11... | collective-permute-start | bytes 73736 | tf_op jit(solution)/shard_map/ppermute | solution.py:129
  6.4 4.8 %collective-permute-start.2 = (f32[2,8,384]{2,1,0:T(8,128)S(1)}, f32[2,8,384]{2,1,0:T(8,128)}, u32[]{:S(2)}, u32[]{:S(2)}) collective-permute-start(f32[2,8,384]{2,1,0:T(8,128)S(1)} %bitcast.232), channel_id=1, source_target_pairs={{0,3},{1,2},{2,1},{3,0},{4,7},{5,6},{6,5},{7,4},{8,11},{9,10},{10,... | collective-permute-start | bytes 73736 | tf_op jit(solution)/shard_map/ppermute | solution.py:129
  7.4 15.8 %copy-start.2 = (bf16[2,2,384,384]{3,2,1,0:T(8,128)(2,1)S(1)}, bf16[2,2,384,384]{3,2,1,0:T(8,128)(2,1)}, u32[]{:S(2)}) copy-start(bf16[2,2,384,384]{3,2,1,0:T(8,128)(2,1)} %param.13) | copy-start | bytes 3538948
  14.2 6.4 %collective-permute-start.4 = (f32[1,2,8,384]{3,1,2,0:T(2,128)}, f32[1,2,8,384]{3,1,2,0:T(2,128)S(1)}, u32[]{:S(2)}, u32[]{:S(2)}) collective-permute-start(f32[1,2,8,384]{3,1,2,0:T(2,128)} %bitcast.218), channel_id=1, source_target_pairs={{0,8},{1,9},{2,10},{3,11},{4,12},{5,13},{6,14},{7,15},{8,0},{9,1},... | collective-permute-start | bytes 73736 | tf_op jit(solution)/shard_map/ppermute | solution.py:141
  17.3 5.8 %collective-permute-start.5 = (f32[1,2,8,384]{3,1,2,0:T(2,128)}, f32[1,2,8,384]{3,1,2,0:T(2,128)S(1)}, u32[]{:S(2)}, u32[]{:S(2)}) collective-permute-start(f32[1,2,8,384]{3,1,2,0:T(2,128)} %bitcast.223), channel_id=1, source_target_pairs={{0,12},{1,13},{2,14},{3,15},{4,8},{5,9},{6,10},{7,11},{8,4},{9,5},... | collective-permute-start | bytes 73736 | tf_op jit(solution)/shard_map/ppermute | solution.py:141
  18.6 4.5 %collective-permute-start.3 = (f32[1,2,8,384]{3,1,2,0:T(2,128)}, f32[1,2,8,384]{3,1,2,0:T(2,128)S(1)}, u32[]{:S(2)}, u32[]{:S(2)}) collective-permute-start(f32[1,2,8,384]{3,1,2,0:T(2,128)} %bitcast.219), channel_id=1, source_target_pairs={{0,4},{1,5},{2,6},{3,7},{4,0},{5,1},{6,2},{7,3},{8,12},{9,13},{10,... | collective-permute-start | bytes 73736 | tf_op jit(solution)/shard_map/ppermute | solution.py:141
  24.6 3.4 %collective-permute-start.8 = (bf16[2,8,384]{2,1,0:T(8,128)(2,1)}, bf16[2,8,384]{2,1,0:T(8,128)(2,1)S(1)}, u32[]{:S(2)}, u32[]{:S(2)}) collective-permute-start(bf16[2,8,384]{2,1,0:T(8,128)(2,1)} %pad_maximum_fusion.1), channel_id=1, source_target_pairs={{0,3},{1,2},{2,1},{3,0},{4,7},{5,6},{6,5},{7,4},{8,11},{9,10},{10,... | collective-permute-start | bytes 36872 | tf_op jit(solution)/shard_map/ppermute | solution.py:129
  24.6 3.9 %collective-permute-start.7 = (bf16[2,8,384]{2,1,0:T(8,128)(2,1)}, bf16[2,8,384]{2,1,0:T(8,128)(2,1)S(1)}, u32[]{:S(2)}, u32[]{:S(2)}) collective-permute-start(bf16[2,8,384]{2,1,0:T(8,128)(2,1)} %pad_maximum_fusion.1), channel_id=1, source_target_pairs={{0,2},{1,3},{2,0},{3,1},{4,6},{5,7},{6,4},{7,5},{8,10},{9,11},{10,... | collective-permute-start | bytes 36872 | tf_op jit(solution)/shard_map/ppermute | solution.py:129
  26.2 2.4 %collective-permute-start.6 = (bf16[2,8,384]{2,1,0:T(8,128)(2,1)}, bf16[2,8,384]{2,1,0:T(8,128)(2,1)S(1)}, u32[]{:S(2)}, u32[]{:S(2)}) collective-permute-start(bf16[2,8,384]{2,1,0:T(8,128)(2,1)} %pad_maximum_fusion.1), channel_id=1, source_target_pairs={{0,1},{1,0},{2,3},{3,2},{4,5},{5,4},{6,7},{7,6},{8,9},{9,8},{10,11... | collective-permute-start | bytes 36872 | tf_op jit(solution)/shard_map/ppermute | solution.py:129
  31.4 9.1 %collective-permute-start.10 = (f32[1,2,8,384]{3,1,2,0:T(2,128)}, f32[1,2,8,384]{3,1,2,0:T(2,128)}, u32[]{:S(2)}, u32[]{:S(2)}) collective-permute-start(f32[1,2,8,384]{3,1,2,0:T(2,128)} %bitcast.216), channel_id=1, source_target_pairs={{0,8},{1,9},{2,10},{3,11},{4,12},{5,13},{6,14},{7,15},{8,0},{9,1},... | collective-permute-start | bytes 73736 | tf_op jit(solution)/shard_map/ppermute | solution.py:141
  32.6 7.9 %collective-permute-start.11 = (f32[1,2,8,384]{3,1,2,0:T(2,128)}, f32[1,2,8,384]{3,1,2,0:T(2,128)}, u32[]{:S(2)}, u32[]{:S(2)}) collective-permute-start(f32[1,2,8,384]{3,1,2,0:T(2,128)} %bitcast.222), channel_id=1, source_target_pairs={{0,12},{1,13},{2,14},{3,15},{4,8},{5,9},{6,10},{7,11},{8,4},{9,5},... | collective-permute-start | bytes 73736 | tf_op jit(solution)/shard_map/ppermute | solution.py:141
  33.6 7.0 %collective-permute-start.9 = (f32[1,2,8,384]{3,1,2,0:T(2,128)}, f32[1,2,8,384]{3,1,2,0:T(2,128)}, u32[]{:S(2)}, u32[]{:S(2)}) collective-permute-start(f32[1,2,8,384]{3,1,2,0:T(2,128)} %bitcast.217), channel_id=1, source_target_pairs={{0,4},{1,5},{2,6},{3,7},{4,0},{5,1},{6,2},{7,3},{8,12},{9,13},{10,... | collective-permute-start | bytes 73736 | tf_op jit(solution)/shard_map/ppermute | solution.py:141
  47.8 5.1 %collective-permute-start.13 = (f32[2,8,384]{2,1,0:T(8,128)S(1)}, f32[2,8,384]{2,1,0:T(8,128)S(1)}, u32[]{:S(2)}, u32[]{:S(2)}) collective-permute-start(f32[2,8,384]{2,1,0:T(8,128)S(1)} %bitcast.234), channel_id=1, source_target_pairs={{0,2},{1,3},{2,0},{3,1},{4,6},{5,7},{6,4},{7,5},{8,10},{9,11},{10,... | collective-permute-start | bytes 73736 | tf_op jit(solution)/shard_map/ppermute | solution.py:129
  49.3 3.6 %collective-permute-start.12 = (f32[2,8,384]{2,1,0:T(8,128)S(1)}, f32[2,8,384]{2,1,0:T(8,128)S(1)}, u32[]{:S(2)}, u32[]{:S(2)}) collective-permute-start(f32[2,8,384]{2,1,0:T(8,128)S(1)} %bitcast.235), channel_id=1, source_target_pairs={{0,1},{1,0},{2,3},{3,2},{4,5},{5,4},{6,7},{7,6},{8,9},{9,8},{10,11... | collective-permute-start | bytes 73736 | tf_op jit(solution)/shard_map/ppermute | solution.py:129
  49.3 3.6 %collective-permute-start.14 = (f32[2,8,384]{2,1,0:T(8,128)S(1)}, f32[2,8,384]{2,1,0:T(8,128)S(1)}, u32[]{:S(2)}, u32[]{:S(2)}) collective-permute-start(f32[2,8,384]{2,1,0:T(8,128)S(1)} %bitcast.236), channel_id=1, source_target_pairs={{0,3},{1,2},{2,1},{3,0},{4,7},{5,6},{6,5},{7,4},{8,11},{9,10},{10,... | collective-permute-start | bytes 73736 | tf_op jit(solution)/shard_map/ppermute | solution.py:129
  52.9 11.6 %copy-start.7 = (bf16[2,4,384]{2,0,1:T(2,128)(2,1)S(1)}, bf16[2,4,384]{2,0,1:T(2,128)(2,1)}, u32[]{:S(2)}) copy-start(bf16[2,4,384]{2,0,1:T(2,128)(2,1)} %copy-done.6) | copy-start | bytes 18436
  53.5 5.3 %collective-permute-start.16 = (f32[1,2,8,384]{3,1,2,0:T(2,128)S(1)}, f32[1,2,8,384]{3,1,2,0:T(2,128)S(1)}, u32[]{:S(2)}, u32[]{:S(2)}) collective-permute-start(f32[1,2,8,384]{3,1,2,0:T(2,128)S(1)} %bitcast.251), channel_id=1, source_target_pairs={{0,8},{1,9},{2,10},{3,11},{4,12},{5,13},{6,14},{7,15},{8,0},{9,1},... | collective-permute-start | bytes 73736 | tf_op jit(solution)/shard_map/ppermute | solution.py:141
  55.7 5.6 %collective-permute-start.17 = (f32[1,2,8,384]{3,1,2,0:T(2,128)S(1)}, f32[1,2,8,384]{3,1,2,0:T(2,128)S(1)}, u32[]{:S(2)}, u32[]{:S(2)}) collective-permute-start(f32[1,2,8,384]{3,1,2,0:T(2,128)S(1)} %bitcast.250), channel_id=1, source_target_pairs={{0,12},{1,13},{2,14},{3,15},{4,8},{5,9},{6,10},{7,11},{8,4},{9,5},... | collective-permute-start | bytes 73736 | tf_op jit(solution)/shard_map/ppermute | solution.py:141
  56.6 4.7 %collective-permute-start.15 = (f32[1,2,8,384]{3,1,2,0:T(2,128)S(1)}, f32[1,2,8,384]{3,1,2,0:T(2,128)S(1)}, u32[]{:S(2)}, u32[]{:S(2)}) collective-permute-start(f32[1,2,8,384]{3,1,2,0:T(2,128)S(1)} %bitcast.248), channel_id=1, source_target_pairs={{0,4},{1,5},{2,6},{3,7},{4,0},{5,1},{6,2},{7,3},{8,12},{9,13},{10,... | collective-permute-start | bytes 73736 | tf_op jit(solution)/shard_map/ppermute | solution.py:141
  57.1 14.2 %collective-permute-start.24 = (f32[8,24,384]{2,1,0:T(8,128)S(1)}, f32[8,24,384]{2,1,0:T(8,128)S(1)}, u32[]{:S(2)}, u32[]{:S(2)}) collective-permute-start(f32[8,24,384]{2,1,0:T(8,128)S(1)} %dynamic-slice_bitcast_fusion), channel_id=1, source_target_pairs={{0,1},{1,0},{2,3},{3,2},{4,5},{5,4},{6,7},{7,6},{8,9},{9,8},{10,11... | collective-permute-start | bytes 884744 | tf_op jit(solution)/shard_map/ppermute | solution.py:120
  62.5 4.7 %collective-permute-start.20 = (bf16[2,8,384]{2,1,0:T(8,128)(2,1)S(1)}, bf16[2,8,384]{2,1,0:T(8,128)(2,1)S(1)}, u32[]{:S(2)}, u32[]{:S(2)}) collective-permute-start(bf16[2,8,384]{2,1,0:T(8,128)(2,1)S(1)} %pad_maximum_fusion.2), channel_id=1, source_target_pairs={{0,3},{1,2},{2,1},{3,0},{4,7},{5,6},{6,5},{7,4},{8,11},{9,10},{10,... | collective-permute-start | bytes 36872 | tf_op jit(solution)/shard_map/ppermute | solution.py:129
  62.6 4.7 %collective-permute-start.19 = (bf16[2,8,384]{2,1,0:T(8,128)(2,1)S(1)}, bf16[2,8,384]{2,1,0:T(8,128)(2,1)S(1)}, u32[]{:S(2)}, u32[]{:S(2)}) collective-permute-start(bf16[2,8,384]{2,1,0:T(8,128)(2,1)S(1)} %pad_maximum_fusion.2), channel_id=1, source_target_pairs={{0,2},{1,3},{2,0},{3,1},{4,6},{5,7},{6,4},{7,5},{8,10},{9,11},{10,... | collective-permute-start | bytes 36872 | tf_op jit(solution)/shard_map/ppermute | solution.py:129
  64.2 3.1 %collective-permute-start.18 = (bf16[2,8,384]{2,1,0:T(8,128)(2,1)S(1)}, bf16[2,8,384]{2,1,0:T(8,128)(2,1)S(1)}, u32[]{:S(2)}, u32[]{:S(2)}) collective-permute-start(bf16[2,8,384]{2,1,0:T(8,128)(2,1)S(1)} %pad_maximum_fusion.2), channel_id=1, source_target_pairs={{0,1},{1,0},{2,3},{3,2},{4,5},{5,4},{6,7},{7,6},{8,9},{9,8},{10,11... | collective-permute-start | bytes 36872 | tf_op jit(solution)/shard_map/ppermute | solution.py:129
  66.1 14.1 %copy-start.3 = (bf16[2,1440,384]{2,1,0:T(8,128)(2,1)S(1)}, bf16[2,1440,384]{2,1,0:T(8,128)(2,1)}, u32[]{:S(2)}) copy-start(bf16[2,1440,384]{2,1,0:T(8,128)(2,1)} %param.11) | copy-start | bytes 6635524
  67.8 5.2 %collective-permute-start.22 = (f32[1,2,8,384]{3,1,2,0:T(2,128)S(1)}, f32[1,2,8,384]{3,1,2,0:T(2,128)S(1)}, u32[]{:S(2)}, u32[]{:S(2)}) collective-permute-start(f32[1,2,8,384]{3,1,2,0:T(2,128)S(1)} %bitcast.249), channel_id=1, source_target_pairs={{0,8},{1,9},{2,10},{3,11},{4,12},{5,13},{6,14},{7,15},{8,0},{9,1},... | collective-permute-start | bytes 73736 | tf_op jit(solution)/shard_map/ppermute | solution.py:141
  68.7 5.6 %collective-permute-start.23 = (f32[1,2,8,384]{3,1,2,0:T(2,128)S(1)}, f32[1,2,8,384]{3,1,2,0:T(2,128)S(1)}, u32[]{:S(2)}, u32[]{:S(2)}) collective-permute-start(f32[1,2,8,384]{3,1,2,0:T(2,128)S(1)} %bitcast.247), channel_id=1, source_target_pairs={{0,12},{1,13},{2,14},{3,15},{4,8},{5,9},{6,10},{7,11},{8,4},{9,5},... | collective-permute-start | bytes 73736 | tf_op jit(solution)/shard_map/ppermute | solution.py:141
  69.9 4.4 %collective-permute-start.21 = (f32[1,2,8,384]{3,1,2,0:T(2,128)S(1)}, f32[1,2,8,384]{3,1,2,0:T(2,128)S(1)}, u32[]{:S(2)}, u32[]{:S(2)}) collective-permute-start(f32[1,2,8,384]{3,1,2,0:T(2,128)S(1)} %bitcast.246), channel_id=1, source_target_pairs={{0,4},{1,5},{2,6},{3,7},{4,0},{5,1},{6,2},{7,3},{8,12},{9,13},{10,... | collective-permute-start | bytes 73736 | tf_op jit(solution)/shard_map/ppermute | solution.py:141
  71.4 5.2 %collective-permute-start.25 = (f32[4,24,384]{2,1,0:T(8,128)S(1)}, f32[4,24,384]{2,1,0:T(8,128)S(1)}, u32[]{:S(2)}, u32[]{:S(2)}) collective-permute-start(f32[4,24,384]{2,1,0:T(8,128)S(1)} %dynamic-slice_bitcast_fusion.1), channel_id=1, source_target_pairs={{0,2},{1,3},{2,0},{3,1},{4,6},{5,7},{6,4},{7,5},{8,10},{9,11},{10,... | collective-permute-start | bytes 442376 | tf_op jit(solution)/shard_map/ppermute | solution.py:120
  76.7 6.0 %collective-permute-start.26 = (f32[1,24,384]{2,1,0:T(8,128)S(1)}, f32[1,24,384]{2,1,0:T(8,128)S(1)}, u32[]{:S(2)}, u32[]{:S(2)}) collective-permute-start(f32[1,24,384]{2,1,0:T(8,128)S(1)} %get-tuple-element.10), channel_id=1, source_target_pairs={{0,4},{1,5},{2,6},{3,7},{4,0},{5,1},{6,2},{7,3},{8,12},{9,13},{10,... | collective-permute-start | bytes 110600 | tf_op jit(solution)/shard_map/ppermute | solution.py:120
  77.7 5.8 %collective-permute-start.28 = (f32[1,24,384]{2,1,0:T(8,128)S(1)}, f32[1,24,384]{2,1,0:T(8,128)S(1)}, u32[]{:S(2)}, u32[]{:S(2)}) collective-permute-start(f32[1,24,384]{2,1,0:T(8,128)S(1)} %get-tuple-element.11), channel_id=1, source_target_pairs={{0,12},{1,13},{2,14},{3,15},{4,8},{5,9},{6,10},{7,11},{8,4},{9,5},... | collective-permute-start | bytes 110600 | tf_op jit(solution)/shard_map/ppermute | solution.py:120
  79.9 4.9 %collective-permute-start.27 = (f32[1,24,384]{2,1,0:T(8,128)S(1)}, f32[1,24,384]{2,1,0:T(8,128)S(1)}, u32[]{:S(2)}, u32[]{:S(2)}) collective-permute-start(f32[1,24,384]{2,1,0:T(8,128)S(1)} %get-tuple-element.12), channel_id=1, source_target_pairs={{0,8},{1,9},{2,10},{3,11},{4,12},{5,13},{6,14},{7,15},{8,0},{9,1},... | collective-permute-start | bytes 110600 | tf_op jit(solution)/shard_map/ppermute | solution.py:120
  (6 other events, 28.0 us)

commit v12 on v11

--- a/solution.py
+++ b/solution.py
@@ -226,9 +226,14 @@
     filtered = complex_apply(coeffs, spectral_weight, orders).astype(jnp.bfloat16)
     grid_modes = exchange(filtered, rows_plm, to_rows).astype(jnp.bfloat16)
 
-    spatial = jnp.einsum("jfc,kf->jkc", grid_modes, fourier, preferred_element_type=jnp.float32)
-    skip_out = jnp.einsum("jkc,cd->jkd", activations, skip_weight, preferred_element_type=jnp.float32)
-    _, pullback = jax.vjp(gelu_tanh, spatial + skip_out)
+    widened = jnp.concatenate(
+        [activations, jnp.broadcast_to(fourier[None], (lat_rows,) + fourier.shape)], axis=2
+    )
+    stacked_w = jnp.concatenate(
+        [jnp.broadcast_to(skip_weight[None], (lat_rows,) + skip_weight.shape), grid_modes], axis=1
+    )
+    preact = jnp.einsum("jkc,jcd->jkd", widened, stacked_w, preferred_element_type=jnp.float32)
+    _, pullback = jax.vjp(gelu_tanh, preact)
     slope_b = pullback(upstream.astype(jnp.float32))[0].astype(jnp.bfloat16)
 
     skip_terms = jnp.einsum("jkc,jkd->cd", activations, slope_b, preferred_element_type=jnp.float32)

time: 85.9 us -> 85.1 us (level)
  matrix products: 22.2 us -> 19.3 us
  local copies, waits for them, and re-layouts: 15.4 us -> 17.5 us
    dot_general x2 -> x1, matrix products: 10.5 us -> 6.77 us  [local(): jnp.einsum('jkc,jcd->jkd', widened, stacked_w, preferred_element_type=jnp...]
    broadcast_in_dim x0 -> x2, local copies, waits for them, and re-layouts: none -> 1.76 us  [the longest x1 1.02 us: local(): jnp.broadcast_to(skip_weight[None], (lat_rows,) + skip_weight.shape)]
    unnamed x35 -> x34, local copies, waits for them, and re-layouts: 8.01 us -> 9.07 us
    dot_general x1, matrix products: 1.13 us -> 2.04 us  [local(): jnp.einsum('jkc,kf->jfc', activations, fourier, preferred_element_type=jn...]
  transfers between devices with their start and end apart: 29 -> 29, of which waited for: 9 -> 9; matrix products, arithmetic and copies ran while one was open for 27% -> 24% of each run, Pallas kernels for 0% -> 0%
where the time goes in v12:
time: 85.1 us; the launch traced here: 84.7 us
  starting transfers between devices  29.5 us (35%)
  matrix products  19.3 us (23%)
  local copies, waits for them, and re-layouts  17.5 us (21%)
  waiting for transfers between devices  13.7 us (16%)
  other arithmetic  3.56 us (4%)
  between operations  1.1 us (1%)
    ppermute x12, starting transfers between devices, xor_exchange(): lax.ppermute(view[:, k], axis_name, [(i, i ^ mask) for i in range(groups)])  15.2 us
    ppermute x12, starting transfers between devices, xor_exchange(): lax.ppermute(values, axis_name, [(i, i ^ k) for i in range(groups)])  9.09 us
    unnamed x34, local copies, waits for them, and re-layouts  9.07 us
    ppermute x12, waiting for transfers between devices, xor_exchange(): lax.ppermute(view[:, k], axis_name, [(i, i ^ mask) for i in range(groups)])  7.94 us
    dot_general x1, matrix products, local(): jnp.einsum('jkc,jcd->jkd', widened, stacked_w, preferred_element_type=jnp...  6.77 us
    ppermute x5, starting transfers between devices, xor_reduce_scatter(): lax.ppermute(sent, axis_name, [(i, i ^ mask) for i in range(groups)])  5.22 us
    ppermute x5, waiting for transfers between devices, xor_reduce_scatter(): lax.ppermute(sent, axis_name, [(i, i ^ mask) for i in range(groups)])  4.43 us
    dot_general x1, matrix products, local(): jnp.einsum('jfc,kf->jkc', row_grads, fourier, preferred_element_type=jnp....  2.42 us
  transfers between devices with their start and end apart: 29, of which 9 were waited for; matrix products, arithmetic and copies ran while one was open for 24% of the time, Pallas kernels for 0%

profile of v12, /device:TPU:0, one launch (start us, length us, event | category | flops | bytes accessed | tf_op | source)
XLA Modules:
  0.0 84.7 jit_solution(1873792761670682571)
XLA Ops:
  0.6 2.0 %fusion.107 = f32[8,2,384]{2,0,1:T(8,128)S(1)} fusion(bf16[1440,8,1]{0,1,2:T(8,128)(2,1)} %constant.110, bf16[2,1440,384]{2,1,0:T(8,128)(2,1)} %param.10), kind=kOutput, calls=%fused_computation.167 | convolution fusion | flops 17694720 | bytes 2259456 | tf_op jit(solution)/shard_map/jkc,kf->jfc/dot_general | solution.py:224
  2.7 3.0 %collective-permute-start.1 = (f32[2,8,384]{2,1,0:T(8,128)S(1)}, f32[2,8,384]{2,1,0:T(8,128)S(1)}, u32[]{:S(2)}, u32[]{:S(2)}) collective-permute-start(f32[2,8,384]{2,1,0:T(8,128)S(1)} %bitcast.222), channel_id=1, source_target_pairs={{0,2},{1,3},{2,0},{3,1},{4,6},{5,7},{6,4},{7,5},{8,10},{9,11},{10,... | collective-permute-start | bytes 73736 | tf_op jit(solution)/shard_map/ppermute | solution.py:129
  12.1 3.0 %collective-permute-start.4 = (f32[1,2,8,384]{3,1,2,0:T(2,128)}, f32[1,2,8,384]{3,1,2,0:T(2,128)S(1)}, u32[]{:S(2)}, u32[]{:S(2)}) collective-permute-start(f32[1,2,8,384]{3,1,2,0:T(2,128)} %bitcast.210), channel_id=1, source_target_pairs={{0,8},{1,9},{2,10},{3,11},{4,12},{5,13},{6,14},{7,15},{8,0},{9,1},... | collective-permute-start | bytes 73736 | tf_op jit(solution)/shard_map/ppermute | solution.py:141
  15.2 1.3 %collective-permute-start.5 = (f32[1,2,8,384]{3,1,2,0:T(2,128)}, f32[1,2,8,384]{3,1,2,0:T(2,128)S(1)}, u32[]{:S(2)}, u32[]{:S(2)}) collective-permute-start(f32[1,2,8,384]{3,1,2,0:T(2,128)} %bitcast.215), channel_id=1, source_target_pairs={{0,12},{1,13},{2,14},{3,15},{4,8},{5,9},{6,10},{7,11},{8,4},{9,5},... | collective-permute-start | bytes 73736 | tf_op jit(solution)/shard_map/ppermute | solution.py:141
  16.9 1.6 %gather_fusion.1 = f32[64,16]{1,0:T(8,128)S(1)} fusion(f32[32,32,16]{2,1,0:T(8,128)} %constant.83, s32[64]{0:T(128)S(1)} %reshape.197), kind=kCustom, calls=%fused_computation.3 | custom fusion | bytes 8704 | tf_op jit(solution)/shard_map/gather | solution.py:214
  18.5 2.5 %collective-permute-done.5 = f32[1,2,8,384]{3,1,2,0:T(2,128)S(1)} collective-permute-done((f32[1,2,8,384]{3,1,2,0:T(2,128)}, f32[1,2,8,384]{3,1,2,0:T(2,128)S(1)}, u32[]{:S(2)}, u32[]{:S(2)}) %collective-permute-start.5) | collective-permute-done | bytes 24608 | tf_op jit(solution)/shard_map/ppermute | solution.py:141
  22.5 1.5 %collective-permute-start.7 = (bf16[2,8,384]{2,1,0:T(8,128)(2,1)}, bf16[2,8,384]{2,1,0:T(8,128)(2,1)S(1)}, u32[]{:S(2)}, u32[]{:S(2)}) collective-permute-start(bf16[2,8,384]{2,1,0:T(8,128)(2,1)} %pad_maximum_fusion.1), channel_id=1, source_target_pairs={{0,2},{1,3},{2,0},{3,1},{4,6},{5,7},{6,4},{7,5},{8,10},{9,11},{10,... | collective-permute-start | bytes 36872 | tf_op jit(solution)/shard_map/ppermute | solution.py:129
  30.0 1.2 %collective-permute-start.10 = (f32[1,2,8,384]{3,1,2,0:T(2,128)}, f32[1,2,8,384]{3,1,2,0:T(2,128)}, u32[]{:S(2)}, u32[]{:S(2)}) collective-permute-start(f32[1,2,8,384]{3,1,2,0:T(2,128)} %bitcast.208), channel_id=1, source_target_pairs={{0,8},{1,9},{2,10},{3,11},{4,12},{5,13},{6,14},{7,15},{8,0},{9,1},... | collective-permute-start | bytes 73736 | tf_op jit(solution)/shard_map/ppermute | solution.py:141
  31.2 0.9 %collective-permute-start.11 = (f32[1,2,8,384]{3,1,2,0:T(2,128)}, f32[1,2,8,384]{3,1,2,0:T(2,128)}, u32[]{:S(2)}, u32[]{:S(2)}) collective-permute-start(f32[1,2,8,384]{3,1,2,0:T(2,128)} %bitcast.214), channel_id=1, source_target_pairs={{0,12},{1,13},{2,14},{3,15},{4,8},{5,9},{6,10},{7,11},{8,4},{9,5},... | collective-permute-start | bytes 73736 | tf_op jit(solution)/shard_map/ppermute | solution.py:141
  32.1 1.3 %collective-permute-start.9 = (f32[1,2,8,384]{3,1,2,0:T(2,128)}, f32[1,2,8,384]{3,1,2,0:T(2,128)}, u32[]{:S(2)}, u32[]{:S(2)}) collective-permute-start(f32[1,2,8,384]{3,1,2,0:T(2,128)} %bitcast.209), channel_id=1, source_target_pairs={{0,4},{1,5},{2,6},{3,7},{4,0},{5,1},{6,2},{7,3},{8,12},{9,13},{10,... | collective-permute-start | bytes 73736 | tf_op jit(solution)/shard_map/ppermute | solution.py:141
  33.5 2.6 %copy.49 = bf16[2,1440,384]{1,2,0:T(8,128)(2,1)} copy(bf16[2,1440,384]{2,1,0:T(8,128)(2,1)S(1)} %copy-done.2) | data formatting | bytes 4423680 | tf_op args[0]
  36.3 0.9 %copy.125 = f32[4,4,2,2,8]{1,0,2,3,4:T(4,128)S(1)} copy(f32[4,4,2,2,8]{4,3,2,1,0:T(2,128)} %get-tuple-element.31) | data formatting | bytes 4096
  38.1 1.0 %broadcast_in_dim.16 = bf16[2,384,384]{2,1,0:T(8,128)(2,1)S(1)} broadcast(bf16[384,384]{1,0:T(8,128)(2,1)} %param.12), dimensions={1,2} | broadcast | bytes 884736 | tf_op jit(solution)/shard_map/broadcast_in_dim | solution.py:233
  39.9 6.8 %fusion.6 = bf16[2,1440,384]{2,1,0:T(8,128)(2,1)S(1)} fusion(bf16[2,1440,384]{2,1,0:T(8,128)(2,1)} %param.11, bf16[2,1440,8]{1,2,0:T(8,128)(2,1)S(1)} %broadcast_in_dim.15, bf16[2,1440,384]{1,2,0:T(8,128)(2,1)} %copy.49, bf16[2,8,384]{2,1,0:T(8,128)(2,1)S(1)} %copy.66, bf16[2,384,384]{2,1,0:T(8,128)(2,1)S(1)} %broadcast_in_dim.16), kind=kOutput, calls=%fused_computation.15 | convolution fusion | flops 895985664 | bytes 7283712 | tf_op jit(solution)/shard_map/jkc,jcd->jkd/dot_general | solution.py:235
  47.0 1.5 %collective-permute-start.13 = (f32[2,8,384]{2,1,0:T(8,128)S(1)}, f32[2,8,384]{2,1,0:T(8,128)S(1)}, u32[]{:S(2)}, u32[]{:S(2)}) collective-permute-start(f32[2,8,384]{2,1,0:T(8,128)S(1)} %bitcast.226), channel_id=1, source_target_pairs={{0,2},{1,3},{2,0},{3,1},{4,6},{5,7},{6,4},{7,5},{8,10},{9,11},{10,... | collective-permute-start | bytes 73736 | tf_op jit(solution)/shard_map/ppermute | solution.py:129
  49.2 1.5 %fusion.49 = f32[2,1440,384]{2,1,0:T(8,128)S(1)} fusion(bf16[2,1440,384]{2,1,0:T(8,128)(2,1)S(1)} %fusion.6, bf16[384,384]{1,0:T(8,128)(2,1)S(1)} %copy-done.4), kind=kOutput, calls=%fused_computation.68 | convolution fusion | flops 849346560 | bytes 6930432 | tf_op jit(solution)/shard_map/jkd,cd->jkc/dot_general | solution.py:242
  50.7 1.4 %fusion.109 = f32[384,384,1]{0,1,2:T(8,128)S(1)} fusion(bf16[2,1440,384]{2,1,0:T(8,128)(2,1)S(1)} %fusion.6, bf16[2,1440,384]{2,1,0:T(8,128)(2,1)S(1)} %copy-done.2), kind=kOutput, calls=%fused_computation.169 | convolution fusion | flops 849346560 | bytes 5013504 | tf_op jit(solution)/shard_map/jkc,jkd->cd/dot_general | solution.py:239
  52.8 2.2 %collective-permute-start.16 = (f32[1,2,8,384]{3,1,2,0:T(2,128)S(1)}, f32[1,2,8,384]{3,1,2,0:T(2,128)S(1)}, u32[]{:S(2)}, u32[]{:S(2)}) collective-permute-start(f32[1,2,8,384]{3,1,2,0:T(2,128)S(1)} %bitcast.245), channel_id=1, source_target_pairs={{0,8},{1,9},{2,10},{3,11},{4,12},{5,13},{6,14},{7,15},{8,0},{9,1},... | collective-permute-start | bytes 73736 | tf_op jit(solution)/shard_map/ppermute | solution.py:141
  55.0 0.9 %collective-permute-start.17 = (f32[1,2,8,384]{3,1,2,0:T(2,128)S(1)}, f32[1,2,8,384]{3,1,2,0:T(2,128)S(1)}, u32[]{:S(2)}, u32[]{:S(2)}) collective-permute-start(f32[1,2,8,384]{3,1,2,0:T(2,128)S(1)} %bitcast.244), channel_id=1, source_target_pairs={{0,12},{1,13},{2,14},{3,15},{4,8},{5,9},{6,10},{7,11},{8,4},{9,5},... | collective-permute-start | bytes 73736 | tf_op jit(solution)/shard_map/ppermute | solution.py:141
  56.4 1.6 %collective-permute-done.16 = f32[1,2,8,384]{3,1,2,0:T(2,128)S(1)} collective-permute-done((f32[1,2,8,384]{3,1,2,0:T(2,128)S(1)}, f32[1,2,8,384]{3,1,2,0:T(2,128)S(1)}, u32[]{:S(2)}, u32[]{:S(2)}) %collective-permute-start.16) | collective-permute-done | bytes 24608 | tf_op jit(solution)/shard_map/ppermute | solution.py:141
  58.1 2.5 %collective-permute-done.17 = f32[1,2,8,384]{3,1,2,0:T(2,128)S(1)} collective-permute-done((f32[1,2,8,384]{3,1,2,0:T(2,128)S(1)}, f32[1,2,8,384]{3,1,2,0:T(2,128)S(1)}, u32[]{:S(2)}, u32[]{:S(2)}) %collective-permute-start.17) | collective-permute-done | bytes 24608 | tf_op jit(solution)/shard_map/ppermute | solution.py:141
  61.9 1.6 %collective-permute-start.19 = (bf16[2,8,384]{2,1,0:T(8,128)(2,1)S(1)}, bf16[2,8,384]{2,1,0:T(8,128)(2,1)S(1)}, u32[]{:S(2)}, u32[]{:S(2)}) collective-permute-start(bf16[2,8,384]{2,1,0:T(8,128)(2,1)S(1)} %pad_maximum_fusion.2), channel_id=1, source_target_pairs={{0,2},{1,3},{2,0},{3,1},{4,6},{5,7},{6,4},{7,5},{8,10},{9,11},{10,... | collective-permute-start | bytes 36872 | tf_op jit(solution)/shard_map/ppermute | solution.py:129
  65.4 1.1 %copy.90 = bf16[2,2,384,384]{3,2,1,0:T(8,128)(2,1)} copy(bf16[2,2,384,384]{3,2,0,1:T(8,128)(2,1)S(1)} %pad_maximum_fusion) | data formatting | bytes 2359296
  67.9 1.3 %collective-permute-start.23 = (f32[1,2,8,384]{3,1,2,0:T(2,128)S(1)}, f32[1,2,8,384]{3,1,2,0:T(2,128)S(1)}, u32[]{:S(2)}, u32[]{:S(2)}) collective-permute-start(f32[1,2,8,384]{3,1,2,0:T(2,128)S(1)} %bitcast.241), channel_id=1, source_target_pairs={{0,12},{1,13},{2,14},{3,15},{4,8},{5,9},{6,10},{7,11},{8,4},{9,5},... | collective-permute-start | bytes 73736 | tf_op jit(solution)/shard_map/ppermute | solution.py:141
  69.2 1.4 %collective-permute-start.21 = (f32[1,2,8,384]{3,1,2,0:T(2,128)S(1)}, f32[1,2,8,384]{3,1,2,0:T(2,128)S(1)}, u32[]{:S(2)}, u32[]{:S(2)}) collective-permute-start(f32[1,2,8,384]{3,1,2,0:T(2,128)S(1)} %bitcast.240), channel_id=1, source_target_pairs={{0,4},{1,5},{2,6},{3,7},{4,0},{5,1},{6,2},{7,3},{8,12},{9,13},{10,... | collective-permute-start | bytes 73736 | tf_op jit(solution)/shard_map/ppermute | solution.py:141
  70.6 1.6 %collective-permute-start.25 = (f32[4,24,384]{2,1,0:T(8,128)S(1)}, f32[4,24,384]{2,1,0:T(8,128)S(1)}, u32[]{:S(2)}, u32[]{:S(2)}) collective-permute-start(f32[4,24,384]{2,1,0:T(8,128)S(1)} %dynamic-slice_bitcast_fusion.1), channel_id=1, source_target_pairs={{0,2},{1,3},{2,0},{3,1},{4,6},{5,7},{6,4},{7,5},{8,10},{9,11},{10,... | collective-permute-start | bytes 442376 | tf_op jit(solution)/shard_map/ppermute | solution.py:120
  72.2 1.3 %collective-permute-done.23 = f32[1,2,8,384]{3,1,2,0:T(2,128)S(1)} collective-permute-done((f32[1,2,8,384]{3,1,2,0:T(2,128)S(1)}, f32[1,2,8,384]{3,1,2,0:T(2,128)S(1)}, u32[]{:S(2)}, u32[]{:S(2)}) %collective-permute-start.23) | collective-permute-done | bytes 24608 | tf_op jit(solution)/shard_map/ppermute | solution.py:141
  73.6 2.3 %collective-permute-done.25 = f32[4,24,384]{2,1,0:T(8,128)S(1)} collective-permute-done((f32[4,24,384]{2,1,0:T(8,128)S(1)}, f32[4,24,384]{2,1,0:T(8,128)S(1)}, u32[]{:S(2)}, u32[]{:S(2)}) %collective-permute-start.25) | collective-permute-done | bytes 147488 | tf_op jit(solution)/shard_map/ppermute | solution.py:120
  75.9 1.0 %collective-permute-start.26 = (f32[1,24,384]{2,1,0:T(8,128)S(1)}, f32[1,24,384]{2,1,0:T(8,128)S(1)}, u32[]{:S(2)}, u32[]{:S(2)}) collective-permute-start(f32[1,24,384]{2,1,0:T(8,128)S(1)} %get-tuple-element.10), channel_id=1, source_target_pairs={{0,4},{1,5},{2,6},{3,7},{4,0},{5,1},{6,2},{7,3},{8,12},{9,13},{10,... | collective-permute-start | bytes 110600 | tf_op jit(solution)/shard_map/ppermute | solution.py:120
  76.9 2.3 %collective-permute-start.28 = (f32[1,24,384]{2,1,0:T(8,128)S(1)}, f32[1,24,384]{2,1,0:T(8,128)S(1)}, u32[]{:S(2)}, u32[]{:S(2)}) collective-permute-start(f32[1,24,384]{2,1,0:T(8,128)S(1)} %get-tuple-element.11), channel_id=1, source_target_pairs={{0,12},{1,13},{2,14},{3,15},{4,8},{5,9},{6,10},{7,11},{8,4},{9,5},... | collective-permute-start | bytes 110600 | tf_op jit(solution)/shard_map/ppermute | solution.py:120
  79.5 2.4 %fusion.11 = bf16[2,1440,384]{2,1,0:T(8,128)(2,1)} fusion(f32[2,1440,384]{2,1,0:T(8,128)S(1)} %fusion.49, bf16[2,1440,384]{2,1,0:T(8,128)(2,1)S(1)} %copy-done.3, bf16[1440,8,1]{0,1,2:T(8,128)(2,1)S(1)} %copy-done.6, bf16[2,8,384]{2,0,1:T(2,128)(2,1)S(1)} %fusion.72), kind=kOutput, calls=%fused_computation.20 | convolution fusion | flops 22118400 | bytes 8882688 | tf_op jit(solution)/shard_map/jfc,kf->jkc/dot_general | solution.py:248
  82.7 1.4 %collective-permute-done.27 = f32[1,24,384]{2,1,0:T(8,128)S(1)} collective-permute-done((f32[1,24,384]{2,1,0:T(8,128)S(1)}, f32[1,24,384]{2,1,0:T(8,128)S(1)}, u32[]{:S(2)}, u32[]{:S(2)}) %collective-permute-start.27) | collective-permute-done | bytes 36896 | tf_op jit(solution)/shard_map/ppermute | solution.py:120
  (129 shorter events, 24.3 us)
Async XLA Ops:
  2.7 7.1 %collective-permute-start.1 = (f32[2,8,384]{2,1,0:T(8,128)S(1)}, f32[2,8,384]{2,1,0:T(8,128)S(1)}, u32[]{:S(2)}, u32[]{:S(2)}) collective-permute-start(f32[2,8,384]{2,1,0:T(8,128)S(1)} %bitcast.222), channel_id=1, source_target_pairs={{0,2},{1,3},{2,0},{3,1},{4,6},{5,7},{6,4},{7,5},{8,10},{9,11},{10,... | collective-permute-start | bytes 73736 | tf_op jit(solution)/shard_map/ppermute | solution.py:129
  5.7 4.1 %collective-permute-start = (f32[2,8,384]{2,1,0:T(8,128)S(1)}, f32[2,8,384]{2,1,0:T(8,128)S(1)}, u32[]{:S(2)}, u32[]{:S(2)}) collective-permute-start(f32[2,8,384]{2,1,0:T(8,128)S(1)} %bitcast.223), channel_id=1, source_target_pairs={{0,1},{1,0},{2,3},{3,2},{4,5},{5,4},{6,7},{7,6},{8,9},{9,8},{10,11... | collective-permute-start | bytes 73736 | tf_op jit(solution)/shard_map/ppermute | solution.py:129
  5.7 4.1 %collective-permute-start.2 = (f32[2,8,384]{2,1,0:T(8,128)S(1)}, f32[2,8,384]{2,1,0:T(8,128)S(1)}, u32[]{:S(2)}, u32[]{:S(2)}) collective-permute-start(f32[2,8,384]{2,1,0:T(8,128)S(1)} %bitcast.224), channel_id=1, source_target_pairs={{0,3},{1,2},{2,1},{3,0},{4,7},{5,6},{6,5},{7,4},{8,11},{9,10},{10,... | collective-permute-start | bytes 73736 | tf_op jit(solution)/shard_map/ppermute | solution.py:129
  6.8 14.3 %copy-start.1 = (bf16[2,2,384,384]{3,2,1,0:T(8,128)(2,1)S(1)}, bf16[2,2,384,384]{3,2,1,0:T(8,128)(2,1)}, u32[]{:S(2)}) copy-start(bf16[2,2,384,384]{3,2,1,0:T(8,128)(2,1)} %param.13) | copy-start | bytes 3538948
  10.2 23.3 %copy-start.2 = (bf16[2,1440,384]{2,1,0:T(8,128)(2,1)S(1)}, bf16[2,1440,384]{2,1,0:T(8,128)(2,1)}, u32[]{:S(2)}) copy-start(bf16[2,1440,384]{2,1,0:T(8,128)(2,1)} %param.10) | copy-start | bytes 6635524
  12.1 6.4 %collective-permute-start.4 = (f32[1,2,8,384]{3,1,2,0:T(2,128)}, f32[1,2,8,384]{3,1,2,0:T(2,128)S(1)}, u32[]{:S(2)}, u32[]{:S(2)}) collective-permute-start(f32[1,2,8,384]{3,1,2,0:T(2,128)} %bitcast.210), channel_id=1, source_target_pairs={{0,8},{1,9},{2,10},{3,11},{4,12},{5,13},{6,14},{7,15},{8,0},{9,1},... | collective-permute-start | bytes 73736 | tf_op jit(solution)/shard_map/ppermute | solution.py:141
  15.2 5.8 %collective-permute-start.5 = (f32[1,2,8,384]{3,1,2,0:T(2,128)}, f32[1,2,8,384]{3,1,2,0:T(2,128)S(1)}, u32[]{:S(2)}, u32[]{:S(2)}) collective-permute-start(f32[1,2,8,384]{3,1,2,0:T(2,128)} %bitcast.215), channel_id=1, source_target_pairs={{0,12},{1,13},{2,14},{3,15},{4,8},{5,9},{6,10},{7,11},{8,4},{9,5},... | collective-permute-start | bytes 73736 | tf_op jit(solution)/shard_map/ppermute | solution.py:141
  16.5 4.5 %collective-permute-start.3 = (f32[1,2,8,384]{3,1,2,0:T(2,128)}, f32[1,2,8,384]{3,1,2,0:T(2,128)S(1)}, u32[]{:S(2)}, u32[]{:S(2)}) collective-permute-start(f32[1,2,8,384]{3,1,2,0:T(2,128)} %bitcast.211), channel_id=1, source_target_pairs={{0,4},{1,5},{2,6},{3,7},{4,0},{5,1},{6,2},{7,3},{8,12},{9,13},{10,... | collective-permute-start | bytes 73736 | tf_op jit(solution)/shard_map/ppermute | solution.py:141
  22.5 3.4 %collective-permute-start.8 = (bf16[2,8,384]{2,1,0:T(8,128)(2,1)}, bf16[2,8,384]{2,1,0:T(8,128)(2,1)S(1)}, u32[]{:S(2)}, u32[]{:S(2)}) collective-permute-start(bf16[2,8,384]{2,1,0:T(8,128)(2,1)} %pad_maximum_fusion.1), channel_id=1, source_target_pairs={{0,3},{1,2},{2,1},{3,0},{4,7},{5,6},{6,5},{7,4},{8,11},{9,10},{10,... | collective-permute-start | bytes 36872 | tf_op jit(solution)/shard_map/ppermute | solution.py:129
  22.5 3.9 %collective-permute-start.7 = (bf16[2,8,384]{2,1,0:T(8,128)(2,1)}, bf16[2,8,384]{2,1,0:T(8,128)(2,1)S(1)}, u32[]{:S(2)}, u32[]{:S(2)}) collective-permute-start(bf16[2,8,384]{2,1,0:T(8,128)(2,1)} %pad_maximum_fusion.1), channel_id=1, source_target_pairs={{0,2},{1,3},{2,0},{3,1},{4,6},{5,7},{6,4},{7,5},{8,10},{9,11},{10,... | collective-permute-start | bytes 36872 | tf_op jit(solution)/shard_map/ppermute | solution.py:129
  24.0 2.4 %collective-permute-start.6 = (bf16[2,8,384]{2,1,0:T(8,128)(2,1)}, bf16[2,8,384]{2,1,0:T(8,128)(2,1)}, u32[]{:S(2)}, u32[]{:S(2)}) collective-permute-start(bf16[2,8,384]{2,1,0:T(8,128)(2,1)} %pad_maximum_fusion.1), channel_id=1, source_target_pairs={{0,1},{1,0},{2,3},{3,2},{4,5},{5,4},{6,7},{7,6},{8,9},{9,8},{10,11... | collective-permute-start | bytes 36872 | tf_op jit(solution)/shard_map/ppermute | solution.py:129
  30.0 7.3 %collective-permute-start.10 = (f32[1,2,8,384]{3,1,2,0:T(2,128)}, f32[1,2,8,384]{3,1,2,0:T(2,128)}, u32[]{:S(2)}, u32[]{:S(2)}) collective-permute-start(f32[1,2,8,384]{3,1,2,0:T(2,128)} %bitcast.208), channel_id=1, source_target_pairs={{0,8},{1,9},{2,10},{3,11},{4,12},{5,13},{6,14},{7,15},{8,0},{9,1},... | collective-permute-start | bytes 73736 | tf_op jit(solution)/shard_map/ppermute | solution.py:141
  31.2 6.0 %collective-permute-start.11 = (f32[1,2,8,384]{3,1,2,0:T(2,128)}, f32[1,2,8,384]{3,1,2,0:T(2,128)}, u32[]{:S(2)}, u32[]{:S(2)}) collective-permute-start(f32[1,2,8,384]{3,1,2,0:T(2,128)} %bitcast.214), channel_id=1, source_target_pairs={{0,12},{1,13},{2,14},{3,15},{4,8},{5,9},{6,10},{7,11},{8,4},{9,5},... | collective-permute-start | bytes 73736 | tf_op jit(solution)/shard_map/ppermute | solution.py:141
  32.1 5.1 %collective-permute-start.9 = (f32[1,2,8,384]{3,1,2,0:T(2,128)}, f32[1,2,8,384]{3,1,2,0:T(2,128)}, u32[]{:S(2)}, u32[]{:S(2)}) collective-permute-start(f32[1,2,8,384]{3,1,2,0:T(2,128)} %bitcast.209), channel_id=1, source_target_pairs={{0,4},{1,5},{2,6},{3,7},{4,0},{5,1},{6,2},{7,3},{8,12},{9,13},{10,... | collective-permute-start | bytes 73736 | tf_op jit(solution)/shard_map/ppermute | solution.py:141
  47.0 5.1 %collective-permute-start.13 = (f32[2,8,384]{2,1,0:T(8,128)S(1)}, f32[2,8,384]{2,1,0:T(8,128)S(1)}, u32[]{:S(2)}, u32[]{:S(2)}) collective-permute-start(f32[2,8,384]{2,1,0:T(8,128)S(1)} %bitcast.226), channel_id=1, source_target_pairs={{0,2},{1,3},{2,0},{3,1},{4,6},{5,7},{6,4},{7,5},{8,10},{9,11},{10,... | collective-permute-start | bytes 73736 | tf_op jit(solution)/shard_map/ppermute | solution.py:129
  48.6 3.6 %collective-permute-start.12 = (f32[2,8,384]{2,1,0:T(8,128)S(1)}, f32[2,8,384]{2,1,0:T(8,128)S(1)}, u32[]{:S(2)}, u32[]{:S(2)}) collective-permute-start(f32[2,8,384]{2,1,0:T(8,128)S(1)} %bitcast.227), channel_id=1, source_target_pairs={{0,1},{1,0},{2,3},{3,2},{4,5},{5,4},{6,7},{7,6},{8,9},{9,8},{10,11... | collective-permute-start | bytes 73736 | tf_op jit(solution)/shard_map/ppermute | solution.py:129
  48.6 3.6 %collective-permute-start.14 = (f32[2,8,384]{2,1,0:T(8,128)S(1)}, f32[2,8,384]{2,1,0:T(8,128)S(1)}, u32[]{:S(2)}, u32[]{:S(2)}) collective-permute-start(f32[2,8,384]{2,1,0:T(8,128)S(1)} %bitcast.228), channel_id=1, source_target_pairs={{0,3},{1,2},{2,1},{3,0},{4,7},{5,6},{6,5},{7,4},{8,11},{9,10},{10,... | collective-permute-start | bytes 73736 | tf_op jit(solution)/shard_map/ppermute | solution.py:129
  52.8 5.3 %collective-permute-start.16 = (f32[1,2,8,384]{3,1,2,0:T(2,128)S(1)}, f32[1,2,8,384]{3,1,2,0:T(2,128)S(1)}, u32[]{:S(2)}, u32[]{:S(2)}) collective-permute-start(f32[1,2,8,384]{3,1,2,0:T(2,128)S(1)} %bitcast.245), channel_id=1, source_target_pairs={{0,8},{1,9},{2,10},{3,11},{4,12},{5,13},{6,14},{7,15},{8,0},{9,1},... | collective-permute-start | bytes 73736 | tf_op jit(solution)/shard_map/ppermute | solution.py:141
  55.0 5.6 %collective-permute-start.17 = (f32[1,2,8,384]{3,1,2,0:T(2,128)S(1)}, f32[1,2,8,384]{3,1,2,0:T(2,128)S(1)}, u32[]{:S(2)}, u32[]{:S(2)}) collective-permute-start(f32[1,2,8,384]{3,1,2,0:T(2,128)S(1)} %bitcast.244), channel_id=1, source_target_pairs={{0,12},{1,13},{2,14},{3,15},{4,8},{5,9},{6,10},{7,11},{8,4},{9,5},... | collective-permute-start | bytes 73736 | tf_op jit(solution)/shard_map/ppermute | solution.py:141
  55.9 4.7 %collective-permute-start.15 = (f32[1,2,8,384]{3,1,2,0:T(2,128)S(1)}, f32[1,2,8,384]{3,1,2,0:T(2,128)S(1)}, u32[]{:S(2)}, u32[]{:S(2)}) collective-permute-start(f32[1,2,8,384]{3,1,2,0:T(2,128)S(1)} %bitcast.242), channel_id=1, source_target_pairs={{0,4},{1,5},{2,6},{3,7},{4,0},{5,1},{6,2},{7,3},{8,12},{9,13},{10,... | collective-permute-start | bytes 73736 | tf_op jit(solution)/shard_map/ppermute | solution.py:141
  56.3 14.2 %collective-permute-start.24 = (f32[8,24,384]{2,1,0:T(8,128)S(1)}, f32[8,24,384]{2,1,0:T(8,128)S(1)}, u32[]{:S(2)}, u32[]{:S(2)}) collective-permute-start(f32[8,24,384]{2,1,0:T(8,128)S(1)} %dynamic-slice_bitcast_fusion), channel_id=1, source_target_pairs={{0,1},{1,0},{2,3},{3,2},{4,5},{5,4},{6,7},{7,6},{8,9},{9,8},{10,11... | collective-permute-start | bytes 884744 | tf_op jit(solution)/shard_map/ppermute | solution.py:120
  61.8 4.7 %collective-permute-start.20 = (bf16[2,8,384]{2,1,0:T(8,128)(2,1)S(1)}, bf16[2,8,384]{2,1,0:T(8,128)(2,1)S(1)}, u32[]{:S(2)}, u32[]{:S(2)}) collective-permute-start(bf16[2,8,384]{2,1,0:T(8,128)(2,1)S(1)} %pad_maximum_fusion.2), channel_id=1, source_target_pairs={{0,3},{1,2},{2,1},{3,0},{4,7},{5,6},{6,5},{7,4},{8,11},{9,10},{10,... | collective-permute-start | bytes 36872 | tf_op jit(solution)/shard_map/ppermute | solution.py:129
  61.9 4.7 %collective-permute-start.19 = (bf16[2,8,384]{2,1,0:T(8,128)(2,1)S(1)}, bf16[2,8,384]{2,1,0:T(8,128)(2,1)S(1)}, u32[]{:S(2)}, u32[]{:S(2)}) collective-permute-start(bf16[2,8,384]{2,1,0:T(8,128)(2,1)S(1)} %pad_maximum_fusion.2), channel_id=1, source_target_pairs={{0,2},{1,3},{2,0},{3,1},{4,6},{5,7},{6,4},{7,5},{8,10},{9,11},{10,... | collective-permute-start | bytes 36872 | tf_op jit(solution)/shard_map/ppermute | solution.py:129
  63.5 3.1 %collective-permute-start.18 = (bf16[2,8,384]{2,1,0:T(8,128)(2,1)S(1)}, bf16[2,8,384]{2,1,0:T(8,128)(2,1)S(1)}, u32[]{:S(2)}, u32[]{:S(2)}) collective-permute-start(bf16[2,8,384]{2,1,0:T(8,128)(2,1)S(1)} %pad_maximum_fusion.2), channel_id=1, source_target_pairs={{0,1},{1,0},{2,3},{3,2},{4,5},{5,4},{6,7},{7,6},{8,9},{9,8},{10,11... | collective-permute-start | bytes 36872 | tf_op jit(solution)/shard_map/ppermute | solution.py:129
  65.4 14.1 %copy-start.3 = (bf16[2,1440,384]{2,1,0:T(8,128)(2,1)S(1)}, bf16[2,1440,384]{2,1,0:T(8,128)(2,1)}, u32[]{:S(2)}) copy-start(bf16[2,1440,384]{2,1,0:T(8,128)(2,1)} %param.11) | copy-start | bytes 6635524
  67.0 5.2 %collective-permute-start.22 = (f32[1,2,8,384]{3,1,2,0:T(2,128)S(1)}, f32[1,2,8,384]{3,1,2,0:T(2,128)S(1)}, u32[]{:S(2)}, u32[]{:S(2)}) collective-permute-start(f32[1,2,8,384]{3,1,2,0:T(2,128)S(1)} %bitcast.243), channel_id=1, source_target_pairs={{0,8},{1,9},{2,10},{3,11},{4,12},{5,13},{6,14},{7,15},{8,0},{9,1},... | collective-permute-start | bytes 73736 | tf_op jit(solution)/shard_map/ppermute | solution.py:141
  67.9 5.6 %collective-permute-start.23 = (f32[1,2,8,384]{3,1,2,0:T(2,128)S(1)}, f32[1,2,8,384]{3,1,2,0:T(2,128)S(1)}, u32[]{:S(2)}, u32[]{:S(2)}) collective-permute-start(f32[1,2,8,384]{3,1,2,0:T(2,128)S(1)} %bitcast.241), channel_id=1, source_target_pairs={{0,12},{1,13},{2,14},{3,15},{4,8},{5,9},{6,10},{7,11},{8,4},{9,5},... | collective-permute-start | bytes 73736 | tf_op jit(solution)/shard_map/ppermute | solution.py:141
  69.2 4.3 %collective-permute-start.21 = (f32[1,2,8,384]{3,1,2,0:T(2,128)S(1)}, f32[1,2,8,384]{3,1,2,0:T(2,128)S(1)}, u32[]{:S(2)}, u32[]{:S(2)}) collective-permute-start(f32[1,2,8,384]{3,1,2,0:T(2,128)S(1)} %bitcast.240), channel_id=1, source_target_pairs={{0,4},{1,5},{2,6},{3,7},{4,0},{5,1},{6,2},{7,3},{8,12},{9,13},{10,... | collective-permute-start | bytes 73736 | tf_op jit(solution)/shard_map/ppermute | solution.py:141
  70.6 5.2 %collective-permute-start.25 = (f32[4,24,384]{2,1,0:T(8,128)S(1)}, f32[4,24,384]{2,1,0:T(8,128)S(1)}, u32[]{:S(2)}, u32[]{:S(2)}) collective-permute-start(f32[4,24,384]{2,1,0:T(8,128)S(1)} %dynamic-slice_bitcast_fusion.1), channel_id=1, source_target_pairs={{0,2},{1,3},{2,0},{3,1},{4,6},{5,7},{6,4},{7,5},{8,10},{9,11},{10,... | collective-permute-start | bytes 442376 | tf_op jit(solution)/shard_map/ppermute | solution.py:120
  75.9 6.0 %collective-permute-start.26 = (f32[1,24,384]{2,1,0:T(8,128)S(1)}, f32[1,24,384]{2,1,0:T(8,128)S(1)}, u32[]{:S(2)}, u32[]{:S(2)}) collective-permute-start(f32[1,24,384]{2,1,0:T(8,128)S(1)} %get-tuple-element.10), channel_id=1, source_target_pairs={{0,4},{1,5},{2,6},{3,7},{4,0},{5,1},{6,2},{7,3},{8,12},{9,13},{10,... | collective-permute-start | bytes 110600 | tf_op jit(solution)/shard_map/ppermute | solution.py:120
  76.9 5.8 %collective-permute-start.28 = (f32[1,24,384]{2,1,0:T(8,128)S(1)}, f32[1,24,384]{2,1,0:T(8,128)S(1)}, u32[]{:S(2)}, u32[]{:S(2)}) collective-permute-start(f32[1,24,384]{2,1,0:T(8,128)S(1)} %get-tuple-element.11), channel_id=1, source_target_pairs={{0,12},{1,13},{2,14},{3,15},{4,8},{5,9},{6,10},{7,11},{8,4},{9,5},... | collective-permute-start | bytes 110600 | tf_op jit(solution)/shard_map/ppermute | solution.py:120
  79.2 4.9 %collective-permute-start.27 = (f32[1,24,384]{2,1,0:T(8,128)S(1)}, f32[1,24,384]{2,1,0:T(8,128)S(1)}, u32[]{:S(2)}, u32[]{:S(2)}) collective-permute-start(f32[1,24,384]{2,1,0:T(8,128)S(1)} %get-tuple-element.12), channel_id=1, source_target_pairs={{0,8},{1,9},{2,10},{3,11},{4,12},{5,13},{6,14},{7,15},{8,0},{9,1},... | collective-permute-start | bytes 110600 | tf_op jit(solution)/shard_map/ppermute | solution.py:120
  (5 other events, 22.7 us)

commit v13 on v9

--- a/solution.py
+++ b/solution.py
@@ -231,8 +231,12 @@
 
     spatial = jnp.einsum("jfc,kf->jkc", grid_modes, fourier, preferred_element_type=jnp.float32)
     skip_out = jnp.einsum("jkc,cd->jkd", activations, skip_weight, preferred_element_type=jnp.float32)
-    _, pullback = jax.vjp(gelu_tanh, spatial + skip_out)
-    slope_b = pullback(upstream.astype(jnp.float32))[0].astype(jnp.bfloat16)
+    x = spatial + skip_out
+    k_gelu = math.sqrt(2.0 / math.pi)
+    x2 = x * x
+    t = jnp.tanh(k_gelu * (x + 0.044715 * x * x2))
+    half = 0.5 * x * (1.0 - t * t) * (k_gelu * (1.0 + 3.0 * 0.044715 * x2))
+    slope_b = (upstream.astype(jnp.float32) * (0.5 * (1.0 + t) + half)).astype(jnp.bfloat16)
 
     skip_terms = jnp.einsum("jkc,jkd->cd", activations, slope_b, preferred_element_type=jnp.float32)
     skip_blocks = skip_terms.reshape((groups, -1) + skip_terms.shape[1:])

time: 83.9 us -> 83.5 us (level)
  no operation moved by 1% of the time
where the time goes in v13:
time: 83.5 us; the launch traced here: 83 us
  starting transfers between devices  28.5 us (34%)
  matrix products  21.8 us (26%)
  local copies, waits for them, and re-layouts  15.4 us (18%)
  waiting for transfers between devices  12.7 us (15%)
  other arithmetic  3.61 us (4%)
  between operations  1.11 us (1%)
    ppermute x12, starting transfers between devices, xor_exchange(): lax.ppermute(view[:, k], axis_name, [(i, i ^ mask) for i in range(groups)])  15.2 us
    ppermute x12, starting transfers between devices, xor_exchange(): lax.ppermute(values, axis_name, [(i, i ^ k) for i in range(groups)])  9.07 us
    ppermute x12, waiting for transfers between devices, xor_exchange(): lax.ppermute(view[:, k], axis_name, [(i, i ^ mask) for i in range(groups)])  9.05 us
    unnamed x35, local copies, waits for them, and re-layouts  8 us
    dot_general x1, matrix products, local(): jnp.einsum('jfc,kf->jkc', grid_modes, fourier, preferred_element_type=jnp...  5.59 us
    dot_general x1, matrix products, local(): jnp.einsum('jkc,cd->jkd', activations, skip_weight, preferred_element_typ...  4.51 us
    ppermute x4, starting transfers between devices, xor_reduce_scatter(): lax.ppermute(sent, axis_name, [(i, i ^ mask) for i in range(groups)])  4.17 us
    dot_general x1, matrix products, local(): jnp.einsum('jfc,kf->jkc', row_grads, fourier, preferred_element_type=jnp....  2.45 us
  transfers between devices with their start and end apart: 28, of which 9 were waited for; matrix products, arithmetic and copies ran while one was open for 27% of the time, Pallas kernels for 0%

profile of v13, /device:TPU:0, one launch (start us, length us, event | category | flops | bytes accessed | tf_op | source)
XLA Modules:
  0.0 83.0 jit_solution(17362666402307800093)
XLA Ops:
  0.7 1.6 %copy-done = bf16[2,1440,384]{2,1,0:T(8,128)(2,1)S(1)} copy-done((bf16[2,1440,384]{2,1,0:T(8,128)(2,1)S(1)}, bf16[2,1440,384]{2,1,0:T(8,128)(2,1)}, u32[]{:S(2)}) %copy-start) | copy-done | bytes 2211864
  2.3 1.1 %fusion.93 = f32[8,2,384]{2,0,1:T(8,128)S(1)} fusion(bf16[1440,8,1]{0,1,2:T(8,128)(2,1)} %constant.110, bf16[2,1440,384]{2,1,0:T(8,128)(2,1)S(1)} %copy-done), kind=kOutput, calls=%fused_computation.153 | convolution fusion | flops 17694720 | bytes 2259456 | tf_op jit(solution)/shard_map/jkc,kf->jfc/dot_general | solution.py:227
  3.4 3.0 %collective-permute-start.1 = (f32[2,8,384]{2,1,0:T(8,128)S(1)}, f32[2,8,384]{2,1,0:T(8,128)S(1)}, u32[]{:S(2)}, u32[]{:S(2)}) collective-permute-start(f32[2,8,384]{2,1,0:T(8,128)S(1)} %bitcast.241), channel_id=1, source_target_pairs={{0,2},{1,3},{2,0},{3,1},{4,6},{5,7},{6,4},{7,5},{8,10},{9,11},{10,... | collective-permute-start | bytes 73736 | tf_op jit(solution)/shard_map/ppermute | solution.py:132
  8.6 1.6 %gather_fusion = f32[64,16]{1,0:T(8,128)S(1)} fusion(f32[32,32,16]{2,1,0:T(8,128)} %constant.83, s32[64]{0:T(128)S(1)} %reshape.191), kind=kCustom, calls=%fused_computation.2 | custom fusion | bytes 8704 | tf_op jit(solution)/shard_map/gather | solution.py:214
  14.2 3.1 %collective-permute-start.4 = (f32[1,2,8,384]{3,1,2,0:T(2,128)}, f32[1,2,8,384]{3,1,2,0:T(2,128)S(1)}, u32[]{:S(2)}, u32[]{:S(2)}) collective-permute-start(f32[1,2,8,384]{3,1,2,0:T(2,128)} %bitcast.227), channel_id=1, source_target_pairs={{0,8},{1,9},{2,10},{3,11},{4,12},{5,13},{6,14},{7,15},{8,0},{9,1},... | collective-permute-start | bytes 73736 | tf_op jit(solution)/shard_map/ppermute | solution.py:144
  17.3 1.3 %collective-permute-start.5 = (f32[1,2,8,384]{3,1,2,0:T(2,128)}, f32[1,2,8,384]{3,1,2,0:T(2,128)S(1)}, u32[]{:S(2)}, u32[]{:S(2)}) collective-permute-start(f32[1,2,8,384]{3,1,2,0:T(2,128)} %bitcast.232), channel_id=1, source_target_pairs={{0,12},{1,13},{2,14},{3,15},{4,8},{5,9},{6,10},{7,11},{8,4},{9,5},... | collective-permute-start | bytes 73736 | tf_op jit(solution)/shard_map/ppermute | solution.py:144
  19.1 1.6 %gather_fusion.1 = f32[64,16]{1,0:T(8,128)S(1)} fusion(f32[32,32,16]{2,1,0:T(8,128)} %constant.83, s32[64]{0:T(128)S(1)} %reshape.197), kind=kCustom, calls=%fused_computation.3 | custom fusion | bytes 8704 | tf_op jit(solution)/shard_map/gather | solution.py:217
  20.7 2.5 %collective-permute-done.5 = f32[1,2,8,384]{3,1,2,0:T(2,128)S(1)} collective-permute-done((f32[1,2,8,384]{3,1,2,0:T(2,128)}, f32[1,2,8,384]{3,1,2,0:T(2,128)S(1)}, u32[]{:S(2)}, u32[]{:S(2)}) %collective-permute-start.5) | collective-permute-done | bytes 24608 | tf_op jit(solution)/shard_map/ppermute | solution.py:144
  24.6 1.6 %collective-permute-start.7 = (bf16[2,8,384]{2,1,0:T(8,128)(2,1)}, bf16[2,8,384]{2,1,0:T(8,128)(2,1)S(1)}, u32[]{:S(2)}, u32[]{:S(2)}) collective-permute-start(bf16[2,8,384]{2,1,0:T(8,128)(2,1)} %pad_maximum_fusion.1), channel_id=1, source_target_pairs={{0,2},{1,3},{2,0},{3,1},{4,6},{5,7},{6,4},{7,5},{8,10},{9,11},{10,... | collective-permute-start | bytes 36872 | tf_op jit(solution)/shard_map/ppermute | solution.py:132
  31.4 1.2 %collective-permute-start.10 = (f32[1,2,8,384]{3,1,2,0:T(2,128)}, f32[1,2,8,384]{3,1,2,0:T(2,128)}, u32[]{:S(2)}, u32[]{:S(2)}) collective-permute-start(f32[1,2,8,384]{3,1,2,0:T(2,128)} %bitcast.225), channel_id=1, source_target_pairs={{0,8},{1,9},{2,10},{3,11},{4,12},{5,13},{6,14},{7,15},{8,0},{9,1},... | collective-permute-start | bytes 73736 | tf_op jit(solution)/shard_map/ppermute | solution.py:144
  32.6 0.9 %collective-permute-start.11 = (f32[1,2,8,384]{3,1,2,0:T(2,128)}, f32[1,2,8,384]{3,1,2,0:T(2,128)}, u32[]{:S(2)}, u32[]{:S(2)}) collective-permute-start(f32[1,2,8,384]{3,1,2,0:T(2,128)} %bitcast.231), channel_id=1, source_target_pairs={{0,12},{1,13},{2,14},{3,15},{4,8},{5,9},{6,10},{7,11},{8,4},{9,5},... | collective-permute-start | bytes 73736 | tf_op jit(solution)/shard_map/ppermute | solution.py:144
  33.6 1.3 %collective-permute-start.9 = (f32[1,2,8,384]{3,1,2,0:T(2,128)}, f32[1,2,8,384]{3,1,2,0:T(2,128)}, u32[]{:S(2)}, u32[]{:S(2)}) collective-permute-start(f32[1,2,8,384]{3,1,2,0:T(2,128)} %bitcast.226), channel_id=1, source_target_pairs={{0,4},{1,5},{2,6},{3,7},{4,0},{5,1},{6,2},{7,3},{8,12},{9,13},{10,... | collective-permute-start | bytes 73736 | tf_op jit(solution)/shard_map/ppermute | solution.py:144
  34.9 4.5 %fusion.33 = f32[2,1440,384]{2,1,0:T(8,128)} fusion(bf16[2,1440,384]{2,1,0:T(8,128)(2,1)S(1)} %copy-done, bf16[384,384]{1,0:T(8,128)(2,1)} %param.12), kind=kOutput, calls=%fused_computation.53 | convolution fusion | flops 849346560 | bytes 6930432 | tf_op jit(solution)/shard_map/jkc,cd->jkd/dot_general | solution.py:233
  39.6 0.9 %copy.165 = f32[4,4,2,2,8]{1,0,2,3,4:T(4,128)S(1)} copy(f32[4,4,2,2,8]{4,3,2,1,0:T(2,128)} %get-tuple-element.31) | data formatting | bytes 4096
  41.4 5.6 %fusion = bf16[2,1440,384]{2,1,0:T(8,128)(2,1)S(1)} fusion(bf16[2,1440,384]{2,1,0:T(8,128)(2,1)} %param.11, f32[2,1440,384]{2,1,0:T(8,128)} %fusion.33, bf16[1440,8,1]{0,1,2:T(8,128)(2,1)S(1)} %copy-done.5, bf16[2,8,384]{2,0,1:T(2,128)(2,1)S(1)} %fusion.61), kind=kOutput, calls=%fused_computation.6 | convolution fusion | flops 39813120 | bytes 8882688 | tf_op jit(solution)/shard_map/jfc,kf->jkc/dot_general | solution.py:232
  47.4 1.5 %collective-permute-start.13 = (f32[2,8,384]{2,1,0:T(8,128)S(1)}, f32[2,8,384]{2,1,0:T(8,128)S(1)}, u32[]{:S(2)}, u32[]{:S(2)}) collective-permute-start(f32[2,8,384]{2,1,0:T(8,128)S(1)} %bitcast.245), channel_id=1, source_target_pairs={{0,2},{1,3},{2,0},{3,1},{4,6},{5,7},{6,4},{7,5},{8,10},{9,11},{10,... | collective-permute-start | bytes 73736 | tf_op jit(solution)/shard_map/ppermute | solution.py:132
  49.5 1.5 %fusion.31 = f32[2,1440,384]{2,1,0:T(8,128)S(1)} fusion(bf16[2,1440,384]{2,1,0:T(8,128)(2,1)S(1)} %fusion, bf16[384,384]{1,0:T(8,128)(2,1)S(1)} %copy-done.4), kind=kOutput, calls=%fused_computation.51 | convolution fusion | flops 849346560 | bytes 6930432 | tf_op jit(solution)/shard_map/jkd,cd->jkc/dot_general | solution.py:244
  51.1 1.4 %fusion.95 = f32[384,384,1]{0,1,2:T(8,128)S(1)} fusion(bf16[2,1440,384]{2,1,0:T(8,128)(2,1)S(1)} %fusion, bf16[2,1440,384]{2,1,0:T(8,128)(2,1)S(1)} %copy-done), kind=kOutput, calls=%fused_computation.155 | convolution fusion | flops 849346560 | bytes 5013504 | tf_op jit(solution)/shard_map/jkc,jkd->cd/dot_general | solution.py:241
  53.1 2.2 %collective-permute-start.16 = (f32[1,2,8,384]{3,1,2,0:T(2,128)S(1)}, f32[1,2,8,384]{3,1,2,0:T(2,128)S(1)}, u32[]{:S(2)}, u32[]{:S(2)}) collective-permute-start(f32[1,2,8,384]{3,1,2,0:T(2,128)S(1)} %bitcast.262), channel_id=1, source_target_pairs={{0,8},{1,9},{2,10},{3,11},{4,12},{5,13},{6,14},{7,15},{8,0},{9,1},... | collective-permute-start | bytes 73736 | tf_op jit(solution)/shard_map/ppermute | solution.py:144
  55.3 0.9 %collective-permute-start.17 = (f32[1,2,8,384]{3,1,2,0:T(2,128)S(1)}, f32[1,2,8,384]{3,1,2,0:T(2,128)S(1)}, u32[]{:S(2)}, u32[]{:S(2)}) collective-permute-start(f32[1,2,8,384]{3,1,2,0:T(2,128)S(1)} %bitcast.261), channel_id=1, source_target_pairs={{0,12},{1,13},{2,14},{3,15},{4,8},{5,9},{6,10},{7,11},{8,4},{9,5},... | collective-permute-start | bytes 73736 | tf_op jit(solution)/shard_map/ppermute | solution.py:144
  56.7 1.7 %collective-permute-done.16 = f32[1,2,8,384]{3,1,2,0:T(2,128)S(1)} collective-permute-done((f32[1,2,8,384]{3,1,2,0:T(2,128)S(1)}, f32[1,2,8,384]{3,1,2,0:T(2,128)S(1)}, u32[]{:S(2)}, u32[]{:S(2)}) %collective-permute-start.16) | collective-permute-done | bytes 24608 | tf_op jit(solution)/shard_map/ppermute | solution.py:144
  58.4 2.5 %collective-permute-done.17 = f32[1,2,8,384]{3,1,2,0:T(2,128)S(1)} collective-permute-done((f32[1,2,8,384]{3,1,2,0:T(2,128)S(1)}, f32[1,2,8,384]{3,1,2,0:T(2,128)S(1)}, u32[]{:S(2)}, u32[]{:S(2)}) %collective-permute-start.17) | collective-permute-done | bytes 24608 | tf_op jit(solution)/shard_map/ppermute | solution.py:144
  62.2 1.6 %collective-permute-start.19 = (bf16[2,8,384]{2,1,0:T(8,128)(2,1)S(1)}, bf16[2,8,384]{2,1,0:T(8,128)(2,1)S(1)}, u32[]{:S(2)}, u32[]{:S(2)}) collective-permute-start(bf16[2,8,384]{2,1,0:T(8,128)(2,1)S(1)} %pad_maximum_fusion.2), channel_id=1, source_target_pairs={{0,2},{1,3},{2,0},{3,1},{4,6},{5,7},{6,4},{7,5},{8,10},{9,11},{10,... | collective-permute-start | bytes 36872 | tf_op jit(solution)/shard_map/ppermute | solution.py:132
  65.7 1.1 %copy.130 = bf16[2,2,384,384]{3,2,1,0:T(8,128)(2,1)} copy(bf16[2,2,384,384]{3,2,0,1:T(8,128)(2,1)S(1)} %pad_maximum_fusion) | data formatting | bytes 2359296
  67.3 1.6 %collective-permute-start.25 = (bf16[4,24,384]{2,1,0:T(8,128)(2,1)S(1)}, bf16[4,24,384]{2,1,0:T(8,128)(2,1)S(1)}, u32[]{:S(2)}, u32[]{:S(2)}) collective-permute-start(bf16[4,24,384]{2,1,0:T(8,128)(2,1)S(1)} %fusion.38), channel_id=1, source_target_pairs={{0,2},{1,3},{2,0},{3,1},{4,6},{5,7},{6,4},{7,5},{8,10},{9,11},{10,... | collective-permute-start | bytes 221192 | tf_op jit(solution)/shard_map/ppermute | solution.py:122
  69.9 1.3 %collective-permute-start.23 = (f32[1,2,8,384]{3,1,2,0:T(2,128)S(1)}, f32[1,2,8,384]{3,1,2,0:T(2,128)S(1)}, u32[]{:S(2)}, u32[]{:S(2)}) collective-permute-start(f32[1,2,8,384]{3,1,2,0:T(2,128)S(1)} %bitcast.258), channel_id=1, source_target_pairs={{0,12},{1,13},{2,14},{3,15},{4,8},{5,9},{6,10},{7,11},{8,4},{9,5},... | collective-permute-start | bytes 73736 | tf_op jit(solution)/shard_map/ppermute | solution.py:144
  71.2 1.4 %collective-permute-start.21 = (f32[1,2,8,384]{3,1,2,0:T(2,128)S(1)}, f32[1,2,8,384]{3,1,2,0:T(2,128)S(1)}, u32[]{:S(2)}, u32[]{:S(2)}) collective-permute-start(f32[1,2,8,384]{3,1,2,0:T(2,128)S(1)} %bitcast.257), channel_id=1, source_target_pairs={{0,4},{1,5},{2,6},{3,7},{4,0},{5,1},{6,2},{7,3},{8,12},{9,13},{10,... | collective-permute-start | bytes 73736 | tf_op jit(solution)/shard_map/ppermute | solution.py:144
  73.8 1.9 %collective-permute-done.23 = f32[1,2,8,384]{3,1,2,0:T(2,128)S(1)} collective-permute-done((f32[1,2,8,384]{3,1,2,0:T(2,128)S(1)}, f32[1,2,8,384]{3,1,2,0:T(2,128)S(1)}, u32[]{:S(2)}, u32[]{:S(2)}) %collective-permute-start.23) | collective-permute-done | bytes 24608 | tf_op jit(solution)/shard_map/ppermute | solution.py:144
  75.8 1.3 %collective-permute-done.26 = f32[2,24,384]{2,1,0:T(8,128)S(1)} collective-permute-done((f32[2,24,384]{2,1,0:T(8,128)S(1)}, f32[2,24,384]{2,1,0:T(8,128)S(1)}, u32[]{:S(2)}, u32[]{:S(2)}) %collective-permute-start.26) | collective-permute-done | bytes 73760 | tf_op jit(solution)/shard_map/ppermute | solution.py:122
  77.1 1.8 %collective-permute-start.27 = (f32[1,24,384]{2,1,0:T(8,128)S(1)}, f32[1,24,384]{2,1,0:T(8,128)S(1)}, u32[]{:S(2)}, u32[]{:S(2)}) collective-permute-start(f32[1,24,384]{2,1,0:T(8,128)S(1)} %constant_dynamic-slice_fusion), channel_id=1, source_target_pairs={{0,8},{1,9},{2,10},{3,11},{4,12},{5,13},{6,14},{7,15},{8,0},{9,1},... | collective-permute-start | bytes 110600 | tf_op jit(solution)/shard_map/ppermute | solution.py:122
  78.9 2.5 %fusion.2 = bf16[2,1440,384]{2,1,0:T(8,128)(2,1)} fusion(f32[2,1440,384]{2,1,0:T(8,128)S(1)} %fusion.31, bf16[2,1440,384]{2,1,0:T(8,128)(2,1)S(1)} %copy-done.3, bf16[1440,8,1]{0,1,2:T(8,128)(2,1)S(1)} %copy-done.5, bf16[2,8,384]{2,0,1:T(2,128)(2,1)S(1)} %fusion.59), kind=kOutput, calls=%fused_computation.8 | convolution fusion | flops 22118400 | bytes 8882688 | tf_op jit(solution)/shard_map/jfc,kf->jkc/dot_general | solution.py:250
  81.3 1.1 %collective-permute-done.27 = f32[1,24,384]{2,1,0:T(8,128)S(1)} collective-permute-done((f32[1,24,384]{2,1,0:T(8,128)S(1)}, f32[1,24,384]{2,1,0:T(8,128)S(1)}, u32[]{:S(2)}, u32[]{:S(2)}) %collective-permute-start.27) | collective-permute-done | bytes 36896 | tf_op jit(solution)/shard_map/ppermute | solution.py:122
  (128 shorter events, 22.8 us)
Async XLA Ops:
  3.4 7.7 %collective-permute-start.1 = (f32[2,8,384]{2,1,0:T(8,128)S(1)}, f32[2,8,384]{2,1,0:T(8,128)S(1)}, u32[]{:S(2)}, u32[]{:S(2)}) collective-permute-start(f32[2,8,384]{2,1,0:T(8,128)S(1)} %bitcast.241), channel_id=1, source_target_pairs={{0,2},{1,3},{2,0},{3,1},{4,6},{5,7},{6,4},{7,5},{8,10},{9,11},{10,... | collective-permute-start | bytes 73736 | tf_op jit(solution)/shard_map/ppermute | solution.py:132
  6.4 4.8 %collective-permute-start = (f32[2,8,384]{2,1,0:T(8,128)S(1)}, f32[2,8,384]{2,1,0:T(8,128)}, u32[]{:S(2)}, u32[]{:S(2)}) collective-permute-start(f32[2,8,384]{2,1,0:T(8,128)S(1)} %bitcast.242), channel_id=1, source_target_pairs={{0,1},{1,0},{2,3},{3,2},{4,5},{5,4},{6,7},{7,6},{8,9},{9,8},{10,11... | collective-permute-start | bytes 73736 | tf_op jit(solution)/shard_map/ppermute | solution.py:132
  6.4 4.8 %collective-permute-start.2 = (f32[2,8,384]{2,1,0:T(8,128)S(1)}, f32[2,8,384]{2,1,0:T(8,128)}, u32[]{:S(2)}, u32[]{:S(2)}) collective-permute-start(f32[2,8,384]{2,1,0:T(8,128)S(1)} %bitcast.243), channel_id=1, source_target_pairs={{0,3},{1,2},{2,1},{3,0},{4,7},{5,6},{6,5},{7,4},{8,11},{9,10},{10,... | collective-permute-start | bytes 73736 | tf_op jit(solution)/shard_map/ppermute | solution.py:132
  7.4 15.8 %copy-start.2 = (bf16[2,2,384,384]{3,2,1,0:T(8,128)(2,1)S(1)}, bf16[2,2,384,384]{3,2,1,0:T(8,128)(2,1)}, u32[]{:S(2)}) copy-start(bf16[2,2,384,384]{3,2,1,0:T(8,128)(2,1)} %param.13) | copy-start | bytes 3538948
  14.2 6.4 %collective-permute-start.4 = (f32[1,2,8,384]{3,1,2,0:T(2,128)}, f32[1,2,8,384]{3,1,2,0:T(2,128)S(1)}, u32[]{:S(2)}, u32[]{:S(2)}) collective-permute-start(f32[1,2,8,384]{3,1,2,0:T(2,128)} %bitcast.227), channel_id=1, source_target_pairs={{0,8},{1,9},{2,10},{3,11},{4,12},{5,13},{6,14},{7,15},{8,0},{9,1},... | collective-permute-start | bytes 73736 | tf_op jit(solution)/shard_map/ppermute | solution.py:144
  17.3 5.8 %collective-permute-start.5 = (f32[1,2,8,384]{3,1,2,0:T(2,128)}, f32[1,2,8,384]{3,1,2,0:T(2,128)S(1)}, u32[]{:S(2)}, u32[]{:S(2)}) collective-permute-start(f32[1,2,8,384]{3,1,2,0:T(2,128)} %bitcast.232), channel_id=1, source_target_pairs={{0,12},{1,13},{2,14},{3,15},{4,8},{5,9},{6,10},{7,11},{8,4},{9,5},... | collective-permute-start | bytes 73736 | tf_op jit(solution)/shard_map/ppermute | solution.py:144
  18.6 4.5 %collective-permute-start.3 = (f32[1,2,8,384]{3,1,2,0:T(2,128)}, f32[1,2,8,384]{3,1,2,0:T(2,128)S(1)}, u32[]{:S(2)}, u32[]{:S(2)}) collective-permute-start(f32[1,2,8,384]{3,1,2,0:T(2,128)} %bitcast.228), channel_id=1, source_target_pairs={{0,4},{1,5},{2,6},{3,7},{4,0},{5,1},{6,2},{7,3},{8,12},{9,13},{10,... | collective-permute-start | bytes 73736 | tf_op jit(solution)/shard_map/ppermute | solution.py:144
  24.6 3.4 %collective-permute-start.8 = (bf16[2,8,384]{2,1,0:T(8,128)(2,1)}, bf16[2,8,384]{2,1,0:T(8,128)(2,1)S(1)}, u32[]{:S(2)}, u32[]{:S(2)}) collective-permute-start(bf16[2,8,384]{2,1,0:T(8,128)(2,1)} %pad_maximum_fusion.1), channel_id=1, source_target_pairs={{0,3},{1,2},{2,1},{3,0},{4,7},{5,6},{6,5},{7,4},{8,11},{9,10},{10,... | collective-permute-start | bytes 36872 | tf_op jit(solution)/shard_map/ppermute | solution.py:132
  24.6 3.9 %collective-permute-start.7 = (bf16[2,8,384]{2,1,0:T(8,128)(2,1)}, bf16[2,8,384]{2,1,0:T(8,128)(2,1)S(1)}, u32[]{:S(2)}, u32[]{:S(2)}) collective-permute-start(bf16[2,8,384]{2,1,0:T(8,128)(2,1)} %pad_maximum_fusion.1), channel_id=1, source_target_pairs={{0,2},{1,3},{2,0},{3,1},{4,6},{5,7},{6,4},{7,5},{8,10},{9,11},{10,... | collective-permute-start | bytes 36872 | tf_op jit(solution)/shard_map/ppermute | solution.py:132
  26.2 2.4 %collective-permute-start.6 = (bf16[2,8,384]{2,1,0:T(8,128)(2,1)}, bf16[2,8,384]{2,1,0:T(8,128)(2,1)S(1)}, u32[]{:S(2)}, u32[]{:S(2)}) collective-permute-start(bf16[2,8,384]{2,1,0:T(8,128)(2,1)} %pad_maximum_fusion.1), channel_id=1, source_target_pairs={{0,1},{1,0},{2,3},{3,2},{4,5},{5,4},{6,7},{7,6},{8,9},{9,8},{10,11... | collective-permute-start | bytes 36872 | tf_op jit(solution)/shard_map/ppermute | solution.py:132
  31.4 9.1 %collective-permute-start.10 = (f32[1,2,8,384]{3,1,2,0:T(2,128)}, f32[1,2,8,384]{3,1,2,0:T(2,128)}, u32[]{:S(2)}, u32[]{:S(2)}) collective-permute-start(f32[1,2,8,384]{3,1,2,0:T(2,128)} %bitcast.225), channel_id=1, source_target_pairs={{0,8},{1,9},{2,10},{3,11},{4,12},{5,13},{6,14},{7,15},{8,0},{9,1},... | collective-permute-start | bytes 73736 | tf_op jit(solution)/shard_map/ppermute | solution.py:144
  32.6 7.9 %collective-permute-start.11 = (f32[1,2,8,384]{3,1,2,0:T(2,128)}, f32[1,2,8,384]{3,1,2,0:T(2,128)}, u32[]{:S(2)}, u32[]{:S(2)}) collective-permute-start(f32[1,2,8,384]{3,1,2,0:T(2,128)} %bitcast.231), channel_id=1, source_target_pairs={{0,12},{1,13},{2,14},{3,15},{4,8},{5,9},{6,10},{7,11},{8,4},{9,5},... | collective-permute-start | bytes 73736 | tf_op jit(solution)/shard_map/ppermute | solution.py:144
  33.6 7.8 %copy-start.5 = (bf16[1440,8,1]{0,1,2:T(8,128)(2,1)S(1)}, bf16[1440,8,1]{0,1,2:T(8,128)(2,1)}, u32[]{:S(2)}) copy-start(bf16[1440,8,1]{0,1,2:T(8,128)(2,1)} %constant.110) | copy-start | bytes 69124
  33.6 7.0 %collective-permute-start.9 = (f32[1,2,8,384]{3,1,2,0:T(2,128)}, f32[1,2,8,384]{3,1,2,0:T(2,128)}, u32[]{:S(2)}, u32[]{:S(2)}) collective-permute-start(f32[1,2,8,384]{3,1,2,0:T(2,128)} %bitcast.226), channel_id=1, source_target_pairs={{0,4},{1,5},{2,6},{3,7},{4,0},{5,1},{6,2},{7,3},{8,12},{9,13},{10,... | collective-permute-start | bytes 73736 | tf_op jit(solution)/shard_map/ppermute | solution.py:144
  47.4 5.1 %collective-permute-start.13 = (f32[2,8,384]{2,1,0:T(8,128)S(1)}, f32[2,8,384]{2,1,0:T(8,128)S(1)}, u32[]{:S(2)}, u32[]{:S(2)}) collective-permute-start(f32[2,8,384]{2,1,0:T(8,128)S(1)} %bitcast.245), channel_id=1, source_target_pairs={{0,2},{1,3},{2,0},{3,1},{4,6},{5,7},{6,4},{7,5},{8,10},{9,11},{10,... | collective-permute-start | bytes 73736 | tf_op jit(solution)/shard_map/ppermute | solution.py:132
  48.9 3.6 %collective-permute-start.12 = (f32[2,8,384]{2,1,0:T(8,128)S(1)}, f32[2,8,384]{2,1,0:T(8,128)S(1)}, u32[]{:S(2)}, u32[]{:S(2)}) collective-permute-start(f32[2,8,384]{2,1,0:T(8,128)S(1)} %bitcast.246), channel_id=1, source_target_pairs={{0,1},{1,0},{2,3},{3,2},{4,5},{5,4},{6,7},{7,6},{8,9},{9,8},{10,11... | collective-permute-start | bytes 73736 | tf_op jit(solution)/shard_map/ppermute | solution.py:132
  48.9 3.6 %collective-permute-start.14 = (f32[2,8,384]{2,1,0:T(8,128)S(1)}, f32[2,8,384]{2,1,0:T(8,128)S(1)}, u32[]{:S(2)}, u32[]{:S(2)}) collective-permute-start(f32[2,8,384]{2,1,0:T(8,128)S(1)} %bitcast.247), channel_id=1, source_target_pairs={{0,3},{1,2},{2,1},{3,0},{4,7},{5,6},{6,5},{7,4},{8,11},{9,10},{10,... | collective-permute-start | bytes 73736 | tf_op jit(solution)/shard_map/ppermute | solution.py:132
  52.5 11.6 %copy-start.7 = (bf16[2,4,384]{2,0,1:T(2,128)(2,1)S(1)}, bf16[2,4,384]{2,0,1:T(2,128)(2,1)}, u32[]{:S(2)}) copy-start(bf16[2,4,384]{2,0,1:T(2,128)(2,1)} %copy-done.6) | copy-start | bytes 18436
  53.1 5.3 %collective-permute-start.16 = (f32[1,2,8,384]{3,1,2,0:T(2,128)S(1)}, f32[1,2,8,384]{3,1,2,0:T(2,128)S(1)}, u32[]{:S(2)}, u32[]{:S(2)}) collective-permute-start(f32[1,2,8,384]{3,1,2,0:T(2,128)S(1)} %bitcast.262), channel_id=1, source_target_pairs={{0,8},{1,9},{2,10},{3,11},{4,12},{5,13},{6,14},{7,15},{8,0},{9,1},... | collective-permute-start | bytes 73736 | tf_op jit(solution)/shard_map/ppermute | solution.py:144
  55.3 5.6 %collective-permute-start.17 = (f32[1,2,8,384]{3,1,2,0:T(2,128)S(1)}, f32[1,2,8,384]{3,1,2,0:T(2,128)S(1)}, u32[]{:S(2)}, u32[]{:S(2)}) collective-permute-start(f32[1,2,8,384]{3,1,2,0:T(2,128)S(1)} %bitcast.261), channel_id=1, source_target_pairs={{0,12},{1,13},{2,14},{3,15},{4,8},{5,9},{6,10},{7,11},{8,4},{9,5},... | collective-permute-start | bytes 73736 | tf_op jit(solution)/shard_map/ppermute | solution.py:144
  56.2 4.7 %collective-permute-start.15 = (f32[1,2,8,384]{3,1,2,0:T(2,128)S(1)}, f32[1,2,8,384]{3,1,2,0:T(2,128)S(1)}, u32[]{:S(2)}, u32[]{:S(2)}) collective-permute-start(f32[1,2,8,384]{3,1,2,0:T(2,128)S(1)} %bitcast.259), channel_id=1, source_target_pairs={{0,4},{1,5},{2,6},{3,7},{4,0},{5,1},{6,2},{7,3},{8,12},{9,13},{10,... | collective-permute-start | bytes 73736 | tf_op jit(solution)/shard_map/ppermute | solution.py:144
  56.7 10.5 %collective-permute-start.24 = (bf16[8,24,384]{2,1,0:T(8,128)(2,1)S(1)}, bf16[8,24,384]{2,1,0:T(8,128)(2,1)S(1)}, u32[]{:S(2)}, u32[]{:S(2)}) collective-permute-start(bf16[8,24,384]{2,1,0:T(8,128)(2,1)S(1)} %fusion.35), channel_id=1, source_target_pairs={{0,1},{1,0},{2,3},{3,2},{4,5},{5,4},{6,7},{7,6},{8,9},{9,8},{10,11... | collective-permute-start | bytes 442376 | tf_op jit(solution)/shard_map/ppermute | solution.py:122
  62.1 4.7 %collective-permute-start.20 = (bf16[2,8,384]{2,1,0:T(8,128)(2,1)S(1)}, bf16[2,8,384]{2,1,0:T(8,128)(2,1)S(1)}, u32[]{:S(2)}, u32[]{:S(2)}) collective-permute-start(bf16[2,8,384]{2,1,0:T(8,128)(2,1)S(1)} %pad_maximum_fusion.2), channel_id=1, source_target_pairs={{0,3},{1,2},{2,1},{3,0},{4,7},{5,6},{6,5},{7,4},{8,11},{9,10},{10,... | collective-permute-start | bytes 36872 | tf_op jit(solution)/shard_map/ppermute | solution.py:132
  62.2 4.7 %collective-permute-start.19 = (bf16[2,8,384]{2,1,0:T(8,128)(2,1)S(1)}, bf16[2,8,384]{2,1,0:T(8,128)(2,1)S(1)}, u32[]{:S(2)}, u32[]{:S(2)}) collective-permute-start(bf16[2,8,384]{2,1,0:T(8,128)(2,1)S(1)} %pad_maximum_fusion.2), channel_id=1, source_target_pairs={{0,2},{1,3},{2,0},{3,1},{4,6},{5,7},{6,4},{7,5},{8,10},{9,11},{10,... | collective-permute-start | bytes 36872 | tf_op jit(solution)/shard_map/ppermute | solution.py:132
  63.8 3.1 %collective-permute-start.18 = (bf16[2,8,384]{2,1,0:T(8,128)(2,1)S(1)}, bf16[2,8,384]{2,1,0:T(8,128)(2,1)S(1)}, u32[]{:S(2)}, u32[]{:S(2)}) collective-permute-start(bf16[2,8,384]{2,1,0:T(8,128)(2,1)S(1)} %pad_maximum_fusion.2), channel_id=1, source_target_pairs={{0,1},{1,0},{2,3},{3,2},{4,5},{5,4},{6,7},{7,6},{8,9},{9,8},{10,11... | collective-permute-start | bytes 36872 | tf_op jit(solution)/shard_map/ppermute | solution.py:132
  65.7 13.1 %copy-start.3 = (bf16[2,1440,384]{2,1,0:T(8,128)(2,1)S(1)}, bf16[2,1440,384]{2,1,0:T(8,128)(2,1)}, u32[]{:S(2)}) copy-start(bf16[2,1440,384]{2,1,0:T(8,128)(2,1)} %param.11) | copy-start | bytes 6635524
  67.3 5.3 %collective-permute-start.25 = (bf16[4,24,384]{2,1,0:T(8,128)(2,1)S(1)}, bf16[4,24,384]{2,1,0:T(8,128)(2,1)S(1)}, u32[]{:S(2)}, u32[]{:S(2)}) collective-permute-start(bf16[4,24,384]{2,1,0:T(8,128)(2,1)S(1)} %fusion.38), channel_id=1, source_target_pairs={{0,2},{1,3},{2,0},{3,1},{4,6},{5,7},{6,4},{7,5},{8,10},{9,11},{10,... | collective-permute-start | bytes 221192 | tf_op jit(solution)/shard_map/ppermute | solution.py:122
  69.0 4.8 %collective-permute-start.22 = (f32[1,2,8,384]{3,1,2,0:T(2,128)S(1)}, f32[1,2,8,384]{3,1,2,0:T(2,128)S(1)}, u32[]{:S(2)}, u32[]{:S(2)}) collective-permute-start(f32[1,2,8,384]{3,1,2,0:T(2,128)S(1)} %bitcast.260), channel_id=1, source_target_pairs={{0,8},{1,9},{2,10},{3,11},{4,12},{5,13},{6,14},{7,15},{8,0},{9,1},... | collective-permute-start | bytes 73736 | tf_op jit(solution)/shard_map/ppermute | solution.py:144
  69.9 5.8 %collective-permute-start.23 = (f32[1,2,8,384]{3,1,2,0:T(2,128)S(1)}, f32[1,2,8,384]{3,1,2,0:T(2,128)S(1)}, u32[]{:S(2)}, u32[]{:S(2)}) collective-permute-start(f32[1,2,8,384]{3,1,2,0:T(2,128)S(1)} %bitcast.258), channel_id=1, source_target_pairs={{0,12},{1,13},{2,14},{3,15},{4,8},{5,9},{6,10},{7,11},{8,4},{9,5},... | collective-permute-start | bytes 73736 | tf_op jit(solution)/shard_map/ppermute | solution.py:144
  71.2 4.6 %collective-permute-start.21 = (f32[1,2,8,384]{3,1,2,0:T(2,128)S(1)}, f32[1,2,8,384]{3,1,2,0:T(2,128)S(1)}, u32[]{:S(2)}, u32[]{:S(2)}) collective-permute-start(f32[1,2,8,384]{3,1,2,0:T(2,128)S(1)} %bitcast.257), channel_id=1, source_target_pairs={{0,4},{1,5},{2,6},{3,7},{4,0},{5,1},{6,2},{7,3},{8,12},{9,13},{10,... | collective-permute-start | bytes 73736 | tf_op jit(solution)/shard_map/ppermute | solution.py:144
  72.6 4.4 %collective-permute-start.26 = (f32[2,24,384]{2,1,0:T(8,128)S(1)}, f32[2,24,384]{2,1,0:T(8,128)S(1)}, u32[]{:S(2)}, u32[]{:S(2)}) collective-permute-start(f32[2,24,384]{2,1,0:T(8,128)S(1)} %dynamic-slice_bitcast_fusion), channel_id=1, source_target_pairs={{0,4},{1,5},{2,6},{3,7},{4,0},{5,1},{6,2},{7,3},{8,12},{9,13},{10,... | collective-permute-start | bytes 221192 | tf_op jit(solution)/shard_map/ppermute | solution.py:122
  77.1 5.3 %collective-permute-start.27 = (f32[1,24,384]{2,1,0:T(8,128)S(1)}, f32[1,24,384]{2,1,0:T(8,128)S(1)}, u32[]{:S(2)}, u32[]{:S(2)}) collective-permute-start(f32[1,24,384]{2,1,0:T(8,128)S(1)} %constant_dynamic-slice_fusion), channel_id=1, source_target_pairs={{0,8},{1,9},{2,10},{3,11},{4,12},{5,13},{6,14},{7,15},{8,0},{9,1},... | collective-permute-start | bytes 110600 | tf_op jit(solution)/shard_map/ppermute | solution.py:122
  (5 other events, 20.1 us)

commit v14 on v13

--- a/solution.py
+++ b/solution.py
@@ -238,9 +238,11 @@
     half = 0.5 * x * (1.0 - t * t) * (k_gelu * (1.0 + 3.0 * 0.044715 * x2))
     slope_b = (upstream.astype(jnp.float32) * (0.5 * (1.0 + t) + half)).astype(jnp.bfloat16)
 
-    skip_terms = jnp.einsum("jkc,jkd->cd", activations, slope_b, preferred_element_type=jnp.float32)
+    skip_terms = jnp.einsum("jkc,jkd->cd", activations, slope_b, preferred_element_type=jnp.float32) * (
+        1.0 / math.sqrt(lat_total * lon_total)
+    )
     skip_blocks = skip_terms.reshape((groups, -1) + skip_terms.shape[1:])
-    grad_skip = xor_reduce_scatter(skip_blocks, "lat", groups, me, 1, 2) * (1.0 / math.sqrt(lat_total * lon_total))
+    grad_skip = xor_reduce_scatter(skip_blocks, "lat", groups, me, 1, 2)
     through_skip = jnp.einsum("jkd,cd->jkc", slope_b, skip_weight, preferred_element_type=jnp.float32)
 
     mode_grads = jnp.einsum("jkc,kf->jfc", slope_b, fourier, preferred_element_type=jnp.float32)

time: 83.5 us -> 83.5 us (level)
  no operation moved by 1% of the time
where the time goes in v14:
time: 83.5 us; the launch traced here: 83 us
  starting transfers between devices  28.5 us (34%)
  matrix products  21.8 us (26%)
  local copies, waits for them, and re-layouts  15.4 us (18%)
  waiting for transfers between devices  12.7 us (15%)
  other arithmetic  3.6 us (4%)
  between operations  1.11 us (1%)
    ppermute x12, starting transfers between devices, xor_exchange(): lax.ppermute(view[:, k], axis_name, [(i, i ^ mask) for i in range(groups)])  15.2 us
    ppermute x12, starting transfers between devices, xor_exchange(): lax.ppermute(values, axis_name, [(i, i ^ k) for i in range(groups)])  9.07 us
    ppermute x12, waiting for transfers between devices, xor_exchange(): lax.ppermute(view[:, k], axis_name, [(i, i ^ mask) for i in range(groups)])  9.05 us
    unnamed x35, local copies, waits for them, and re-layouts  8 us
    dot_general x1, matrix products, local(): jnp.einsum('jfc,kf->jkc', grid_modes, fourier, preferred_element_type=jnp...  5.59 us
    dot_general x1, matrix products, local(): jnp.einsum('jkc,cd->jkd', activations, skip_weight, preferred_element_typ...  4.51 us
    ppermute x4, starting transfers between devices, xor_reduce_scatter(): lax.ppermute(sent, axis_name, [(i, i ^ mask) for i in range(groups)])  4.17 us
    dot_general x1, matrix products, local(): jnp.einsum('jfc,kf->jkc', row_grads, fourier, preferred_element_type=jnp....  2.45 us
  transfers between devices with their start and end apart: 28, of which 9 were waited for; matrix products, arithmetic and copies ran while one was open for 27% of the time, Pallas kernels for 0%

profile of v14, /device:TPU:0, one launch (start us, length us, event | category | flops | bytes accessed | tf_op | source)
XLA Modules:
  0.0 83.0 jit_solution(6669177207619022183)
XLA Ops:
  0.7 1.6 %copy-done = bf16[2,1440,384]{2,1,0:T(8,128)(2,1)S(1)} copy-done((bf16[2,1440,384]{2,1,0:T(8,128)(2,1)S(1)}, bf16[2,1440,384]{2,1,0:T(8,128)(2,1)}, u32[]{:S(2)}) %copy-start) | copy-done | bytes 2211864
  2.3 1.1 %fusion.94 = f32[8,2,384]{2,0,1:T(8,128)S(1)} fusion(bf16[1440,8,1]{0,1,2:T(8,128)(2,1)} %constant.110, bf16[2,1440,384]{2,1,0:T(8,128)(2,1)S(1)} %copy-done), kind=kOutput, calls=%fused_computation.155 | convolution fusion | flops 17694720 | bytes 2259456 | tf_op jit(solution)/shard_map/jkc,kf->jfc/dot_general | solution.py:227
  3.4 3.0 %collective-permute-start.1 = (f32[2,8,384]{2,1,0:T(8,128)S(1)}, f32[2,8,384]{2,1,0:T(8,128)S(1)}, u32[]{:S(2)}, u32[]{:S(2)}) collective-permute-start(f32[2,8,384]{2,1,0:T(8,128)S(1)} %bitcast.243), channel_id=1, source_target_pairs={{0,2},{1,3},{2,0},{3,1},{4,6},{5,7},{6,4},{7,5},{8,10},{9,11},{10,... | collective-permute-start | bytes 73736 | tf_op jit(solution)/shard_map/ppermute | solution.py:132
  8.6 1.6 %gather_fusion = f32[64,16]{1,0:T(8,128)S(1)} fusion(f32[32,32,16]{2,1,0:T(8,128)} %constant.83, s32[64]{0:T(128)S(1)} %reshape.189), kind=kCustom, calls=%fused_computation.2 | custom fusion | bytes 8704 | tf_op jit(solution)/shard_map/gather | solution.py:214
  14.2 3.1 %collective-permute-start.4 = (f32[1,2,8,384]{3,1,2,0:T(2,128)}, f32[1,2,8,384]{3,1,2,0:T(2,128)S(1)}, u32[]{:S(2)}, u32[]{:S(2)}) collective-permute-start(f32[1,2,8,384]{3,1,2,0:T(2,128)} %bitcast.229), channel_id=1, source_target_pairs={{0,8},{1,9},{2,10},{3,11},{4,12},{5,13},{6,14},{7,15},{8,0},{9,1},... | collective-permute-start | bytes 73736 | tf_op jit(solution)/shard_map/ppermute | solution.py:144
  17.3 1.3 %collective-permute-start.5 = (f32[1,2,8,384]{3,1,2,0:T(2,128)}, f32[1,2,8,384]{3,1,2,0:T(2,128)S(1)}, u32[]{:S(2)}, u32[]{:S(2)}) collective-permute-start(f32[1,2,8,384]{3,1,2,0:T(2,128)} %bitcast.234), channel_id=1, source_target_pairs={{0,12},{1,13},{2,14},{3,15},{4,8},{5,9},{6,10},{7,11},{8,4},{9,5},... | collective-permute-start | bytes 73736 | tf_op jit(solution)/shard_map/ppermute | solution.py:144
  19.1 1.6 %gather_fusion.1 = f32[64,16]{1,0:T(8,128)S(1)} fusion(f32[32,32,16]{2,1,0:T(8,128)} %constant.83, s32[64]{0:T(128)S(1)} %reshape.195), kind=kCustom, calls=%fused_computation.3 | custom fusion | bytes 8704 | tf_op jit(solution)/shard_map/gather | solution.py:217
  20.7 2.5 %collective-permute-done.5 = f32[1,2,8,384]{3,1,2,0:T(2,128)S(1)} collective-permute-done((f32[1,2,8,384]{3,1,2,0:T(2,128)}, f32[1,2,8,384]{3,1,2,0:T(2,128)S(1)}, u32[]{:S(2)}, u32[]{:S(2)}) %collective-permute-start.5) | collective-permute-done | bytes 24608 | tf_op jit(solution)/shard_map/ppermute | solution.py:144
  24.6 1.6 %collective-permute-start.7 = (bf16[2,8,384]{2,1,0:T(8,128)(2,1)}, bf16[2,8,384]{2,1,0:T(8,128)(2,1)S(1)}, u32[]{:S(2)}, u32[]{:S(2)}) collective-permute-start(bf16[2,8,384]{2,1,0:T(8,128)(2,1)} %pad_maximum_fusion.1), channel_id=1, source_target_pairs={{0,2},{1,3},{2,0},{3,1},{4,6},{5,7},{6,4},{7,5},{8,10},{9,11},{10,... | collective-permute-start | bytes 36872 | tf_op jit(solution)/shard_map/ppermute | solution.py:132
  31.4 1.2 %collective-permute-start.10 = (f32[1,2,8,384]{3,1,2,0:T(2,128)}, f32[1,2,8,384]{3,1,2,0:T(2,128)}, u32[]{:S(2)}, u32[]{:S(2)}) collective-permute-start(f32[1,2,8,384]{3,1,2,0:T(2,128)} %bitcast.227), channel_id=1, source_target_pairs={{0,8},{1,9},{2,10},{3,11},{4,12},{5,13},{6,14},{7,15},{8,0},{9,1},... | collective-permute-start | bytes 73736 | tf_op jit(solution)/shard_map/ppermute | solution.py:144
  32.6 0.9 %collective-permute-start.11 = (f32[1,2,8,384]{3,1,2,0:T(2,128)}, f32[1,2,8,384]{3,1,2,0:T(2,128)}, u32[]{:S(2)}, u32[]{:S(2)}) collective-permute-start(f32[1,2,8,384]{3,1,2,0:T(2,128)} %bitcast.233), channel_id=1, source_target_pairs={{0,12},{1,13},{2,14},{3,15},{4,8},{5,9},{6,10},{7,11},{8,4},{9,5},... | collective-permute-start | bytes 73736 | tf_op jit(solution)/shard_map/ppermute | solution.py:144
  33.6 1.3 %collective-permute-start.9 = (f32[1,2,8,384]{3,1,2,0:T(2,128)}, f32[1,2,8,384]{3,1,2,0:T(2,128)}, u32[]{:S(2)}, u32[]{:S(2)}) collective-permute-start(f32[1,2,8,384]{3,1,2,0:T(2,128)} %bitcast.228), channel_id=1, source_target_pairs={{0,4},{1,5},{2,6},{3,7},{4,0},{5,1},{6,2},{7,3},{8,12},{9,13},{10,... | collective-permute-start | bytes 73736 | tf_op jit(solution)/shard_map/ppermute | solution.py:144
  34.9 4.5 %fusion.34 = f32[2,1440,384]{2,1,0:T(8,128)} fusion(bf16[2,1440,384]{2,1,0:T(8,128)(2,1)S(1)} %copy-done, bf16[384,384]{1,0:T(8,128)(2,1)} %param.12), kind=kOutput, calls=%fused_computation.55 | convolution fusion | flops 849346560 | bytes 6930432 | tf_op jit(solution)/shard_map/jkc,cd->jkd/dot_general | solution.py:233
  39.6 0.9 %copy.165 = f32[4,4,2,2,8]{1,0,2,3,4:T(4,128)S(1)} copy(f32[4,4,2,2,8]{4,3,2,1,0:T(2,128)} %get-tuple-element.31) | data formatting | bytes 4096
  41.4 5.6 %fusion = bf16[2,1440,384]{2,1,0:T(8,128)(2,1)S(1)} fusion(bf16[2,1440,384]{2,1,0:T(8,128)(2,1)} %param.11, f32[2,1440,384]{2,1,0:T(8,128)} %fusion.34, bf16[1440,8,1]{0,1,2:T(8,128)(2,1)S(1)} %copy-done.5, bf16[2,8,384]{2,0,1:T(2,128)(2,1)S(1)} %fusion.62), kind=kOutput, calls=%fused_computation.6 | convolution fusion | flops 39813120 | bytes 8882688 | tf_op jit(solution)/shard_map/jfc,kf->jkc/dot_general | solution.py:232
  47.4 1.5 %collective-permute-start.13 = (f32[2,8,384]{2,1,0:T(8,128)S(1)}, f32[2,8,384]{2,1,0:T(8,128)S(1)}, u32[]{:S(2)}, u32[]{:S(2)}) collective-permute-start(f32[2,8,384]{2,1,0:T(8,128)S(1)} %bitcast.247), channel_id=1, source_target_pairs={{0,2},{1,3},{2,0},{3,1},{4,6},{5,7},{6,4},{7,5},{8,10},{9,11},{10,... | collective-permute-start | bytes 73736 | tf_op jit(solution)/shard_map/ppermute | solution.py:132
  49.5 1.5 %fusion.32 = f32[2,1440,384]{2,1,0:T(8,128)S(1)} fusion(bf16[2,1440,384]{2,1,0:T(8,128)(2,1)S(1)} %fusion, bf16[384,384]{1,0:T(8,128)(2,1)S(1)} %copy-done.4), kind=kOutput, calls=%fused_computation.53 | convolution fusion | flops 849346560 | bytes 6930432 | tf_op jit(solution)/shard_map/jkd,cd->jkc/dot_general | solution.py:246
  51.1 1.4 %fusion.5 = f32[384,384]{0,1:T(8,128)S(1)} fusion(bf16[2,1440,384]{2,1,0:T(8,128)(2,1)S(1)} %fusion, bf16[2,1440,384]{2,1,0:T(8,128)(2,1)S(1)} %copy-done), kind=kOutput, calls=%fused_computation.15 | convolution fusion | flops 849494016 | bytes 5013504 | tf_op jit(solution)/shard_map/jkc,jkd->cd/dot_general | solution.py:241
  53.1 2.2 %collective-permute-start.16 = (f32[1,2,8,384]{3,1,2,0:T(2,128)S(1)}, f32[1,2,8,384]{3,1,2,0:T(2,128)S(1)}, u32[]{:S(2)}, u32[]{:S(2)}) collective-permute-start(f32[1,2,8,384]{3,1,2,0:T(2,128)S(1)} %bitcast.264), channel_id=1, source_target_pairs={{0,8},{1,9},{2,10},{3,11},{4,12},{5,13},{6,14},{7,15},{8,0},{9,1},... | collective-permute-start | bytes 73736 | tf_op jit(solution)/shard_map/ppermute | solution.py:144
  55.3 0.9 %collective-permute-start.17 = (f32[1,2,8,384]{3,1,2,0:T(2,128)S(1)}, f32[1,2,8,384]{3,1,2,0:T(2,128)S(1)}, u32[]{:S(2)}, u32[]{:S(2)}) collective-permute-start(f32[1,2,8,384]{3,1,2,0:T(2,128)S(1)} %bitcast.263), channel_id=1, source_target_pairs={{0,12},{1,13},{2,14},{3,15},{4,8},{5,9},{6,10},{7,11},{8,4},{9,5},... | collective-permute-start | bytes 73736 | tf_op jit(solution)/shard_map/ppermute | solution.py:144
  56.7 1.7 %collective-permute-done.16 = f32[1,2,8,384]{3,1,2,0:T(2,128)S(1)} collective-permute-done((f32[1,2,8,384]{3,1,2,0:T(2,128)S(1)}, f32[1,2,8,384]{3,1,2,0:T(2,128)S(1)}, u32[]{:S(2)}, u32[]{:S(2)}) %collective-permute-start.16) | collective-permute-done | bytes 24608 | tf_op jit(solution)/shard_map/ppermute | solution.py:144
  58.4 2.5 %collective-permute-done.17 = f32[1,2,8,384]{3,1,2,0:T(2,128)S(1)} collective-permute-done((f32[1,2,8,384]{3,1,2,0:T(2,128)S(1)}, f32[1,2,8,384]{3,1,2,0:T(2,128)S(1)}, u32[]{:S(2)}, u32[]{:S(2)}) %collective-permute-start.17) | collective-permute-done | bytes 24608 | tf_op jit(solution)/shard_map/ppermute | solution.py:144
  62.2 1.6 %collective-permute-start.19 = (bf16[2,8,384]{2,1,0:T(8,128)(2,1)S(1)}, bf16[2,8,384]{2,1,0:T(8,128)(2,1)S(1)}, u32[]{:S(2)}, u32[]{:S(2)}) collective-permute-start(bf16[2,8,384]{2,1,0:T(8,128)(2,1)S(1)} %pad_maximum_fusion.2), channel_id=1, source_target_pairs={{0,2},{1,3},{2,0},{3,1},{4,6},{5,7},{6,4},{7,5},{8,10},{9,11},{10,... | collective-permute-start | bytes 36872 | tf_op jit(solution)/shard_map/ppermute | solution.py:132
  65.7 1.1 %copy.130 = bf16[2,2,384,384]{3,2,1,0:T(8,128)(2,1)} copy(bf16[2,2,384,384]{3,2,0,1:T(8,128)(2,1)S(1)} %pad_maximum_fusion) | data formatting | bytes 2359296
  67.3 1.6 %collective-permute-start.25 = (bf16[4,24,384]{2,1,0:T(8,128)(2,1)S(1)}, bf16[4,24,384]{2,1,0:T(8,128)(2,1)S(1)}, u32[]{:S(2)}, u32[]{:S(2)}) collective-permute-start(bf16[4,24,384]{2,1,0:T(8,128)(2,1)S(1)} %fusion.39), channel_id=1, source_target_pairs={{0,2},{1,3},{2,0},{3,1},{4,6},{5,7},{6,4},{7,5},{8,10},{9,11},{10,... | collective-permute-start | bytes 221192 | tf_op jit(solution)/shard_map/ppermute | solution.py:122
  69.9 1.3 %collective-permute-start.23 = (f32[1,2,8,384]{3,1,2,0:T(2,128)S(1)}, f32[1,2,8,384]{3,1,2,0:T(2,128)S(1)}, u32[]{:S(2)}, u32[]{:S(2)}) collective-permute-start(f32[1,2,8,384]{3,1,2,0:T(2,128)S(1)} %bitcast.260), channel_id=1, source_target_pairs={{0,12},{1,13},{2,14},{3,15},{4,8},{5,9},{6,10},{7,11},{8,4},{9,5},... | collective-permute-start | bytes 73736 | tf_op jit(solution)/shard_map/ppermute | solution.py:144
  71.2 1.4 %collective-permute-start.21 = (f32[1,2,8,384]{3,1,2,0:T(2,128)S(1)}, f32[1,2,8,384]{3,1,2,0:T(2,128)S(1)}, u32[]{:S(2)}, u32[]{:S(2)}) collective-permute-start(f32[1,2,8,384]{3,1,2,0:T(2,128)S(1)} %bitcast.259), channel_id=1, source_target_pairs={{0,4},{1,5},{2,6},{3,7},{4,0},{5,1},{6,2},{7,3},{8,12},{9,13},{10,... | collective-permute-start | bytes 73736 | tf_op jit(solution)/shard_map/ppermute | solution.py:144
  73.8 1.9 %collective-permute-done.23 = f32[1,2,8,384]{3,1,2,0:T(2,128)S(1)} collective-permute-done((f32[1,2,8,384]{3,1,2,0:T(2,128)S(1)}, f32[1,2,8,384]{3,1,2,0:T(2,128)S(1)}, u32[]{:S(2)}, u32[]{:S(2)}) %collective-permute-start.23) | collective-permute-done | bytes 24608 | tf_op jit(solution)/shard_map/ppermute | solution.py:144
  75.8 1.3 %collective-permute-done.26 = f32[2,24,384]{2,1,0:T(8,128)S(1)} collective-permute-done((f32[2,24,384]{2,1,0:T(8,128)S(1)}, f32[2,24,384]{2,1,0:T(8,128)S(1)}, u32[]{:S(2)}, u32[]{:S(2)}) %collective-permute-start.26) | collective-permute-done | bytes 73760 | tf_op jit(solution)/shard_map/ppermute | solution.py:122
  77.1 1.8 %collective-permute-start.27 = (f32[1,24,384]{2,1,0:T(8,128)S(1)}, f32[1,24,384]{2,1,0:T(8,128)S(1)}, u32[]{:S(2)}, u32[]{:S(2)}) collective-permute-start(f32[1,24,384]{2,1,0:T(8,128)S(1)} %constant_dynamic-slice_fusion), channel_id=1, source_target_pairs={{0,8},{1,9},{2,10},{3,11},{4,12},{5,13},{6,14},{7,15},{8,0},{9,1},... | collective-permute-start | bytes 110600 | tf_op jit(solution)/shard_map/ppermute | solution.py:122
  78.9 2.5 %fusion.2 = bf16[2,1440,384]{2,1,0:T(8,128)(2,1)} fusion(f32[2,1440,384]{2,1,0:T(8,128)S(1)} %fusion.32, bf16[2,1440,384]{2,1,0:T(8,128)(2,1)S(1)} %copy-done.3, bf16[1440,8,1]{0,1,2:T(8,128)(2,1)S(1)} %copy-done.5, bf16[2,8,384]{2,0,1:T(2,128)(2,1)S(1)} %fusion.60), kind=kOutput, calls=%fused_computation.8 | convolution fusion | flops 22118400 | bytes 8882688 | tf_op jit(solution)/shard_map/jfc,kf->jkc/dot_general | solution.py:252
  81.3 1.1 %collective-permute-done.27 = f32[1,24,384]{2,1,0:T(8,128)S(1)} collective-permute-done((f32[1,24,384]{2,1,0:T(8,128)S(1)}, f32[1,24,384]{2,1,0:T(8,128)S(1)}, u32[]{:S(2)}, u32[]{:S(2)}) %collective-permute-start.27) | collective-permute-done | bytes 36896 | tf_op jit(solution)/shard_map/ppermute | solution.py:122
  (128 shorter events, 22.8 us)
Async XLA Ops:
  3.4 7.7 %collective-permute-start.1 = (f32[2,8,384]{2,1,0:T(8,128)S(1)}, f32[2,8,384]{2,1,0:T(8,128)S(1)}, u32[]{:S(2)}, u32[]{:S(2)}) collective-permute-start(f32[2,8,384]{2,1,0:T(8,128)S(1)} %bitcast.243), channel_id=1, source_target_pairs={{0,2},{1,3},{2,0},{3,1},{4,6},{5,7},{6,4},{7,5},{8,10},{9,11},{10,... | collective-permute-start | bytes 73736 | tf_op jit(solution)/shard_map/ppermute | solution.py:132
  6.4 4.8 %collective-permute-start = (f32[2,8,384]{2,1,0:T(8,128)S(1)}, f32[2,8,384]{2,1,0:T(8,128)}, u32[]{:S(2)}, u32[]{:S(2)}) collective-permute-start(f32[2,8,384]{2,1,0:T(8,128)S(1)} %bitcast.244), channel_id=1, source_target_pairs={{0,1},{1,0},{2,3},{3,2},{4,5},{5,4},{6,7},{7,6},{8,9},{9,8},{10,11... | collective-permute-start | bytes 73736 | tf_op jit(solution)/shard_map/ppermute | solution.py:132
  6.4 4.8 %collective-permute-start.2 = (f32[2,8,384]{2,1,0:T(8,128)S(1)}, f32[2,8,384]{2,1,0:T(8,128)}, u32[]{:S(2)}, u32[]{:S(2)}) collective-permute-start(f32[2,8,384]{2,1,0:T(8,128)S(1)} %bitcast.245), channel_id=1, source_target_pairs={{0,3},{1,2},{2,1},{3,0},{4,7},{5,6},{6,5},{7,4},{8,11},{9,10},{10,... | collective-permute-start | bytes 73736 | tf_op jit(solution)/shard_map/ppermute | solution.py:132
  7.4 15.8 %copy-start.2 = (bf16[2,2,384,384]{3,2,1,0:T(8,128)(2,1)S(1)}, bf16[2,2,384,384]{3,2,1,0:T(8,128)(2,1)}, u32[]{:S(2)}) copy-start(bf16[2,2,384,384]{3,2,1,0:T(8,128)(2,1)} %param.13) | copy-start | bytes 3538948
  14.2 6.4 %collective-permute-start.4 = (f32[1,2,8,384]{3,1,2,0:T(2,128)}, f32[1,2,8,384]{3,1,2,0:T(2,128)S(1)}, u32[]{:S(2)}, u32[]{:S(2)}) collective-permute-start(f32[1,2,8,384]{3,1,2,0:T(2,128)} %bitcast.229), channel_id=1, source_target_pairs={{0,8},{1,9},{2,10},{3,11},{4,12},{5,13},{6,14},{7,15},{8,0},{9,1},... | collective-permute-start | bytes 73736 | tf_op jit(solution)/shard_map/ppermute | solution.py:144
  17.3 5.8 %collective-permute-start.5 = (f32[1,2,8,384]{3,1,2,0:T(2,128)}, f32[1,2,8,384]{3,1,2,0:T(2,128)S(1)}, u32[]{:S(2)}, u32[]{:S(2)}) collective-permute-start(f32[1,2,8,384]{3,1,2,0:T(2,128)} %bitcast.234), channel_id=1, source_target_pairs={{0,12},{1,13},{2,14},{3,15},{4,8},{5,9},{6,10},{7,11},{8,4},{9,5},... | collective-permute-start | bytes 73736 | tf_op jit(solution)/shard_map/ppermute | solution.py:144
  18.6 4.5 %collective-permute-start.3 = (f32[1,2,8,384]{3,1,2,0:T(2,128)}, f32[1,2,8,384]{3,1,2,0:T(2,128)S(1)}, u32[]{:S(2)}, u32[]{:S(2)}) collective-permute-start(f32[1,2,8,384]{3,1,2,0:T(2,128)} %bitcast.230), channel_id=1, source_target_pairs={{0,4},{1,5},{2,6},{3,7},{4,0},{5,1},{6,2},{7,3},{8,12},{9,13},{10,... | collective-permute-start | bytes 73736 | tf_op jit(solution)/shard_map/ppermute | solution.py:144
  24.6 3.4 %collective-permute-start.8 = (bf16[2,8,384]{2,1,0:T(8,128)(2,1)}, bf16[2,8,384]{2,1,0:T(8,128)(2,1)S(1)}, u32[]{:S(2)}, u32[]{:S(2)}) collective-permute-start(bf16[2,8,384]{2,1,0:T(8,128)(2,1)} %pad_maximum_fusion.1), channel_id=1, source_target_pairs={{0,3},{1,2},{2,1},{3,0},{4,7},{5,6},{6,5},{7,4},{8,11},{9,10},{10,... | collective-permute-start | bytes 36872 | tf_op jit(solution)/shard_map/ppermute | solution.py:132
  24.6 3.9 %collective-permute-start.7 = (bf16[2,8,384]{2,1,0:T(8,128)(2,1)}, bf16[2,8,384]{2,1,0:T(8,128)(2,1)S(1)}, u32[]{:S(2)}, u32[]{:S(2)}) collective-permute-start(bf16[2,8,384]{2,1,0:T(8,128)(2,1)} %pad_maximum_fusion.1), channel_id=1, source_target_pairs={{0,2},{1,3},{2,0},{3,1},{4,6},{5,7},{6,4},{7,5},{8,10},{9,11},{10,... | collective-permute-start | bytes 36872 | tf_op jit(solution)/shard_map/ppermute | solution.py:132
  26.2 2.4 %collective-permute-start.6 = (bf16[2,8,384]{2,1,0:T(8,128)(2,1)}, bf16[2,8,384]{2,1,0:T(8,128)(2,1)S(1)}, u32[]{:S(2)}, u32[]{:S(2)}) collective-permute-start(bf16[2,8,384]{2,1,0:T(8,128)(2,1)} %pad_maximum_fusion.1), channel_id=1, source_target_pairs={{0,1},{1,0},{2,3},{3,2},{4,5},{5,4},{6,7},{7,6},{8,9},{9,8},{10,11... | collective-permute-start | bytes 36872 | tf_op jit(solution)/shard_map/ppermute | solution.py:132
  31.4 9.1 %collective-permute-start.10 = (f32[1,2,8,384]{3,1,2,0:T(2,128)}, f32[1,2,8,384]{3,1,2,0:T(2,128)}, u32[]{:S(2)}, u32[]{:S(2)}) collective-permute-start(f32[1,2,8,384]{3,1,2,0:T(2,128)} %bitcast.227), channel_id=1, source_target_pairs={{0,8},{1,9},{2,10},{3,11},{4,12},{5,13},{6,14},{7,15},{8,0},{9,1},... | collective-permute-start | bytes 73736 | tf_op jit(solution)/shard_map/ppermute | solution.py:144
  32.6 7.9 %collective-permute-start.11 = (f32[1,2,8,384]{3,1,2,0:T(2,128)}, f32[1,2,8,384]{3,1,2,0:T(2,128)}, u32[]{:S(2)}, u32[]{:S(2)}) collective-permute-start(f32[1,2,8,384]{3,1,2,0:T(2,128)} %bitcast.233), channel_id=1, source_target_pairs={{0,12},{1,13},{2,14},{3,15},{4,8},{5,9},{6,10},{7,11},{8,4},{9,5},... | collective-permute-start | bytes 73736 | tf_op jit(solution)/shard_map/ppermute | solution.py:144
  33.6 7.8 %copy-start.5 = (bf16[1440,8,1]{0,1,2:T(8,128)(2,1)S(1)}, bf16[1440,8,1]{0,1,2:T(8,128)(2,1)}, u32[]{:S(2)}) copy-start(bf16[1440,8,1]{0,1,2:T(8,128)(2,1)} %constant.110) | copy-start | bytes 69124
  33.6 7.0 %collective-permute-start.9 = (f32[1,2,8,384]{3,1,2,0:T(2,128)}, f32[1,2,8,384]{3,1,2,0:T(2,128)}, u32[]{:S(2)}, u32[]{:S(2)}) collective-permute-start(f32[1,2,8,384]{3,1,2,0:T(2,128)} %bitcast.228), channel_id=1, source_target_pairs={{0,4},{1,5},{2,6},{3,7},{4,0},{5,1},{6,2},{7,3},{8,12},{9,13},{10,... | collective-permute-start | bytes 73736 | tf_op jit(solution)/shard_map/ppermute | solution.py:144
  47.4 5.1 %collective-permute-start.13 = (f32[2,8,384]{2,1,0:T(8,128)S(1)}, f32[2,8,384]{2,1,0:T(8,128)S(1)}, u32[]{:S(2)}, u32[]{:S(2)}) collective-permute-start(f32[2,8,384]{2,1,0:T(8,128)S(1)} %bitcast.247), channel_id=1, source_target_pairs={{0,2},{1,3},{2,0},{3,1},{4,6},{5,7},{6,4},{7,5},{8,10},{9,11},{10,... | collective-permute-start | bytes 73736 | tf_op jit(solution)/shard_map/ppermute | solution.py:132
  48.9 3.6 %collective-permute-start.12 = (f32[2,8,384]{2,1,0:T(8,128)S(1)}, f32[2,8,384]{2,1,0:T(8,128)S(1)}, u32[]{:S(2)}, u32[]{:S(2)}) collective-permute-start(f32[2,8,384]{2,1,0:T(8,128)S(1)} %bitcast.248), channel_id=1, source_target_pairs={{0,1},{1,0},{2,3},{3,2},{4,5},{5,4},{6,7},{7,6},{8,9},{9,8},{10,11... | collective-permute-start | bytes 73736 | tf_op jit(solution)/shard_map/ppermute | solution.py:132
  48.9 3.6 %collective-permute-start.14 = (f32[2,8,384]{2,1,0:T(8,128)S(1)}, f32[2,8,384]{2,1,0:T(8,128)S(1)}, u32[]{:S(2)}, u32[]{:S(2)}) collective-permute-start(f32[2,8,384]{2,1,0:T(8,128)S(1)} %bitcast.249), channel_id=1, source_target_pairs={{0,3},{1,2},{2,1},{3,0},{4,7},{5,6},{6,5},{7,4},{8,11},{9,10},{10,... | collective-permute-start | bytes 73736 | tf_op jit(solution)/shard_map/ppermute | solution.py:132
  52.5 11.6 %copy-start.7 = (bf16[2,4,384]{2,0,1:T(2,128)(2,1)S(1)}, bf16[2,4,384]{2,0,1:T(2,128)(2,1)}, u32[]{:S(2)}) copy-start(bf16[2,4,384]{2,0,1:T(2,128)(2,1)} %copy-done.6) | copy-start | bytes 18436
  53.1 5.3 %collective-permute-start.16 = (f32[1,2,8,384]{3,1,2,0:T(2,128)S(1)}, f32[1,2,8,384]{3,1,2,0:T(2,128)S(1)}, u32[]{:S(2)}, u32[]{:S(2)}) collective-permute-start(f32[1,2,8,384]{3,1,2,0:T(2,128)S(1)} %bitcast.264), channel_id=1, source_target_pairs={{0,8},{1,9},{2,10},{3,11},{4,12},{5,13},{6,14},{7,15},{8,0},{9,1},... | collective-permute-start | bytes 73736 | tf_op jit(solution)/shard_map/ppermute | solution.py:144
  55.3 5.6 %collective-permute-start.17 = (f32[1,2,8,384]{3,1,2,0:T(2,128)S(1)}, f32[1,2,8,384]{3,1,2,0:T(2,128)S(1)}, u32[]{:S(2)}, u32[]{:S(2)}) collective-permute-start(f32[1,2,8,384]{3,1,2,0:T(2,128)S(1)} %bitcast.263), channel_id=1, source_target_pairs={{0,12},{1,13},{2,14},{3,15},{4,8},{5,9},{6,10},{7,11},{8,4},{9,5},... | collective-permute-start | bytes 73736 | tf_op jit(solution)/shard_map/ppermute | solution.py:144
  56.2 4.7 %collective-permute-start.15 = (f32[1,2,8,384]{3,1,2,0:T(2,128)S(1)}, f32[1,2,8,384]{3,1,2,0:T(2,128)S(1)}, u32[]{:S(2)}, u32[]{:S(2)}) collective-permute-start(f32[1,2,8,384]{3,1,2,0:T(2,128)S(1)} %bitcast.261), channel_id=1, source_target_pairs={{0,4},{1,5},{2,6},{3,7},{4,0},{5,1},{6,2},{7,3},{8,12},{9,13},{10,... | collective-permute-start | bytes 73736 | tf_op jit(solution)/shard_map/ppermute | solution.py:144
  56.7 10.5 %collective-permute-start.24 = (bf16[8,24,384]{2,1,0:T(8,128)(2,1)S(1)}, bf16[8,24,384]{2,1,0:T(8,128)(2,1)S(1)}, u32[]{:S(2)}, u32[]{:S(2)}) collective-permute-start(bf16[8,24,384]{2,1,0:T(8,128)(2,1)S(1)} %fusion.36), channel_id=1, source_target_pairs={{0,1},{1,0},{2,3},{3,2},{4,5},{5,4},{6,7},{7,6},{8,9},{9,8},{10,11... | collective-permute-start | bytes 442376 | tf_op jit(solution)/shard_map/ppermute | solution.py:122
  62.1 4.7 %collective-permute-start.20 = (bf16[2,8,384]{2,1,0:T(8,128)(2,1)S(1)}, bf16[2,8,384]{2,1,0:T(8,128)(2,1)S(1)}, u32[]{:S(2)}, u32[]{:S(2)}) collective-permute-start(bf16[2,8,384]{2,1,0:T(8,128)(2,1)S(1)} %pad_maximum_fusion.2), channel_id=1, source_target_pairs={{0,3},{1,2},{2,1},{3,0},{4,7},{5,6},{6,5},{7,4},{8,11},{9,10},{10,... | collective-permute-start | bytes 36872 | tf_op jit(solution)/shard_map/ppermute | solution.py:132
  62.2 4.7 %collective-permute-start.19 = (bf16[2,8,384]{2,1,0:T(8,128)(2,1)S(1)}, bf16[2,8,384]{2,1,0:T(8,128)(2,1)S(1)}, u32[]{:S(2)}, u32[]{:S(2)}) collective-permute-start(bf16[2,8,384]{2,1,0:T(8,128)(2,1)S(1)} %pad_maximum_fusion.2), channel_id=1, source_target_pairs={{0,2},{1,3},{2,0},{3,1},{4,6},{5,7},{6,4},{7,5},{8,10},{9,11},{10,... | collective-permute-start | bytes 36872 | tf_op jit(solution)/shard_map/ppermute | solution.py:132
  63.8 3.1 %collective-permute-start.18 = (bf16[2,8,384]{2,1,0:T(8,128)(2,1)S(1)}, bf16[2,8,384]{2,1,0:T(8,128)(2,1)S(1)}, u32[]{:S(2)}, u32[]{:S(2)}) collective-permute-start(bf16[2,8,384]{2,1,0:T(8,128)(2,1)S(1)} %pad_maximum_fusion.2), channel_id=1, source_target_pairs={{0,1},{1,0},{2,3},{3,2},{4,5},{5,4},{6,7},{7,6},{8,9},{9,8},{10,11... | collective-permute-start | bytes 36872 | tf_op jit(solution)/shard_map/ppermute | solution.py:132
  65.7 13.1 %copy-start.3 = (bf16[2,1440,384]{2,1,0:T(8,128)(2,1)S(1)}, bf16[2,1440,384]{2,1,0:T(8,128)(2,1)}, u32[]{:S(2)}) copy-start(bf16[2,1440,384]{2,1,0:T(8,128)(2,1)} %param.11) | copy-start | bytes 6635524
  67.3 5.3 %collective-permute-start.25 = (bf16[4,24,384]{2,1,0:T(8,128)(2,1)S(1)}, bf16[4,24,384]{2,1,0:T(8,128)(2,1)S(1)}, u32[]{:S(2)}, u32[]{:S(2)}) collective-permute-start(bf16[4,24,384]{2,1,0:T(8,128)(2,1)S(1)} %fusion.39), channel_id=1, source_target_pairs={{0,2},{1,3},{2,0},{3,1},{4,6},{5,7},{6,4},{7,5},{8,10},{9,11},{10,... | collective-permute-start | bytes 221192 | tf_op jit(solution)/shard_map/ppermute | solution.py:122
  69.0 4.8 %collective-permute-start.22 = (f32[1,2,8,384]{3,1,2,0:T(2,128)S(1)}, f32[1,2,8,384]{3,1,2,0:T(2,128)S(1)}, u32[]{:S(2)}, u32[]{:S(2)}) collective-permute-start(f32[1,2,8,384]{3,1,2,0:T(2,128)S(1)} %bitcast.262), channel_id=1, source_target_pairs={{0,8},{1,9},{2,10},{3,11},{4,12},{5,13},{6,14},{7,15},{8,0},{9,1},... | collective-permute-start | bytes 73736 | tf_op jit(solution)/shard_map/ppermute | solution.py:144
  69.9 5.8 %collective-permute-start.23 = (f32[1,2,8,384]{3,1,2,0:T(2,128)S(1)}, f32[1,2,8,384]{3,1,2,0:T(2,128)S(1)}, u32[]{:S(2)}, u32[]{:S(2)}) collective-permute-start(f32[1,2,8,384]{3,1,2,0:T(2,128)S(1)} %bitcast.260), channel_id=1, source_target_pairs={{0,12},{1,13},{2,14},{3,15},{4,8},{5,9},{6,10},{7,11},{8,4},{9,5},... | collective-permute-start | bytes 73736 | tf_op jit(solution)/shard_map/ppermute | solution.py:144
  71.2 4.6 %collective-permute-start.21 = (f32[1,2,8,384]{3,1,2,0:T(2,128)S(1)}, f32[1,2,8,384]{3,1,2,0:T(2,128)S(1)}, u32[]{:S(2)}, u32[]{:S(2)}) collective-permute-start(f32[1,2,8,384]{3,1,2,0:T(2,128)S(1)} %bitcast.259), channel_id=1, source_target_pairs={{0,4},{1,5},{2,6},{3,7},{4,0},{5,1},{6,2},{7,3},{8,12},{9,13},{10,... | collective-permute-start | bytes 73736 | tf_op jit(solution)/shard_map/ppermute | solution.py:144
  72.6 4.4 %collective-permute-start.26 = (f32[2,24,384]{2,1,0:T(8,128)S(1)}, f32[2,24,384]{2,1,0:T(8,128)S(1)}, u32[]{:S(2)}, u32[]{:S(2)}) collective-permute-start(f32[2,24,384]{2,1,0:T(8,128)S(1)} %dynamic-slice_bitcast_fusion), channel_id=1, source_target_pairs={{0,4},{1,5},{2,6},{3,7},{4,0},{5,1},{6,2},{7,3},{8,12},{9,13},{10,... | collective-permute-start | bytes 221192 | tf_op jit(solution)/shard_map/ppermute | solution.py:122
  77.1 5.3 %collective-permute-start.27 = (f32[1,24,384]{2,1,0:T(8,128)S(1)}, f32[1,24,384]{2,1,0:T(8,128)S(1)}, u32[]{:S(2)}, u32[]{:S(2)}) collective-permute-start(f32[1,24,384]{2,1,0:T(8,128)S(1)} %constant_dynamic-slice_fusion), channel_id=1, source_target_pairs={{0,8},{1,9},{2,10},{3,11},{4,12},{5,13},{6,14},{7,15},{8,0},{9,1},... | collective-permute-start | bytes 110600 | tf_op jit(solution)/shard_map/ppermute | solution.py:122
  (5 other events, 20.1 us)

commit v15 on v13

--- a/solution.py
+++ b/solution.py
@@ -240,7 +240,7 @@
 
     skip_terms = jnp.einsum("jkc,jkd->cd", activations, slope_b, preferred_element_type=jnp.float32)
     skip_blocks = skip_terms.reshape((groups, -1) + skip_terms.shape[1:])
-    grad_skip = xor_reduce_scatter(skip_blocks, "lat", groups, me, 1, 2) * (1.0 / math.sqrt(lat_total * lon_total))
+    grad_skip = xor_reduce_scatter(skip_blocks, "lat", groups, me, 1, bits) * (1.0 / math.sqrt(lat_total * lon_total))
     through_skip = jnp.einsum("jkd,cd->jkc", slope_b, skip_weight, preferred_element_type=jnp.float32)
 
     mode_grads = jnp.einsum("jkc,kf->jfc", slope_b, fourier, preferred_element_type=jnp.float32)

time: 83.5 us -> 82.5 us (0.988)
  waiting for transfers between devices: 12.7 us -> 11.7 us
    ppermute x4, waiting for transfers between devices: 2.34 us -> 1.36 us  [xor_reduce_scatter(): lax.ppermute(sent, axis_name, [(i, i ^ mask) for i in range(groups)])]
  transfers between devices with their start and end apart: 28 -> 28, of which waited for: 9 -> 9; matrix products, arithmetic and copies ran while one was open for 27% -> 28% of each run, Pallas kernels for 0% -> 0%
where the time goes in v15:
time: 82.5 us; the launch traced here: 82 us
  starting transfers between devices  28.5 us (35%)
  matrix products  21.8 us (26%)
  local copies, waits for them, and re-layouts  15.4 us (19%)
  waiting for transfers between devices  11.7 us (14%)
  other arithmetic  3.61 us (4%)
  between operations  1.11 us (1%)
    ppermute x12, starting transfers between devices, xor_exchange(): lax.ppermute(view[:, k], axis_name, [(i, i ^ mask) for i in range(groups)])  15.2 us
    ppermute x12, starting transfers between devices, xor_exchange(): lax.ppermute(values, axis_name, [(i, i ^ k) for i in range(groups)])  9.07 us
    ppermute x12, waiting for transfers between devices, xor_exchange(): lax.ppermute(view[:, k], axis_name, [(i, i ^ mask) for i in range(groups)])  9.05 us
    unnamed x35, local copies, waits for them, and re-layouts  8 us
    dot_general x1, matrix products, local(): jnp.einsum('jfc,kf->jkc', grid_modes, fourier, preferred_element_type=jnp...  5.59 us
    dot_general x1, matrix products, local(): jnp.einsum('jkc,cd->jkd', activations, skip_weight, preferred_element_typ...  4.51 us
    ppermute x4, starting transfers between devices, xor_reduce_scatter(): lax.ppermute(sent, axis_name, [(i, i ^ mask) for i in range(groups)])  4.17 us
    dot_general x1, matrix products, local(): jnp.einsum('jfc,kf->jkc', row_grads, fourier, preferred_element_type=jnp....  2.45 us
  transfers between devices with their start and end apart: 28, of which 9 were waited for; matrix products, arithmetic and copies ran while one was open for 28% of the time, Pallas kernels for 0%

profile of v15, /device:TPU:0, one launch (start us, length us, event | category | flops | bytes accessed | tf_op | source)
XLA Modules:
  0.0 82.0 jit_solution(15402892780490297806)
XLA Ops:
  0.7 1.6 %copy-done = bf16[2,1440,384]{2,1,0:T(8,128)(2,1)S(1)} copy-done((bf16[2,1440,384]{2,1,0:T(8,128)(2,1)S(1)}, bf16[2,1440,384]{2,1,0:T(8,128)(2,1)}, u32[]{:S(2)}) %copy-start) | copy-done | bytes 2211864
  2.3 1.1 %fusion.94 = f32[8,2,384]{2,0,1:T(8,128)S(1)} fusion(bf16[1440,8,1]{0,1,2:T(8,128)(2,1)} %constant.110, bf16[2,1440,384]{2,1,0:T(8,128)(2,1)S(1)} %copy-done), kind=kOutput, calls=%fused_computation.154 | convolution fusion | flops 17694720 | bytes 2259456 | tf_op jit(solution)/shard_map/jkc,kf->jfc/dot_general | solution.py:227
  3.4 3.0 %collective-permute-start.1 = (f32[2,8,384]{2,1,0:T(8,128)S(1)}, f32[2,8,384]{2,1,0:T(8,128)S(1)}, u32[]{:S(2)}, u32[]{:S(2)}) collective-permute-start(f32[2,8,384]{2,1,0:T(8,128)S(1)} %bitcast.241), channel_id=1, source_target_pairs={{0,2},{1,3},{2,0},{3,1},{4,6},{5,7},{6,4},{7,5},{8,10},{9,11},{10,... | collective-permute-start | bytes 73736 | tf_op jit(solution)/shard_map/ppermute | solution.py:132
  8.6 1.6 %gather_fusion = f32[64,16]{1,0:T(8,128)S(1)} fusion(f32[32,32,16]{2,1,0:T(8,128)} %constant.83, s32[64]{0:T(128)S(1)} %reshape.194), kind=kCustom, calls=%fused_computation.2 | custom fusion | bytes 8704 | tf_op jit(solution)/shard_map/gather | solution.py:214
  14.2 3.1 %collective-permute-start.4 = (f32[1,2,8,384]{3,1,2,0:T(2,128)}, f32[1,2,8,384]{3,1,2,0:T(2,128)S(1)}, u32[]{:S(2)}, u32[]{:S(2)}) collective-permute-start(f32[1,2,8,384]{3,1,2,0:T(2,128)} %bitcast.227), channel_id=1, source_target_pairs={{0,8},{1,9},{2,10},{3,11},{4,12},{5,13},{6,14},{7,15},{8,0},{9,1},... | collective-permute-start | bytes 73736 | tf_op jit(solution)/shard_map/ppermute | solution.py:144
  17.3 1.3 %collective-permute-start.5 = (f32[1,2,8,384]{3,1,2,0:T(2,128)}, f32[1,2,8,384]{3,1,2,0:T(2,128)S(1)}, u32[]{:S(2)}, u32[]{:S(2)}) collective-permute-start(f32[1,2,8,384]{3,1,2,0:T(2,128)} %bitcast.232), channel_id=1, source_target_pairs={{0,12},{1,13},{2,14},{3,15},{4,8},{5,9},{6,10},{7,11},{8,4},{9,5},... | collective-permute-start | bytes 73736 | tf_op jit(solution)/shard_map/ppermute | solution.py:144
  19.1 1.6 %gather_fusion.1 = f32[64,16]{1,0:T(8,128)S(1)} fusion(f32[32,32,16]{2,1,0:T(8,128)} %constant.83, s32[64]{0:T(128)S(1)} %reshape.200), kind=kCustom, calls=%fused_computation.3 | custom fusion | bytes 8704 | tf_op jit(solution)/shard_map/gather | solution.py:217
  20.7 2.5 %collective-permute-done.5 = f32[1,2,8,384]{3,1,2,0:T(2,128)S(1)} collective-permute-done((f32[1,2,8,384]{3,1,2,0:T(2,128)}, f32[1,2,8,384]{3,1,2,0:T(2,128)S(1)}, u32[]{:S(2)}, u32[]{:S(2)}) %collective-permute-start.5) | collective-permute-done | bytes 24608 | tf_op jit(solution)/shard_map/ppermute | solution.py:144
  24.6 1.6 %collective-permute-start.7 = (bf16[2,8,384]{2,1,0:T(8,128)(2,1)}, bf16[2,8,384]{2,1,0:T(8,128)(2,1)S(1)}, u32[]{:S(2)}, u32[]{:S(2)}) collective-permute-start(bf16[2,8,384]{2,1,0:T(8,128)(2,1)} %pad_maximum_fusion.1), channel_id=1, source_target_pairs={{0,2},{1,3},{2,0},{3,1},{4,6},{5,7},{6,4},{7,5},{8,10},{9,11},{10,... | collective-permute-start | bytes 36872 | tf_op jit(solution)/shard_map/ppermute | solution.py:132
  31.4 1.2 %collective-permute-start.10 = (f32[1,2,8,384]{3,1,2,0:T(2,128)}, f32[1,2,8,384]{3,1,2,0:T(2,128)}, u32[]{:S(2)}, u32[]{:S(2)}) collective-permute-start(f32[1,2,8,384]{3,1,2,0:T(2,128)} %bitcast.225), channel_id=1, source_target_pairs={{0,8},{1,9},{2,10},{3,11},{4,12},{5,13},{6,14},{7,15},{8,0},{9,1},... | collective-permute-start | bytes 73736 | tf_op jit(solution)/shard_map/ppermute | solution.py:144
  32.6 0.9 %collective-permute-start.11 = (f32[1,2,8,384]{3,1,2,0:T(2,128)}, f32[1,2,8,384]{3,1,2,0:T(2,128)}, u32[]{:S(2)}, u32[]{:S(2)}) collective-permute-start(f32[1,2,8,384]{3,1,2,0:T(2,128)} %bitcast.231), channel_id=1, source_target_pairs={{0,12},{1,13},{2,14},{3,15},{4,8},{5,9},{6,10},{7,11},{8,4},{9,5},... | collective-permute-start | bytes 73736 | tf_op jit(solution)/shard_map/ppermute | solution.py:144
  33.6 1.3 %collective-permute-start.9 = (f32[1,2,8,384]{3,1,2,0:T(2,128)}, f32[1,2,8,384]{3,1,2,0:T(2,128)}, u32[]{:S(2)}, u32[]{:S(2)}) collective-permute-start(f32[1,2,8,384]{3,1,2,0:T(2,128)} %bitcast.226), channel_id=1, source_target_pairs={{0,4},{1,5},{2,6},{3,7},{4,0},{5,1},{6,2},{7,3},{8,12},{9,13},{10,... | collective-permute-start | bytes 73736 | tf_op jit(solution)/shard_map/ppermute | solution.py:144
  34.9 4.5 %fusion.33 = f32[2,1440,384]{2,1,0:T(8,128)} fusion(bf16[2,1440,384]{2,1,0:T(8,128)(2,1)S(1)} %copy-done, bf16[384,384]{1,0:T(8,128)(2,1)} %param.12), kind=kOutput, calls=%fused_computation.53 | convolution fusion | flops 849346560 | bytes 6930432 | tf_op jit(solution)/shard_map/jkc,cd->jkd/dot_general | solution.py:233
  39.6 0.9 %copy.165 = f32[4,4,2,2,8]{1,0,2,3,4:T(4,128)S(1)} copy(f32[4,4,2,2,8]{4,3,2,1,0:T(2,128)} %get-tuple-element.31) | data formatting | bytes 4096
  41.4 5.6 %fusion = bf16[2,1440,384]{2,1,0:T(8,128)(2,1)S(1)} fusion(bf16[2,1440,384]{2,1,0:T(8,128)(2,1)} %param.11, f32[2,1440,384]{2,1,0:T(8,128)} %fusion.33, bf16[1440,8,1]{0,1,2:T(8,128)(2,1)S(1)} %copy-done.5, bf16[2,8,384]{2,0,1:T(2,128)(2,1)S(1)} %fusion.62), kind=kOutput, calls=%fused_computation.6 | convolution fusion | flops 39813120 | bytes 8882688 | tf_op jit(solution)/shard_map/jfc,kf->jkc/dot_general | solution.py:232
  47.4 1.5 %collective-permute-start.13 = (f32[2,8,384]{2,1,0:T(8,128)S(1)}, f32[2,8,384]{2,1,0:T(8,128)S(1)}, u32[]{:S(2)}, u32[]{:S(2)}) collective-permute-start(f32[2,8,384]{2,1,0:T(8,128)S(1)} %bitcast.245), channel_id=1, source_target_pairs={{0,2},{1,3},{2,0},{3,1},{4,6},{5,7},{6,4},{7,5},{8,10},{9,11},{10,... | collective-permute-start | bytes 73736 | tf_op jit(solution)/shard_map/ppermute | solution.py:132
  49.5 1.5 %fusion.31 = f32[2,1440,384]{2,1,0:T(8,128)S(1)} fusion(bf16[2,1440,384]{2,1,0:T(8,128)(2,1)S(1)} %fusion, bf16[384,384]{1,0:T(8,128)(2,1)S(1)} %copy-done.4), kind=kOutput, calls=%fused_computation.51 | convolution fusion | flops 849346560 | bytes 6930432 | tf_op jit(solution)/shard_map/jkd,cd->jkc/dot_general | solution.py:244
  51.1 1.4 %fusion.96 = f32[384,384,1]{0,1,2:T(8,128)S(1)} fusion(bf16[2,1440,384]{2,1,0:T(8,128)(2,1)S(1)} %fusion, bf16[2,1440,384]{2,1,0:T(8,128)(2,1)S(1)} %copy-done), kind=kOutput, calls=%fused_computation.156 | convolution fusion | flops 849346560 | bytes 5013504 | tf_op jit(solution)/shard_map/jkc,jkd->cd/dot_general | solution.py:241
  53.1 2.2 %collective-permute-start.16 = (f32[1,2,8,384]{3,1,2,0:T(2,128)S(1)}, f32[1,2,8,384]{3,1,2,0:T(2,128)S(1)}, u32[]{:S(2)}, u32[]{:S(2)}) collective-permute-start(f32[1,2,8,384]{3,1,2,0:T(2,128)S(1)} %bitcast.262), channel_id=1, source_target_pairs={{0,8},{1,9},{2,10},{3,11},{4,12},{5,13},{6,14},{7,15},{8,0},{9,1},... | collective-permute-start | bytes 73736 | tf_op jit(solution)/shard_map/ppermute | solution.py:144
  55.3 0.9 %collective-permute-start.17 = (f32[1,2,8,384]{3,1,2,0:T(2,128)S(1)}, f32[1,2,8,384]{3,1,2,0:T(2,128)S(1)}, u32[]{:S(2)}, u32[]{:S(2)}) collective-permute-start(f32[1,2,8,384]{3,1,2,0:T(2,128)S(1)} %bitcast.261), channel_id=1, source_target_pairs={{0,12},{1,13},{2,14},{3,15},{4,8},{5,9},{6,10},{7,11},{8,4},{9,5},... | collective-permute-start | bytes 73736 | tf_op jit(solution)/shard_map/ppermute | solution.py:144
  56.7 1.7 %collective-permute-done.16 = f32[1,2,8,384]{3,1,2,0:T(2,128)S(1)} collective-permute-done((f32[1,2,8,384]{3,1,2,0:T(2,128)S(1)}, f32[1,2,8,384]{3,1,2,0:T(2,128)S(1)}, u32[]{:S(2)}, u32[]{:S(2)}) %collective-permute-start.16) | collective-permute-done | bytes 24608 | tf_op jit(solution)/shard_map/ppermute | solution.py:144
  58.4 2.5 %collective-permute-done.17 = f32[1,2,8,384]{3,1,2,0:T(2,128)S(1)} collective-permute-done((f32[1,2,8,384]{3,1,2,0:T(2,128)S(1)}, f32[1,2,8,384]{3,1,2,0:T(2,128)S(1)}, u32[]{:S(2)}, u32[]{:S(2)}) %collective-permute-start.17) | collective-permute-done | bytes 24608 | tf_op jit(solution)/shard_map/ppermute | solution.py:144
  62.2 1.6 %collective-permute-start.19 = (bf16[2,8,384]{2,1,0:T(8,128)(2,1)S(1)}, bf16[2,8,384]{2,1,0:T(8,128)(2,1)S(1)}, u32[]{:S(2)}, u32[]{:S(2)}) collective-permute-start(bf16[2,8,384]{2,1,0:T(8,128)(2,1)S(1)} %pad_maximum_fusion.2), channel_id=1, source_target_pairs={{0,2},{1,3},{2,0},{3,1},{4,6},{5,7},{6,4},{7,5},{8,10},{9,11},{10,... | collective-permute-start | bytes 36872 | tf_op jit(solution)/shard_map/ppermute | solution.py:132
  65.7 1.1 %copy.130 = bf16[2,2,384,384]{3,2,1,0:T(8,128)(2,1)} copy(bf16[2,2,384,384]{3,2,0,1:T(8,128)(2,1)S(1)} %pad_maximum_fusion) | data formatting | bytes 2359296
  67.3 1.6 %collective-permute-start.25 = (bf16[4,24,384]{2,1,0:T(8,128)(2,1)S(1)}, bf16[4,24,384]{2,1,0:T(8,128)(2,1)S(1)}, u32[]{:S(2)}, u32[]{:S(2)}) collective-permute-start(bf16[4,24,384]{2,1,0:T(8,128)(2,1)S(1)} %fusion.38), channel_id=1, source_target_pairs={{0,2},{1,3},{2,0},{3,1},{4,6},{5,7},{6,4},{7,5},{8,10},{9,11},{10,... | collective-permute-start | bytes 221192 | tf_op jit(solution)/shard_map/ppermute | solution.py:122
  69.0 0.9 %collective-permute-start.22 = (f32[1,2,8,384]{3,1,2,0:T(2,128)S(1)}, f32[1,2,8,384]{3,1,2,0:T(2,128)S(1)}, u32[]{:S(2)}, u32[]{:S(2)}) collective-permute-start(f32[1,2,8,384]{3,1,2,0:T(2,128)S(1)} %bitcast.260), channel_id=1, source_target_pairs={{0,8},{1,9},{2,10},{3,11},{4,12},{5,13},{6,14},{7,15},{8,0},{9,1},... | collective-permute-start | bytes 73736 | tf_op jit(solution)/shard_map/ppermute | solution.py:144
  69.9 1.3 %collective-permute-start.23 = (f32[1,2,8,384]{3,1,2,0:T(2,128)S(1)}, f32[1,2,8,384]{3,1,2,0:T(2,128)S(1)}, u32[]{:S(2)}, u32[]{:S(2)}) collective-permute-start(f32[1,2,8,384]{3,1,2,0:T(2,128)S(1)} %bitcast.258), channel_id=1, source_target_pairs={{0,12},{1,13},{2,14},{3,15},{4,8},{5,9},{6,10},{7,11},{8,4},{9,5},... | collective-permute-start | bytes 73736 | tf_op jit(solution)/shard_map/ppermute | solution.py:144
  71.2 1.4 %collective-permute-start.21 = (f32[1,2,8,384]{3,1,2,0:T(2,128)S(1)}, f32[1,2,8,384]{3,1,2,0:T(2,128)S(1)}, u32[]{:S(2)}, u32[]{:S(2)}) collective-permute-start(f32[1,2,8,384]{3,1,2,0:T(2,128)S(1)} %bitcast.257), channel_id=1, source_target_pairs={{0,4},{1,5},{2,6},{3,7},{4,0},{5,1},{6,2},{7,3},{8,12},{9,13},{10,... | collective-permute-start | bytes 73736 | tf_op jit(solution)/shard_map/ppermute | solution.py:144
  73.8 1.9 %collective-permute-done.23 = f32[1,2,8,384]{3,1,2,0:T(2,128)S(1)} collective-permute-done((f32[1,2,8,384]{3,1,2,0:T(2,128)S(1)}, f32[1,2,8,384]{3,1,2,0:T(2,128)S(1)}, u32[]{:S(2)}, u32[]{:S(2)}) %collective-permute-start.23) | collective-permute-done | bytes 24608 | tf_op jit(solution)/shard_map/ppermute | solution.py:144
  75.8 0.9 %collective-permute-done.26 = bf16[2,24,384]{2,1,0:T(8,128)(2,1)S(1)} collective-permute-done((bf16[2,24,384]{2,1,0:T(8,128)(2,1)S(1)}, bf16[2,24,384]{2,1,0:T(8,128)(2,1)S(1)}, u32[]{:S(2)}, u32[]{:S(2)}) %collective-permute-start.26) | collective-permute-done | bytes 36896 | tf_op jit(solution)/shard_map/ppermute | solution.py:122
  76.7 1.8 %collective-permute-start.27 = (bf16[1,24,384]{2,1,0:T(8,128)(2,1)S(1)}, bf16[1,24,384]{2,1,0:T(8,128)(2,1)S(1)}, u32[]{:S(2)}, u32[]{:S(2)}) collective-permute-start(bf16[1,24,384]{2,1,0:T(8,128)(2,1)S(1)} %dynamic-slice_convert_fusion.2), channel_id=1, source_target_pairs={{0,8},{1,9},{2,10},{3,11},{4,12},{5,13},{6,14},{7,15},{8,0},{9,1},... | collective-permute-start | bytes 55304 | tf_op jit(solution)/shard_map/ppermute | solution.py:122
  78.5 2.5 %fusion.2 = bf16[2,1440,384]{2,1,0:T(8,128)(2,1)} fusion(f32[2,1440,384]{2,1,0:T(8,128)S(1)} %fusion.31, bf16[2,1440,384]{2,1,0:T(8,128)(2,1)S(1)} %copy-done.3, bf16[1440,8,1]{0,1,2:T(8,128)(2,1)S(1)} %copy-done.5, bf16[2,8,384]{2,0,1:T(2,128)(2,1)S(1)} %fusion.60), kind=kOutput, calls=%fused_computation.8 | convolution fusion | flops 22118400 | bytes 8882688 | tf_op jit(solution)/shard_map/jfc,kf->jkc/dot_general | solution.py:250
  (128 shorter events, 22.4 us)
Async XLA Ops:
  3.4 7.7 %collective-permute-start.1 = (f32[2,8,384]{2,1,0:T(8,128)S(1)}, f32[2,8,384]{2,1,0:T(8,128)S(1)}, u32[]{:S(2)}, u32[]{:S(2)}) collective-permute-start(f32[2,8,384]{2,1,0:T(8,128)S(1)} %bitcast.241), channel_id=1, source_target_pairs={{0,2},{1,3},{2,0},{3,1},{4,6},{5,7},{6,4},{7,5},{8,10},{9,11},{10,... | collective-permute-start | bytes 73736 | tf_op jit(solution)/shard_map/ppermute | solution.py:132
  6.4 4.8 %collective-permute-start = (f32[2,8,384]{2,1,0:T(8,128)S(1)}, f32[2,8,384]{2,1,0:T(8,128)}, u32[]{:S(2)}, u32[]{:S(2)}) collective-permute-start(f32[2,8,384]{2,1,0:T(8,128)S(1)} %bitcast.242), channel_id=1, source_target_pairs={{0,1},{1,0},{2,3},{3,2},{4,5},{5,4},{6,7},{7,6},{8,9},{9,8},{10,11... | collective-permute-start | bytes 73736 | tf_op jit(solution)/shard_map/ppermute | solution.py:132
  6.4 4.8 %collective-permute-start.2 = (f32[2,8,384]{2,1,0:T(8,128)S(1)}, f32[2,8,384]{2,1,0:T(8,128)}, u32[]{:S(2)}, u32[]{:S(2)}) collective-permute-start(f32[2,8,384]{2,1,0:T(8,128)S(1)} %bitcast.243), channel_id=1, source_target_pairs={{0,3},{1,2},{2,1},{3,0},{4,7},{5,6},{6,5},{7,4},{8,11},{9,10},{10,... | collective-permute-start | bytes 73736 | tf_op jit(solution)/shard_map/ppermute | solution.py:132
  7.4 15.8 %copy-start.2 = (bf16[2,2,384,384]{3,2,1,0:T(8,128)(2,1)S(1)}, bf16[2,2,384,384]{3,2,1,0:T(8,128)(2,1)}, u32[]{:S(2)}) copy-start(bf16[2,2,384,384]{3,2,1,0:T(8,128)(2,1)} %param.13) | copy-start | bytes 3538948
  14.2 6.4 %collective-permute-start.4 = (f32[1,2,8,384]{3,1,2,0:T(2,128)}, f32[1,2,8,384]{3,1,2,0:T(2,128)S(1)}, u32[]{:S(2)}, u32[]{:S(2)}) collective-permute-start(f32[1,2,8,384]{3,1,2,0:T(2,128)} %bitcast.227), channel_id=1, source_target_pairs={{0,8},{1,9},{2,10},{3,11},{4,12},{5,13},{6,14},{7,15},{8,0},{9,1},... | collective-permute-start | bytes 73736 | tf_op jit(solution)/shard_map/ppermute | solution.py:144
  17.3 5.8 %collective-permute-start.5 = (f32[1,2,8,384]{3,1,2,0:T(2,128)}, f32[1,2,8,384]{3,1,2,0:T(2,128)S(1)}, u32[]{:S(2)}, u32[]{:S(2)}) collective-permute-start(f32[1,2,8,384]{3,1,2,0:T(2,128)} %bitcast.232), channel_id=1, source_target_pairs={{0,12},{1,13},{2,14},{3,15},{4,8},{5,9},{6,10},{7,11},{8,4},{9,5},... | collective-permute-start | bytes 73736 | tf_op jit(solution)/shard_map/ppermute | solution.py:144
  18.6 4.5 %collective-permute-start.3 = (f32[1,2,8,384]{3,1,2,0:T(2,128)}, f32[1,2,8,384]{3,1,2,0:T(2,128)S(1)}, u32[]{:S(2)}, u32[]{:S(2)}) collective-permute-start(f32[1,2,8,384]{3,1,2,0:T(2,128)} %bitcast.228), channel_id=1, source_target_pairs={{0,4},{1,5},{2,6},{3,7},{4,0},{5,1},{6,2},{7,3},{8,12},{9,13},{10,... | collective-permute-start | bytes 73736 | tf_op jit(solution)/shard_map/ppermute | solution.py:144
  24.6 3.4 %collective-permute-start.8 = (bf16[2,8,384]{2,1,0:T(8,128)(2,1)}, bf16[2,8,384]{2,1,0:T(8,128)(2,1)S(1)}, u32[]{:S(2)}, u32[]{:S(2)}) collective-permute-start(bf16[2,8,384]{2,1,0:T(8,128)(2,1)} %pad_maximum_fusion.1), channel_id=1, source_target_pairs={{0,3},{1,2},{2,1},{3,0},{4,7},{5,6},{6,5},{7,4},{8,11},{9,10},{10,... | collective-permute-start | bytes 36872 | tf_op jit(solution)/shard_map/ppermute | solution.py:132
  24.6 3.9 %collective-permute-start.7 = (bf16[2,8,384]{2,1,0:T(8,128)(2,1)}, bf16[2,8,384]{2,1,0:T(8,128)(2,1)S(1)}, u32[]{:S(2)}, u32[]{:S(2)}) collective-permute-start(bf16[2,8,384]{2,1,0:T(8,128)(2,1)} %pad_maximum_fusion.1), channel_id=1, source_target_pairs={{0,2},{1,3},{2,0},{3,1},{4,6},{5,7},{6,4},{7,5},{8,10},{9,11},{10,... | collective-permute-start | bytes 36872 | tf_op jit(solution)/shard_map/ppermute | solution.py:132
  26.2 2.4 %collective-permute-start.6 = (bf16[2,8,384]{2,1,0:T(8,128)(2,1)}, bf16[2,8,384]{2,1,0:T(8,128)(2,1)S(1)}, u32[]{:S(2)}, u32[]{:S(2)}) collective-permute-start(bf16[2,8,384]{2,1,0:T(8,128)(2,1)} %pad_maximum_fusion.1), channel_id=1, source_target_pairs={{0,1},{1,0},{2,3},{3,2},{4,5},{5,4},{6,7},{7,6},{8,9},{9,8},{10,11... | collective-permute-start | bytes 36872 | tf_op jit(solution)/shard_map/ppermute | solution.py:132
  31.4 9.1 %collective-permute-start.10 = (f32[1,2,8,384]{3,1,2,0:T(2,128)}, f32[1,2,8,384]{3,1,2,0:T(2,128)}, u32[]{:S(2)}, u32[]{:S(2)}) collective-permute-start(f32[1,2,8,384]{3,1,2,0:T(2,128)} %bitcast.225), channel_id=1, source_target_pairs={{0,8},{1,9},{2,10},{3,11},{4,12},{5,13},{6,14},{7,15},{8,0},{9,1},... | collective-permute-start | bytes 73736 | tf_op jit(solution)/shard_map/ppermute | solution.py:144
  32.6 7.9 %collective-permute-start.11 = (f32[1,2,8,384]{3,1,2,0:T(2,128)}, f32[1,2,8,384]{3,1,2,0:T(2,128)}, u32[]{:S(2)}, u32[]{:S(2)}) collective-permute-start(f32[1,2,8,384]{3,1,2,0:T(2,128)} %bitcast.231), channel_id=1, source_target_pairs={{0,12},{1,13},{2,14},{3,15},{4,8},{5,9},{6,10},{7,11},{8,4},{9,5},... | collective-permute-start | bytes 73736 | tf_op jit(solution)/shard_map/ppermute | solution.py:144
  33.6 7.8 %copy-start.5 = (bf16[1440,8,1]{0,1,2:T(8,128)(2,1)S(1)}, bf16[1440,8,1]{0,1,2:T(8,128)(2,1)}, u32[]{:S(2)}) copy-start(bf16[1440,8,1]{0,1,2:T(8,128)(2,1)} %constant.110) | copy-start | bytes 69124
  33.6 7.0 %collective-permute-start.9 = (f32[1,2,8,384]{3,1,2,0:T(2,128)}, f32[1,2,8,384]{3,1,2,0:T(2,128)}, u32[]{:S(2)}, u32[]{:S(2)}) collective-permute-start(f32[1,2,8,384]{3,1,2,0:T(2,128)} %bitcast.226), channel_id=1, source_target_pairs={{0,4},{1,5},{2,6},{3,7},{4,0},{5,1},{6,2},{7,3},{8,12},{9,13},{10,... | collective-permute-start | bytes 73736 | tf_op jit(solution)/shard_map/ppermute | solution.py:144
  47.4 5.1 %collective-permute-start.13 = (f32[2,8,384]{2,1,0:T(8,128)S(1)}, f32[2,8,384]{2,1,0:T(8,128)S(1)}, u32[]{:S(2)}, u32[]{:S(2)}) collective-permute-start(f32[2,8,384]{2,1,0:T(8,128)S(1)} %bitcast.245), channel_id=1, source_target_pairs={{0,2},{1,3},{2,0},{3,1},{4,6},{5,7},{6,4},{7,5},{8,10},{9,11},{10,... | collective-permute-start | bytes 73736 | tf_op jit(solution)/shard_map/ppermute | solution.py:132
  48.9 3.6 %collective-permute-start.12 = (f32[2,8,384]{2,1,0:T(8,128)S(1)}, f32[2,8,384]{2,1,0:T(8,128)S(1)}, u32[]{:S(2)}, u32[]{:S(2)}) collective-permute-start(f32[2,8,384]{2,1,0:T(8,128)S(1)} %bitcast.246), channel_id=1, source_target_pairs={{0,1},{1,0},{2,3},{3,2},{4,5},{5,4},{6,7},{7,6},{8,9},{9,8},{10,11... | collective-permute-start | bytes 73736 | tf_op jit(solution)/shard_map/ppermute | solution.py:132
  48.9 3.6 %collective-permute-start.14 = (f32[2,8,384]{2,1,0:T(8,128)S(1)}, f32[2,8,384]{2,1,0:T(8,128)S(1)}, u32[]{:S(2)}, u32[]{:S(2)}) collective-permute-start(f32[2,8,384]{2,1,0:T(8,128)S(1)} %bitcast.247), channel_id=1, source_target_pairs={{0,3},{1,2},{2,1},{3,0},{4,7},{5,6},{6,5},{7,4},{8,11},{9,10},{10,... | collective-permute-start | bytes 73736 | tf_op jit(solution)/shard_map/ppermute | solution.py:132
  52.5 11.6 %copy-start.7 = (bf16[2,4,384]{2,0,1:T(2,128)(2,1)S(1)}, bf16[2,4,384]{2,0,1:T(2,128)(2,1)}, u32[]{:S(2)}) copy-start(bf16[2,4,384]{2,0,1:T(2,128)(2,1)} %copy-done.6) | copy-start | bytes 18436
  53.1 5.3 %collective-permute-start.16 = (f32[1,2,8,384]{3,1,2,0:T(2,128)S(1)}, f32[1,2,8,384]{3,1,2,0:T(2,128)S(1)}, u32[]{:S(2)}, u32[]{:S(2)}) collective-permute-start(f32[1,2,8,384]{3,1,2,0:T(2,128)S(1)} %bitcast.262), channel_id=1, source_target_pairs={{0,8},{1,9},{2,10},{3,11},{4,12},{5,13},{6,14},{7,15},{8,0},{9,1},... | collective-permute-start | bytes 73736 | tf_op jit(solution)/shard_map/ppermute | solution.py:144
  55.3 5.6 %collective-permute-start.17 = (f32[1,2,8,384]{3,1,2,0:T(2,128)S(1)}, f32[1,2,8,384]{3,1,2,0:T(2,128)S(1)}, u32[]{:S(2)}, u32[]{:S(2)}) collective-permute-start(f32[1,2,8,384]{3,1,2,0:T(2,128)S(1)} %bitcast.261), channel_id=1, source_target_pairs={{0,12},{1,13},{2,14},{3,15},{4,8},{5,9},{6,10},{7,11},{8,4},{9,5},... | collective-permute-start | bytes 73736 | tf_op jit(solution)/shard_map/ppermute | solution.py:144
  56.2 4.7 %collective-permute-start.15 = (f32[1,2,8,384]{3,1,2,0:T(2,128)S(1)}, f32[1,2,8,384]{3,1,2,0:T(2,128)S(1)}, u32[]{:S(2)}, u32[]{:S(2)}) collective-permute-start(f32[1,2,8,384]{3,1,2,0:T(2,128)S(1)} %bitcast.259), channel_id=1, source_target_pairs={{0,4},{1,5},{2,6},{3,7},{4,0},{5,1},{6,2},{7,3},{8,12},{9,13},{10,... | collective-permute-start | bytes 73736 | tf_op jit(solution)/shard_map/ppermute | solution.py:144
  56.7 10.5 %collective-permute-start.24 = (bf16[8,24,384]{2,1,0:T(8,128)(2,1)S(1)}, bf16[8,24,384]{2,1,0:T(8,128)(2,1)S(1)}, u32[]{:S(2)}, u32[]{:S(2)}) collective-permute-start(bf16[8,24,384]{2,1,0:T(8,128)(2,1)S(1)} %fusion.35), channel_id=1, source_target_pairs={{0,1},{1,0},{2,3},{3,2},{4,5},{5,4},{6,7},{7,6},{8,9},{9,8},{10,11... | collective-permute-start | bytes 442376 | tf_op jit(solution)/shard_map/ppermute | solution.py:122
  62.1 4.7 %collective-permute-start.20 = (bf16[2,8,384]{2,1,0:T(8,128)(2,1)S(1)}, bf16[2,8,384]{2,1,0:T(8,128)(2,1)S(1)}, u32[]{:S(2)}, u32[]{:S(2)}) collective-permute-start(bf16[2,8,384]{2,1,0:T(8,128)(2,1)S(1)} %pad_maximum_fusion.2), channel_id=1, source_target_pairs={{0,3},{1,2},{2,1},{3,0},{4,7},{5,6},{6,5},{7,4},{8,11},{9,10},{10,... | collective-permute-start | bytes 36872 | tf_op jit(solution)/shard_map/ppermute | solution.py:132
  62.2 4.7 %collective-permute-start.19 = (bf16[2,8,384]{2,1,0:T(8,128)(2,1)S(1)}, bf16[2,8,384]{2,1,0:T(8,128)(2,1)S(1)}, u32[]{:S(2)}, u32[]{:S(2)}) collective-permute-start(bf16[2,8,384]{2,1,0:T(8,128)(2,1)S(1)} %pad_maximum_fusion.2), channel_id=1, source_target_pairs={{0,2},{1,3},{2,0},{3,1},{4,6},{5,7},{6,4},{7,5},{8,10},{9,11},{10,... | collective-permute-start | bytes 36872 | tf_op jit(solution)/shard_map/ppermute | solution.py:132
  63.8 3.1 %collective-permute-start.18 = (bf16[2,8,384]{2,1,0:T(8,128)(2,1)S(1)}, bf16[2,8,384]{2,1,0:T(8,128)(2,1)S(1)}, u32[]{:S(2)}, u32[]{:S(2)}) collective-permute-start(bf16[2,8,384]{2,1,0:T(8,128)(2,1)S(1)} %pad_maximum_fusion.2), channel_id=1, source_target_pairs={{0,1},{1,0},{2,3},{3,2},{4,5},{5,4},{6,7},{7,6},{8,9},{9,8},{10,11... | collective-permute-start | bytes 36872 | tf_op jit(solution)/shard_map/ppermute | solution.py:132
  65.7 12.7 %copy-start.3 = (bf16[2,1440,384]{2,1,0:T(8,128)(2,1)S(1)}, bf16[2,1440,384]{2,1,0:T(8,128)(2,1)}, u32[]{:S(2)}) copy-start(bf16[2,1440,384]{2,1,0:T(8,128)(2,1)} %param.11) | copy-start | bytes 6635524
  67.3 5.3 %collective-permute-start.25 = (bf16[4,24,384]{2,1,0:T(8,128)(2,1)S(1)}, bf16[4,24,384]{2,1,0:T(8,128)(2,1)S(1)}, u32[]{:S(2)}, u32[]{:S(2)}) collective-permute-start(bf16[4,24,384]{2,1,0:T(8,128)(2,1)S(1)} %fusion.38), channel_id=1, source_target_pairs={{0,2},{1,3},{2,0},{3,1},{4,6},{5,7},{6,4},{7,5},{8,10},{9,11},{10,... | collective-permute-start | bytes 221192 | tf_op jit(solution)/shard_map/ppermute | solution.py:122
  69.0 4.8 %collective-permute-start.22 = (f32[1,2,8,384]{3,1,2,0:T(2,128)S(1)}, f32[1,2,8,384]{3,1,2,0:T(2,128)S(1)}, u32[]{:S(2)}, u32[]{:S(2)}) collective-permute-start(f32[1,2,8,384]{3,1,2,0:T(2,128)S(1)} %bitcast.260), channel_id=1, source_target_pairs={{0,8},{1,9},{2,10},{3,11},{4,12},{5,13},{6,14},{7,15},{8,0},{9,1},... | collective-permute-start | bytes 73736 | tf_op jit(solution)/shard_map/ppermute | solution.py:144
  69.9 5.8 %collective-permute-start.23 = (f32[1,2,8,384]{3,1,2,0:T(2,128)S(1)}, f32[1,2,8,384]{3,1,2,0:T(2,128)S(1)}, u32[]{:S(2)}, u32[]{:S(2)}) collective-permute-start(f32[1,2,8,384]{3,1,2,0:T(2,128)S(1)} %bitcast.258), channel_id=1, source_target_pairs={{0,12},{1,13},{2,14},{3,15},{4,8},{5,9},{6,10},{7,11},{8,4},{9,5},... | collective-permute-start | bytes 73736 | tf_op jit(solution)/shard_map/ppermute | solution.py:144
  71.2 4.6 %collective-permute-start.21 = (f32[1,2,8,384]{3,1,2,0:T(2,128)S(1)}, f32[1,2,8,384]{3,1,2,0:T(2,128)S(1)}, u32[]{:S(2)}, u32[]{:S(2)}) collective-permute-start(f32[1,2,8,384]{3,1,2,0:T(2,128)S(1)} %bitcast.257), channel_id=1, source_target_pairs={{0,4},{1,5},{2,6},{3,7},{4,0},{5,1},{6,2},{7,3},{8,12},{9,13},{10,... | collective-permute-start | bytes 73736 | tf_op jit(solution)/shard_map/ppermute | solution.py:144
  72.6 4.0 %collective-permute-start.26 = (bf16[2,24,384]{2,1,0:T(8,128)(2,1)S(1)}, bf16[2,24,384]{2,1,0:T(8,128)(2,1)S(1)}, u32[]{:S(2)}, u32[]{:S(2)}) collective-permute-start(bf16[2,24,384]{2,1,0:T(8,128)(2,1)S(1)} %fusion.41), channel_id=1, source_target_pairs={{0,4},{1,5},{2,6},{3,7},{4,0},{5,1},{6,2},{7,3},{8,12},{9,13},{10,... | collective-permute-start | bytes 110600 | tf_op jit(solution)/shard_map/ppermute | solution.py:122
  76.7 4.7 %collective-permute-start.27 = (bf16[1,24,384]{2,1,0:T(8,128)(2,1)S(1)}, bf16[1,24,384]{2,1,0:T(8,128)(2,1)S(1)}, u32[]{:S(2)}, u32[]{:S(2)}) collective-permute-start(bf16[1,24,384]{2,1,0:T(8,128)(2,1)S(1)} %dynamic-slice_convert_fusion.2), channel_id=1, source_target_pairs={{0,8},{1,9},{2,10},{3,11},{4,12},{5,13},{6,14},{7,15},{8,0},{9,1},... | collective-permute-start | bytes 55304 | tf_op jit(solution)/shard_map/ppermute | solution.py:122
  (5 other events, 20.1 us)

commit v16 on v15

--- a/solution.py
+++ b/solution.py
@@ -126,6 +126,18 @@
     return cur[0]
 
 
+def reversed_halving(cur, axis_name, groups, me, bits):
+    for r in range(bits):
+        dev_bit = bits - 1 - r
+        view = cur.reshape((cur.shape[0] // 2, 2) + cur.shape[1:])
+        bit = (me >> dev_bit) & 1
+        total = lax.dynamic_index_in_dim(view, bit, axis=1, keepdims=False)
+        sent = lax.dynamic_index_in_dim(view, 1 - bit, axis=1, keepdims=False).astype(jnp.bfloat16)
+        mask = 1 << dev_bit
+        cur = total + lax.ppermute(sent, axis_name, [(i, i ^ mask) for i in range(groups)]).astype(jnp.float32)
+    return cur[0]
+
+
 def xor_exchange(values, table, axis_name, groups, me, lo, spec):
     parts = [values]
     for k in range(1, 1 << lo):
@@ -240,7 +252,9 @@
 
     skip_terms = jnp.einsum("jkc,jkd->cd", activations, slope_b, preferred_element_type=jnp.float32)
     skip_blocks = skip_terms.reshape((groups, -1) + skip_terms.shape[1:])
-    grad_skip = xor_reduce_scatter(skip_blocks, "lat", groups, me, 1, bits) * (1.0 / math.sqrt(lat_total * lon_total))
+    flips = skip_blocks.reshape((2,) * bits + skip_blocks.shape[1:])
+    flips = flips.transpose(tuple(range(bits))[::-1] + (bits, bits + 1)).reshape(skip_blocks.shape)
+    grad_skip = reversed_halving(flips, "lat", groups, me, bits) * (1.0 / math.sqrt(lat_total * lon_total))
     through_skip = jnp.einsum("jkd,cd->jkc", slope_b, skip_weight, preferred_element_type=jnp.float32)
 
     mode_grads = jnp.einsum("jkc,kf->jfc", slope_b, fourier, preferred_element_type=jnp.float32)

time: 82.5 us -> 80.4 us (0.975)
  waiting for transfers between devices: 11.7 us -> 8 us
  starting transfers between devices: 28.5 us -> 29.9 us
    ppermute x12, waiting for transfers between devices: 9.05 us -> 6.63 us  [xor_exchange(): lax.ppermute(view[:, k], axis_name, [(i, i ^ mask) for i in range(groups)])]
    ppermute x4, waiting for transfers between devices: 1.36 us -> 0.1 us  [reversed_halving(): lax.ppermute(sent, axis_name, [(i, i ^ mask) for i in range(groups)])]
    ppermute x12, starting transfers between devices: 15.2 us -> 16.1 us  [xor_exchange(): lax.ppermute(view[:, k], axis_name, [(i, i ^ mask) for i in range(groups)])]
  transfers between devices with their start and end apart: 28 -> 28, of which waited for: 9 -> 6; matrix products, arithmetic and copies ran while one was open for 28% -> 28% of each run, Pallas kernels for 0% -> 0%
where the time goes in v16:
time: 80.4 us; the launch traced here: 79.9 us
  starting transfers between devices  29.9 us (37%)
  matrix products  21.8 us (27%)
  local copies, waits for them, and re-layouts  15.4 us (19%)
  waiting for transfers between devices  8 us (10%)
  other arithmetic  3.61 us (4%)
  between operations  1.13 us (1%)
    ppermute x12, starting transfers between devices, xor_exchange(): lax.ppermute(view[:, k], axis_name, [(i, i ^ mask) for i in range(groups)])  16.1 us
    ppermute x12, starting transfers between devices, xor_exchange(): lax.ppermute(values, axis_name, [(i, i ^ k) for i in range(groups)])  9.07 us
    unnamed x35, local copies, waits for them, and re-layouts  8 us
    ppermute x12, waiting for transfers between devices, xor_exchange(): lax.ppermute(view[:, k], axis_name, [(i, i ^ mask) for i in range(groups)])  6.63 us
    dot_general x1, matrix products, local(): jnp.einsum('jfc,kf->jkc', grid_modes, fourier, preferred_element_type=jnp...  5.59 us
    ppermute x4, starting transfers between devices, reversed_halving(): lax.ppermute(sent, axis_name, [(i, i ^ mask) for i in range(groups)])  4.76 us
    dot_general x1, matrix products, local(): jnp.einsum('jkc,cd->jkd', activations, skip_weight, preferred_element_typ...  4.51 us
    dot_general x1, matrix products, local(): jnp.einsum('jfc,kf->jkc', row_grads, fourier, preferred_element_type=jnp....  2.46 us
  transfers between devices with their start and end apart: 28, of which 6 were waited for; matrix products, arithmetic and copies ran while one was open for 28% of the time, Pallas kernels for 0%

profile of v16, /device:TPU:0, one launch (start us, length us, event | category | flops | bytes accessed | tf_op | source)
XLA Modules:
  0.0 79.9 jit_solution(3762336901744706427)
XLA Ops:
  0.7 1.6 %copy-done = bf16[2,1440,384]{2,1,0:T(8,128)(2,1)S(1)} copy-done((bf16[2,1440,384]{2,1,0:T(8,128)(2,1)S(1)}, bf16[2,1440,384]{2,1,0:T(8,128)(2,1)}, u32[]{:S(2)}) %copy-start) | copy-done | bytes 2211864
  2.3 1.1 %fusion.94 = f32[8,2,384]{2,0,1:T(8,128)S(1)} fusion(bf16[1440,8,1]{0,1,2:T(8,128)(2,1)} %constant.114, bf16[2,1440,384]{2,1,0:T(8,128)(2,1)S(1)} %copy-done), kind=kOutput, calls=%fused_computation.154 | convolution fusion | flops 17694720 | bytes 2259456 | tf_op jit(solution)/shard_map/jkc,kf->jfc/dot_general | solution.py:239
  3.4 3.0 %collective-permute-start.1 = (f32[2,8,384]{2,1,0:T(8,128)S(1)}, f32[2,8,384]{2,1,0:T(8,128)S(1)}, u32[]{:S(2)}, u32[]{:S(2)}) collective-permute-start(f32[2,8,384]{2,1,0:T(8,128)S(1)} %bitcast.245), channel_id=1, source_target_pairs={{0,2},{1,3},{2,0},{3,1},{4,6},{5,7},{6,4},{7,5},{8,10},{9,11},{10,... | collective-permute-start | bytes 73736 | tf_op jit(solution)/shard_map/ppermute | solution.py:144
  8.6 1.6 %gather_fusion = f32[64,16]{1,0:T(8,128)S(1)} fusion(f32[32,32,16]{2,1,0:T(8,128)} %constant.87, s32[64]{0:T(128)S(1)} %reshape.194), kind=kCustom, calls=%fused_computation.2 | custom fusion | bytes 8704 | tf_op jit(solution)/shard_map/gather | solution.py:226
  10.2 0.7 fusion.90
  11.1 0.8 maximum_bitcast_fusion
  14.2 3.1 %collective-permute-start.4 = (f32[1,2,8,384]{3,1,2,0:T(2,128)}, f32[1,2,8,384]{3,1,2,0:T(2,128)S(1)}, u32[]{:S(2)}, u32[]{:S(2)}) collective-permute-start(f32[1,2,8,384]{3,1,2,0:T(2,128)} %bitcast.230), channel_id=1, source_target_pairs={{0,8},{1,9},{2,10},{3,11},{4,12},{5,13},{6,14},{7,15},{8,0},{9,1},... | collective-permute-start | bytes 73736 | tf_op jit(solution)/shard_map/ppermute | solution.py:156
  17.3 1.3 %collective-permute-start.5 = (f32[1,2,8,384]{3,1,2,0:T(2,128)}, f32[1,2,8,384]{3,1,2,0:T(2,128)S(1)}, u32[]{:S(2)}, u32[]{:S(2)}) collective-permute-start(f32[1,2,8,384]{3,1,2,0:T(2,128)} %bitcast.235), channel_id=1, source_target_pairs={{0,12},{1,13},{2,14},{3,15},{4,8},{5,9},{6,10},{7,11},{8,4},{9,5},... | collective-permute-start | bytes 73736 | tf_op jit(solution)/shard_map/ppermute | solution.py:156
  19.1 1.6 %gather_fusion.1 = f32[64,16]{1,0:T(8,128)S(1)} fusion(f32[32,32,16]{2,1,0:T(8,128)} %constant.87, s32[64]{0:T(128)S(1)} %reshape.200), kind=kCustom, calls=%fused_computation.3 | custom fusion | bytes 8704 | tf_op jit(solution)/shard_map/gather | solution.py:229
  20.7 2.5 %collective-permute-done.5 = f32[1,2,8,384]{3,1,2,0:T(2,128)S(1)} collective-permute-done((f32[1,2,8,384]{3,1,2,0:T(2,128)}, f32[1,2,8,384]{3,1,2,0:T(2,128)S(1)}, u32[]{:S(2)}, u32[]{:S(2)}) %collective-permute-start.5) | collective-permute-done | bytes 24608 | tf_op jit(solution)/shard_map/ppermute | solution.py:156
  24.6 1.6 %collective-permute-start.7 = (bf16[2,8,384]{2,1,0:T(8,128)(2,1)}, bf16[2,8,384]{2,1,0:T(8,128)(2,1)S(1)}, u32[]{:S(2)}, u32[]{:S(2)}) collective-permute-start(bf16[2,8,384]{2,1,0:T(8,128)(2,1)} %pad_maximum_fusion.1), channel_id=1, source_target_pairs={{0,2},{1,3},{2,0},{3,1},{4,6},{5,7},{6,4},{7,5},{8,10},{9,11},{10,... | collective-permute-start | bytes 36872 | tf_op jit(solution)/shard_map/ppermute | solution.py:144
  31.4 1.2 %collective-permute-start.10 = (f32[1,2,8,384]{3,1,2,0:T(2,128)}, f32[1,2,8,384]{3,1,2,0:T(2,128)}, u32[]{:S(2)}, u32[]{:S(2)}) collective-permute-start(f32[1,2,8,384]{3,1,2,0:T(2,128)} %bitcast.228), channel_id=1, source_target_pairs={{0,8},{1,9},{2,10},{3,11},{4,12},{5,13},{6,14},{7,15},{8,0},{9,1},... | collective-permute-start | bytes 73736 | tf_op jit(solution)/shard_map/ppermute | solution.py:156
  32.6 0.9 %collective-permute-start.11 = (f32[1,2,8,384]{3,1,2,0:T(2,128)}, f32[1,2,8,384]{3,1,2,0:T(2,128)}, u32[]{:S(2)}, u32[]{:S(2)}) collective-permute-start(f32[1,2,8,384]{3,1,2,0:T(2,128)} %bitcast.234), channel_id=1, source_target_pairs={{0,12},{1,13},{2,14},{3,15},{4,8},{5,9},{6,10},{7,11},{8,4},{9,5},... | collective-permute-start | bytes 73736 | tf_op jit(solution)/shard_map/ppermute | solution.py:156
  33.6 1.3 %collective-permute-start.9 = (f32[1,2,8,384]{3,1,2,0:T(2,128)}, f32[1,2,8,384]{3,1,2,0:T(2,128)}, u32[]{:S(2)}, u32[]{:S(2)}) collective-permute-start(f32[1,2,8,384]{3,1,2,0:T(2,128)} %bitcast.229), channel_id=1, source_target_pairs={{0,4},{1,5},{2,6},{3,7},{4,0},{5,1},{6,2},{7,3},{8,12},{9,13},{10,... | collective-permute-start | bytes 73736 | tf_op jit(solution)/shard_map/ppermute | solution.py:156
  34.9 4.5 %fusion.33 = f32[2,1440,384]{2,1,0:T(8,128)} fusion(bf16[2,1440,384]{2,1,0:T(8,128)(2,1)S(1)} %copy-done, bf16[384,384]{1,0:T(8,128)(2,1)} %param.12), kind=kOutput, calls=%fused_computation.52 | convolution fusion | flops 849346560 | bytes 6930432 | tf_op jit(solution)/shard_map/jkc,cd->jkd/dot_general | solution.py:245
  39.6 0.9 %copy.125 = f32[4,4,2,2,8]{1,0,2,3,4:T(4,128)S(1)} copy(f32[4,4,2,2,8]{4,3,2,1,0:T(2,128)} %get-tuple-element.28) | data formatting | bytes 4096
  40.5 0.8 %fusion.62 = bf16[2,8,384]{2,0,1:T(2,128)(2,1)S(1)} fusion(f32[1,2,8,384]{3,1,2,0:T(2,128)} %collective-permute-done.11, f32[1,2,8,384]{3,1,2,0:T(2,128)} %collective-permute-done.10, f32[1,2,8,384]{3,1,2,0:T(2,128)} %collective-permute-done.9, f32[1,1,2,8,384]{4,1,2,3,0:T(1,128)} %get-tuple-element.18), kind=kLoop, calls=%fused_computation.110 | loop fusion | flops 24576 | bytes 110592 | tf_op jit(solution)/shard_map/convert_element_type | solution.py:242
  41.3 5.6 %fusion = bf16[2,1440,384]{2,1,0:T(8,128)(2,1)S(1)} fusion(bf16[2,1440,384]{2,1,0:T(8,128)(2,1)} %param.11, f32[2,1440,384]{2,1,0:T(8,128)} %fusion.33, bf16[1440,8,1]{0,1,2:T(8,128)(2,1)S(1)} %copy-done.5, bf16[2,8,384]{2,0,1:T(2,128)(2,1)S(1)} %fusion.62), kind=kOutput, calls=%fused_computation.6 | convolution fusion | flops 39813120 | bytes 8882688 | tf_op jit(solution)/shard_map/jfc,kf->jkc/dot_general | solution.py:244
  47.4 1.5 %collective-permute-start.13 = (f32[2,8,384]{2,1,0:T(8,128)S(1)}, f32[2,8,384]{2,1,0:T(8,128)S(1)}, u32[]{:S(2)}, u32[]{:S(2)}) collective-permute-start(f32[2,8,384]{2,1,0:T(8,128)S(1)} %bitcast.249), channel_id=1, source_target_pairs={{0,2},{1,3},{2,0},{3,1},{4,6},{5,7},{6,4},{7,5},{8,10},{9,11},{10,... | collective-permute-start | bytes 73736 | tf_op jit(solution)/shard_map/ppermute | solution.py:144
  49.5 1.5 %fusion.31 = f32[2,1440,384]{2,1,0:T(8,128)S(1)} fusion(bf16[2,1440,384]{2,1,0:T(8,128)(2,1)S(1)} %fusion, bf16[384,384]{1,0:T(8,128)(2,1)S(1)} %copy-done.4), kind=kOutput, calls=%fused_computation.50 | convolution fusion | flops 849346560 | bytes 6930432 | tf_op jit(solution)/shard_map/jkd,cd->jkc/dot_general | solution.py:258
  51.0 1.4 %fusion.96 = f32[384,384,1]{0,1,2:T(8,128)S(1)} fusion(bf16[2,1440,384]{2,1,0:T(8,128)(2,1)S(1)} %fusion, bf16[2,1440,384]{2,1,0:T(8,128)(2,1)S(1)} %copy-done), kind=kOutput, calls=%fused_computation.156 | convolution fusion | flops 849346560 | bytes 5013504 | tf_op jit(solution)/shard_map/jkc,jkd->cd/dot_general | solution.py:253
  53.1 2.2 %collective-permute-start.16 = (f32[1,2,8,384]{3,1,2,0:T(2,128)S(1)}, f32[1,2,8,384]{3,1,2,0:T(2,128)S(1)}, u32[]{:S(2)}, u32[]{:S(2)}) collective-permute-start(f32[1,2,8,384]{3,1,2,0:T(2,128)S(1)} %bitcast.266), channel_id=1, source_target_pairs={{0,8},{1,9},{2,10},{3,11},{4,12},{5,13},{6,14},{7,15},{8,0},{9,1},... | collective-permute-start | bytes 73736 | tf_op jit(solution)/shard_map/ppermute | solution.py:156
  55.3 0.9 %collective-permute-start.17 = (f32[1,2,8,384]{3,1,2,0:T(2,128)S(1)}, f32[1,2,8,384]{3,1,2,0:T(2,128)S(1)}, u32[]{:S(2)}, u32[]{:S(2)}) collective-permute-start(f32[1,2,8,384]{3,1,2,0:T(2,128)S(1)} %bitcast.265), channel_id=1, source_target_pairs={{0,12},{1,13},{2,14},{3,15},{4,8},{5,9},{6,10},{7,11},{8,4},{9,5},... | collective-permute-start | bytes 73736 | tf_op jit(solution)/shard_map/ppermute | solution.py:156
  56.7 3.1 %collective-permute-start.24 = (bf16[8,24,384]{2,1,0:T(8,128)(2,1)S(1)}, bf16[8,24,384]{2,1,0:T(8,128)(2,1)S(1)}, u32[]{:S(2)}, u32[]{:S(2)}) collective-permute-start(bf16[8,24,384]{2,1,0:T(8,128)(2,1)S(1)} %fusion.35), channel_id=1, source_target_pairs={{0,8},{1,9},{2,10},{3,11},{4,12},{5,13},{6,14},{7,15},{8,0},{9,1},... | collective-permute-start | bytes 442376 | tf_op jit(solution)/shard_map/ppermute | solution.py:137
  59.8 1.5 %collective-permute-done.17 = f32[1,2,8,384]{3,1,2,0:T(2,128)S(1)} collective-permute-done((f32[1,2,8,384]{3,1,2,0:T(2,128)S(1)}, f32[1,2,8,384]{3,1,2,0:T(2,128)S(1)}, u32[]{:S(2)}, u32[]{:S(2)}) %collective-permute-start.17) | collective-permute-done | bytes 24608 | tf_op jit(solution)/shard_map/ppermute | solution.py:156
  62.6 1.6 %collective-permute-start.19 = (bf16[2,8,384]{2,1,0:T(8,128)(2,1)S(1)}, bf16[2,8,384]{2,1,0:T(8,128)(2,1)S(1)}, u32[]{:S(2)}, u32[]{:S(2)}) collective-permute-start(bf16[2,8,384]{2,1,0:T(8,128)(2,1)S(1)} %pad_maximum_fusion.2), channel_id=1, source_target_pairs={{0,2},{1,3},{2,0},{3,1},{4,6},{5,7},{6,4},{7,5},{8,10},{9,11},{10,... | collective-permute-start | bytes 36872 | tf_op jit(solution)/shard_map/ppermute | solution.py:144
  66.1 1.1 %copy.90 = bf16[2,2,384,384]{3,2,1,0:T(8,128)(2,1)} copy(bf16[2,2,384,384]{3,2,0,1:T(8,128)(2,1)S(1)} %pad_maximum_fusion) | data formatting | bytes 2359296
  67.9 3.1 %collective-permute-start.22 = (f32[1,2,8,384]{3,1,2,0:T(2,128)S(1)}, f32[1,2,8,384]{3,1,2,0:T(2,128)S(1)}, u32[]{:S(2)}, u32[]{:S(2)}) collective-permute-start(f32[1,2,8,384]{3,1,2,0:T(2,128)S(1)} %bitcast.264), channel_id=1, source_target_pairs={{0,8},{1,9},{2,10},{3,11},{4,12},{5,13},{6,14},{7,15},{8,0},{9,1},... | collective-permute-start | bytes 73736 | tf_op jit(solution)/shard_map/ppermute | solution.py:156
  71.0 1.3 %collective-permute-start.23 = (f32[1,2,8,384]{3,1,2,0:T(2,128)S(1)}, f32[1,2,8,384]{3,1,2,0:T(2,128)S(1)}, u32[]{:S(2)}, u32[]{:S(2)}) collective-permute-start(f32[1,2,8,384]{3,1,2,0:T(2,128)S(1)} %bitcast.262), channel_id=1, source_target_pairs={{0,12},{1,13},{2,14},{3,15},{4,8},{5,9},{6,10},{7,11},{8,4},{9,5},... | collective-permute-start | bytes 73736 | tf_op jit(solution)/shard_map/ppermute | solution.py:156
  72.5 1.5 %collective-permute-start.26 = (bf16[2,24,384]{2,1,0:T(8,128)(2,1)S(1)}, bf16[2,24,384]{2,1,0:T(8,128)(2,1)S(1)}, u32[]{:S(2)}, u32[]{:S(2)}) collective-permute-start(bf16[2,24,384]{2,1,0:T(8,128)(2,1)S(1)} %fusion.41), channel_id=1, source_target_pairs={{0,2},{1,3},{2,0},{3,1},{4,6},{5,7},{6,4},{7,5},{8,10},{9,11},{10,... | collective-permute-start | bytes 110600 | tf_op jit(solution)/shard_map/ppermute | solution.py:137
  74.0 2.6 %collective-permute-done.23 = f32[1,2,8,384]{3,1,2,0:T(2,128)S(1)} collective-permute-done((f32[1,2,8,384]{3,1,2,0:T(2,128)S(1)}, f32[1,2,8,384]{3,1,2,0:T(2,128)S(1)}, u32[]{:S(2)}, u32[]{:S(2)}) %collective-permute-start.23) | collective-permute-done | bytes 24608 | tf_op jit(solution)/shard_map/ppermute | solution.py:156
  76.8 2.5 %fusion.2 = bf16[2,1440,384]{2,1,0:T(8,128)(2,1)} fusion(f32[2,1440,384]{2,1,0:T(8,128)S(1)} %fusion.31, bf16[2,1440,384]{2,1,0:T(8,128)(2,1)S(1)} %copy-done.3, bf16[1440,8,1]{0,1,2:T(8,128)(2,1)S(1)} %copy-done.5, bf16[2,8,384]{2,0,1:T(2,128)(2,1)S(1)} %fusion.60), kind=kOutput, calls=%fused_computation.8 | convolution fusion | flops 22118400 | bytes 8882688 | tf_op jit(solution)/shard_map/jfc,kf->jkc/dot_general | solution.py:264
  (129 shorter events, 18.7 us)
Async XLA Ops:
  3.4 7.7 %collective-permute-start.1 = (f32[2,8,384]{2,1,0:T(8,128)S(1)}, f32[2,8,384]{2,1,0:T(8,128)S(1)}, u32[]{:S(2)}, u32[]{:S(2)}) collective-permute-start(f32[2,8,384]{2,1,0:T(8,128)S(1)} %bitcast.245), channel_id=1, source_target_pairs={{0,2},{1,3},{2,0},{3,1},{4,6},{5,7},{6,4},{7,5},{8,10},{9,11},{10,... | collective-permute-start | bytes 73736 | tf_op jit(solution)/shard_map/ppermute | solution.py:144
  6.4 4.8 %collective-permute-start = (f32[2,8,384]{2,1,0:T(8,128)S(1)}, f32[2,8,384]{2,1,0:T(8,128)}, u32[]{:S(2)}, u32[]{:S(2)}) collective-permute-start(f32[2,8,384]{2,1,0:T(8,128)S(1)} %bitcast.246), channel_id=1, source_target_pairs={{0,1},{1,0},{2,3},{3,2},{4,5},{5,4},{6,7},{7,6},{8,9},{9,8},{10,11... | collective-permute-start | bytes 73736 | tf_op jit(solution)/shard_map/ppermute | solution.py:144
  6.4 4.8 %collective-permute-start.2 = (f32[2,8,384]{2,1,0:T(8,128)S(1)}, f32[2,8,384]{2,1,0:T(8,128)}, u32[]{:S(2)}, u32[]{:S(2)}) collective-permute-start(f32[2,8,384]{2,1,0:T(8,128)S(1)} %bitcast.247), channel_id=1, source_target_pairs={{0,3},{1,2},{2,1},{3,0},{4,7},{5,6},{6,5},{7,4},{8,11},{9,10},{10,... | collective-permute-start | bytes 73736 | tf_op jit(solution)/shard_map/ppermute | solution.py:144
  7.4 15.8 %copy-start.2 = (bf16[2,2,384,384]{3,2,1,0:T(8,128)(2,1)S(1)}, bf16[2,2,384,384]{3,2,1,0:T(8,128)(2,1)}, u32[]{:S(2)}) copy-start(bf16[2,2,384,384]{3,2,1,0:T(8,128)(2,1)} %param.13) | copy-start | bytes 3538948
  14.2 6.4 %collective-permute-start.4 = (f32[1,2,8,384]{3,1,2,0:T(2,128)}, f32[1,2,8,384]{3,1,2,0:T(2,128)S(1)}, u32[]{:S(2)}, u32[]{:S(2)}) collective-permute-start(f32[1,2,8,384]{3,1,2,0:T(2,128)} %bitcast.230), channel_id=1, source_target_pairs={{0,8},{1,9},{2,10},{3,11},{4,12},{5,13},{6,14},{7,15},{8,0},{9,1},... | collective-permute-start | bytes 73736 | tf_op jit(solution)/shard_map/ppermute | solution.py:156
  17.3 5.8 %collective-permute-start.5 = (f32[1,2,8,384]{3,1,2,0:T(2,128)}, f32[1,2,8,384]{3,1,2,0:T(2,128)S(1)}, u32[]{:S(2)}, u32[]{:S(2)}) collective-permute-start(f32[1,2,8,384]{3,1,2,0:T(2,128)} %bitcast.235), channel_id=1, source_target_pairs={{0,12},{1,13},{2,14},{3,15},{4,8},{5,9},{6,10},{7,11},{8,4},{9,5},... | collective-permute-start | bytes 73736 | tf_op jit(solution)/shard_map/ppermute | solution.py:156
  18.6 4.5 %collective-permute-start.3 = (f32[1,2,8,384]{3,1,2,0:T(2,128)}, f32[1,2,8,384]{3,1,2,0:T(2,128)S(1)}, u32[]{:S(2)}, u32[]{:S(2)}) collective-permute-start(f32[1,2,8,384]{3,1,2,0:T(2,128)} %bitcast.231), channel_id=1, source_target_pairs={{0,4},{1,5},{2,6},{3,7},{4,0},{5,1},{6,2},{7,3},{8,12},{9,13},{10,... | collective-permute-start | bytes 73736 | tf_op jit(solution)/shard_map/ppermute | solution.py:156
  24.6 3.4 %collective-permute-start.8 = (bf16[2,8,384]{2,1,0:T(8,128)(2,1)}, bf16[2,8,384]{2,1,0:T(8,128)(2,1)S(1)}, u32[]{:S(2)}, u32[]{:S(2)}) collective-permute-start(bf16[2,8,384]{2,1,0:T(8,128)(2,1)} %pad_maximum_fusion.1), channel_id=1, source_target_pairs={{0,3},{1,2},{2,1},{3,0},{4,7},{5,6},{6,5},{7,4},{8,11},{9,10},{10,... | collective-permute-start | bytes 36872 | tf_op jit(solution)/shard_map/ppermute | solution.py:144
  24.6 3.9 %collective-permute-start.7 = (bf16[2,8,384]{2,1,0:T(8,128)(2,1)}, bf16[2,8,384]{2,1,0:T(8,128)(2,1)S(1)}, u32[]{:S(2)}, u32[]{:S(2)}) collective-permute-start(bf16[2,8,384]{2,1,0:T(8,128)(2,1)} %pad_maximum_fusion.1), channel_id=1, source_target_pairs={{0,2},{1,3},{2,0},{3,1},{4,6},{5,7},{6,4},{7,5},{8,10},{9,11},{10,... | collective-permute-start | bytes 36872 | tf_op jit(solution)/shard_map/ppermute | solution.py:144
  26.2 2.4 %collective-permute-start.6 = (bf16[2,8,384]{2,1,0:T(8,128)(2,1)}, bf16[2,8,384]{2,1,0:T(8,128)(2,1)S(1)}, u32[]{:S(2)}, u32[]{:S(2)}) collective-permute-start(bf16[2,8,384]{2,1,0:T(8,128)(2,1)} %pad_maximum_fusion.1), channel_id=1, source_target_pairs={{0,1},{1,0},{2,3},{3,2},{4,5},{5,4},{6,7},{7,6},{8,9},{9,8},{10,11... | collective-permute-start | bytes 36872 | tf_op jit(solution)/shard_map/ppermute | solution.py:144
  31.4 9.1 %collective-permute-start.10 = (f32[1,2,8,384]{3,1,2,0:T(2,128)}, f32[1,2,8,384]{3,1,2,0:T(2,128)}, u32[]{:S(2)}, u32[]{:S(2)}) collective-permute-start(f32[1,2,8,384]{3,1,2,0:T(2,128)} %bitcast.228), channel_id=1, source_target_pairs={{0,8},{1,9},{2,10},{3,11},{4,12},{5,13},{6,14},{7,15},{8,0},{9,1},... | collective-permute-start | bytes 73736 | tf_op jit(solution)/shard_map/ppermute | solution.py:156
  32.6 7.9 %collective-permute-start.11 = (f32[1,2,8,384]{3,1,2,0:T(2,128)}, f32[1,2,8,384]{3,1,2,0:T(2,128)}, u32[]{:S(2)}, u32[]{:S(2)}) collective-permute-start(f32[1,2,8,384]{3,1,2,0:T(2,128)} %bitcast.234), channel_id=1, source_target_pairs={{0,12},{1,13},{2,14},{3,15},{4,8},{5,9},{6,10},{7,11},{8,4},{9,5},... | collective-permute-start | bytes 73736 | tf_op jit(solution)/shard_map/ppermute | solution.py:156
  33.6 7.8 %copy-start.5 = (bf16[1440,8,1]{0,1,2:T(8,128)(2,1)S(1)}, bf16[1440,8,1]{0,1,2:T(8,128)(2,1)}, u32[]{:S(2)}) copy-start(bf16[1440,8,1]{0,1,2:T(8,128)(2,1)} %constant.114) | copy-start | bytes 69124
  33.6 7.0 %collective-permute-start.9 = (f32[1,2,8,384]{3,1,2,0:T(2,128)}, f32[1,2,8,384]{3,1,2,0:T(2,128)}, u32[]{:S(2)}, u32[]{:S(2)}) collective-permute-start(f32[1,2,8,384]{3,1,2,0:T(2,128)} %bitcast.229), channel_id=1, source_target_pairs={{0,4},{1,5},{2,6},{3,7},{4,0},{5,1},{6,2},{7,3},{8,12},{9,13},{10,... | collective-permute-start | bytes 73736 | tf_op jit(solution)/shard_map/ppermute | solution.py:156
  47.4 5.2 %collective-permute-start.13 = (f32[2,8,384]{2,1,0:T(8,128)S(1)}, f32[2,8,384]{2,1,0:T(8,128)S(1)}, u32[]{:S(2)}, u32[]{:S(2)}) collective-permute-start(f32[2,8,384]{2,1,0:T(8,128)S(1)} %bitcast.249), channel_id=1, source_target_pairs={{0,2},{1,3},{2,0},{3,1},{4,6},{5,7},{6,4},{7,5},{8,10},{9,11},{10,... | collective-permute-start | bytes 73736 | tf_op jit(solution)/shard_map/ppermute | solution.py:144
  48.9 3.6 %collective-permute-start.12 = (f32[2,8,384]{2,1,0:T(8,128)S(1)}, f32[2,8,384]{2,1,0:T(8,128)S(1)}, u32[]{:S(2)}, u32[]{:S(2)}) collective-permute-start(f32[2,8,384]{2,1,0:T(8,128)S(1)} %bitcast.250), channel_id=1, source_target_pairs={{0,1},{1,0},{2,3},{3,2},{4,5},{5,4},{6,7},{7,6},{8,9},{9,8},{10,11... | collective-permute-start | bytes 73736 | tf_op jit(solution)/shard_map/ppermute | solution.py:144
  48.9 3.7 %collective-permute-start.14 = (f32[2,8,384]{2,1,0:T(8,128)S(1)}, f32[2,8,384]{2,1,0:T(8,128)S(1)}, u32[]{:S(2)}, u32[]{:S(2)}) collective-permute-start(f32[2,8,384]{2,1,0:T(8,128)S(1)} %bitcast.251), channel_id=1, source_target_pairs={{0,3},{1,2},{2,1},{3,0},{4,7},{5,6},{6,5},{7,4},{8,11},{9,10},{10,... | collective-permute-start | bytes 73736 | tf_op jit(solution)/shard_map/ppermute | solution.py:144
  52.5 12.0 %copy-start.7 = (bf16[2,4,384]{2,0,1:T(2,128)(2,1)S(1)}, bf16[2,4,384]{2,0,1:T(2,128)(2,1)}, u32[]{:S(2)}) copy-start(bf16[2,4,384]{2,0,1:T(2,128)(2,1)} %copy-done.6) | copy-start | bytes 18436
  53.1 6.7 %collective-permute-start.16 = (f32[1,2,8,384]{3,1,2,0:T(2,128)S(1)}, f32[1,2,8,384]{3,1,2,0:T(2,128)S(1)}, u32[]{:S(2)}, u32[]{:S(2)}) collective-permute-start(f32[1,2,8,384]{3,1,2,0:T(2,128)S(1)} %bitcast.266), channel_id=1, source_target_pairs={{0,8},{1,9},{2,10},{3,11},{4,12},{5,13},{6,14},{7,15},{8,0},{9,1},... | collective-permute-start | bytes 73736 | tf_op jit(solution)/shard_map/ppermute | solution.py:156
  55.3 6.0 %collective-permute-start.17 = (f32[1,2,8,384]{3,1,2,0:T(2,128)S(1)}, f32[1,2,8,384]{3,1,2,0:T(2,128)S(1)}, u32[]{:S(2)}, u32[]{:S(2)}) collective-permute-start(f32[1,2,8,384]{3,1,2,0:T(2,128)S(1)} %bitcast.265), channel_id=1, source_target_pairs={{0,12},{1,13},{2,14},{3,15},{4,8},{5,9},{6,10},{7,11},{8,4},{9,5},... | collective-permute-start | bytes 73736 | tf_op jit(solution)/shard_map/ppermute | solution.py:156
  56.2 5.1 %collective-permute-start.15 = (f32[1,2,8,384]{3,1,2,0:T(2,128)S(1)}, f32[1,2,8,384]{3,1,2,0:T(2,128)S(1)}, u32[]{:S(2)}, u32[]{:S(2)}) collective-permute-start(f32[1,2,8,384]{3,1,2,0:T(2,128)S(1)} %bitcast.263), channel_id=1, source_target_pairs={{0,4},{1,5},{2,6},{3,7},{4,0},{5,1},{6,2},{7,3},{8,12},{9,13},{10,... | collective-permute-start | bytes 73736 | tf_op jit(solution)/shard_map/ppermute | solution.py:156
  56.7 10.9 %collective-permute-start.24 = (bf16[8,24,384]{2,1,0:T(8,128)(2,1)S(1)}, bf16[8,24,384]{2,1,0:T(8,128)(2,1)S(1)}, u32[]{:S(2)}, u32[]{:S(2)}) collective-permute-start(bf16[8,24,384]{2,1,0:T(8,128)(2,1)S(1)} %fusion.35), channel_id=1, source_target_pairs={{0,8},{1,9},{2,10},{3,11},{4,12},{5,13},{6,14},{7,15},{8,0},{9,1},... | collective-permute-start | bytes 442376 | tf_op jit(solution)/shard_map/ppermute | solution.py:137
  62.5 4.7 %collective-permute-start.20 = (bf16[2,8,384]{2,1,0:T(8,128)(2,1)S(1)}, bf16[2,8,384]{2,1,0:T(8,128)(2,1)S(1)}, u32[]{:S(2)}, u32[]{:S(2)}) collective-permute-start(bf16[2,8,384]{2,1,0:T(8,128)(2,1)S(1)} %pad_maximum_fusion.2), channel_id=1, source_target_pairs={{0,3},{1,2},{2,1},{3,0},{4,7},{5,6},{6,5},{7,4},{8,11},{9,10},{10,... | collective-permute-start | bytes 36872 | tf_op jit(solution)/shard_map/ppermute | solution.py:144
  62.6 4.7 %collective-permute-start.19 = (bf16[2,8,384]{2,1,0:T(8,128)(2,1)S(1)}, bf16[2,8,384]{2,1,0:T(8,128)(2,1)S(1)}, u32[]{:S(2)}, u32[]{:S(2)}) collective-permute-start(bf16[2,8,384]{2,1,0:T(8,128)(2,1)S(1)} %pad_maximum_fusion.2), channel_id=1, source_target_pairs={{0,2},{1,3},{2,0},{3,1},{4,6},{5,7},{6,4},{7,5},{8,10},{9,11},{10,... | collective-permute-start | bytes 36872 | tf_op jit(solution)/shard_map/ppermute | solution.py:144
  64.2 3.1 %collective-permute-start.18 = (bf16[2,8,384]{2,1,0:T(8,128)(2,1)S(1)}, bf16[2,8,384]{2,1,0:T(8,128)(2,1)S(1)}, u32[]{:S(2)}, u32[]{:S(2)}) collective-permute-start(bf16[2,8,384]{2,1,0:T(8,128)(2,1)S(1)} %pad_maximum_fusion.2), channel_id=1, source_target_pairs={{0,1},{1,0},{2,3},{3,2},{4,5},{5,4},{6,7},{7,6},{8,9},{9,8},{10,11... | collective-permute-start | bytes 36872 | tf_op jit(solution)/shard_map/ppermute | solution.py:144
  66.1 10.7 %copy-start.3 = (bf16[2,1440,384]{2,1,0:T(8,128)(2,1)S(1)}, bf16[2,1440,384]{2,1,0:T(8,128)(2,1)}, u32[]{:S(2)}) copy-start(bf16[2,1440,384]{2,1,0:T(8,128)(2,1)} %param.11) | copy-start | bytes 6635524
  67.7 4.8 %collective-permute-start.25 = (bf16[4,24,384]{2,1,0:T(8,128)(2,1)S(1)}, bf16[4,24,384]{2,1,0:T(8,128)(2,1)S(1)}, u32[]{:S(2)}, u32[]{:S(2)}) collective-permute-start(bf16[4,24,384]{2,1,0:T(8,128)(2,1)S(1)} %fusion.38), channel_id=1, source_target_pairs={{0,4},{1,5},{2,6},{3,7},{4,0},{5,1},{6,2},{7,3},{8,12},{9,13},{10,... | collective-permute-start | bytes 221192 | tf_op jit(solution)/shard_map/ppermute | solution.py:137
  67.9 6.1 %collective-permute-start.22 = (f32[1,2,8,384]{3,1,2,0:T(2,128)S(1)}, f32[1,2,8,384]{3,1,2,0:T(2,128)S(1)}, u32[]{:S(2)}, u32[]{:S(2)}) collective-permute-start(f32[1,2,8,384]{3,1,2,0:T(2,128)S(1)} %bitcast.264), channel_id=1, source_target_pairs={{0,8},{1,9},{2,10},{3,11},{4,12},{5,13},{6,14},{7,15},{8,0},{9,1},... | collective-permute-start | bytes 73736 | tf_op jit(solution)/shard_map/ppermute | solution.py:156
  71.0 5.6 %collective-permute-start.23 = (f32[1,2,8,384]{3,1,2,0:T(2,128)S(1)}, f32[1,2,8,384]{3,1,2,0:T(2,128)S(1)}, u32[]{:S(2)}, u32[]{:S(2)}) collective-permute-start(f32[1,2,8,384]{3,1,2,0:T(2,128)S(1)} %bitcast.262), channel_id=1, source_target_pairs={{0,12},{1,13},{2,14},{3,15},{4,8},{5,9},{6,10},{7,11},{8,4},{9,5},... | collective-permute-start | bytes 73736 | tf_op jit(solution)/shard_map/ppermute | solution.py:156
  72.3 4.3 %collective-permute-start.21 = (f32[1,2,8,384]{3,1,2,0:T(2,128)S(1)}, f32[1,2,8,384]{3,1,2,0:T(2,128)S(1)}, u32[]{:S(2)}, u32[]{:S(2)}) collective-permute-start(f32[1,2,8,384]{3,1,2,0:T(2,128)S(1)} %bitcast.261), channel_id=1, source_target_pairs={{0,4},{1,5},{2,6},{3,7},{4,0},{5,1},{6,2},{7,3},{8,12},{9,13},{10,... | collective-permute-start | bytes 73736 | tf_op jit(solution)/shard_map/ppermute | solution.py:156
  72.5 4.2 %collective-permute-start.26 = (bf16[2,24,384]{2,1,0:T(8,128)(2,1)S(1)}, bf16[2,24,384]{2,1,0:T(8,128)(2,1)S(1)}, u32[]{:S(2)}, u32[]{:S(2)}) collective-permute-start(bf16[2,24,384]{2,1,0:T(8,128)(2,1)S(1)} %fusion.41), channel_id=1, source_target_pairs={{0,2},{1,3},{2,0},{3,1},{4,6},{5,7},{6,4},{7,5},{8,10},{9,11},{10,... | collective-permute-start | bytes 110600 | tf_op jit(solution)/shard_map/ppermute | solution.py:137
  76.7 2.5 %collective-permute-start.27 = (bf16[1,24,384]{2,1,0:T(8,128)(2,1)S(1)}, bf16[1,24,384]{2,1,0:T(8,128)(2,1)S(1)}, u32[]{:S(2)}, u32[]{:S(2)}) collective-permute-start(bf16[1,24,384]{2,1,0:T(8,128)(2,1)S(1)} %dynamic-slice_convert_fusion.2), channel_id=1, source_target_pairs={{0,1},{1,0},{2,3},{3,2},{4,5},{5,4},{6,7},{7,6},{8,9},{9,8},{10,11... | collective-permute-start | bytes 55304 | tf_op jit(solution)/shard_map/ppermute | solution.py:137
  (5 other events, 20.1 us)
